TPU v7x, 32 devices: a whole 2x2x4 slice. The times are simulated.
32 devices in a mesh: row: 16 (over z, y, x), col: 2 (over core).
Axes of the slice: x: 2, y: 2, z: 4, core: 2. Of those that a mesh axis runs over, the one named last changes fastest.
Arguments:
- matrix: bfloat16 [16384, 2048], P('row', 'col'), may hold values from -6 to 6
- fill_mask: int32 [64, 16], P('row', 'col'), may hold values from 0 to 1, as said below
- col_rows: int32 [16], replicated, may hold values from 0 to 127, as said below
- inverses: bfloat16 [2, 128, 128], replicated, may hold values from -0.05 to 0.15625
Outputs:
- factor: bfloat16 [16384, 2048], P('row', 'col')
Inputs may be any that keep to these rules, and one draw needn't show every extreme that they name: `fill_mask`: each column panel's density of filled blocks is drawn for that column from 1/8 to 8/8. `col_rows`: exactly 1 entries lie in each aligned run of 8 slabs.
All inputs are finite; a program needn't handle non-finite values.
Results may differ from a plain program's by a relative error of at most 0.0035.
Values may be sent and summed in bfloat16 or wider, within the bound.
No kernel may reach another device: no remote copies, remote signals or barrier semaphores. Data moves between devices by JAX's collectives and lax.ppermute only.
A program may use at most 64 MiB of HBM per device.

v0:
```python
import jax
import jax.numpy as jnp
from jax import lax
from jax.sharding import PartitionSpec as P

RB = 256
PW = 128


def from_root(shard, axis, root):
    mine = lax.axis_index(axis) == root
    return lax.psum(jnp.where(mine, shard, jnp.zeros_like(shard)), axis)


def contract(left, right):
    return lax.dot_general(
        left, right, (((1,), (1,)), ((), ())), preferred_element_type=jnp.float32
    )


def fetch_slabs(panel_tiles, col_rows):
    row_count = lax.axis_size("row")
    row_index = lax.axis_index("row")
    col_index = lax.axis_index("col")
    slab_tiles = panel_tiles.reshape(-1, PW, PW)
    per_device = slab_tiles.shape[0]
    all_cols = col_rows.shape[0]
    col_panels = all_cols // lax.axis_size("col")
    owner_row = col_rows // per_device
    slab_place = col_rows % per_device
    per_owner = all_cols // row_count
    position = jnp.arange(all_cols, dtype=jnp.int32)
    earlier = (owner_row[None, :] == owner_row[:, None]) & (position[None, :] < position[:, None])
    slab_rank = jnp.sum(earlier.astype(jnp.int32), axis=1)
    is_owned = (owner_row == row_index).astype(jnp.int32)
    rank_match = (slab_rank[:, None] == jnp.arange(per_owner, dtype=jnp.int32)[None, :]).astype(
        jnp.int32
    ) * is_owned[:, None]
    place_match = (slab_place[:, None] == jnp.arange(per_device, dtype=jnp.int32)[None, :]).astype(
        jnp.int32
    )
    select_table = jnp.dot(rank_match.T, place_match).astype(jnp.bfloat16)
    owned_slabs = jnp.einsum(
        "qs,sij->qij", select_table, slab_tiles, preferred_element_type=jnp.float32
    ).astype(jnp.bfloat16)
    everyone = lax.all_gather(owned_slabs, "row", axis=0, tiled=True)
    wanted_owner = lax.dynamic_slice_in_dim(owner_row, col_index * col_panels, col_panels)
    wanted_rank = lax.dynamic_slice_in_dim(slab_rank, col_index * col_panels, col_panels)
    gather_slot = wanted_owner * per_owner + wanted_rank
    pick_table = (
        gather_slot[:, None] == jnp.arange(row_count * per_owner, dtype=jnp.int32)[None, :]
    ).astype(jnp.bfloat16)
    result = jnp.einsum(
        "tq,qij->tij", pick_table, everyone, preferred_element_type=jnp.float32
    ).astype(jnp.bfloat16)
    return result


def shards(matrix, fill_mask, col_rows, inverses):
    col_index = lax.axis_index("col")
    local_rows = matrix.shape[0]
    width = matrix.shape[1]
    col_panels = fill_mask.shape[1]
    rows_mask = jnp.repeat(fill_mask.astype(jnp.float32), RB, axis=0)
    first_local = (
        jnp.dot(matrix[:, :PW], jnp.triu(inverses[0]), preferred_element_type=jnp.float32)
        * rows_mask[:, 0:1]
    ).astype(jnp.bfloat16)
    first_panel = from_root(first_local, "col", 0)
    diag_first = fetch_slabs(first_panel, col_rows)
    column_sum = matrix[:, :PW].astype(jnp.float32) - contract(first_panel, diag_first[0])
    panel_update = column_sum.astype(jnp.bfloat16)
    second_local = (
        jnp.dot(panel_update, jnp.triu(inverses[1]), preferred_element_type=jnp.float32)
        * rows_mask[:, 0:1]
    ).astype(jnp.bfloat16)
    second_panel = from_root(second_local, "col", 1)
    diag_second = fetch_slabs(second_panel, col_rows)
    both_panels = jnp.concatenate((first_panel, second_panel), axis=1)
    both_diag = jnp.concatenate((diag_first, diag_second), axis=2).reshape(-1, 2 * PW)
    schur_sum = matrix.astype(jnp.float32) - contract(both_panels, both_diag)
    masked = (
        (schur_sum.reshape(local_rows, col_panels, PW) * rows_mask[:, :, None])
        .astype(jnp.bfloat16)
        .reshape(local_rows, width)
    )
    leading = jnp.where(
        col_index == 0, first_panel, jnp.where(col_index == 1, second_panel, masked[:, :PW])
    )
    return jnp.concatenate((leading, masked[:, PW:]), axis=1)


def solution(mesh):
    in_specs = (P("row", "col"), P("row", "col"), P(), P())
    out_specs = P("row", "col")
    return jax.shard_map(shards, mesh=mesh, in_specs=in_specs, out_specs=out_specs, check_vma=False)
```

profile of v0, /device:TPU:0, one launch (start us, length us, event | category | flops | bytes accessed | tf_op | source)
XLA Modules:
  0.0 149.6 jit_solution(10960983689356108654)
XLA Ops:
  6.5 0.7 convert_element_type.58
  7.3 2.0 %fusion.6 = bf16[1024,128]{0,1:T(8,128)(2,1)} fusion(f32[1024]{0:T(1024)S(1)} %bitcast.68, pred[]{:T(512)S(6)} %eq.32, bf16[1024,1024]{1,0:T(8,128)(2,1)} %param.4, bf16[2,128,128]{2,1,0:T(8,128)(2,1)} %param.7, s32[128]{0:T(128)S(1)} %iota_add_fusion), kind=kOutput, calls=%fused_computation.13 | convolution fusion | flops 33980416 | bytes 561665 | tf_op jit(solution)/shard_map/dot_general | solution.py:66
  9.4 0.7 and_select_fusion.1
  10.1 0.2 convert_reduce_fusion
  10.3 0.2 convolution_bitcast_fusion
  10.5 20.1 %all-reduce.3.cloned.1.call-done = bf16[1024,128]{0,1:T(8,128)(2,1)} async-done(((bf16[1024,128]{0,1:T(8,128)(2,1)}), bf16[1024,128]{0,1:T(8,128)(2,1)}) %all-reduce.3.cloned.1.call-update) | async-done | bytes 262160 | tf_op jit(solution)/shard_map/psum | solution.py:12
  30.7 1.1 copy.24
  31.8 0.2 fusion.47
  32.0 0.1 copy.20
  32.1 44.0 %all-gather = bf16[2048,128]{1,0:T(8,128)(2,1)S(1)} all-gather(bf16[128,128]{1,0:T(8,128)(2,1)S(1)} %bitcast.66), channel_id=2, replica_groups=mesh['row'=16,'col'=2] {'row'}, dimensions={0}, use_global_device_ids=true | all-gather | bytes 557056 | tf_op jit(solution)/shard_map/all_gather | solution.py:46
  76.1 0.4 convolution_convert_fusion.1
  76.6 2.1 %fusion.4 = bf16[1024,128]{0,1:T(8,128)(2,1)} fusion(bf16[1024,128]{0,1:T(8,128)(2,1)S(1)} %copy-done, f32[1024]{0:T(1024)S(1)} %bitcast.69, pred[]{:T(512)S(6)} %eq.33, bf16[1024,1024]{1,0:T(8,128)(2,1)} %param.4, bf16[1,128,128]{2,0,1:T(2,128)(2,1)S(1)} %slice.31, bf16[2,128,128]{2,1,0:T(8,128)(2,1)S(1)} %copy-done.2, s32[128]{0:T(128)S(1)} %iota_add_fusion), kind=kOutput, calls=%fused_computation.11 | convolution fusion | flops 67928064 | bytes 889345 | tf_op jit(solution)/shard_map/dot_general | solution.py:74
  78.7 2.9 %copy.16 = bf16[1024,1024]{0,1:T(8,128)(2,1)S(1)} copy(bf16[1024,1024]{1,0:T(8,128)(2,1)} %param.4) | data formatting | bytes 4194304 | tf_op args[0]
  81.6 11.4 %all-reduce.5.cloned.1.call-done = bf16[1024,128]{0,1:T(8,128)(2,1)} async-done(((bf16[1024,128]{0,1:T(8,128)(2,1)}), bf16[1024,128]{0,1:T(8,128)(2,1)}) %all-reduce.5.cloned.1.call-update) | async-done | bytes 262160 | tf_op jit(solution)/shard_map/psum | solution.py:12
  93.0 1.1 copy.25
  94.1 0.2 fusion.48
  94.3 0.1 copy.22
  94.4 44.0 %all-gather.1 = bf16[2048,128]{1,0:T(8,128)(2,1)S(1)} all-gather(bf16[128,128]{1,0:T(8,128)(2,1)S(1)} %bitcast.67), channel_id=3, replica_groups=mesh['row'=16,'col'=2] {'row'}, dimensions={0}, use_global_device_ids=true | all-gather | bytes 557056 | tf_op jit(solution)/shard_map/all_gather | solution.py:46
  138.4 0.4 convolution_convert_fusion
  138.9 0.1 copy.18
  139.0 0.7 fusion
  139.8 0.1 slice.33
  140.0 0.2 pad_maximum_fusion
  140.2 2.6 %copy.19 = bf16[1024,1024]{1,0:T(8,128)(2,1)} copy(bf16[1024,1024]{0,1:T(8,128)(2,1)S(1)} %pad_maximum_fusion) | data formatting | bytes 4194304 | tf_op jit(solution)/shard_map/concatenate | solution.py:90
  (17 shorter events, 0.4 us)
Async XLA Ops:
  6.5 70.0 %copy-start.2 = (bf16[2,128,128]{2,1,0:T(8,128)(2,1)S(1)}, bf16[2,128,128]{2,1,0:T(8,128)(2,1)}, u32[]{:S(2)}) copy-start(bf16[2,128,128]{2,1,0:T(8,128)(2,1)} %param.7) | copy-start | bytes 196612
  6.5 24.1 %all-reduce.3.cloned.1.call-start = ((), (), s32[]{:S(2)}) async-start(), calls=%async_computation | async-start | bytes 524288 | tf_op jit(solution)/shard_map/psum | solution.py:12
  9.4 83.7 %all-reduce.5.cloned.1.call-start = ((), (), s32[]{:S(2)}) async-start(), calls=%async_computation.1 | async-start | bytes 524288 | tf_op jit(solution)/shard_map/psum | solution.py:12
  30.7 45.9 %copy-start = (bf16[1024,128]{0,1:T(8,128)(2,1)S(1)}, bf16[1024,128]{0,1:T(8,128)(2,1)}, u32[]{:S(2)}) copy-start(bf16[1024,128]{0,1:T(8,128)(2,1)} %all-reduce.3.cloned.1.call-done) | copy-start | bytes 786436
  93.0 46.0 %copy-start.1 = (bf16[1024,128]{0,1:T(8,128)(2,1)S(1)}, bf16[1024,128]{0,1:T(8,128)(2,1)}, u32[]{:S(2)}) copy-start(bf16[1024,128]{0,1:T(8,128)(2,1)} %all-reduce.5.cloned.1.call-done) | copy-start | bytes 786436
Sparse Core Ops, SparseCore 0:
  9.7 20.9 all-reduce.2
  78.8 14.1 all-reduce.4
where the time goes:
time: 150 us
  blocking collectives  88 us (59%)
  waiting for transfers between devices  31.6 us (21%)
  between operations  13.5 us (9%)
  local copies, waits for them, and re-layouts  8.17 us (5%)
  matrix products  6.28 us (4%)
  other arithmetic  1.96 us (1%)
    all_gather x2, blocking collectives, fetch_slabs(): everyone = lax.all_gather(owned_slabs, 'row', axis=0, tiled=True)  88 us
    psum x2, waiting for transfers between devices, from_root(): return lax.psum(jnp.where(mine, shard, jnp.zeros_like(shard)), axis)  31.6 us
    unnamed x9, local copies, waits for them, and re-layouts  5.01 us
  transfers between devices with their start and end apart: 2, of which 2 were waited for; matrix products, arithmetic and copies ran while one was open for 3% of the time, Pallas kernels for 0%

commit v1 on v0

v1 whole, which is shorter than its diff:
```python
import jax
import jax.numpy as jnp
from jax import lax
from jax.sharding import PartitionSpec as P

RB = 256
PW = 128
FIRST_COL = 0
SECOND_COL = 1
MASK_ROWS = 16


def contract(left, right):
    return lax.dot_general(
        left, right, (((1,), (1,)), ((), ())), preferred_element_type=jnp.float32
    )


def lead_columns(payload):
    col_count = lax.axis_size("col")
    if col_count == 2:
        other = lax.ppermute(payload, "col", [(0, 1), (1, 0)])
        first = lax.axis_index("col") == FIRST_COL
        return jnp.where(first, payload, other), jnp.where(first, other, payload)
    gathered = lax.all_gather(payload, "col", axis=0, tiled=False)
    return gathered[FIRST_COL], gathered[SECOND_COL]


def gather_rows(piece):
    row_count = lax.axis_size("row")
    me = lax.axis_index("row")
    bits = row_count.bit_length() - 1
    if (1 << bits) != row_count:
        everyone = lax.all_gather(piece, "row", axis=0, tiled=False)
        return everyone, lambda owner: owner
    held = piece[None]
    order = list(range(bits))[::-1]
    for bit in order:
        step = 1 << bit
        perm = [(i, i ^ step) for i in range(row_count)]
        held = jnp.concatenate((held, lax.ppermute(held, "row", perm)), axis=0)

    def slot_of(owner):
        diff = jnp.bitwise_xor(owner, me)
        slot = jnp.zeros_like(diff)
        for position, bit in enumerate(order):
            slot = slot + ((diff >> bit) & 1) * (1 << position)
        return slot

    return held, slot_of


def shards(matrix, fill_mask, col_rows, inverses):
    col_index = lax.axis_index("col")
    row_index = lax.axis_index("row")
    local_rows, width = matrix.shape
    col_panels = width // PW
    block_rows = local_rows // RB
    local_slabs = local_rows // PW
    upper_first = jnp.triu(inverses[0])
    upper_second = jnp.triu(inverses[1])

    mask_f = fill_mask.astype(jnp.bfloat16)
    mask_rows = jnp.zeros((MASK_ROWS, PW), jnp.bfloat16)
    mask_rows = mask_rows.at[:block_rows].set(jnp.broadcast_to(mask_f[:, 0:1], (block_rows, PW)))
    payload = jnp.concatenate((matrix[:, :PW], mask_rows), axis=0)
    first_cols, second_cols = lead_columns(payload)

    owner_row = col_rows // local_slabs
    slab_place = col_rows % local_slabs
    owned = owner_row == row_index
    place = jnp.sum(jnp.where(owned, slab_place, 0))
    block = place // (RB // PW)
    first_slab = lax.dynamic_slice_in_dim(first_cols, place * PW, PW, 0)
    second_slab = lax.dynamic_slice_in_dim(second_cols, place * PW, PW, 0)
    first_flag = lax.dynamic_slice_in_dim(first_cols, local_rows + block, 1, 0)
    second_flag = lax.dynamic_slice_in_dim(second_cols, local_rows + block, 1, 0)
    flags = jnp.concatenate(
        (first_flag, second_flag, jnp.zeros((MASK_ROWS - 2, PW), jnp.bfloat16)), axis=0
    )
    piece = jnp.concatenate((first_slab, second_slab, flags), axis=0)
    held, slot_of = gather_rows(piece)

    wanted = col_index * col_panels + jnp.arange(col_panels, dtype=jnp.int32)
    wanted = jnp.concatenate((wanted, jnp.full((1,), SECOND_COL * col_panels, jnp.int32)))
    slots = slot_of(owner_row[wanted])
    pick = (slots[:, None] == jnp.arange(held.shape[0], dtype=jnp.int32)[None, :]).astype(
        jnp.bfloat16
    )
    picked = jnp.einsum(
        "tq,qij->tij", pick, held, preferred_element_type=jnp.float32
    ).astype(jnp.bfloat16)
    slab_first = picked[:, :PW]
    slab_second = picked[:, PW : 2 * PW]
    flag_first = picked[:, 2 * PW, 0].astype(jnp.float32)
    flag_second = picked[:, 2 * PW + 1, 0].astype(jnp.float32)

    diag_first = (
        jnp.einsum("tij,jk->tik", slab_first, upper_first, preferred_element_type=jnp.float32)
        * flag_first[:, None, None]
    ).astype(jnp.bfloat16)
    pivot = diag_first[col_panels]
    diag_update = (
        slab_second.astype(jnp.float32)
        - jnp.einsum("tij,kj->tik", diag_first, pivot, preferred_element_type=jnp.float32)
    ).astype(jnp.bfloat16)
    diag_second = (
        jnp.einsum("tij,jk->tik", diag_update, upper_second, preferred_element_type=jnp.float32)
        * flag_second[:, None, None]
    ).astype(jnp.bfloat16)

    rows_first = jnp.repeat(first_cols[local_rows : local_rows + block_rows, 0:1], RB, axis=0)
    rows_second = jnp.repeat(second_cols[local_rows : local_rows + block_rows, 0:1], RB, axis=0)
    first_panel = (
        jnp.dot(first_cols[:local_rows], upper_first, preferred_element_type=jnp.float32)
        * rows_first.astype(jnp.float32)
    ).astype(jnp.bfloat16)
    panel_update = (
        second_cols[:local_rows].astype(jnp.float32) - contract(first_panel, pivot)
    ).astype(jnp.bfloat16)
    second_panel = (
        jnp.dot(panel_update, upper_second, preferred_element_type=jnp.float32)
        * rows_second.astype(jnp.float32)
    ).astype(jnp.bfloat16)

    both_panels = jnp.concatenate((first_panel, second_panel), axis=1)
    both_diag = jnp.concatenate(
        (diag_first[:col_panels], diag_second[:col_panels]), axis=2
    ).reshape(-1, 2 * PW)
    schur_sum = matrix.astype(jnp.float32) - contract(both_panels, both_diag)
    rows_mask = jnp.repeat(fill_mask.astype(jnp.float32), RB, axis=0)
    masked = (
        (schur_sum.reshape(local_rows, col_panels, PW) * rows_mask[:, :, None])
        .astype(jnp.bfloat16)
        .reshape(local_rows, width)
    )
    leading = jnp.where(
        col_index == FIRST_COL,
        first_panel,
        jnp.where(col_index == SECOND_COL, second_panel, masked[:, :PW]),
    )
    return jnp.concatenate((leading, masked[:, PW:]), axis=1)


def solution(mesh):
    in_specs = (P("row", "col"), P("row", "col"), P(), P())
    out_specs = P("row", "col")
    return jax.shard_map(shards, mesh=mesh, in_specs=in_specs, out_specs=out_specs, check_vma=False)
```

time: 150 us -> 65.3 us (0.44)
  blocking collectives: 88 us -> 0 us
  between operations: 13.5 us -> 3.57 us
  local copies, waits for them, and re-layouts: 8.17 us -> 16.5 us
  starting transfers between devices: 0.04 us -> 7.54 us
  waiting for transfers between devices: 31.6 us -> 24.1 us
  other arithmetic: 1.96 us -> 7.68 us
    all_gather x2 -> x0, blocking collectives: 88 us -> none  [fetch_slabs(): everyone = lax.all_gather(owned_slabs, 'row', axis=0, tiled=True)]
    psum x2 -> x0, waiting for transfers between devices: 31.6 us -> none  [from_root(): return lax.psum(jnp.where(mine, shard, jnp.zeros_like(shard)), axis)]
    ppermute x0 -> x5, waiting for transfers between devices: none -> 24.1 us  [the longest x4 24.1 us: gather_rows(): held = jnp.concatenate((held, lax.ppermute(held, 'row', perm)), axis=0)]
    concatenate x1 -> x3, local copies, waits for them, and re-layouts: 0.1 us -> 8.14 us  [the longest x1 6.73 us: gather_rows(): held = jnp.concatenate((held, lax.ppermute(held, 'row', perm)), axis=0)]
    ppermute x0 -> x5, starting transfers between devices: none -> 7.54 us  [the longest x4 7.02 us: gather_rows(): held = jnp.concatenate((held, lax.ppermute(held, 'row', perm)), axis=0)]
    concatenate x1 -> x7, other arithmetic: 0.08 us -> 3.2 us  [the longest x3 2.16 us: gather_rows(): held = jnp.concatenate((held, lax.ppermute(held, 'row', perm)), axis=0)]
    unnamed x9 -> x25, local copies, waits for them, and re-layouts: 5.01 us -> 3.66 us
    dot_general x7 -> x6, matrix products: 5.55 us -> 4.54 us  [the longest x1 1.42 us: shards(): jnp.dot(panel_update, upper_second, preferred_element_type=jnp.float32)]
  transfers between devices with their start and end apart: 2 -> 5, of which waited for: 2 -> 4; matrix products, arithmetic and copies ran while one was open for 3% -> 11% of each run, Pallas kernels for 0% -> 0%
where the time goes in v1:
time: 65.3 us; the launch traced here: 64.6 us
  waiting for transfers between devices  24.1 us (37%)
  local copies, waits for them, and re-layouts  16.5 us (25%)
  other arithmetic  7.68 us (12%)
  starting transfers between devices  7.54 us (12%)
  matrix products  5.25 us (8%)
  between operations  3.57 us (5%)
    ppermute x4, waiting for transfers between devices, gather_rows(): held = jnp.concatenate((held, lax.ppermute(held, 'row', perm)), axis=0)  24.1 us
    ppermute x4, starting transfers between devices, gather_rows(): held = jnp.concatenate((held, lax.ppermute(held, 'row', perm)), axis=0)  7.02 us
    concatenate x1, local copies, waits for them, and re-layouts, gather_rows(): held = jnp.concatenate((held, lax.ppermute(held, 'row', perm)), axis=0)  6.73 us
    unnamed x25, local copies, waits for them, and re-layouts  3.66 us
    concatenate x1, local copies, waits for them, and re-layouts, shards(): return jnp.concatenate((leading, masked[:, PW:]), axis=1)  2.56 us
    concatenate x3, other arithmetic, gather_rows(): held = jnp.concatenate((held, lax.ppermute(held, 'row', perm)), axis=0)  2.16 us
    dot_general x1, matrix products, shards(): jnp.dot(panel_update, upper_second, preferred_element_type=jnp.float32)  1.42 us
    convert_element_type x1, other arithmetic, shards(): rows_mask = jnp.repeat(fill_mask.astype(jnp.float32), RB, axis=0)  1.34 us
  transfers between devices with their start and end apart: 5, of which 4 were waited for; matrix products, arithmetic and copies ran while one was open for 11% of the time, Pallas kernels for 0%

profile of v1, /device:TPU:0, one launch (start us, length us, event | category | flops | bytes accessed | tf_op | source)
XLA Modules:
  0.0 64.6 jit_solution(17599077366081319309)
XLA Ops:
  0.0 1.3 %fusion.45 = (f32[4,8]{1,0:T(4,128)}, bf16[4,8]{1,0:T(4,128)(2,1)S(1)}) fusion(s32[4,8]{1,0:T(4,128)} %param.7), kind=kLoop, calls=%fused_computation.78 | loop fusion | flops 64 | bytes 320 | tf_op jit(solution)/shard_map/convert_element_type | solution.py:131
  1.5 1.0 %slice.67 = bf16[1024,128]{1,0:T(8,128)(2,1)S(1)} slice(bf16[1024,1024]{1,0:T(8,128)(2,1)} %param.6), slice={[0:1024], [0:128]} | slice | bytes 524288 | tf_op jit(solution)/shard_map/slice | solution.py:66
  3.2 1.3 %fusion.39 = (s32[]{:T(128)}, s32[16]{0:T(128)S(1)}) fusion(s32[]{:T(128)S(6)} %axis_index.33, s32[16]{0:T(128)} %param.8), kind=kLoop, calls=%fused_computation.72 | loop fusion | flops 351 | bytes 136 | tf_op jit(solution)/shard_map/reduce_sum | solution.py:72
  8.3 3.7 %collective-permute-start.1 = (bf16[1,272,128]{2,0,1:T(2,128)(2,1)S(1)}, bf16[1,272,128]{2,0,1:T(2,128)(2,1)S(1)}, u32[]{:S(2)}, u32[]{:S(2)}) collective-permute-start(bf16[1,272,128]{2,0,1:T(2,128)(2,1)S(1)} %copy.15), channel_id=1, source_target_pairs={{0,16},{2,18},{4,20},{6,22},{8,24},{10,26},{12,28},{14,30},{16,0},... | collective-permute-start | bytes 208904 | tf_op jit(solution)/shard_map/ppermute | solution.py:41
  12.0 7.3 %collective-permute-done.1 = bf16[1,272,128]{2,0,1:T(2,128)(2,1)S(1)} collective-permute-done((bf16[1,272,128]{2,0,1:T(2,128)(2,1)S(1)}, bf16[1,272,128]{2,0,1:T(2,128)(2,1)S(1)}, u32[]{:S(2)}, u32[]{:S(2)}) %collective-permute-start.1) | collective-permute-done | bytes 69664 | tf_op jit(solution)/shard_map/ppermute | solution.py:41
  19.6 0.8 %collective-permute-start.2 = (bf16[2,272,128]{2,0,1:T(2,128)(2,1)S(1)}, bf16[2,272,128]{2,0,1:T(2,128)(2,1)S(1)}, u32[]{:S(2)}, u32[]{:S(2)}) collective-permute-start(bf16[2,272,128]{2,0,1:T(2,128)(2,1)S(1)} %pad_maximum_fusion.5), channel_id=1, source_target_pairs={{0,8},{2,10},{4,12},{6,14},{8,0},{10,2},{12,4},{14,6},{16,24},{18,... | collective-permute-start | bytes 417800 | tf_op jit(solution)/shard_map/ppermute | solution.py:41
  20.5 0.7 %gather_fusion = s32[9]{0:T(128)S(1)} fusion(s32[16]{0:T(128)S(1)} %get-tuple-element.20, s32[1024]{0:T(1024)S(1)} %pad_clamp_fusion), kind=kCustom, calls=%fused_computation | custom fusion | bytes 108 | tf_op jit(solution)/shard_map/gather | solution.py:86
  21.2 4.0 %collective-permute-done.2 = bf16[2,272,128]{2,0,1:T(2,128)(2,1)S(1)} collective-permute-done((bf16[2,272,128]{2,0,1:T(2,128)(2,1)S(1)}, bf16[2,272,128]{2,0,1:T(2,128)(2,1)S(1)}, u32[]{:S(2)}, u32[]{:S(2)}) %collective-permute-start.2) | collective-permute-done | bytes 139296 | tf_op jit(solution)/shard_map/ppermute | solution.py:41
  25.2 1.2 %pad_maximum_fusion.3 = bf16[4,272,128]{2,0,1:T(4,128)(2,1)} fusion(bf16[2,272,128]{2,0,1:T(2,128)(2,1)S(1)} %collective-permute-done.2, bf16[1,272,128]{2,0,1:T(2,128)(2,1)S(1)} %collective-permute-done.1, bf16[1,272,128]{2,0,1:T(2,128)(2,1)S(1)} %copy.15), kind=kLoop, calls=%fused_computation.24 | loop fusion | flops 835584 | bytes 557056 | tf_op jit(solution)/shard_map/concatenate | solution.py:41
  26.4 1.4 %collective-permute-start.3 = (bf16[4,272,128]{2,0,1:T(4,128)(2,1)}, bf16[4,272,128]{2,0,1:T(4,128)(2,1)S(1)}, u32[]{:S(2)}, u32[]{:S(2)}) collective-permute-start(bf16[4,272,128]{2,0,1:T(4,128)(2,1)} %pad_maximum_fusion.3), channel_id=1, source_target_pairs={{0,4},{2,6},{4,0},{6,2},{8,12},{10,14},{12,8},{14,10},{16,20},{18,... | collective-permute-start | bytes 835592 | tf_op jit(solution)/shard_map/ppermute | solution.py:41
  28.3 2.9 %copy.18 = bf16[1024,1024]{0,1:T(8,128)(2,1)S(1)} copy(bf16[1024,1024]{1,0:T(8,128)(2,1)} %param.6) | data formatting | bytes 4194304 | tf_op args[0]
  31.3 2.9 %collective-permute-done.3 = bf16[4,272,128]{2,0,1:T(4,128)(2,1)S(1)} collective-permute-done((bf16[4,272,128]{2,0,1:T(4,128)(2,1)}, bf16[4,272,128]{2,0,1:T(4,128)(2,1)S(1)}, u32[]{:S(2)}, u32[]{:S(2)}) %collective-permute-start.3) | collective-permute-done | bytes 278560 | tf_op jit(solution)/shard_map/ppermute | solution.py:41
  34.2 0.7 %pad_maximum_fusion.1 = bf16[8,272,128]{2,0,1:T(8,128)(2,1)S(1)} fusion(bf16[4,272,128]{2,0,1:T(4,128)(2,1)S(1)} %collective-permute-done.3, bf16[2,272,128]{2,0,1:T(2,128)(2,1)S(1)} %collective-permute-done.2, bf16[1,272,128]{2,0,1:T(2,128)(2,1)S(1)} %collective-permute-done.1, bf16[1,272,128]{2,0,1:T(2,128)(2,1)S(1)} %copy.15), kind=kLoop, calls=%fused_computation.13 | loop fusion | flops 2228224 | bytes 1114112 | tf_op jit(solution)/shard_map/concatenate | solution.py:41
  34.8 1.2 %collective-permute-start.4 = (bf16[8,272,128]{2,0,1:T(8,128)(2,1)S(1)}, bf16[8,272,128]{2,0,1:T(8,128)(2,1)}, u32[]{:S(2)}, u32[]{:S(2)}) collective-permute-start(bf16[8,272,128]{2,0,1:T(8,128)(2,1)S(1)} %pad_maximum_fusion.1), channel_id=1, source_target_pairs={{0,2},{2,0},{4,6},{6,4},{8,10},{10,8},{12,14},{14,12},{16,18},{18,... | collective-permute-start | bytes 1671176 | tf_op jit(solution)/shard_map/ppermute | solution.py:41
  36.1 0.6 copy.29
  36.8 1.0 %fusion.2 = bf16[1024,128]{0,1:T(8,128)(2,1)} fusion(bf16[1040,128]{1,0:T(8,128)(2,1)S(1)} %get-tuple-element.22, f32[1024]{0:T(1024)S(1)} %bitcast.56, bf16[2,128,128]{2,1,0:T(8,128)(2,1)S(1)} %copy-done.4, s32[128]{0:T(128)S(1)} %iota_add_fusion), kind=kOutput, calls=%fused_computation.9 | convolution fusion | flops 33849344 | bytes 561664 | tf_op jit(solution)/shard_map/dot_general | solution.py:115
  37.8 9.9 %collective-permute-done.4 = bf16[8,272,128]{2,0,1:T(8,128)(2,1)} collective-permute-done((bf16[8,272,128]{2,0,1:T(8,128)(2,1)S(1)}, bf16[8,272,128]{2,0,1:T(8,128)(2,1)}, u32[]{:S(2)}, u32[]{:S(2)}) %collective-permute-start.4) | collective-permute-done | bytes 557088 | tf_op jit(solution)/shard_map/ppermute | solution.py:41
  47.7 6.7 %concatenate.63 = bf16[16,272,128]{2,0,1:T(8,128)(2,1)S(1)} concatenate(bf16[1,272,128]{2,0,1:T(2,128)(2,1)S(1)} %copy.15, bf16[1,272,128]{2,0,1:T(2,128)(2,1)S(1)} %collective-permute-done.1, bf16[2,272,128]{2,0,1:T(2,128)(2,1)} %copy-done.1, bf16[4,272,128]{2,0,1:T(4,128)(2,1)} %copy-done.2, bf16[8,272,128]{2,0,1:T(8,128)(2,1)} %collective-permute-done.4), dimensions={0} | concatenate | bytes 2228224 | tf_op jit(solution)/shard_map/concatenate | solution.py:41
  54.4 1.1 %convolution_convert_fusion = bf16[9,272,128]{2,0,1:T(8,128)(2,1)S(1)} fusion(bf16[16,272,128]{2,0,1:T(8,128)(2,1)S(1)} %concatenate.63, s32[9]{0:T(128)} %multiply_add_fusion), kind=kOutput, calls=%fused_computation.4 | convolution fusion | flops 10340496 | bytes 1740836 | tf_op jit(solution)/shard_map/tq,qij->tij/dot_general | solution.py:90
  57.3 0.8 %pad_maximum_fusion.2 = bf16[8,128,256]{1,2,0:T(8,128)(2,1)} fusion(bf16[8,128,128]{1,2,0:T(8,128)(2,1)S(1)} %fusion.5, bf16[8,128,128]{1,2,0:T(8,128)(2,1)S(1)} %slice.93), kind=kLoop, calls=%fused_computation.16 | loop fusion | flops 1048576 | bytes 1048576 | tf_op jit(solution)/shard_map/concatenate | solution.py:127
  58.1 1.2 %copy.21 = bf16[8,128,256]{2,1,0:T(8,128)(2,1)S(1)} copy(bf16[8,128,256]{1,2,0:T(8,128)(2,1)} %pad_maximum_fusion.2) | data formatting | bytes 1048576 | tf_op jit(solution)/shard_map/concatenate | solution.py:127
  59.4 1.4 %fusion.3 = bf16[1024,128]{0,1:T(8,128)(2,1)S(1)} fusion(bf16[1040,128]{1,0:T(8,128)(2,1)} %copy-done.3, f32[1024]{0:T(1024)S(1)} %bitcast.57, bf16[1024,128]{0,1:T(8,128)(2,1)S(1)} %copy-done, bf16[9,128,128]{1,2,0:T(8,128)(2,1)S(1)} %fusion.1, bf16[2,128,128]{2,1,0:T(8,128)(2,1)S(1)} %copy-done.4, s32[128]{0:T(128)S(1)} %copy-done.8), kind=kOutput, calls=%fused_computation.10 | convolution fusion | flops 67796992 | bytes 856576 | tf_op jit(solution)/shard_map/dot_general | solution.py:122
  60.9 0.7 %fusion = bf16[1024,1024]{0,1:T(8,128)(2,1)S(1)} fusion(bf16[1024,1024]{0,1:T(8,128)(2,1)S(1)} %copy.18, bf16[1024,256]{1,0:T(8,128)(2,1)S(1)} %bitcast.53, f32[1024,8]{0,1:T(8,128)S(1)} %bitcast.55, bf16[1024,128]{0,1:T(8,128)(2,1)S(1)} %fusion.3, bf16[1024,128]{0,1:T(8,128)(2,1)S(1)} %copy-done), kind=kOutput, calls=%fused_computation.2 | convolution fusion | flops 542113792 | bytes 5275648 | tf_op jit(solution)/shard_map/dot_general | solution.py:14
  62.1 2.6 %copy.22 = bf16[1024,1024]{1,0:T(8,128)(2,1)} copy(bf16[1024,1024]{0,1:T(8,128)(2,1)S(1)} %pad_maximum_fusion) | data formatting | bytes 4194304 | tf_op jit(solution)/shard_map/concatenate | solution.py:142
  (53 shorter events, 4.7 us)
Async XLA Ops:
  2.6 5.1 %collective-permute-start = (bf16[1040,128]{1,0:T(8,128)(2,1)S(1)}, bf16[1040,128]{1,0:T(8,128)(2,1)S(1)}, u32[]{:S(2)}, u32[]{:S(2)}) collective-permute-start(bf16[1040,128]{1,0:T(8,128)(2,1)S(1)} %pad_maximum_fusion.4), channel_id=1, source_target_pairs={{0,1},{1,0},{2,3},{3,2},{4,5},{5,4},{6,7},{7,6},{8,9},{9,8},{10,11... | collective-permute-start | bytes 798728 | tf_op jit(solution)/shard_map/ppermute | solution.py:22
  8.0 23.2 %copy-start.3 = (bf16[1040,128]{1,0:T(8,128)(2,1)}, bf16[1040,128]{1,0:T(8,128)(2,1)S(1)}, u32[]{:S(2)}) copy-start(bf16[1040,128]{1,0:T(8,128)(2,1)S(1)} %get-tuple-element.21) | copy-start | bytes 798724
  8.3 11.0 %collective-permute-start.1 = (bf16[1,272,128]{2,0,1:T(2,128)(2,1)S(1)}, bf16[1,272,128]{2,0,1:T(2,128)(2,1)S(1)}, u32[]{:S(2)}, u32[]{:S(2)}) collective-permute-start(bf16[1,272,128]{2,0,1:T(2,128)(2,1)S(1)} %copy.15), channel_id=1, source_target_pairs={{0,16},{2,18},{4,20},{6,22},{8,24},{10,26},{12,28},{14,30},{16,0},... | collective-permute-start | bytes 208904 | tf_op jit(solution)/shard_map/ppermute | solution.py:41
  19.6 5.6 %collective-permute-start.2 = (bf16[2,272,128]{2,0,1:T(2,128)(2,1)S(1)}, bf16[2,272,128]{2,0,1:T(2,128)(2,1)S(1)}, u32[]{:S(2)}, u32[]{:S(2)}) collective-permute-start(bf16[2,272,128]{2,0,1:T(2,128)(2,1)S(1)} %pad_maximum_fusion.5), channel_id=1, source_target_pairs={{0,8},{2,10},{4,12},{6,14},{8,0},{10,2},{12,4},{14,6},{16,24},{18,... | collective-permute-start | bytes 417800 | tf_op jit(solution)/shard_map/ppermute | solution.py:41
  25.2 9.0 %copy-start.1 = (bf16[2,272,128]{2,0,1:T(2,128)(2,1)}, bf16[2,272,128]{2,0,1:T(2,128)(2,1)S(1)}, u32[]{:S(2)}) copy-start(bf16[2,272,128]{2,0,1:T(2,128)(2,1)S(1)} %collective-permute-done.2) | copy-start | bytes 417796
  26.4 7.8 %collective-permute-start.3 = (bf16[4,272,128]{2,0,1:T(4,128)(2,1)}, bf16[4,272,128]{2,0,1:T(4,128)(2,1)S(1)}, u32[]{:S(2)}, u32[]{:S(2)}) collective-permute-start(bf16[4,272,128]{2,0,1:T(4,128)(2,1)} %pad_maximum_fusion.3), channel_id=1, source_target_pairs={{0,4},{2,6},{4,0},{6,2},{8,12},{10,14},{12,8},{14,10},{16,20},{18,... | collective-permute-start | bytes 835592 | tf_op jit(solution)/shard_map/ppermute | solution.py:41
  28.3 8.5 %copy-start.4 = (bf16[2,128,128]{2,1,0:T(8,128)(2,1)S(1)}, bf16[2,128,128]{2,1,0:T(8,128)(2,1)}, u32[]{:S(2)}) copy-start(bf16[2,128,128]{2,1,0:T(8,128)(2,1)} %param.9) | copy-start | bytes 196612
  31.2 6.6 %copy-start.6 = (s32[128]{0:T(128)}, s32[128]{0:T(128)S(1)}, u32[]{:S(2)}) copy-start(s32[128]{0:T(128)S(1)} %iota_add_fusion) | copy-start | bytes 1540
  34.2 3.6 %copy-start.2 = (bf16[4,272,128]{2,0,1:T(4,128)(2,1)}, bf16[4,272,128]{2,0,1:T(4,128)(2,1)S(1)}, u32[]{:S(2)}) copy-start(bf16[4,272,128]{2,0,1:T(4,128)(2,1)S(1)} %collective-permute-done.3) | copy-start | bytes 835588
  34.8 12.8 %collective-permute-start.4 = (bf16[8,272,128]{2,0,1:T(8,128)(2,1)S(1)}, bf16[8,272,128]{2,0,1:T(8,128)(2,1)}, u32[]{:S(2)}, u32[]{:S(2)}) collective-permute-start(bf16[8,272,128]{2,0,1:T(8,128)(2,1)S(1)} %pad_maximum_fusion.1), channel_id=1, source_target_pairs={{0,2},{2,0},{4,6},{6,4},{8,10},{10,8},{12,14},{14,12},{16,18},{18,... | collective-permute-start | bytes 1671176 | tf_op jit(solution)/shard_map/ppermute | solution.py:41
  54.4 1.3 %copy-start.7 = (s32[128]{0:T(128)S(1)}, s32[128]{0:T(128)}, u32[]{:S(2)}) copy-start(s32[128]{0:T(128)} %copy-done.6) | copy-start | bytes 1540
  56.8 2.6 %copy-start = (bf16[1024,128]{0,1:T(8,128)(2,1)S(1)}, bf16[1024,128]{0,1:T(8,128)(2,1)}, u32[]{:S(2)}) copy-start(bf16[1024,128]{0,1:T(8,128)(2,1)} %fusion.2) | copy-start | bytes 786436
  56.8 2.6 %copy-start.8 = (s32[128]{0:T(128)S(1)}, s32[128]{0:T(128)}, u32[]{:S(2)}) copy-start(s32[128]{0:T(128)} %copy-done.6) | copy-start | bytes 1540
  56.8 2.6 %copy-start.9 = (f32[1,2,4,128]{3,1,2,0:T(2,128)S(1)}, f32[1,2,4,128]{3,1,2,0:T(2,128)}, u32[]{:S(2)}) copy-start(f32[1,2,4,128]{3,1,2,0:T(2,128)} %copy.29) | copy-start | bytes 12292
  57.2 3.7 %copy-start.5 = (f32[4,8]{1,0:T(4,128)S(1)}, f32[4,8]{1,0:T(4,128)}, u32[]{:S(2)}) copy-start(f32[4,8]{1,0:T(4,128)} %get-tuple-element.23) | copy-start | bytes 388

commit v2 on v1

v2 whole, which is shorter than its diff:
```python
import jax
import jax.numpy as jnp
from jax import lax
from jax.sharding import PartitionSpec as P

RB = 256
PW = 128
FIRST_COL = 0
SECOND_COL = 1
MASK_ROWS = 16


def contract(left, right):
    return lax.dot_general(
        left, right, (((1,), (1,)), ((), ())), preferred_element_type=jnp.float32
    )


def round_orders(bits):
    even = list(range(bits))[::-1]
    odd = list(even)
    for position in range(0, bits - 1, 2):
        odd[position], odd[position + 1] = odd[position + 1], odd[position]
    return even, odd


def gather_rows(piece, row_count, col_count):
    me = lax.axis_index("row")
    parity = lax.axis_index("col") % 2
    bits = row_count.bit_length() - 1
    even, odd = round_orders(bits)
    held = piece[None]
    for step in range(bits):
        perm = []
        for r in range(row_count):
            for k in range(col_count):
                bit = (even if k % 2 == 0 else odd)[step]
                perm.append((r * col_count + k, (r ^ (1 << bit)) * col_count + k))
        held = jnp.concatenate((held, lax.ppermute(held, ("row", "col"), perm)), axis=0)

    def slot_of(owner, order_parity):
        diff = jnp.bitwise_xor(owner, me)
        slot_even = jnp.zeros_like(diff)
        slot_odd = jnp.zeros_like(diff)
        for position in range(bits):
            slot_even = slot_even + ((diff >> even[position]) & 1) * (1 << position)
            slot_odd = slot_odd + ((diff >> odd[position]) & 1) * (1 << position)
        return jnp.where(order_parity == 0, slot_even, slot_odd)

    return held, slot_of, parity


def shards(matrix, fill_mask, col_rows, inverses):
    col_index = lax.axis_index("col")
    row_index = lax.axis_index("row")
    row_count = lax.axis_size("row")
    col_count = lax.axis_size("col")
    local_rows, width = matrix.shape
    col_panels = width // PW
    block_rows = local_rows // RB
    local_slabs = local_rows // PW
    upper_first = jnp.triu(inverses[0])
    upper_second = jnp.triu(inverses[1])
    mask_f = fill_mask.astype(jnp.bfloat16)

    owner_row = col_rows // local_slabs
    slab_place = col_rows % local_slabs
    place = jnp.sum(jnp.where(owner_row == row_index, slab_place, 0))
    block = place // (RB // PW)
    own_slab = lax.dynamic_slice_in_dim(matrix[:, :PW], place * PW, PW, 0)
    own_flag = lax.dynamic_slice_in_dim(mask_f[:, 0:1], block, 1, 0)
    flag_rows = jnp.zeros((MASK_ROWS, PW), jnp.bfloat16).at[0:1].set(
        jnp.broadcast_to(own_flag, (1, PW))
    )
    piece = jnp.concatenate((own_slab, flag_rows), axis=0)
    held, slot_of, parity = gather_rows(piece, row_count, col_count)

    mask_rows = jnp.zeros((MASK_ROWS, PW), jnp.bfloat16)
    mask_rows = mask_rows.at[:block_rows].set(jnp.broadcast_to(mask_f[:, 0:1], (block_rows, PW)))
    payload = jnp.concatenate((matrix[:, :PW], mask_rows), axis=0)

    def wanted_of(group):
        own = group * col_panels + jnp.arange(col_panels, dtype=jnp.int32)
        return jnp.concatenate((own, jnp.full((1,), SECOND_COL * col_panels, jnp.int32)))

    def pick(pieces, wanted, order_parity):
        slots = slot_of(owner_row[wanted], order_parity)
        return jnp.take(pieces, slots, axis=0)

    wanted = wanted_of(col_index)
    if col_count == 2:
        swap = [(0, 1), (1, 0)]
        other = lax.ppermute(payload, "col", swap)
        first = col_index == FIRST_COL
        first_cols = jnp.where(first, payload, other)
        second_cols = jnp.where(first, other, payload)
        mine = pick(held, wanted, parity)
        for_partner = pick(held, wanted_of(1 - col_index), parity)
        theirs = lax.ppermute(for_partner, "col", swap)
        pieces_first = jnp.where(first, mine, theirs)
        pieces_second = jnp.where(first, theirs, mine)
    else:
        lead = lax.all_gather(payload, "col", axis=0, tiled=False)
        first_cols, second_cols = lead[FIRST_COL], lead[SECOND_COL]
        everyone = lax.all_gather(held, "col", axis=0, tiled=False)
        pieces_first = pick(everyone[FIRST_COL], wanted, FIRST_COL % 2)
        pieces_second = pick(everyone[SECOND_COL], wanted, SECOND_COL % 2)

    slab_first = pieces_first[:, :PW]
    slab_second = pieces_second[:, :PW]
    flag_first = pieces_first[:, PW, 0].astype(jnp.float32)
    flag_second = pieces_second[:, PW, 0].astype(jnp.float32)

    diag_first = (
        jnp.einsum("tij,jk->tik", slab_first, upper_first, preferred_element_type=jnp.float32)
        * flag_first[:, None, None]
    ).astype(jnp.bfloat16)
    pivot = diag_first[col_panels]
    diag_update = (
        slab_second.astype(jnp.float32)
        - jnp.einsum("tij,kj->tik", diag_first, pivot, preferred_element_type=jnp.float32)
    ).astype(jnp.bfloat16)
    diag_second = (
        jnp.einsum("tij,jk->tik", diag_update, upper_second, preferred_element_type=jnp.float32)
        * flag_second[:, None, None]
    ).astype(jnp.bfloat16)

    rows_first = jnp.repeat(first_cols[local_rows : local_rows + block_rows, 0:1], RB, axis=0)
    rows_second = jnp.repeat(second_cols[local_rows : local_rows + block_rows, 0:1], RB, axis=0)
    first_panel = (
        jnp.dot(first_cols[:local_rows], upper_first, preferred_element_type=jnp.float32)
        * rows_first.astype(jnp.float32)
    ).astype(jnp.bfloat16)
    panel_update = (
        second_cols[:local_rows].astype(jnp.float32) - contract(first_panel, pivot)
    ).astype(jnp.bfloat16)
    second_panel = (
        jnp.dot(panel_update, upper_second, preferred_element_type=jnp.float32)
        * rows_second.astype(jnp.float32)
    ).astype(jnp.bfloat16)

    both_panels = jnp.concatenate((first_panel, second_panel), axis=1)
    both_diag_t = jnp.concatenate(
        (
            jnp.transpose(diag_first[:col_panels], (2, 0, 1)),
            jnp.transpose(diag_second[:col_panels], (2, 0, 1)),
        ),
        axis=0,
    ).reshape(2 * PW, width)
    schur_sum = matrix.astype(jnp.float32) - jnp.dot(
        both_panels, both_diag_t, preferred_element_type=jnp.float32
    )
    rows_mask = jnp.repeat(fill_mask.astype(jnp.float32), RB, axis=0)
    masked = (
        (schur_sum.reshape(local_rows, col_panels, PW) * rows_mask[:, :, None])
        .astype(jnp.bfloat16)
        .reshape(local_rows, width)
    )
    leading = jnp.where(
        col_index == FIRST_COL,
        first_panel,
        jnp.where(col_index == SECOND_COL, second_panel, masked[:, :PW]),
    )
    return jnp.concatenate((leading, masked[:, PW:]), axis=1)


def solution(mesh):
    in_specs = (P("row", "col"), P("row", "col"), P(), P())
    out_specs = P("row", "col")
    return jax.shard_map(shards, mesh=mesh, in_specs=in_specs, out_specs=out_specs, check_vma=False)
```

time: 65.3 us -> 52.6 us (0.81)
  waiting for transfers between devices: 24.1 us -> 10.5 us
  local copies, waits for them, and re-layouts: 16.5 us -> 11.9 us
  other arithmetic: 7.68 us -> 11.3 us
  starting transfers between devices: 7.54 us -> 8.96 us
    ppermute x5 -> x6, waiting for transfers between devices: 24.1 us -> 10.5 us  [the longest x4 10.4 us: gather_rows(): lax.ppermute(held, ('row', 'col'), perm)]
    concatenate x3 -> x2, local copies, waits for them, and re-layouts: 8.14 us -> 1.28 us  [the longest x1 1.24 us: shards(): jnp.concatenate((jnp.transpose(diag_first[:col_panels], (2, 0, 1)), jnp.t...]
    select_n x2 -> x4, other arithmetic: 0.28 us -> 3.72 us  [the longest x1 1.4 us: pick(): return jnp.take(pieces, slots, axis=0)]
    gather x1 -> x4, local copies, waits for them, and re-layouts: 0.66 us -> 2.78 us  [the longest x2 1.47 us: pick(): return jnp.take(pieces, slots, axis=0)]
    concatenate x5 -> x7, other arithmetic: 2.99 us -> 1.55 us  [the longest x1 0.83 us: shards(): jnp.concatenate((jnp.transpose(diag_first[:col_panels], (2, 0, 1)), jnp.t...]
    ppermute x5 -> x6, starting transfers between devices: 7.54 us -> 8.96 us  [the longest x4 8.88 us: gather_rows(): lax.ppermute(held, ('row', 'col'), perm)]
    dot_general x3 -> x1, matrix products: 2.11 us -> 0.72 us  [shards(): jnp.dot(both_panels, both_diag_t, preferred_element_type=jnp.float32)]
    gather x1 -> x4, other arithmetic: 0.01 us -> 1.2 us  [shards(): slots = slot_of(owner_row[wanted])]
  transfers between devices with their start and end apart: 5 -> 6, of which waited for: 4 -> 4; matrix products, arithmetic and copies ran while one was open for 11% -> 21% of each run, Pallas kernels for 0% -> 0%
where the time goes in v2:
time: 52.6 us; the launch traced here: 52 us
  local copies, waits for them, and re-layouts  11.9 us (23%)
  other arithmetic  11.3 us (21%)
  waiting for transfers between devices  10.5 us (20%)
  starting transfers between devices  8.96 us (17%)
  matrix products  5.79 us (11%)
  between operations  3.54 us (7%)
    ppermute x4, waiting for transfers between devices, gather_rows(): lax.ppermute(held, ('row', 'col'), perm)  10.4 us
    ppermute x4, starting transfers between devices, gather_rows(): lax.ppermute(held, ('row', 'col'), perm)  8.88 us
    unnamed x14, local copies, waits for them, and re-layouts  3.47 us
    concatenate x1, local copies, waits for them, and re-layouts, shards(): return jnp.concatenate((leading, masked[:, PW:]), axis=1)  2.56 us
    gather x2, local copies, waits for them, and re-layouts, pick(): return jnp.take(pieces, slots, axis=0)  1.47 us
    dot_general x1, matrix products, shards(): jnp.einsum('tij,jk->tik', diag_update, upper_second, preferred_element_ty...  1.45 us
    dot_general x1, matrix products, shards(): jnp.dot(panel_update, upper_second, preferred_element_type=jnp.float32)  1.42 us
    select_n x1, other arithmetic, pick(): return jnp.take(pieces, slots, axis=0)  1.4 us
  transfers between devices with their start and end apart: 6, of which 4 were waited for; matrix products, arithmetic and copies ran while one was open for 21% of the time, Pallas kernels for 0%

profile of v2, /device:TPU:0, one launch (start us, length us, event | category | flops | bytes accessed | tf_op | source)
XLA Modules:
  0.0 52.0 jit_solution(14186509637632825365)
XLA Ops:
  0.0 1.3 %fusion.42 = (s32[]{:T(128)}, s32[16]{0:T(128)S(1)}) fusion(s32[]{:T(128)S(6)} %axis_index.33, s32[16]{0:T(128)} %param.12), kind=kLoop, calls=%fused_computation.95 | loop fusion | flops 351 | bytes 136 | tf_op jit(solution)/shard_map/reduce_sum | solution.py:68
  4.6 0.8 %fusion.48 = (f32[4,8]{1,0:T(4,128)S(1)}, bf16[4,8]{1,0:T(4,128)(2,1)S(1)}) fusion(s32[4,8]{1,0:T(4,128)} %param.11), kind=kLoop, calls=%fused_computation.102 | loop fusion | flops 64 | bytes 320 | tf_op jit(solution)/shard_map/convert_element_type | solution.py:153
  6.6 1.0 %slice.85 = bf16[1024,128]{1,0:T(8,128)(2,1)S(1)} slice(bf16[1024,1024]{1,0:T(8,128)(2,1)} %param.10), slice={[0:1024], [0:128]} | slice | bytes 524288 | tf_op jit(solution)/shard_map/slice | solution.py:80
  7.7 4.1 %collective-permute-start.1 = (bf16[1,144,128]{2,1,0:T(8,128)(2,1)S(1)}, bf16[1,144,128]{2,1,0:T(8,128)(2,1)S(1)}, u32[]{:S(2)}, u32[]{:S(2)}) collective-permute-start(bf16[1,144,128]{2,1,0:T(8,128)(2,1)S(1)} %maximum_bitcast_fusion), channel_id=1, source_target_pairs={{0,16},{1,9},{2,18},{3,11},{4,20},{5,13},{6,22},{7,15},{8,24},{9,1... | collective-permute-start | bytes 110600 | tf_op jit(solution)/shard_map/ppermute | solution.py:39
  15.9 2.9 %copy.10 = bf16[1024,1024]{0,1:T(8,128)(2,1)S(1)} copy(bf16[1024,1024]{1,0:T(8,128)(2,1)} %param.10) | data formatting | bytes 4194304 | tf_op args[0]
  18.8 1.6 %collective-permute-start.2 = (bf16[2,144,128]{2,1,0:T(8,128)(2,1)S(1)}, bf16[2,144,128]{2,1,0:T(8,128)(2,1)S(1)}, u32[]{:S(2)}, u32[]{:S(2)}) collective-permute-start(bf16[2,144,128]{2,1,0:T(8,128)(2,1)S(1)} %pad_maximum_fusion.5), channel_id=1, source_target_pairs={{0,8},{1,17},{2,10},{3,19},{4,12},{5,21},{6,14},{7,23},{8,0},{9,25... | collective-permute-start | bytes 221192 | tf_op jit(solution)/shard_map/ppermute | solution.py:39
  21.0 3.0 %collective-permute-done.2 = bf16[2,144,128]{2,1,0:T(8,128)(2,1)S(1)} collective-permute-done((bf16[2,144,128]{2,1,0:T(8,128)(2,1)S(1)}, bf16[2,144,128]{2,1,0:T(8,128)(2,1)S(1)}, u32[]{:S(2)}, u32[]{:S(2)}) %collective-permute-start.2) | collective-permute-done | bytes 73760 | tf_op jit(solution)/shard_map/ppermute | solution.py:39
  24.0 1.6 %collective-permute-start.3 = (bf16[4,144,128]{2,1,0:T(8,128)(2,1)S(1)}, bf16[4,144,128]{2,1,0:T(8,128)(2,1)S(1)}, u32[]{:S(2)}, u32[]{:S(2)}) collective-permute-start(bf16[4,144,128]{2,1,0:T(8,128)(2,1)S(1)} %pad_maximum_fusion.4), channel_id=1, source_target_pairs={{0,4},{1,3},{2,6},{3,1},{4,0},{5,7},{6,2},{7,5},{8,12},{9,11},{10,... | collective-permute-start | bytes 442376 | tf_op jit(solution)/shard_map/ppermute | solution.py:39
  25.6 3.6 %collective-permute-done.3 = bf16[4,144,128]{2,1,0:T(8,128)(2,1)S(1)} collective-permute-done((bf16[4,144,128]{2,1,0:T(8,128)(2,1)S(1)}, bf16[4,144,128]{2,1,0:T(8,128)(2,1)S(1)}, u32[]{:S(2)}, u32[]{:S(2)}) %collective-permute-start.3) | collective-permute-done | bytes 147488 | tf_op jit(solution)/shard_map/ppermute | solution.py:39
  29.3 1.6 %collective-permute-start.4 = (bf16[8,144,128]{2,1,0:T(8,128)(2,1)S(1)}, bf16[8,144,128]{2,1,0:T(8,128)(2,1)S(1)}, u32[]{:S(2)}, u32[]{:S(2)}) collective-permute-start(bf16[8,144,128]{2,1,0:T(8,128)(2,1)S(1)} %pad_maximum_fusion.2), channel_id=1, source_target_pairs={{0,2},{1,5},{2,0},{3,7},{4,6},{5,1},{6,4},{7,3},{8,10},{9,13},{10,... | collective-permute-start | bytes 884744 | tf_op jit(solution)/shard_map/ppermute | solution.py:39
  30.8 1.2 %broadcast_select_fusion.5 = (bf16[1040,128]{1,0:T(8,128)(2,1)S(1)}, bf16[1040,128]{1,0:T(8,128)(2,1)S(1)}) fusion(bf16[1040,128]{1,0:T(8,128)(2,1)} %collective-permute-done, pred[]{:T(512)S(6)} %eq.21, bf16[1040]{0:T(1024)(128)(2,1)S(1)} %fusion.33, bf16[1024,128]{1,0:T(8,128)(2,1)S(1)} %slice.85), kind=kLoop, calls=%fused_computation.32 | loop fusion | flops 798720 | bytes 1062945 | tf_op jit(solution)/shard_map/jit(_where)/select_n | solution.py:95
  32.2 3.8 %collective-permute-done.4 = bf16[8,144,128]{2,1,0:T(8,128)(2,1)S(1)} collective-permute-done((bf16[8,144,128]{2,1,0:T(8,128)(2,1)S(1)}, bf16[8,144,128]{2,1,0:T(8,128)(2,1)S(1)}, u32[]{:S(2)}, u32[]{:S(2)}) %collective-permute-start.4) | collective-permute-done | bytes 294944 | tf_op jit(solution)/shard_map/ppermute | solution.py:39
  36.1 0.7 %gather_fusion.3 = bf16[9,144,128]{2,1,0:T(8,128)(2,1)S(1)} fusion(bf16[16,144,128]{2,1,0:T(8,128)(2,1)S(1)} %constant_dynamic-update-slice_fusion, s32[1024]{0:T(1024)} %pad_clamp_fusion), kind=kCustom, calls=%fused_computation.1.clone | custom fusion | bytes 663588 | tf_op jit(solution)/shard_map/jit(_take)/gather | solution.py:88
  36.8 1.4 %broadcast_select_fusion = bf16[9,144,128]{2,1,0:T(8,128)(2,1)} fusion(bf16[9,144,128]{2,1,0:T(8,128)(2,1)S(1)} %gather_fusion.3, pred[9]{0:T(512)(128)(4,1)} %get-tuple-element.32), kind=kLoop, calls=%fused_computation.21 | loop fusion | flops 165888 | bytes 663561 | tf_op jit(solution)/shard_map/jit(_take)/select_n | solution.py:88
  38.3 1.1 %fusion.2 = bf16[1024,128]{0,1:T(8,128)(2,1)S(1)} fusion(bf16[1040,128]{1,0:T(8,128)(2,1)S(1)} %get-tuple-element.38, f32[1024]{0:T(1024)S(1)} %bitcast.64, bf16[2,128,128]{2,1,0:T(8,128)(2,1)} %param.13, s32[128]{0:T(128)} %iota_add_fusion), kind=kOutput, calls=%fused_computation.11 | convolution fusion | flops 33849344 | bytes 561664 | tf_op jit(solution)/shard_map/dot_general | solution.py:131
  39.4 0.7 %gather_fusion.2 = bf16[9,144,128]{2,1,0:T(8,128)(2,1)S(1)} fusion(bf16[16,144,128]{2,1,0:T(8,128)(2,1)S(1)} %constant_dynamic-update-slice_fusion, s32[1024]{0:T(1024)} %pad_clamp_fusion.2), kind=kCustom, calls=%fused_computation.clone | custom fusion | bytes 663588 | tf_op jit(solution)/shard_map/jit(_take)/gather | solution.py:88
  40.2 1.1 %broadcast_select_fusion.2 = (bf16[9,144,128]{2,1,0:T(8,128)(2,1)S(1)}, bf16[9,144,128]{2,1,0:T(8,128)(2,1)S(1)}) fusion(bf16[9,144,128]{2,1,0:T(8,128)(2,1)} %collective-permute-done.5, pred[]{:T(512)S(6)} %eq.21, bf16[9,144,128]{2,1,0:T(8,128)(2,1)S(1)} %gather_fusion.2, pred[9]{0:T(512)(128)(4,1)} %get-tuple-element.30), kind=kLoop, calls=%fused_computation.23 | loop fusion | flops 497664 | bytes 1327114 | tf_op jit(solution)/shard_map/jit(_where)/select_n | solution.py:101
  42.0 1.1 %fusion.1 = bf16[9,128,128]{1,2,0:T(8,128)(2,1)S(1)} fusion(bf16[9,144,128]{2,1,0:T(8,128)(2,1)S(1)} %get-tuple-element.37, f32[9]{0:T(128)S(1)} %fusion.39, bf16[2,128,128]{2,1,0:T(8,128)(2,1)} %param.13, s32[128]{0:T(128)} %iota_add_fusion), kind=kOutput, calls=%fused_computation.10 | convolution fusion | flops 38076416 | bytes 623616 | tf_op jit(solution)/shard_map/tij,jk->tik/dot_general | solution.py:115
  43.2 1.4 %fusion.8 = f32[9,128,128]{1,2,0:T(8,128)S(1)} fusion(bf16[9,128,128]{1,2,0:T(8,128)(2,1)S(1)} %fusion.1, bf16[9,144,128]{2,1,0:T(8,128)(2,1)} %copy-done, bf16[2,128,128]{2,1,0:T(8,128)(2,1)} %param.13, s32[128]{0:T(128)} %iota_add_fusion), kind=kOutput, calls=%fused_computation.25 | convolution fusion | flops 75972608 | bytes 1245696 | tf_op jit(solution)/shard_map/tij,jk->tik/dot_general | solution.py:124
  44.8 0.8 %pad_maximum_fusion.1 = bf16[256,8,128]{2,0,1:T(8,128)(2,1)} fusion(bf16[128,8,128]{2,0,1:T(8,128)(2,1)S(1)} %fusion.13, bf16[128,8,128]{2,0,1:T(8,128)(2,1)S(1)} %slice_bitcast_fusion), kind=kLoop, calls=%fused_computation.16 | loop fusion | flops 1048576 | bytes 1048576 | tf_op jit(solution)/shard_map/concatenate | solution.py:143
  45.6 1.2 %copy.12 = bf16[256,8,128]{0,2,1:T(8,128)(2,1)S(1)} copy(bf16[256,8,128]{2,0,1:T(8,128)(2,1)} %pad_maximum_fusion.1) | data formatting | bytes 1048576 | tf_op jit(solution)/shard_map/concatenate | solution.py:143
  46.8 1.4 %fusion.3 = bf16[1024,128]{0,1:T(8,128)(2,1)S(1)} fusion(bf16[1040,128]{1,0:T(8,128)(2,1)} %copy-done.1, f32[1024]{0:T(1024)S(1)} %bitcast.65, bf16[1024,128]{0,1:T(8,128)(2,1)S(1)} %fusion.2, bf16[9,128,128]{1,2,0:T(8,128)(2,1)S(1)} %fusion.1, bf16[2,128,128]{2,1,0:T(8,128)(2,1)} %param.13, s32[128]{0:T(128)S(1)} %copy-done.2), kind=kOutput, calls=%fused_computation.12 | convolution fusion | flops 67796992 | bytes 856576 | tf_op jit(solution)/shard_map/dot_general | solution.py:138
  48.3 0.7 %fusion = bf16[1024,1024]{0,1:T(8,128)(2,1)S(1)} fusion(bf16[1024,1024]{0,1:T(8,128)(2,1)S(1)} %copy.10, bf16[256,1024]{0,1:T(8,128)(2,1)S(1)} %bitcast.62, f32[1024,8]{0,1:T(8,128)S(1)} %bitcast.63, bf16[1024,128]{0,1:T(8,128)(2,1)S(1)} %fusion.3, bf16[1024,128]{0,1:T(8,128)(2,1)S(1)} %fusion.2), kind=kOutput, calls=%fused_computation.5 | convolution fusion | flops 542113792 | bytes 5275648 | tf_op jit(solution)/shard_map/dot_general | solution.py:150
  49.5 2.6 %copy.13 = bf16[1024,1024]{1,0:T(8,128)(2,1)} copy(bf16[1024,1024]{0,1:T(8,128)(2,1)S(1)} %pad_maximum_fusion) | data formatting | bytes 4194304 | tf_op jit(solution)/shard_map/concatenate | solution.py:164
  (51 shorter events, 7.7 us)
Async XLA Ops:
  7.7 11.1 %collective-permute-start.1 = (bf16[1,144,128]{2,1,0:T(8,128)(2,1)S(1)}, bf16[1,144,128]{2,1,0:T(8,128)(2,1)S(1)}, u32[]{:S(2)}, u32[]{:S(2)}) collective-permute-start(bf16[1,144,128]{2,1,0:T(8,128)(2,1)S(1)} %maximum_bitcast_fusion), channel_id=1, source_target_pairs={{0,16},{1,9},{2,18},{3,11},{4,20},{5,13},{6,22},{7,15},{8,24},{9,1... | collective-permute-start | bytes 110600 | tf_op jit(solution)/shard_map/ppermute | solution.py:39
  12.0 18.8 %collective-permute-start = (bf16[1040,128]{1,0:T(8,128)(2,1)S(1)}, bf16[1040,128]{1,0:T(8,128)(2,1)}, u32[]{:S(2)}, u32[]{:S(2)}) collective-permute-start(bf16[1040,128]{1,0:T(8,128)(2,1)S(1)} %pad_maximum_fusion.3), channel_id=1, source_target_pairs={{0,1},{1,0},{2,3},{3,2},{4,5},{5,4},{6,7},{7,6},{8,9},{9,8},{10,11... | collective-permute-start | bytes 798728 | tf_op jit(solution)/shard_map/ppermute | solution.py:93
  18.8 5.2 %collective-permute-start.2 = (bf16[2,144,128]{2,1,0:T(8,128)(2,1)S(1)}, bf16[2,144,128]{2,1,0:T(8,128)(2,1)S(1)}, u32[]{:S(2)}, u32[]{:S(2)}) collective-permute-start(bf16[2,144,128]{2,1,0:T(8,128)(2,1)S(1)} %pad_maximum_fusion.5), channel_id=1, source_target_pairs={{0,8},{1,17},{2,10},{3,19},{4,12},{5,21},{6,14},{7,23},{8,0},{9,25... | collective-permute-start | bytes 221192 | tf_op jit(solution)/shard_map/ppermute | solution.py:39
  24.0 5.2 %collective-permute-start.3 = (bf16[4,144,128]{2,1,0:T(8,128)(2,1)S(1)}, bf16[4,144,128]{2,1,0:T(8,128)(2,1)S(1)}, u32[]{:S(2)}, u32[]{:S(2)}) collective-permute-start(bf16[4,144,128]{2,1,0:T(8,128)(2,1)S(1)} %pad_maximum_fusion.4), channel_id=1, source_target_pairs={{0,4},{1,3},{2,6},{3,1},{4,0},{5,7},{6,2},{7,5},{8,12},{9,11},{10,... | collective-permute-start | bytes 442376 | tf_op jit(solution)/shard_map/ppermute | solution.py:39
  29.3 6.8 %collective-permute-start.4 = (bf16[8,144,128]{2,1,0:T(8,128)(2,1)S(1)}, bf16[8,144,128]{2,1,0:T(8,128)(2,1)S(1)}, u32[]{:S(2)}, u32[]{:S(2)}) collective-permute-start(bf16[8,144,128]{2,1,0:T(8,128)(2,1)S(1)} %pad_maximum_fusion.2), channel_id=1, source_target_pairs={{0,2},{1,5},{2,0},{3,7},{4,6},{5,1},{6,4},{7,3},{8,10},{9,13},{10,... | collective-permute-start | bytes 884744 | tf_op jit(solution)/shard_map/ppermute | solution.py:39
  32.0 4.0 %copy-start.1 = (bf16[1040,128]{1,0:T(8,128)(2,1)}, bf16[1040,128]{1,0:T(8,128)(2,1)S(1)}, u32[]{:S(2)}) copy-start(bf16[1040,128]{1,0:T(8,128)(2,1)S(1)} %get-tuple-element.39) | copy-start | bytes 798724
  38.2 2.0 %collective-permute-start.5 = (bf16[9,144,128]{2,1,0:T(8,128)(2,1)}, bf16[9,144,128]{2,1,0:T(8,128)(2,1)}, u32[]{:S(2)}, u32[]{:S(2)}) collective-permute-start(bf16[9,144,128]{2,1,0:T(8,128)(2,1)} %broadcast_select_fusion), channel_id=1, source_target_pairs={{0,1},{1,0},{2,3},{3,2},{4,5},{5,4},{6,7},{7,6},{8,9},{9,8},{10,11... | collective-permute-start | bytes 995336 | tf_op jit(solution)/shard_map/ppermute | solution.py:99
  41.3 0.7 %copy-start = (bf16[9,144,128]{2,1,0:T(8,128)(2,1)}, bf16[9,144,128]{2,1,0:T(8,128)(2,1)S(1)}, u32[]{:S(2)}) copy-start(bf16[9,144,128]{2,1,0:T(8,128)(2,1)S(1)} %get-tuple-element.36) | copy-start | bytes 995332
  43.1 3.7 %copy-start.2 = (s32[128]{0:T(128)S(1)}, s32[128]{0:T(128)}, u32[]{:S(2)}) copy-start(s32[128]{0:T(128)} %iota_add_fusion) | copy-start | bytes 1540

commit v3 on v2

v3 whole, which is shorter than its diff:
```python
import jax
import jax.numpy as jnp
from jax import lax
from jax.experimental import pallas as pl
from jax.experimental.pallas import tpu as pltpu
from jax.sharding import PartitionSpec as P

RB = 256
PW = 128
FIRST_COL = 0
SECOND_COL = 1
MASK_ROWS = 16


def round_orders(bits):
    even = list(range(bits))[::-1]
    odd = list(even)
    for position in range(0, bits - 1, 2):
        odd[position], odd[position + 1] = odd[position + 1], odd[position]
    return even, odd


def gather_rows(piece, row_count, col_count):
    me = lax.axis_index("row")
    parity = lax.axis_index("col") % 2
    bits = row_count.bit_length() - 1
    even, odd = round_orders(bits)
    held = piece[None]
    for step in range(bits):
        perm = []
        for r in range(row_count):
            for k in range(col_count):
                bit = (even if k % 2 == 0 else odd)[step]
                perm.append((r * col_count + k, (r ^ (1 << bit)) * col_count + k))
        held = jnp.concatenate((held, lax.ppermute(held, ("row", "col"), perm)), axis=0)

    def slot_of(owner, order_parity):
        diff = jnp.bitwise_xor(owner, me)
        slot_even = jnp.zeros_like(diff)
        slot_odd = jnp.zeros_like(diff)
        for position in range(bits):
            slot_even = slot_even + ((diff >> even[position]) & 1) * (1 << position)
            slot_odd = slot_odd + ((diff >> odd[position]) & 1) * (1 << position)
        return jnp.where(order_parity == 0, slot_even, slot_odd)

    return held, slot_of, parity


def shards(matrix, fill_mask, col_rows, inverses):
    col_index = lax.axis_index("col")
    row_index = lax.axis_index("row")
    row_count = lax.axis_size("row")
    col_count = lax.axis_size("col")
    local_rows, width = matrix.shape
    col_panels = width // PW
    block_rows = local_rows // RB
    local_slabs = local_rows // PW
    mask_f = fill_mask.astype(jnp.bfloat16)

    owner_row = col_rows // local_slabs
    slab_place = col_rows % local_slabs
    place = jnp.sum(jnp.where(owner_row == row_index, slab_place, 0))
    block = place // (RB // PW)
    own_slab = lax.dynamic_slice_in_dim(matrix[:, :PW], place * PW, PW, 0)
    own_flag = lax.dynamic_slice_in_dim(mask_f[:, 0:1], block, 1, 0)
    flag_rows = jnp.zeros((MASK_ROWS, PW), jnp.bfloat16).at[0:1].set(
        jnp.broadcast_to(own_flag, (1, PW))
    )
    piece = jnp.concatenate((own_slab, flag_rows), axis=0)
    held, slot_of, parity = gather_rows(piece, row_count, col_count)

    mask_rows = jnp.zeros((MASK_ROWS, PW), jnp.bfloat16)
    mask_rows = mask_rows.at[:block_rows].set(jnp.broadcast_to(mask_f[:, 0:1], (block_rows, PW)))
    payload = jnp.concatenate((matrix[:, :PW], mask_rows), axis=0)

    def wanted_of(group):
        own = group * col_panels + jnp.arange(col_panels, dtype=jnp.int32)
        return jnp.concatenate((own, jnp.full((1,), SECOND_COL * col_panels, jnp.int32)))

    def pick(pieces, wanted, order_parity):
        slots = slot_of(owner_row[wanted], order_parity)
        return jnp.take(pieces, slots, axis=0)

    wanted = wanted_of(col_index)
    if col_count == 2:
        swap = [(0, 1), (1, 0)]
        cols_a = payload
        cols_b = lax.ppermute(payload, "col", swap)
        pieces_a = pick(held, wanted, parity)
        for_partner = pick(held, wanted_of(1 - col_index), parity)
        pieces_b = lax.ppermute(for_partner, "col", swap)
        order = col_index
    else:
        lead = lax.all_gather(payload, "col", axis=0, tiled=False)
        cols_a, cols_b = lead[FIRST_COL], lead[SECOND_COL]
        everyone = lax.all_gather(held, "col", axis=0, tiled=False)
        pieces_a = pick(everyone[FIRST_COL], wanted, FIRST_COL % 2)
        pieces_b = pick(everyone[SECOND_COL], wanted, SECOND_COL % 2)
        order = jnp.zeros_like(col_index)

    table = jnp.stack((order, col_index)).astype(jnp.int32)
    return factor_call(
        matrix, cols_a, cols_b, pieces_a, pieces_b, inverses, fill_mask, table
    )


def factor_kernel(
    matrix_ref, cols_a_ref, cols_b_ref, pieces_a_ref, pieces_b_ref, inv_ref, mask_ref, table_ref, out_ref
):
    local_rows, width = matrix_ref.shape
    col_panels = width // PW
    block_rows = local_rows // RB
    picks = pieces_a_ref.shape[0]
    swapped = table_ref[0] != 0
    col_index = table_ref[1]

    def dot(left, right):
        return jnp.dot(left, right, preferred_element_type=jnp.float32)

    def dot_t(left, right):
        return lax.dot_general(
            left, right, (((1,), (1,)), ((), ())), preferred_element_type=jnp.float32
        )

    upper = (
        lax.broadcasted_iota(jnp.int32, (PW, PW), 0) <= lax.broadcasted_iota(jnp.int32, (PW, PW), 1)
    )
    zero = jnp.zeros((PW, PW), jnp.bfloat16)
    upper_first = jnp.where(upper, inv_ref[0], zero)
    upper_second = jnp.where(upper, inv_ref[1], zero)

    def first_second(a_ref, b_ref, index):
        a_val, b_val = a_ref[index], b_ref[index]
        return jnp.where(swapped, b_val, a_val), jnp.where(swapped, a_val, b_val)

    diag_first, diag_second = [], []
    for t in range(picks):
        piece_first, piece_second = first_second(pieces_a_ref, pieces_b_ref, t)
        flag_first = piece_first[PW : PW + 1].astype(jnp.float32)
        diag_first.append((dot(piece_first[:PW], upper_first) * flag_first).astype(jnp.bfloat16))
    pivot = diag_first[col_panels]
    for t in range(col_panels):
        piece_first, piece_second = first_second(pieces_a_ref, pieces_b_ref, t)
        flag_second = piece_second[PW : PW + 1].astype(jnp.float32)
        update = (
            piece_second[:PW].astype(jnp.float32) - dot_t(diag_first[t], pivot)
        ).astype(jnp.bfloat16)
        diag_second.append((dot(update, upper_second) * flag_second).astype(jnp.bfloat16))
    both_diag = [
        jnp.concatenate((diag_first[t], diag_second[t]), axis=1) for t in range(col_panels)
    ]

    for b in range(block_rows):
        rows = slice(b * RB, (b + 1) * RB)
        cols_first, cols_second = first_second(cols_a_ref, cols_b_ref, rows)
        flags_first, flags_second = first_second(
            cols_a_ref, cols_b_ref, slice(local_rows + b, local_rows + b + 1)
        )
        first_panel = (dot(cols_first, upper_first) * flags_first.astype(jnp.float32)).astype(
            jnp.bfloat16
        )
        panel_update = (
            cols_second.astype(jnp.float32) - dot_t(first_panel, pivot)
        ).astype(jnp.bfloat16)
        second_panel = (
            dot(panel_update, upper_second) * flags_second.astype(jnp.float32)
        ).astype(jnp.bfloat16)
        both_panels = jnp.concatenate((first_panel, second_panel), axis=1)
        for j in range(col_panels):
            cols = slice(j * PW, (j + 1) * PW)
            schur = matrix_ref[rows, cols].astype(jnp.float32) - dot_t(both_panels, both_diag[j])
            tile = (schur * mask_ref[b, j].astype(jnp.float32)).astype(jnp.bfloat16)
            if j == 0:
                tile = jnp.where(
                    col_index == FIRST_COL,
                    first_panel,
                    jnp.where(col_index == SECOND_COL, second_panel, tile),
                )
            out_ref[rows, cols] = tile


def factor_call(matrix, cols_a, cols_b, pieces_a, pieces_b, inverses, fill_mask, table):
    local_rows, width = matrix.shape
    vmem = pl.BlockSpec(memory_space=pltpu.VMEM)
    smem = pl.BlockSpec(memory_space=pltpu.SMEM)
    flops = 2 * local_rows * width * 2 * PW + 6 * local_rows * PW * PW
    return pl.pallas_call(
        factor_kernel,
        out_shape=jax.ShapeDtypeStruct((local_rows, width), jnp.bfloat16),
        in_specs=[vmem] * 6 + [smem, smem],
        out_specs=vmem,
        cost_estimate=pl.CostEstimate(
            flops=flops, bytes_accessed=4 * local_rows * width, transcendentals=0
        ),
    )(matrix, cols_a, cols_b, pieces_a, pieces_b, inverses, fill_mask, table)


def solution(mesh):
    in_specs = (P("row", "col"), P("row", "col"), P(), P())
    out_specs = P("row", "col")
    return jax.shard_map(shards, mesh=mesh, in_specs=in_specs, out_specs=out_specs, check_vma=False)
```

time: 52.6 us -> 42.9 us (0.82)
  Pallas kernels: 0 us -> 7.31 us
  other arithmetic: 11.3 us -> 4.81 us
  local copies, waits for them, and re-layouts: 11.9 us -> 5.69 us
  matrix products: 5.79 us -> 0 us
  starting transfers between devices: 8.96 us -> 9.98 us
  waiting for transfers between devices: 10.5 us -> 11.4 us
    pallas_call x0 -> x1, Pallas kernels: none -> 7.31 us  [factor_call(): pl.pallas_call(factor_kernel, out_shape=jax.ShapeDtypeStruct((local_rows,...]
    dot_general x5 -> x0, matrix products: 5.79 us -> none  [the longest x1 1.45 us: shards(): jnp.einsum('tij,jk->tik', diag_update, upper_second, preferred_element_ty...]
    concatenate x2 -> x0, local copies, waits for them, and re-layouts: 3.81 us -> none  [the longest x1 2.56 us: shards(): return jnp.concatenate((leading, masked[:, PW:]), axis=1)]
    select_n x3 -> x0, other arithmetic: 2.32 us -> none  [the longest x1 1.16 us: shards(): first_cols = jnp.where(first, payload, other)]
    unnamed x14 -> x9, local copies, waits for them, and re-layouts: 3.47 us -> 1.49 us
    gather x2, other arithmetic: 1.19 us -> 0.01 us
    and x2 -> x1, other arithmetic: 1.05 us -> 0.02 us  [pick(): return jnp.take(pieces, slots, axis=0)]
    concatenate x2 -> x0, other arithmetic: 1 us -> none  [the longest x1 0.83 us: shards(): jnp.concatenate((jnp.transpose(diag_first[:col_panels], (2, 0, 1)), jnp.t...]
  transfers between devices with their start and end apart: 6 -> 6, of which waited for: 4 -> 3; matrix products, arithmetic and copies ran while one was open for 21% -> 11% of each run, Pallas kernels for 0% -> 0%
where the time goes in v3:
time: 42.9 us; the launch traced here: 42.6 us
  waiting for transfers between devices  11.4 us (27%)
  starting transfers between devices  9.98 us (23%)
  Pallas kernels  7.31 us (17%)
  local copies, waits for them, and re-layouts  5.69 us (13%)
  other arithmetic  4.81 us (11%)
  between operations  3.45 us (8%)
    ppermute x4, waiting for transfers between devices, gather_rows(): lax.ppermute(held, ('row', 'col'), perm)  11.4 us
    ppermute x4, starting transfers between devices, gather_rows(): lax.ppermute(held, ('row', 'col'), perm)  9.84 us
    pallas_call x1, Pallas kernels, factor_call(): pl.pallas_call(factor_kernel, out_shape=jax.ShapeDtypeStruct((local_rows,...  7.31 us
    unnamed x9, local copies, waits for them, and re-layouts  1.49 us
    gather x2, local copies, waits for them, and re-layouts, pick(): slots = slot_of(owner_row[wanted], order_parity)  1.32 us
    reduce_sum x1, other arithmetic, shards(): place = jnp.sum(jnp.where(owner_row == row_index, slab_place, 0))  1.3 us
    gather x2, local copies, waits for them, and re-layouts, pick(): return jnp.take(pieces, slots, axis=0)  1.22 us
    slice x1, local copies, waits for them, and re-layouts, shards(): payload = jnp.concatenate((matrix[:, :PW], mask_rows), axis=0)  0.97 us
  transfers between devices with their start and end apart: 6, of which 3 were waited for; matrix products, arithmetic and copies ran while one was open for 11% of the time, Pallas kernels for 0%

profile of v3, /device:TPU:0, one launch (start us, length us, event | category | flops | bytes accessed | tf_op | source)
XLA Modules:
  0.0 42.6 jit_solution(6078518320942564784)
XLA Ops:
  0.0 1.3 %fusion.3 = (s32[]{:T(128)}, s32[16]{0:T(128)S(1)}) fusion(s32[]{:T(128)S(6)} %axis_index.15, s32[16]{0:T(128)} %param.12), kind=kLoop, calls=%fused_computation.46 | loop fusion | flops 351 | bytes 136 | tf_op jit(solution)/shard_map/reduce_sum | solution.py:62
  3.9 0.7 %convert_element_type.3 = bf16[4,8]{1,0:T(4,128)(2,1)S(1)} convert(s32[4,8]{1,0:T(4,128)} %mask_ref.1) | non-fusion elementwise | flops 32 | bytes 192 | tf_op jit(solution)/shard_map/convert_element_type | solution.py:58
  4.6 0.1 fusion.4
  5.4 0.5 %constant_dynamic-slice_fusion = bf16[1,1]{1,0:T(2,128)(2,1)} fusion(bf16[4,1]{1,0:T(4,128)(2,1)S(1)} %get-tuple-element.36, s32[]{:T(128)S(6)} %select_n.76), kind=kLoop, calls=%fused_computation.44 | loop fusion | bytes 8 | tf_op jit(solution)/shard_map/dynamic_slice | solution.py:65
  5.9 0.7 %compare_select_fusion.4 = bf16[144]{0:T(256)(128)(2,1)S(1)} fusion(bf16[1]{0:T(256)(128)(2,1)} %bitcast.2), kind=kLoop, calls=%fused_computation.26 | loop fusion | flops 288 | bytes 290 | tf_op jit(solution)/shard_map/concatenate | solution.py:69
  6.5 1.0 %slice.40 = bf16[1024,128]{1,0:T(8,128)(2,1)S(1)} slice(bf16[1024,1024]{1,0:T(8,128)(2,1)} %matrix_ref.1), slice={[0:1024], [0:128]} | slice | bytes 524288 | tf_op jit(solution)/shard_map/slice | solution.py:74
  7.6 4.1 %collective-permute-start.1 = (bf16[1,144,128]{2,1,0:T(8,128)(2,1)S(1)}, bf16[1,144,128]{2,1,0:T(8,128)(2,1)S(1)}, u32[]{:S(2)}, u32[]{:S(2)}) collective-permute-start(bf16[1,144,128]{2,1,0:T(8,128)(2,1)S(1)} %maximum_bitcast_fusion), channel_id=1, source_target_pairs={{0,16},{1,9},{2,18},{3,11},{4,20},{5,13},{6,22},{7,15},{8,24},{9,1... | collective-permute-start | bytes 110600 | tf_op jit(solution)/shard_map/ppermute | solution.py:35
  11.7 0.2 pad_maximum_fusion.1.cols_a_ref
  12.3 0.7 %gather_fusion = s32[9]{0:T(128)S(1)} fusion(s32[16]{0:T(128)S(1)} %get-tuple-element.35, s32[1024]{0:T(1024)S(1)} %pad_clamp_fusion.3), kind=kCustom, calls=%fused_computation.2 | custom fusion | bytes 108 | tf_op jit(solution)/shard_map/gather | solution.py:81
  13.0 0.7 %gather_fusion.1 = s32[9]{0:T(128)S(1)} fusion(s32[16]{0:T(128)S(1)} %get-tuple-element.35, s32[1024]{0:T(1024)S(1)} %pad_clamp_fusion.1), kind=kCustom, calls=%fused_computation.3 | custom fusion | bytes 108 | tf_op jit(solution)/shard_map/gather | solution.py:81
  13.7 2.0 %collective-permute-start.2 = (bf16[2,144,128]{2,1,0:T(8,128)(2,1)S(1)}, bf16[2,144,128]{2,1,0:T(8,128)(2,1)S(1)}, u32[]{:S(2)}, u32[]{:S(2)}) collective-permute-start(bf16[2,144,128]{2,1,0:T(8,128)(2,1)S(1)} %pad_maximum_fusion.3), channel_id=1, source_target_pairs={{0,8},{1,17},{2,10},{3,19},{4,12},{5,21},{6,14},{7,23},{8,0},{9,25... | collective-permute-start | bytes 221192 | tf_op jit(solution)/shard_map/ppermute | solution.py:35
  15.7 3.2 %collective-permute-done.2 = bf16[2,144,128]{2,1,0:T(8,128)(2,1)S(1)} collective-permute-done((bf16[2,144,128]{2,1,0:T(8,128)(2,1)S(1)}, bf16[2,144,128]{2,1,0:T(8,128)(2,1)S(1)}, u32[]{:S(2)}, u32[]{:S(2)}) %collective-permute-start.2) | collective-permute-done | bytes 73760 | tf_op jit(solution)/shard_map/ppermute | solution.py:35
  18.9 1.9 %collective-permute-start.3 = (bf16[4,144,128]{2,1,0:T(8,128)(2,1)S(1)}, bf16[4,144,128]{2,1,0:T(8,128)(2,1)S(1)}, u32[]{:S(2)}, u32[]{:S(2)}) collective-permute-start(bf16[4,144,128]{2,1,0:T(8,128)(2,1)S(1)} %pad_maximum_fusion.2), channel_id=1, source_target_pairs={{0,4},{1,3},{2,6},{3,1},{4,0},{5,7},{6,2},{7,5},{8,12},{9,11},{10,... | collective-permute-start | bytes 442376 | tf_op jit(solution)/shard_map/ppermute | solution.py:35
  20.8 3.3 %collective-permute-done.3 = bf16[4,144,128]{2,1,0:T(8,128)(2,1)S(1)} collective-permute-done((bf16[4,144,128]{2,1,0:T(8,128)(2,1)S(1)}, bf16[4,144,128]{2,1,0:T(8,128)(2,1)S(1)}, u32[]{:S(2)}, u32[]{:S(2)}) %collective-permute-start.3) | collective-permute-done | bytes 147488 | tf_op jit(solution)/shard_map/ppermute | solution.py:35
  24.2 1.9 %collective-permute-start.4 = (bf16[8,144,128]{2,1,0:T(8,128)(2,1)S(1)}, bf16[8,144,128]{2,1,0:T(8,128)(2,1)S(1)}, u32[]{:S(2)}, u32[]{:S(2)}) collective-permute-start(bf16[8,144,128]{2,1,0:T(8,128)(2,1)S(1)} %pad_maximum_fusion), channel_id=1, source_target_pairs={{0,2},{1,5},{2,0},{3,7},{4,6},{5,1},{6,4},{7,3},{8,10},{9,13},{10,... | collective-permute-start | bytes 884744 | tf_op jit(solution)/shard_map/ppermute | solution.py:35
  26.1 4.9 %collective-permute-done.4 = bf16[8,144,128]{2,1,0:T(8,128)(2,1)S(1)} collective-permute-done((bf16[8,144,128]{2,1,0:T(8,128)(2,1)S(1)}, bf16[8,144,128]{2,1,0:T(8,128)(2,1)S(1)}, u32[]{:S(2)}, u32[]{:S(2)}) %collective-permute-start.4) | collective-permute-done | bytes 294944 | tf_op jit(solution)/shard_map/ppermute | solution.py:35
  31.0 0.6 %gather_fusion.3 = bf16[9,144,128]{2,1,0:T(8,128)(2,1)S(1)} fusion(bf16[16,144,128]{2,1,0:T(8,128)(2,1)S(1)} %constant_dynamic-update-slice_fusion, s32[1024]{0:T(1024)S(1)} %pad_clamp_fusion), kind=kCustom, calls=%fused_computation.1.clone | custom fusion | bytes 663588 | tf_op jit(solution)/shard_map/jit(_take)/gather | solution.py:82
  31.6 0.1 broadcast_select_fusion
  31.8 0.6 %pad_add_fusion.2.table_ref = s32[2]{0:T(128)} fusion(s32[1]{0:T(128)} %bitcast.6), kind=kLoop, calls=%fused_computation.41 | loop fusion | flops 2 | bytes 12 | tf_op jit(solution)/shard_map/stack | solution.py:101
  32.4 0.6 %gather_fusion.2 = bf16[9,144,128]{2,1,0:T(8,128)(2,1)S(1)} fusion(bf16[16,144,128]{2,1,0:T(8,128)(2,1)S(1)} %constant_dynamic-update-slice_fusion, s32[1024]{0:T(1024)S(1)} %pad_clamp_fusion.2), kind=kCustom, calls=%fused_computation.clone | custom fusion | bytes 663588 | tf_op jit(solution)/shard_map/jit(_take)/gather | solution.py:82
  33.0 0.8 %broadcast_select_fusion.1.pieces_a_ref = bf16[9,144,128]{2,1,0:T(8,128)(2,1)} fusion(bf16[9,144,128]{2,1,0:T(8,128)(2,1)S(1)} %gather_fusion.2, pred[9]{0:T(512)(128)(4,1)S(1)} %get-tuple-element.38), kind=kLoop, calls=%fused_computation.5 | loop fusion | flops 165888 | bytes 663561 | tf_op jit(solution)/shard_map/jit(_take)/select_n | solution.py:82
  33.9 0.7 %copy-done.2 = bf16[1040,128]{1,0:T(8,128)(2,1)} copy-done((bf16[1040,128]{1,0:T(8,128)(2,1)}, bf16[1040,128]{1,0:T(8,128)(2,1)S(1)}, u32[]{:S(2)}) %copy-start.2) | copy-done | bytes 266264
  34.6 0.7 %copy-done.1 = bf16[9,144,128]{2,1,0:T(8,128)(2,1)} copy-done((bf16[9,144,128]{2,1,0:T(8,128)(2,1)}, bf16[9,144,128]{2,1,0:T(8,128)(2,1)S(1)}, u32[]{:S(2)}) %copy-start.1) | copy-done | bytes 331800
  35.3 7.3 %shard_map.46 = bf16[1024,1024]{1,0:T(8,128)(2,1)} custom-call(bf16[1024,1024]{1,0:T(8,128)(2,1)} %matrix_ref.1, bf16[1040,128]{1,0:T(8,128)(2,1)} %copy-done, bf16[1040,128]{1,0:T(8,128)(2,1)} %copy-done.2, bf16[9,144,128]{2,1,0:T(8,128)(2,1)} %broadcast_select_fusion.1.pieces_a_ref, bf16[9,144,128]{2,1,0:T(8,128)(2,1)} %copy-done.1, ...), custom_call_target="tpu_custom_call" | custom-call | flops 637534208 | bytes 4194304 | tf_op jit(solution)/shard_map/pallas_call | solution.py:187
  (29 shorter events, 0.7 us)
Async XLA Ops:
  7.6 6.0 %collective-permute-start.1 = (bf16[1,144,128]{2,1,0:T(8,128)(2,1)S(1)}, bf16[1,144,128]{2,1,0:T(8,128)(2,1)S(1)}, u32[]{:S(2)}, u32[]{:S(2)}) collective-permute-start(bf16[1,144,128]{2,1,0:T(8,128)(2,1)S(1)} %maximum_bitcast_fusion), channel_id=1, source_target_pairs={{0,16},{1,9},{2,18},{3,11},{4,20},{5,13},{6,22},{7,15},{8,24},{9,1... | collective-permute-start | bytes 110600 | tf_op jit(solution)/shard_map/ppermute | solution.py:35
  12.0 19.8 %copy-start = (bf16[1040,128]{1,0:T(8,128)(2,1)}, bf16[1040,128]{1,0:T(8,128)(2,1)S(1)}, u32[]{:S(2)}) copy-start(bf16[1040,128]{1,0:T(8,128)(2,1)S(1)} %pad_maximum_fusion.1.cols_a_ref) | copy-start | bytes 798724
  12.0 21.9 %collective-permute-start = (bf16[1040,128]{1,0:T(8,128)(2,1)S(1)}, bf16[1040,128]{1,0:T(8,128)(2,1)S(1)}, u32[]{:S(2)}, u32[]{:S(2)}) collective-permute-start(bf16[1040,128]{1,0:T(8,128)(2,1)S(1)} %pad_maximum_fusion.1.cols_a_ref), channel_id=1, source_target_pairs={{0,1},{1,0},{2,3},{3,2},{4,5},{5,4},{6,7},{7,6},{8,9},{9,8},{10,11... | collective-permute-start | bytes 798728 | tf_op jit(solution)/shard_map/ppermute | solution.py:88
  13.7 5.2 %collective-permute-start.2 = (bf16[2,144,128]{2,1,0:T(8,128)(2,1)S(1)}, bf16[2,144,128]{2,1,0:T(8,128)(2,1)S(1)}, u32[]{:S(2)}, u32[]{:S(2)}) collective-permute-start(bf16[2,144,128]{2,1,0:T(8,128)(2,1)S(1)} %pad_maximum_fusion.3), channel_id=1, source_target_pairs={{0,8},{1,17},{2,10},{3,19},{4,12},{5,21},{6,14},{7,23},{8,0},{9,25... | collective-permute-start | bytes 221192 | tf_op jit(solution)/shard_map/ppermute | solution.py:35
  18.9 5.2 %collective-permute-start.3 = (bf16[4,144,128]{2,1,0:T(8,128)(2,1)S(1)}, bf16[4,144,128]{2,1,0:T(8,128)(2,1)S(1)}, u32[]{:S(2)}, u32[]{:S(2)}) collective-permute-start(bf16[4,144,128]{2,1,0:T(8,128)(2,1)S(1)} %pad_maximum_fusion.2), channel_id=1, source_target_pairs={{0,4},{1,3},{2,6},{3,1},{4,0},{5,7},{6,2},{7,5},{8,12},{9,11},{10,... | collective-permute-start | bytes 442376 | tf_op jit(solution)/shard_map/ppermute | solution.py:35
  24.2 6.8 %collective-permute-start.4 = (bf16[8,144,128]{2,1,0:T(8,128)(2,1)S(1)}, bf16[8,144,128]{2,1,0:T(8,128)(2,1)S(1)}, u32[]{:S(2)}, u32[]{:S(2)}) collective-permute-start(bf16[8,144,128]{2,1,0:T(8,128)(2,1)S(1)} %pad_maximum_fusion), channel_id=1, source_target_pairs={{0,2},{1,5},{2,0},{3,7},{4,6},{5,1},{6,4},{7,3},{8,10},{9,13},{10,... | collective-permute-start | bytes 884744 | tf_op jit(solution)/shard_map/ppermute | solution.py:35
  31.7 2.1 %collective-permute-start.5 = (bf16[9,144,128]{2,1,0:T(8,128)(2,1)S(1)}, bf16[9,144,128]{2,1,0:T(8,128)(2,1)S(1)}, u32[]{:S(2)}, u32[]{:S(2)}) collective-permute-start(bf16[9,144,128]{2,1,0:T(8,128)(2,1)S(1)} %broadcast_select_fusion), channel_id=1, source_target_pairs={{0,1},{1,0},{2,3},{3,2},{4,5},{5,4},{6,7},{7,6},{8,9},{9,8},{10,11... | collective-permute-start | bytes 995336 | tf_op jit(solution)/shard_map/ppermute | solution.py:91
  33.9 0.7 %copy-start.2 = (bf16[1040,128]{1,0:T(8,128)(2,1)}, bf16[1040,128]{1,0:T(8,128)(2,1)S(1)}, u32[]{:S(2)}) copy-start(bf16[1040,128]{1,0:T(8,128)(2,1)S(1)} %collective-permute-done.cols_b_ref) | copy-start | bytes 798724
  34.6 0.7 %copy-start.1 = (bf16[9,144,128]{2,1,0:T(8,128)(2,1)}, bf16[9,144,128]{2,1,0:T(8,128)(2,1)S(1)}, u32[]{:S(2)}) copy-start(bf16[9,144,128]{2,1,0:T(8,128)(2,1)S(1)} %collective-permute-done.5.pieces_b_ref) | copy-start | bytes 995332

commit v4 on v3

--- a/solution.py
+++ b/solution.py
@@ -58,14 +58,24 @@
     mask_f = fill_mask.astype(jnp.bfloat16)
 
     owner_row = col_rows // local_slabs
-    slab_place = col_rows % local_slabs
-    place = jnp.sum(jnp.where(owner_row == row_index, slab_place, 0))
-    block = place // (RB // PW)
-    own_slab = lax.dynamic_slice_in_dim(matrix[:, :PW], place * PW, PW, 0)
-    own_flag = lax.dynamic_slice_in_dim(mask_f[:, 0:1], block, 1, 0)
-    flag_rows = jnp.zeros((MASK_ROWS, PW), jnp.bfloat16).at[0:1].set(
-        jnp.broadcast_to(own_flag, (1, PW))
+    local_ids = row_index * local_slabs + jnp.arange(local_slabs, dtype=jnp.int32)
+    choose = jnp.sum((col_rows[None, :] == local_ids[:, None]).astype(jnp.int32), axis=1)
+    choose_f = choose.astype(jnp.bfloat16)
+    own_slab = jnp.einsum(
+        "s,sij->ij",
+        choose_f,
+        matrix[:, :PW].reshape(local_slabs, PW, PW),
+        preferred_element_type=jnp.float32,
+    ).astype(jnp.bfloat16)
+    slab_mask = jnp.repeat(fill_mask[:, 0], RB // PW).astype(jnp.bfloat16)
+    flag_block = jnp.where(
+        lax.broadcasted_iota(jnp.int32, (local_slabs, MASK_ROWS, PW), 1) == 0,
+        slab_mask[:, None, None],
+        jnp.bfloat16(0),
     )
+    flag_rows = jnp.einsum(
+        "s,sij->ij", choose_f, flag_block, preferred_element_type=jnp.float32
+    ).astype(jnp.bfloat16)
     piece = jnp.concatenate((own_slab, flag_rows), axis=0)
     held, slot_of, parity = gather_rows(piece, row_count, col_count)
 

time: 42.9 us -> 39.1 us (0.911)
  between operations: 3.45 us -> 0.17 us
  waiting for transfers between devices: 11.4 us -> 12.4 us
  starting transfers between devices: 9.98 us -> 9.03 us
  other arithmetic: 4.81 us -> 4.3 us
    ppermute x4, waiting for transfers between devices: 11.4 us -> 12.4 us  [gather_rows(): lax.ppermute(held, ('row', 'col'), perm)]
    ppermute x4, starting transfers between devices: 9.84 us -> 8.89 us  [gather_rows(): lax.ppermute(held, ('row', 'col'), perm)]
    select_n x0 -> x2, other arithmetic: none -> 0.76 us  [the longest x1 0.68 us: shards(): owner_row = col_rows // local_slabs]
    concatenate x1 -> x0, other arithmetic: 0.65 us -> none  [shards(): piece = jnp.concatenate((own_slab, flag_rows), axis=0)]
    dynamic_slice x2 -> x0, local copies, waits for them, and re-layouts: 0.53 us -> none  [the longest x1 0.52 us: shards(): own_flag = lax.dynamic_slice_in_dim(mask_f[:, 0:1], block, 1, 0)]
    reduce_sum x1, other arithmetic: 1.3 us -> 0.84 us  [shards(): jnp.sum((col_rows[None, :] == local_ids[:, None]).astype(jnp.int32), axis=1)]
  transfers between devices with their start and end apart: 6 -> 6, of which waited for: 3 -> 3; matrix products, arithmetic and copies ran while one was open for 11% -> 14% of each run, Pallas kernels for 0% -> 0%
where the time goes in v4:
time: 39.1 us; the launch traced here: 38.9 us
  waiting for transfers between devices  12.4 us (32%)
  starting transfers between devices  9.03 us (23%)
  Pallas kernels  7.31 us (19%)
  local copies, waits for them, and re-layouts  5.31 us (14%)
  other arithmetic  4.3 us (11%)
    ppermute x4, waiting for transfers between devices, gather_rows(): lax.ppermute(held, ('row', 'col'), perm)  12.4 us
    ppermute x4, starting transfers between devices, gather_rows(): lax.ppermute(held, ('row', 'col'), perm)  8.89 us
    pallas_call x1, Pallas kernels, factor_call(): pl.pallas_call(factor_kernel, out_shape=jax.ShapeDtypeStruct((local_rows,...  7.31 us
    unnamed x9, local copies, waits for them, and re-layouts  1.48 us
    gather x2, local copies, waits for them, and re-layouts, pick(): slots = slot_of(owner_row[wanted], order_parity)  1.32 us
    gather x2, local copies, waits for them, and re-layouts, pick(): return jnp.take(pieces, slots, axis=0)  1.22 us
    slice x1, local copies, waits for them, and re-layouts, shards(): payload = jnp.concatenate((matrix[:, :PW], mask_rows), axis=0)  0.97 us
    select_n x2, other arithmetic, pick(): return jnp.take(pieces, slots, axis=0)  0.91 us
  transfers between devices with their start and end apart: 6, of which 3 were waited for; matrix products, arithmetic and copies ran while one was open for 14% of the time, Pallas kernels for 0%

profile of v4, /device:TPU:0, one launch (start us, length us, event | category | flops | bytes accessed | tf_op | source)
XLA Modules:
  0.0 38.9 jit_solution(15582424753965746869)
XLA Ops:
  0.0 0.7 %convert_element_type.25 = bf16[4,8]{1,0:T(4,128)(2,1)S(1)} convert(s32[4,8]{1,0:T(4,128)} %mask_ref.1) | non-fusion elementwise | flops 32 | bytes 192 | tf_op jit(solution)/shard_map/convert_element_type | solution.py:58
  0.7 0.1 slice_reduce_fusion
  1.0 0.8 %convert_reduce_fusion = s32[8]{0:T(128)S(1)} fusion(s32[16]{0:T(128)} %param.10, s32[8]{0:T(128)S(1)} %iota_add_fusion), kind=kLoop, calls=%fused_computation.27 | loop fusion | flops 376 | bytes 128 | tf_op jit(solution)/shard_map/reduce_sum | solution.py:62
  1.9 0.1 fusion.2
  2.0 1.0 %slice.25 = bf16[1024,128]{1,0:T(8,128)(2,1)S(1)} slice(bf16[1024,1024]{1,0:T(8,128)(2,1)} %matrix_ref.1), slice={[0:1024], [0:128]} | slice | bytes 524288 | tf_op jit(solution)/shard_map/slice | solution.py:84
  3.0 0.3 fusion
  3.3 4.1 %collective-permute-start.1 = (bf16[1,144,128]{2,1,0:T(8,128)(2,1)S(1)}, bf16[1,144,128]{2,1,0:T(8,128)(2,1)S(1)}, u32[]{:S(2)}, u32[]{:S(2)}) collective-permute-start(bf16[1,144,128]{2,1,0:T(8,128)(2,1)S(1)} %maximum_bitcast_fusion), channel_id=1, source_target_pairs={{0,16},{1,9},{2,18},{3,11},{4,20},{5,13},{6,22},{7,15},{8,24},{9,1... | collective-permute-start | bytes 110600 | tf_op jit(solution)/shard_map/ppermute | solution.py:35
  7.4 0.2 pad_maximum_fusion.1.cols_a_ref
  7.7 0.7 %and_select_fusion = s32[16]{0:T(128)S(1)} fusion(s32[16]{0:T(128)} %param.10), kind=kLoop, calls=%fused_computation.34 | loop fusion | flops 240 | bytes 128 | tf_op jit(solution)/shard_map/jit(floor_divide)/jit(_where)/select_n | solution.py:60
  8.6 0.7 %gather_fusion.1 = s32[9]{0:T(128)S(1)} fusion(s32[16]{0:T(128)S(1)} %and_select_fusion, s32[1024]{0:T(1024)S(1)} %pad_clamp_fusion.1), kind=kCustom, calls=%fused_computation.3 | custom fusion | bytes 108 | tf_op jit(solution)/shard_map/gather | solution.py:91
  9.2 0.7 %gather_fusion = s32[9]{0:T(128)S(1)} fusion(s32[16]{0:T(128)S(1)} %and_select_fusion, s32[1024]{0:T(1024)S(1)} %pad_clamp_fusion.3), kind=kCustom, calls=%fused_computation.2 | custom fusion | bytes 108 | tf_op jit(solution)/shard_map/gather | solution.py:91
  10.0 1.6 %collective-permute-start.2 = (bf16[2,144,128]{2,1,0:T(8,128)(2,1)S(1)}, bf16[2,144,128]{2,1,0:T(8,128)(2,1)S(1)}, u32[]{:S(2)}, u32[]{:S(2)}) collective-permute-start(bf16[2,144,128]{2,1,0:T(8,128)(2,1)S(1)} %pad_maximum_fusion.3), channel_id=1, source_target_pairs={{0,8},{1,17},{2,10},{3,19},{4,12},{5,21},{6,14},{7,23},{8,0},{9,25... | collective-permute-start | bytes 221192 | tf_op jit(solution)/shard_map/ppermute | solution.py:35
  11.6 3.6 %collective-permute-done.2 = bf16[2,144,128]{2,1,0:T(8,128)(2,1)S(1)} collective-permute-done((bf16[2,144,128]{2,1,0:T(8,128)(2,1)S(1)}, bf16[2,144,128]{2,1,0:T(8,128)(2,1)S(1)}, u32[]{:S(2)}, u32[]{:S(2)}) %collective-permute-start.2) | collective-permute-done | bytes 73760 | tf_op jit(solution)/shard_map/ppermute | solution.py:35
  15.2 1.6 %collective-permute-start.3 = (bf16[4,144,128]{2,1,0:T(8,128)(2,1)S(1)}, bf16[4,144,128]{2,1,0:T(8,128)(2,1)S(1)}, u32[]{:S(2)}, u32[]{:S(2)}) collective-permute-start(bf16[4,144,128]{2,1,0:T(8,128)(2,1)S(1)} %pad_maximum_fusion.2), channel_id=1, source_target_pairs={{0,4},{1,3},{2,6},{3,1},{4,0},{5,7},{6,2},{7,5},{8,12},{9,11},{10,... | collective-permute-start | bytes 442376 | tf_op jit(solution)/shard_map/ppermute | solution.py:35
  16.8 3.6 %collective-permute-done.3 = bf16[4,144,128]{2,1,0:T(8,128)(2,1)S(1)} collective-permute-done((bf16[4,144,128]{2,1,0:T(8,128)(2,1)S(1)}, bf16[4,144,128]{2,1,0:T(8,128)(2,1)S(1)}, u32[]{:S(2)}, u32[]{:S(2)}) %collective-permute-start.3) | collective-permute-done | bytes 147488 | tf_op jit(solution)/shard_map/ppermute | solution.py:35
  20.4 1.6 %collective-permute-start.4 = (bf16[8,144,128]{2,1,0:T(8,128)(2,1)S(1)}, bf16[8,144,128]{2,1,0:T(8,128)(2,1)S(1)}, u32[]{:S(2)}, u32[]{:S(2)}) collective-permute-start(bf16[8,144,128]{2,1,0:T(8,128)(2,1)S(1)} %pad_maximum_fusion), channel_id=1, source_target_pairs={{0,2},{1,5},{2,0},{3,7},{4,6},{5,1},{6,4},{7,3},{8,10},{9,13},{10,... | collective-permute-start | bytes 884744 | tf_op jit(solution)/shard_map/ppermute | solution.py:35
  22.0 5.2 %collective-permute-done.4 = bf16[8,144,128]{2,1,0:T(8,128)(2,1)S(1)} collective-permute-done((bf16[8,144,128]{2,1,0:T(8,128)(2,1)S(1)}, bf16[8,144,128]{2,1,0:T(8,128)(2,1)S(1)}, u32[]{:S(2)}, u32[]{:S(2)}) %collective-permute-start.4) | collective-permute-done | bytes 294944 | tf_op jit(solution)/shard_map/ppermute | solution.py:35
  27.3 0.6 %gather_fusion.3 = bf16[9,144,128]{2,1,0:T(8,128)(2,1)S(1)} fusion(bf16[16,144,128]{2,1,0:T(8,128)(2,1)S(1)} %constant_dynamic-update-slice_fusion, s32[1024]{0:T(1024)S(1)} %pad_clamp_fusion), kind=kCustom, calls=%fused_computation.1.clone | custom fusion | bytes 663588 | tf_op jit(solution)/shard_map/jit(_take)/gather | solution.py:92
  28.1 0.6 %pad_add_fusion.2.table_ref = s32[2]{0:T(128)} fusion(s32[1]{0:T(128)} %bitcast.12), kind=kLoop, calls=%fused_computation.45 | loop fusion | flops 2 | bytes 12 | tf_op jit(solution)/shard_map/stack | solution.py:111
  28.7 0.6 %gather_fusion.2 = bf16[9,144,128]{2,1,0:T(8,128)(2,1)S(1)} fusion(bf16[16,144,128]{2,1,0:T(8,128)(2,1)S(1)} %constant_dynamic-update-slice_fusion, s32[1024]{0:T(1024)S(1)} %pad_clamp_fusion.2), kind=kCustom, calls=%fused_computation.clone | custom fusion | bytes 663588 | tf_op jit(solution)/shard_map/jit(_take)/gather | solution.py:92
  29.3 0.8 %broadcast_select_fusion.1.pieces_a_ref = bf16[9,144,128]{2,1,0:T(8,128)(2,1)} fusion(bf16[9,144,128]{2,1,0:T(8,128)(2,1)S(1)} %gather_fusion.2, pred[9]{0:T(512)(128)(4,1)S(1)} %get-tuple-element.22), kind=kLoop, calls=%fused_computation.5 | loop fusion | flops 165888 | bytes 663561 | tf_op jit(solution)/shard_map/jit(_take)/select_n | solution.py:92
  30.1 0.7 %copy-done.2 = bf16[1040,128]{1,0:T(8,128)(2,1)} copy-done((bf16[1040,128]{1,0:T(8,128)(2,1)}, bf16[1040,128]{1,0:T(8,128)(2,1)S(1)}, u32[]{:S(2)}) %copy-start.2) | copy-done | bytes 266264
  30.8 0.7 %copy-done.1 = bf16[9,144,128]{2,1,0:T(8,128)(2,1)} copy-done((bf16[9,144,128]{2,1,0:T(8,128)(2,1)}, bf16[9,144,128]{2,1,0:T(8,128)(2,1)S(1)}, u32[]{:S(2)}) %copy-start.1) | copy-done | bytes 331800
  31.6 7.3 %shard_map.46 = bf16[1024,1024]{1,0:T(8,128)(2,1)} custom-call(bf16[1024,1024]{1,0:T(8,128)(2,1)} %matrix_ref.1, bf16[1040,128]{1,0:T(8,128)(2,1)} %copy-done, bf16[1040,128]{1,0:T(8,128)(2,1)} %copy-done.2, bf16[9,144,128]{2,1,0:T(8,128)(2,1)} %broadcast_select_fusion.1.pieces_a_ref, bf16[9,144,128]{2,1,0:T(8,128)(2,1)} %copy-done.1, ...), custom_call_target="tpu_custom_call" | custom-call | flops 637534208 | bytes 4194304 | tf_op jit(solution)/shard_map/pallas_call | solution.py:197
  (36 shorter events, 0.9 us)
Async XLA Ops:
  3.3 6.6 %collective-permute-start.1 = (bf16[1,144,128]{2,1,0:T(8,128)(2,1)S(1)}, bf16[1,144,128]{2,1,0:T(8,128)(2,1)S(1)}, u32[]{:S(2)}, u32[]{:S(2)}) collective-permute-start(bf16[1,144,128]{2,1,0:T(8,128)(2,1)S(1)} %maximum_bitcast_fusion), channel_id=1, source_target_pairs={{0,16},{1,9},{2,18},{3,11},{4,20},{5,13},{6,22},{7,15},{8,24},{9,1... | collective-permute-start | bytes 110600 | tf_op jit(solution)/shard_map/ppermute | solution.py:35
  7.6 20.4 %copy-start = (bf16[1040,128]{1,0:T(8,128)(2,1)}, bf16[1040,128]{1,0:T(8,128)(2,1)S(1)}, u32[]{:S(2)}) copy-start(bf16[1040,128]{1,0:T(8,128)(2,1)S(1)} %pad_maximum_fusion.1.cols_a_ref) | copy-start | bytes 798724
  7.6 22.5 %collective-permute-start = (bf16[1040,128]{1,0:T(8,128)(2,1)S(1)}, bf16[1040,128]{1,0:T(8,128)(2,1)S(1)}, u32[]{:S(2)}, u32[]{:S(2)}) collective-permute-start(bf16[1040,128]{1,0:T(8,128)(2,1)S(1)} %pad_maximum_fusion.1.cols_a_ref), channel_id=1, source_target_pairs={{0,1},{1,0},{2,3},{3,2},{4,5},{5,4},{6,7},{7,6},{8,9},{9,8},{10,11... | collective-permute-start | bytes 798728 | tf_op jit(solution)/shard_map/ppermute | solution.py:98
  10.0 5.2 %collective-permute-start.2 = (bf16[2,144,128]{2,1,0:T(8,128)(2,1)S(1)}, bf16[2,144,128]{2,1,0:T(8,128)(2,1)S(1)}, u32[]{:S(2)}, u32[]{:S(2)}) collective-permute-start(bf16[2,144,128]{2,1,0:T(8,128)(2,1)S(1)} %pad_maximum_fusion.3), channel_id=1, source_target_pairs={{0,8},{1,17},{2,10},{3,19},{4,12},{5,21},{6,14},{7,23},{8,0},{9,25... | collective-permute-start | bytes 221192 | tf_op jit(solution)/shard_map/ppermute | solution.py:35
  15.2 5.2 %collective-permute-start.3 = (bf16[4,144,128]{2,1,0:T(8,128)(2,1)S(1)}, bf16[4,144,128]{2,1,0:T(8,128)(2,1)S(1)}, u32[]{:S(2)}, u32[]{:S(2)}) collective-permute-start(bf16[4,144,128]{2,1,0:T(8,128)(2,1)S(1)} %pad_maximum_fusion.2), channel_id=1, source_target_pairs={{0,4},{1,3},{2,6},{3,1},{4,0},{5,7},{6,2},{7,5},{8,12},{9,11},{10,... | collective-permute-start | bytes 442376 | tf_op jit(solution)/shard_map/ppermute | solution.py:35
  20.4 6.8 %collective-permute-start.4 = (bf16[8,144,128]{2,1,0:T(8,128)(2,1)S(1)}, bf16[8,144,128]{2,1,0:T(8,128)(2,1)S(1)}, u32[]{:S(2)}, u32[]{:S(2)}) collective-permute-start(bf16[8,144,128]{2,1,0:T(8,128)(2,1)S(1)} %pad_maximum_fusion), channel_id=1, source_target_pairs={{0,2},{1,5},{2,0},{3,7},{4,6},{5,1},{6,4},{7,3},{8,10},{9,13},{10,... | collective-permute-start | bytes 884744 | tf_op jit(solution)/shard_map/ppermute | solution.py:35
  28.0 2.1 %collective-permute-start.5 = (bf16[9,144,128]{2,1,0:T(8,128)(2,1)S(1)}, bf16[9,144,128]{2,1,0:T(8,128)(2,1)S(1)}, u32[]{:S(2)}, u32[]{:S(2)}) collective-permute-start(bf16[9,144,128]{2,1,0:T(8,128)(2,1)S(1)} %broadcast_select_fusion), channel_id=1, source_target_pairs={{0,1},{1,0},{2,3},{3,2},{4,5},{5,4},{6,7},{7,6},{8,9},{9,8},{10,11... | collective-permute-start | bytes 995336 | tf_op jit(solution)/shard_map/ppermute | solution.py:101
  30.1 0.7 %copy-start.2 = (bf16[1040,128]{1,0:T(8,128)(2,1)}, bf16[1040,128]{1,0:T(8,128)(2,1)S(1)}, u32[]{:S(2)}) copy-start(bf16[1040,128]{1,0:T(8,128)(2,1)S(1)} %collective-permute-done.cols_b_ref) | copy-start | bytes 798724
  30.8 0.7 %copy-start.1 = (bf16[9,144,128]{2,1,0:T(8,128)(2,1)}, bf16[9,144,128]{2,1,0:T(8,128)(2,1)S(1)}, u32[]{:S(2)}) copy-start(bf16[9,144,128]{2,1,0:T(8,128)(2,1)S(1)} %collective-permute-done.5.pieces_b_ref) | copy-start | bytes 995332

commit v5 on v4

--- a/solution.py
+++ b/solution.py
@@ -1,3 +1,5 @@
+import functools
+
 import jax
 import jax.numpy as jnp
 from jax import lax
@@ -99,30 +101,27 @@
         pieces_a = pick(held, wanted, parity)
         for_partner = pick(held, wanted_of(1 - col_index), parity)
         pieces_b = lax.ppermute(for_partner, "col", swap)
-        order = col_index
     else:
         lead = lax.all_gather(payload, "col", axis=0, tiled=False)
         cols_a, cols_b = lead[FIRST_COL], lead[SECOND_COL]
         everyone = lax.all_gather(held, "col", axis=0, tiled=False)
         pieces_a = pick(everyone[FIRST_COL], wanted, FIRST_COL % 2)
         pieces_b = pick(everyone[SECOND_COL], wanted, SECOND_COL % 2)
-        order = jnp.zeros_like(col_index)
-
-    table = jnp.stack((order, col_index)).astype(jnp.int32)
+
     return factor_call(
-        matrix, cols_a, cols_b, pieces_a, pieces_b, inverses, fill_mask, table
+        matrix, cols_a, cols_b, pieces_a, pieces_b, inverses, fill_mask, col_count == 2
     )
 
 
 def factor_kernel(
-    matrix_ref, cols_a_ref, cols_b_ref, pieces_a_ref, pieces_b_ref, inv_ref, mask_ref, table_ref, out_ref
+    matrix_ref, cols_a_ref, cols_b_ref, pieces_a_ref, pieces_b_ref, inv_ref, mask_ref, out_ref, *, by_col
 ):
     local_rows, width = matrix_ref.shape
     col_panels = width // PW
     block_rows = local_rows // RB
     picks = pieces_a_ref.shape[0]
-    swapped = table_ref[0] != 0
-    col_index = table_ref[1]
+    col_index = lax.axis_index("col")
+    swapped = (col_index != FIRST_COL) if by_col else False
 
     def dot(left, right):
         return jnp.dot(left, right, preferred_element_type=jnp.float32)
@@ -132,6 +131,12 @@
             left, right, (((1,), (1,)), ((), ())), preferred_element_type=jnp.float32
         )
 
+    def first_second(a_ref, b_ref, index):
+        a_val, b_val = a_ref[index], b_ref[index]
+        if not by_col:
+            return a_val, b_val
+        return jnp.where(swapped, b_val, a_val), jnp.where(swapped, a_val, b_val)
+
     upper = (
         lax.broadcasted_iota(jnp.int32, (PW, PW), 0) <= lax.broadcasted_iota(jnp.int32, (PW, PW), 1)
     )
@@ -139,70 +144,74 @@
     upper_first = jnp.where(upper, inv_ref[0], zero)
     upper_second = jnp.where(upper, inv_ref[1], zero)
 
-    def first_second(a_ref, b_ref, index):
-        a_val, b_val = a_ref[index], b_ref[index]
-        return jnp.where(swapped, b_val, a_val), jnp.where(swapped, a_val, b_val)
-
-    diag_first, diag_second = [], []
-    for t in range(picks):
-        piece_first, piece_second = first_second(pieces_a_ref, pieces_b_ref, t)
-        flag_first = piece_first[PW : PW + 1].astype(jnp.float32)
-        diag_first.append((dot(piece_first[:PW], upper_first) * flag_first).astype(jnp.bfloat16))
+    slabs_first, slabs_second = first_second(
+        pieces_a_ref, pieces_b_ref, (slice(None), slice(0, PW), slice(None))
+    )
+    flags_first, flags_second = first_second(
+        pieces_a_ref, pieces_b_ref, (slice(None), slice(PW, PW + 1), slice(None))
+    )
+    diag_first = (
+        dot(slabs_first.reshape(picks * PW, PW), upper_first).reshape(picks, PW, PW)
+        * flags_first.astype(jnp.float32)
+    ).astype(jnp.bfloat16)
     pivot = diag_first[col_panels]
-    for t in range(col_panels):
-        piece_first, piece_second = first_second(pieces_a_ref, pieces_b_ref, t)
-        flag_second = piece_second[PW : PW + 1].astype(jnp.float32)
-        update = (
-            piece_second[:PW].astype(jnp.float32) - dot_t(diag_first[t], pivot)
-        ).astype(jnp.bfloat16)
-        diag_second.append((dot(update, upper_second) * flag_second).astype(jnp.bfloat16))
-    both_diag = [
-        jnp.concatenate((diag_first[t], diag_second[t]), axis=1) for t in range(col_panels)
-    ]
-
-    for b in range(block_rows):
-        rows = slice(b * RB, (b + 1) * RB)
-        cols_first, cols_second = first_second(cols_a_ref, cols_b_ref, rows)
-        flags_first, flags_second = first_second(
-            cols_a_ref, cols_b_ref, slice(local_rows + b, local_rows + b + 1)
-        )
-        first_panel = (dot(cols_first, upper_first) * flags_first.astype(jnp.float32)).astype(
-            jnp.bfloat16
-        )
-        panel_update = (
-            cols_second.astype(jnp.float32) - dot_t(first_panel, pivot)
-        ).astype(jnp.bfloat16)
-        second_panel = (
-            dot(panel_update, upper_second) * flags_second.astype(jnp.float32)
-        ).astype(jnp.bfloat16)
-        both_panels = jnp.concatenate((first_panel, second_panel), axis=1)
-        for j in range(col_panels):
-            cols = slice(j * PW, (j + 1) * PW)
-            schur = matrix_ref[rows, cols].astype(jnp.float32) - dot_t(both_panels, both_diag[j])
-            tile = (schur * mask_ref[b, j].astype(jnp.float32)).astype(jnp.bfloat16)
+    own_first = diag_first[:col_panels].reshape(col_panels * PW, PW)
+    diag_update = (
+        slabs_second[:col_panels].reshape(col_panels * PW, PW).astype(jnp.float32)
+        - dot_t(own_first, pivot)
+    ).astype(jnp.bfloat16)
+    diag_second = (
+        dot(diag_update, upper_second).reshape(col_panels, PW, PW)
+        * flags_second[:col_panels].astype(jnp.float32)
+    ).astype(jnp.bfloat16)
+
+    cols_first, cols_second = first_second(cols_a_ref, cols_b_ref, slice(0, local_rows))
+    rows_first, rows_second = first_second(
+        cols_a_ref, cols_b_ref, slice(local_rows, local_rows + block_rows)
+    )
+    first_panel = (
+        dot(cols_first, upper_first).reshape(block_rows, RB, PW)
+        * rows_first.astype(jnp.float32)[:, None, :]
+    ).astype(jnp.bfloat16).reshape(local_rows, PW)
+    panel_update = (
+        cols_second.astype(jnp.float32) - dot_t(first_panel, pivot)
+    ).astype(jnp.bfloat16)
+    second_panel = (
+        dot(panel_update, upper_second).reshape(block_rows, RB, PW)
+        * rows_second.astype(jnp.float32)[:, None, :]
+    ).astype(jnp.bfloat16).reshape(local_rows, PW)
+    both_panels = jnp.concatenate((first_panel, second_panel), axis=1)
+
+    for j in range(col_panels):
+        cols = slice(j * PW, (j + 1) * PW)
+        both_diag = jnp.concatenate((diag_first[j], diag_second[j]), axis=1)
+        schur = matrix_ref[:, cols].astype(jnp.float32) - dot_t(both_panels, both_diag)
+        for b in range(block_rows):
+            rows = slice(b * RB, (b + 1) * RB)
+            tile = (schur[rows] * mask_ref[b, j].astype(jnp.float32)).astype(jnp.bfloat16)
             if j == 0:
                 tile = jnp.where(
                     col_index == FIRST_COL,
-                    first_panel,
-                    jnp.where(col_index == SECOND_COL, second_panel, tile),
+                    first_panel[rows],
+                    jnp.where(col_index == SECOND_COL, second_panel[rows], tile),
                 )
             out_ref[rows, cols] = tile
 
 
-def factor_call(matrix, cols_a, cols_b, pieces_a, pieces_b, inverses, fill_mask, table):
+def factor_call(matrix, cols_a, cols_b, pieces_a, pieces_b, inverses, fill_mask, by_col):
     local_rows, width = matrix.shape
     vmem = pl.BlockSpec(memory_space=pltpu.VMEM)
     smem = pl.BlockSpec(memory_space=pltpu.SMEM)
     flops = 2 * local_rows * width * 2 * PW + 6 * local_rows * PW * PW
     return pl.pallas_call(
-        factor_kernel,
+        functools.partial(factor_kernel, by_col=by_col),
         out_shape=jax.ShapeDtypeStruct((local_rows, width), jnp.bfloat16),
-        in_specs=[vmem] * 6 + [smem, smem],
+        in_specs=[vmem] * 6 + [smem],
         out_specs=vmem,
         cost_estimate=pl.CostEstimate(
             flops=flops, bytes_accessed=4 * local_rows * width, transcendentals=0
         ),
-    )(matrix, cols_a, cols_b, pieces_a, pieces_b, inverses, fill_mask, table)
+    )(matrix, cols_a, cols_b, pieces_a, pieces_b, inverses, fill_mask)
 
 
 def solution(mesh):

time: 39.1 us -> 36.4 us (0.931)
  Pallas kernels: 7.31 us -> 5.24 us
  other arithmetic: 4.3 us -> 3.7 us
    pallas_call x1, Pallas kernels: 7.31 us -> 5.24 us  [factor_call(): pl.pallas_call(functools.partial(factor_kernel, by_col=by_col), out_shape...]
    another operation x1 -> x0, other arithmetic: 0.6 us -> none  [shards(): table = jnp.stack((order, col_index)).astype(jnp.int32)]
  transfers between devices with their start and end apart: 6 -> 6, of which waited for: 3 -> 4; matrix products, arithmetic and copies ran while one was open for 14% -> 13% of each run, Pallas kernels for 0% -> 0%
where the time goes in v5:
time: 36.4 us; the launch traced here: 36.2 us
  waiting for transfers between devices  12.5 us (34%)
  starting transfers between devices  9.03 us (25%)
  Pallas kernels  5.24 us (14%)
  local copies, waits for them, and re-layouts  5.15 us (14%)
  other arithmetic  3.7 us (10%)
  matrix products  0.38 us (1%)
    ppermute x4, waiting for transfers between devices, gather_rows(): lax.ppermute(held, ('row', 'col'), perm)  12.3 us
    ppermute x4, starting transfers between devices, gather_rows(): lax.ppermute(held, ('row', 'col'), perm)  8.89 us
    pallas_call x1, Pallas kernels, factor_call(): pl.pallas_call(functools.partial(factor_kernel, by_col=by_col), out_shape...  5.24 us
    gather x2, local copies, waits for them, and re-layouts, pick(): slots = slot_of(owner_row[wanted], order_parity)  1.32 us
    unnamed x9, local copies, waits for them, and re-layouts  1.32 us
    gather x2, local copies, waits for them, and re-layouts, pick(): return jnp.take(pieces, slots, axis=0)  1.22 us
    slice x1, local copies, waits for them, and re-layouts, shards(): payload = jnp.concatenate((matrix[:, :PW], mask_rows), axis=0)  0.97 us
    select_n x2, other arithmetic, pick(): return jnp.take(pieces, slots, axis=0)  0.91 us
  transfers between devices with their start and end apart: 6, of which 4 were waited for; matrix products, arithmetic and copies ran while one was open for 13% of the time, Pallas kernels for 0%

profile of v5, /device:TPU:0, one launch (start us, length us, event | category | flops | bytes accessed | tf_op | source)
XLA Modules:
  0.0 36.2 jit_solution(10089177860420984885)
XLA Ops:
  0.0 0.7 %convert_element_type.25 = bf16[4,8]{1,0:T(4,128)(2,1)S(1)} convert(s32[4,8]{1,0:T(4,128)} %mask_ref.1) | non-fusion elementwise | flops 32 | bytes 192 | tf_op jit(solution)/shard_map/convert_element_type | solution.py:60
  0.7 0.1 slice_reduce_fusion
  1.0 0.8 %convert_reduce_fusion = s32[8]{0:T(128)S(1)} fusion(s32[16]{0:T(128)} %param.10, s32[8]{0:T(128)S(1)} %iota_add_fusion), kind=kLoop, calls=%fused_computation.27 | loop fusion | flops 376 | bytes 128 | tf_op jit(solution)/shard_map/reduce_sum | solution.py:64
  1.9 0.1 fusion.2
  2.0 1.0 %slice.25 = bf16[1024,128]{1,0:T(8,128)(2,1)S(1)} slice(bf16[1024,1024]{1,0:T(8,128)(2,1)} %matrix_ref.1), slice={[0:1024], [0:128]} | slice | bytes 524288 | tf_op jit(solution)/shard_map/slice | solution.py:86
  3.0 0.3 fusion
  3.3 4.1 %collective-permute-start.1 = (bf16[1,144,128]{2,1,0:T(8,128)(2,1)S(1)}, bf16[1,144,128]{2,1,0:T(8,128)(2,1)S(1)}, u32[]{:S(2)}, u32[]{:S(2)}) collective-permute-start(bf16[1,144,128]{2,1,0:T(8,128)(2,1)S(1)} %maximum_bitcast_fusion), channel_id=1, source_target_pairs={{0,16},{1,9},{2,18},{3,11},{4,20},{5,13},{6,22},{7,15},{8,24},{9,1... | collective-permute-start | bytes 110600 | tf_op jit(solution)/shard_map/ppermute | solution.py:37
  7.4 0.2 pad_maximum_fusion.1.cols_a_ref
  7.7 0.7 %and_select_fusion = s32[16]{0:T(128)S(1)} fusion(s32[16]{0:T(128)} %param.10), kind=kLoop, calls=%fused_computation.34 | loop fusion | flops 240 | bytes 128 | tf_op jit(solution)/shard_map/jit(floor_divide)/jit(_where)/select_n | solution.py:62
  8.6 0.7 %gather_fusion.1 = s32[9]{0:T(128)S(1)} fusion(s32[16]{0:T(128)S(1)} %and_select_fusion, s32[1024]{0:T(1024)S(1)} %pad_clamp_fusion.1), kind=kCustom, calls=%fused_computation.3 | custom fusion | bytes 108 | tf_op jit(solution)/shard_map/gather | solution.py:93
  9.2 0.7 %gather_fusion = s32[9]{0:T(128)S(1)} fusion(s32[16]{0:T(128)S(1)} %and_select_fusion, s32[1024]{0:T(1024)S(1)} %pad_clamp_fusion.3), kind=kCustom, calls=%fused_computation.2 | custom fusion | bytes 108 | tf_op jit(solution)/shard_map/gather | solution.py:93
  9.9 1.6 %collective-permute-start.2 = (bf16[2,144,128]{2,1,0:T(8,128)(2,1)S(1)}, bf16[2,144,128]{2,1,0:T(8,128)(2,1)S(1)}, u32[]{:S(2)}, u32[]{:S(2)}) collective-permute-start(bf16[2,144,128]{2,1,0:T(8,128)(2,1)S(1)} %pad_maximum_fusion.3), channel_id=1, source_target_pairs={{0,8},{1,17},{2,10},{3,19},{4,12},{5,21},{6,14},{7,23},{8,0},{9,25... | collective-permute-start | bytes 221192 | tf_op jit(solution)/shard_map/ppermute | solution.py:37
  11.6 3.5 %collective-permute-done.2 = bf16[2,144,128]{2,1,0:T(8,128)(2,1)S(1)} collective-permute-done((bf16[2,144,128]{2,1,0:T(8,128)(2,1)S(1)}, bf16[2,144,128]{2,1,0:T(8,128)(2,1)S(1)}, u32[]{:S(2)}, u32[]{:S(2)}) %collective-permute-start.2) | collective-permute-done | bytes 73760 | tf_op jit(solution)/shard_map/ppermute | solution.py:37
  15.2 1.6 %collective-permute-start.3 = (bf16[4,144,128]{2,1,0:T(8,128)(2,1)S(1)}, bf16[4,144,128]{2,1,0:T(8,128)(2,1)S(1)}, u32[]{:S(2)}, u32[]{:S(2)}) collective-permute-start(bf16[4,144,128]{2,1,0:T(8,128)(2,1)S(1)} %pad_maximum_fusion.2), channel_id=1, source_target_pairs={{0,4},{1,3},{2,6},{3,1},{4,0},{5,7},{6,2},{7,5},{8,12},{9,11},{10,... | collective-permute-start | bytes 442376 | tf_op jit(solution)/shard_map/ppermute | solution.py:37
  16.8 3.6 %collective-permute-done.3 = bf16[4,144,128]{2,1,0:T(8,128)(2,1)S(1)} collective-permute-done((bf16[4,144,128]{2,1,0:T(8,128)(2,1)S(1)}, bf16[4,144,128]{2,1,0:T(8,128)(2,1)S(1)}, u32[]{:S(2)}, u32[]{:S(2)}) %collective-permute-start.3) | collective-permute-done | bytes 147488 | tf_op jit(solution)/shard_map/ppermute | solution.py:37
  20.4 1.6 %collective-permute-start.4 = (bf16[8,144,128]{2,1,0:T(8,128)(2,1)S(1)}, bf16[8,144,128]{2,1,0:T(8,128)(2,1)S(1)}, u32[]{:S(2)}, u32[]{:S(2)}) collective-permute-start(bf16[8,144,128]{2,1,0:T(8,128)(2,1)S(1)} %pad_maximum_fusion), channel_id=1, source_target_pairs={{0,2},{1,5},{2,0},{3,7},{4,6},{5,1},{6,4},{7,3},{8,10},{9,13},{10,... | collective-permute-start | bytes 884744 | tf_op jit(solution)/shard_map/ppermute | solution.py:37
  22.0 5.2 %collective-permute-done.4 = bf16[8,144,128]{2,1,0:T(8,128)(2,1)S(1)} collective-permute-done((bf16[8,144,128]{2,1,0:T(8,128)(2,1)S(1)}, bf16[8,144,128]{2,1,0:T(8,128)(2,1)S(1)}, u32[]{:S(2)}, u32[]{:S(2)}) %collective-permute-start.4) | collective-permute-done | bytes 294944 | tf_op jit(solution)/shard_map/ppermute | solution.py:37
  27.2 0.6 %gather_fusion.3 = bf16[9,144,128]{2,1,0:T(8,128)(2,1)S(1)} fusion(bf16[16,144,128]{2,1,0:T(8,128)(2,1)S(1)} %constant_dynamic-update-slice_fusion, s32[1024]{0:T(1024)S(1)} %pad_clamp_fusion), kind=kCustom, calls=%fused_computation.1.clone | custom fusion | bytes 663588 | tf_op jit(solution)/shard_map/jit(_take)/gather | solution.py:94
  28.1 0.6 %gather_fusion.2 = bf16[9,144,128]{2,1,0:T(8,128)(2,1)S(1)} fusion(bf16[16,144,128]{2,1,0:T(8,128)(2,1)S(1)} %constant_dynamic-update-slice_fusion, s32[1024]{0:T(1024)S(1)} %pad_clamp_fusion.2), kind=kCustom, calls=%fused_computation.clone | custom fusion | bytes 663588 | tf_op jit(solution)/shard_map/jit(_take)/gather | solution.py:94
  28.7 0.8 %broadcast_select_fusion.1.pieces_a_ref = bf16[9,144,128]{2,1,0:T(8,128)(2,1)} fusion(bf16[9,144,128]{2,1,0:T(8,128)(2,1)S(1)} %gather_fusion.2, pred[9]{0:T(512)(128)(4,1)S(1)} %get-tuple-element.22), kind=kLoop, calls=%fused_computation.5 | loop fusion | flops 165888 | bytes 663561 | tf_op jit(solution)/shard_map/jit(_take)/select_n | solution.py:94
  29.5 0.2 collective-permute-done.5.pieces_b_ref
  29.7 0.5 %copy-done.2 = bf16[1040,128]{1,0:T(8,128)(2,1)} copy-done((bf16[1040,128]{1,0:T(8,128)(2,1)}, bf16[1040,128]{1,0:T(8,128)(2,1)S(1)}, u32[]{:S(2)}) %copy-start.2) | copy-done | bytes 266264
  30.2 0.7 %copy-done.1 = bf16[9,144,128]{2,1,0:T(8,128)(2,1)} copy-done((bf16[9,144,128]{2,1,0:T(8,128)(2,1)}, bf16[9,144,128]{2,1,0:T(8,128)(2,1)S(1)}, u32[]{:S(2)}) %copy-start.1) | copy-done | bytes 331800
  30.9 5.2 %shard_map.46 = bf16[1024,1024]{1,0:T(8,128)(2,1)} custom-call(bf16[1024,1024]{1,0:T(8,128)(2,1)} %matrix_ref.1, bf16[1040,128]{1,0:T(8,128)(2,1)} %copy-done, bf16[1040,128]{1,0:T(8,128)(2,1)} %copy-done.2, bf16[9,144,128]{2,1,0:T(8,128)(2,1)} %broadcast_select_fusion.1.pieces_a_ref, bf16[9,144,128]{2,1,0:T(8,128)(2,1)} %copy-done.1, ...), custom_call_target="tpu_custom_call" | custom-call | flops 637534208 | bytes 4194304 | tf_op jit(solution)/shard_map/pallas_call | solution.py:206
  (35 shorter events, 0.9 us)
Async XLA Ops:
  3.3 6.6 %collective-permute-start.1 = (bf16[1,144,128]{2,1,0:T(8,128)(2,1)S(1)}, bf16[1,144,128]{2,1,0:T(8,128)(2,1)S(1)}, u32[]{:S(2)}, u32[]{:S(2)}) collective-permute-start(bf16[1,144,128]{2,1,0:T(8,128)(2,1)S(1)} %maximum_bitcast_fusion), channel_id=1, source_target_pairs={{0,16},{1,9},{2,18},{3,11},{4,20},{5,13},{6,22},{7,15},{8,24},{9,1... | collective-permute-start | bytes 110600 | tf_op jit(solution)/shard_map/ppermute | solution.py:37
  7.6 20.4 %copy-start = (bf16[1040,128]{1,0:T(8,128)(2,1)}, bf16[1040,128]{1,0:T(8,128)(2,1)S(1)}, u32[]{:S(2)}) copy-start(bf16[1040,128]{1,0:T(8,128)(2,1)S(1)} %pad_maximum_fusion.1.cols_a_ref) | copy-start | bytes 798724
  7.6 21.9 %collective-permute-start = (bf16[1040,128]{1,0:T(8,128)(2,1)S(1)}, bf16[1040,128]{1,0:T(8,128)(2,1)S(1)}, u32[]{:S(2)}, u32[]{:S(2)}) collective-permute-start(bf16[1040,128]{1,0:T(8,128)(2,1)S(1)} %pad_maximum_fusion.1.cols_a_ref), channel_id=1, source_target_pairs={{0,1},{1,0},{2,3},{3,2},{4,5},{5,4},{6,7},{7,6},{8,9},{9,8},{10,11... | collective-permute-start | bytes 798728 | tf_op jit(solution)/shard_map/ppermute | solution.py:100
  9.9 5.2 %collective-permute-start.2 = (bf16[2,144,128]{2,1,0:T(8,128)(2,1)S(1)}, bf16[2,144,128]{2,1,0:T(8,128)(2,1)S(1)}, u32[]{:S(2)}, u32[]{:S(2)}) collective-permute-start(bf16[2,144,128]{2,1,0:T(8,128)(2,1)S(1)} %pad_maximum_fusion.3), channel_id=1, source_target_pairs={{0,8},{1,17},{2,10},{3,19},{4,12},{5,21},{6,14},{7,23},{8,0},{9,25... | collective-permute-start | bytes 221192 | tf_op jit(solution)/shard_map/ppermute | solution.py:37
  15.2 5.2 %collective-permute-start.3 = (bf16[4,144,128]{2,1,0:T(8,128)(2,1)S(1)}, bf16[4,144,128]{2,1,0:T(8,128)(2,1)S(1)}, u32[]{:S(2)}, u32[]{:S(2)}) collective-permute-start(bf16[4,144,128]{2,1,0:T(8,128)(2,1)S(1)} %pad_maximum_fusion.2), channel_id=1, source_target_pairs={{0,4},{1,3},{2,6},{3,1},{4,0},{5,7},{6,2},{7,5},{8,12},{9,11},{10,... | collective-permute-start | bytes 442376 | tf_op jit(solution)/shard_map/ppermute | solution.py:37
  20.4 6.8 %collective-permute-start.4 = (bf16[8,144,128]{2,1,0:T(8,128)(2,1)S(1)}, bf16[8,144,128]{2,1,0:T(8,128)(2,1)S(1)}, u32[]{:S(2)}, u32[]{:S(2)}) collective-permute-start(bf16[8,144,128]{2,1,0:T(8,128)(2,1)S(1)} %pad_maximum_fusion), channel_id=1, source_target_pairs={{0,2},{1,5},{2,0},{3,7},{4,6},{5,1},{6,4},{7,3},{8,10},{9,13},{10,... | collective-permute-start | bytes 884744 | tf_op jit(solution)/shard_map/ppermute | solution.py:37
  28.0 1.7 %collective-permute-start.5 = (bf16[9,144,128]{2,1,0:T(8,128)(2,1)S(1)}, bf16[9,144,128]{2,1,0:T(8,128)(2,1)S(1)}, u32[]{:S(2)}, u32[]{:S(2)}) collective-permute-start(bf16[9,144,128]{2,1,0:T(8,128)(2,1)S(1)} %broadcast_select_fusion), channel_id=1, source_target_pairs={{0,1},{1,0},{2,3},{3,2},{4,5},{5,4},{6,7},{7,6},{8,9},{9,8},{10,11... | collective-permute-start | bytes 995336 | tf_op jit(solution)/shard_map/ppermute | solution.py:103
  29.5 0.7 %copy-start.2 = (bf16[1040,128]{1,0:T(8,128)(2,1)}, bf16[1040,128]{1,0:T(8,128)(2,1)S(1)}, u32[]{:S(2)}) copy-start(bf16[1040,128]{1,0:T(8,128)(2,1)S(1)} %collective-permute-done.cols_b_ref) | copy-start | bytes 798724
  30.2 0.7 %copy-start.1 = (bf16[9,144,128]{2,1,0:T(8,128)(2,1)}, bf16[9,144,128]{2,1,0:T(8,128)(2,1)S(1)}, u32[]{:S(2)}) copy-start(bf16[9,144,128]{2,1,0:T(8,128)(2,1)S(1)} %collective-permute-done.5.pieces_b_ref) | copy-start | bytes 995332

commit v6 on v5

--- a/solution.py
+++ b/solution.py
@@ -27,14 +27,25 @@
     parity = lax.axis_index("col") % 2
     bits = row_count.bit_length() - 1
     even, odd = round_orders(bits)
-    held = piece[None]
-    for step in range(bits):
+    def exchange(value, masks):
         perm = []
         for r in range(row_count):
             for k in range(col_count):
-                bit = (even if k % 2 == 0 else odd)[step]
-                perm.append((r * col_count + k, (r ^ (1 << bit)) * col_count + k))
-        held = jnp.concatenate((held, lax.ppermute(held, ("row", "col"), perm)), axis=0)
+                perm.append((r * col_count + k, (r ^ masks[k % 2]) * col_count + k))
+        return lax.ppermute(value, ("row", "col"), perm)
+
+    held = piece[None]
+    first = 0
+    if bits >= 2:
+        parts = [held]
+        for chosen in ((0,), (1,), (0, 1)):
+            masks = [sum(1 << order[p] for p in chosen) for order in (even, odd)]
+            parts.append(exchange(held, masks))
+        held = jnp.concatenate(parts, axis=0)
+        first = 2
+    for step in range(first, bits):
+        masks = [1 << order[step] for order in (even, odd)]
+        held = jnp.concatenate((held, exchange(held, masks)), axis=0)
 
     def slot_of(owner, order_parity):
         diff = jnp.bitwise_xor(owner, me)

time: 36.4 us -> 34.6 us (0.951)
  waiting for transfers between devices: 12.5 us -> 10.6 us
    ppermute x4 -> x5, waiting for transfers between devices: 12.3 us -> 10.4 us  [exchange(): return lax.ppermute(value, ('row', 'col'), perm)]
    ppermute x4 -> x5, starting transfers between devices: 8.89 us -> 8.9 us  [exchange(): return lax.ppermute(value, ('row', 'col'), perm)]
  transfers between devices with their start and end apart: 6 -> 7, of which waited for: 4 -> 5; matrix products, arithmetic and copies ran while one was open for 13% -> 14% of each run, Pallas kernels for 0% -> 0%
where the time goes in v6:
time: 34.6 us; the launch traced here: 34.3 us
  waiting for transfers between devices  10.6 us (31%)
  starting transfers between devices  9.04 us (26%)
  Pallas kernels  5.24 us (15%)
  local copies, waits for them, and re-layouts  5.22 us (15%)
  other arithmetic  3.68 us (11%)
  matrix products  0.38 us (1%)
    ppermute x5, waiting for transfers between devices, exchange(): return lax.ppermute(value, ('row', 'col'), perm)  10.4 us
    ppermute x5, starting transfers between devices, exchange(): return lax.ppermute(value, ('row', 'col'), perm)  8.9 us
    pallas_call x1, Pallas kernels, factor_call(): pl.pallas_call(functools.partial(factor_kernel, by_col=by_col), out_shape...  5.24 us
    unnamed x9, local copies, waits for them, and re-layouts  1.33 us
    gather x2, local copies, waits for them, and re-layouts, pick(): slots = slot_of(owner_row[wanted], order_parity)  1.32 us
    gather x2, local copies, waits for them, and re-layouts, pick(): return jnp.take(pieces, slots, axis=0)  1.22 us
    slice x1, local copies, waits for them, and re-layouts, shards(): payload = jnp.concatenate((matrix[:, :PW], mask_rows), axis=0)  0.97 us
    select_n x2, other arithmetic, pick(): return jnp.take(pieces, slots, axis=0)  0.93 us
  transfers between devices with their start and end apart: 7, of which 5 were waited for; matrix products, arithmetic and copies ran while one was open for 14% of the time, Pallas kernels for 0%

profile of v6, /device:TPU:0, one launch (start us, length us, event | category | flops | bytes accessed | tf_op | source)
XLA Modules:
  0.0 34.3 jit_solution(1708972709635986117)
XLA Ops:
  0.0 0.7 %convert_element_type.25 = bf16[4,8]{1,0:T(4,128)(2,1)S(1)} convert(s32[4,8]{1,0:T(4,128)} %mask_ref.1) | non-fusion elementwise | flops 32 | bytes 192 | tf_op jit(solution)/shard_map/convert_element_type | solution.py:71
  1.0 0.8 %convert_reduce_fusion = s32[8]{0:T(128)S(1)} fusion(s32[16]{0:T(128)} %param.10, s32[8]{0:T(128)S(1)} %iota_add_fusion), kind=kLoop, calls=%fused_computation.31 | loop fusion | flops 376 | bytes 128 | tf_op jit(solution)/shard_map/reduce_sum | solution.py:75
  1.9 0.1 fusion.2
  2.0 1.0 %slice.25 = bf16[1024,128]{1,0:T(8,128)(2,1)S(1)} slice(bf16[1024,1024]{1,0:T(8,128)(2,1)} %matrix_ref.1), slice={[0:1024], [0:128]} | slice | bytes 524288 | tf_op jit(solution)/shard_map/slice | solution.py:97
  3.0 0.3 fusion
  3.3 5.1 %collective-permute-start.3 = (bf16[1,144,128]{2,1,0:T(8,128)(2,1)S(1)}, bf16[1,144,128]{2,1,0:T(8,128)(2,1)S(1)}, u32[]{:S(2)}, u32[]{:S(2)}) collective-permute-start(bf16[1,144,128]{2,1,0:T(8,128)(2,1)S(1)} %maximum_bitcast_fusion), channel_id=1, source_target_pairs={{0,24},{1,25},{2,26},{3,27},{4,28},{5,29},{6,30},{7,31},{8,16},{9,... | collective-permute-start | bytes 110600 | tf_op jit(solution)/shard_map/ppermute | solution.py:35
  8.4 0.6 %collective-permute-start.1 = (bf16[1,144,128]{2,1,0:T(8,128)(2,1)S(1)}, bf16[1,144,128]{2,1,0:T(8,128)(2,1)S(1)}, u32[]{:S(2)}, u32[]{:S(2)}) collective-permute-start(bf16[1,144,128]{2,1,0:T(8,128)(2,1)S(1)} %maximum_bitcast_fusion), channel_id=1, source_target_pairs={{0,16},{1,9},{2,18},{3,11},{4,20},{5,13},{6,22},{7,15},{8,24},{9,1... | collective-permute-start | bytes 110600 | tf_op jit(solution)/shard_map/ppermute | solution.py:35
  9.1 0.2 pad_maximum_fusion.cols_a_ref
  9.4 0.7 %and_select_fusion = s32[16]{0:T(128)S(1)} fusion(s32[16]{0:T(128)} %param.10), kind=kLoop, calls=%fused_computation.38 | loop fusion | flops 240 | bytes 128 | tf_op jit(solution)/shard_map/jit(floor_divide)/jit(_where)/select_n | solution.py:73
  10.3 0.7 %gather_fusion.1 = s32[9]{0:T(128)S(1)} fusion(s32[16]{0:T(128)S(1)} %and_select_fusion, s32[1024]{0:T(1024)S(1)} %pad_clamp_fusion.1), kind=kCustom, calls=%fused_computation.3 | custom fusion | bytes 108 | tf_op jit(solution)/shard_map/gather | solution.py:104
  10.9 0.7 %gather_fusion = s32[9]{0:T(128)S(1)} fusion(s32[16]{0:T(128)S(1)} %and_select_fusion, s32[1024]{0:T(1024)S(1)} %pad_clamp_fusion.3), kind=kCustom, calls=%fused_computation.2 | custom fusion | bytes 108 | tf_op jit(solution)/shard_map/gather | solution.py:104
  11.6 0.8 %collective-permute-done.2 = bf16[1,144,128]{2,1,0:T(8,128)(2,1)S(1)} collective-permute-done((bf16[1,144,128]{2,1,0:T(8,128)(2,1)S(1)}, bf16[1,144,128]{2,1,0:T(8,128)(2,1)S(1)}, u32[]{:S(2)}, u32[]{:S(2)}) %collective-permute-start.2) | collective-permute-done | bytes 36896 | tf_op jit(solution)/shard_map/ppermute | solution.py:35
  12.4 0.9 %collective-permute-done.1 = bf16[1,144,128]{2,1,0:T(8,128)(2,1)S(1)} collective-permute-done((bf16[1,144,128]{2,1,0:T(8,128)(2,1)S(1)}, bf16[1,144,128]{2,1,0:T(8,128)(2,1)S(1)}, u32[]{:S(2)}, u32[]{:S(2)}) %collective-permute-start.1) | collective-permute-done | bytes 36896 | tf_op jit(solution)/shard_map/ppermute | solution.py:35
  13.3 1.6 %collective-permute-start.4 = (bf16[4,144,128]{2,1,0:T(8,128)(2,1)S(1)}, bf16[4,144,128]{2,1,0:T(8,128)(2,1)S(1)}, u32[]{:S(2)}, u32[]{:S(2)}) collective-permute-start(bf16[4,144,128]{2,1,0:T(8,128)(2,1)S(1)} %pad_maximum_fusion.1), channel_id=1, source_target_pairs={{0,4},{1,3},{2,6},{3,1},{4,0},{5,7},{6,2},{7,5},{8,12},{9,11},{10,... | collective-permute-start | bytes 442376 | tf_op jit(solution)/shard_map/ppermute | solution.py:35
  14.9 3.6 %collective-permute-done.4 = bf16[4,144,128]{2,1,0:T(8,128)(2,1)S(1)} collective-permute-done((bf16[4,144,128]{2,1,0:T(8,128)(2,1)S(1)}, bf16[4,144,128]{2,1,0:T(8,128)(2,1)S(1)}, u32[]{:S(2)}, u32[]{:S(2)}) %collective-permute-start.4) | collective-permute-done | bytes 147488 | tf_op jit(solution)/shard_map/ppermute | solution.py:35
  18.6 1.6 %collective-permute-start.5 = (bf16[8,144,128]{2,1,0:T(8,128)(2,1)S(1)}, bf16[8,144,128]{2,1,0:T(8,128)(2,1)S(1)}, u32[]{:S(2)}, u32[]{:S(2)}) collective-permute-start(bf16[8,144,128]{2,1,0:T(8,128)(2,1)S(1)} %get-tuple-element.22), channel_id=1, source_target_pairs={{0,2},{1,5},{2,0},{3,7},{4,6},{5,1},{6,4},{7,3},{8,10},{9,13},{10,... | collective-permute-start | bytes 884744 | tf_op jit(solution)/shard_map/ppermute | solution.py:35
  20.2 5.2 %collective-permute-done.5 = bf16[8,144,128]{2,1,0:T(8,128)(2,1)S(1)} collective-permute-done((bf16[8,144,128]{2,1,0:T(8,128)(2,1)S(1)}, bf16[8,144,128]{2,1,0:T(8,128)(2,1)S(1)}, u32[]{:S(2)}, u32[]{:S(2)}) %collective-permute-start.5) | collective-permute-done | bytes 294944 | tf_op jit(solution)/shard_map/ppermute | solution.py:35
  25.4 0.6 %gather_fusion.3 = bf16[9,144,128]{2,1,0:T(8,128)(2,1)S(1)} fusion(bf16[16,144,128]{2,1,0:T(8,128)(2,1)S(1)} %constant_dynamic-update-slice_fusion.5, s32[1024]{0:T(1024)S(1)} %pad_clamp_fusion), kind=kCustom, calls=%fused_computation.1.clone | custom fusion | bytes 663588 | tf_op jit(solution)/shard_map/jit(_take)/gather | solution.py:105
  26.2 0.6 %gather_fusion.2 = bf16[9,144,128]{2,1,0:T(8,128)(2,1)S(1)} fusion(bf16[16,144,128]{2,1,0:T(8,128)(2,1)S(1)} %constant_dynamic-update-slice_fusion.5, s32[1024]{0:T(1024)S(1)} %pad_clamp_fusion.2), kind=kCustom, calls=%fused_computation.clone | custom fusion | bytes 663588 | tf_op jit(solution)/shard_map/jit(_take)/gather | solution.py:105
  26.8 0.8 %broadcast_select_fusion.1.pieces_a_ref = bf16[9,144,128]{2,1,0:T(8,128)(2,1)} fusion(bf16[9,144,128]{2,1,0:T(8,128)(2,1)S(1)} %gather_fusion.2, pred[9]{0:T(512)(128)(4,1)S(1)} %get-tuple-element.32), kind=kLoop, calls=%fused_computation.5 | loop fusion | flops 165888 | bytes 663561 | tf_op jit(solution)/shard_map/jit(_take)/select_n | solution.py:105
  27.7 0.2 collective-permute-done.6.pieces_b_ref
  27.8 0.6 %copy-done.2 = bf16[1040,128]{1,0:T(8,128)(2,1)} copy-done((bf16[1040,128]{1,0:T(8,128)(2,1)}, bf16[1040,128]{1,0:T(8,128)(2,1)S(1)}, u32[]{:S(2)}) %copy-start.2) | copy-done | bytes 266264
  28.4 0.7 %copy-done.1 = bf16[9,144,128]{2,1,0:T(8,128)(2,1)} copy-done((bf16[9,144,128]{2,1,0:T(8,128)(2,1)}, bf16[9,144,128]{2,1,0:T(8,128)(2,1)S(1)}, u32[]{:S(2)}) %copy-start.1) | copy-done | bytes 331800
  29.1 5.2 %shard_map.46 = bf16[1024,1024]{1,0:T(8,128)(2,1)} custom-call(bf16[1024,1024]{1,0:T(8,128)(2,1)} %matrix_ref.1, bf16[1040,128]{1,0:T(8,128)(2,1)} %copy-done, bf16[1040,128]{1,0:T(8,128)(2,1)} %copy-done.2, bf16[9,144,128]{2,1,0:T(8,128)(2,1)} %broadcast_select_fusion.1.pieces_a_ref, bf16[9,144,128]{2,1,0:T(8,128)(2,1)} %copy-done.1, ...), custom_call_target="tpu_custom_call" | custom-call | flops 637534208 | bytes 4194304 | tf_op jit(solution)/shard_map/pallas_call | solution.py:217
  (36 shorter events, 1.0 us)
Async XLA Ops:
  3.3 8.3 %collective-permute-start.3 = (bf16[1,144,128]{2,1,0:T(8,128)(2,1)S(1)}, bf16[1,144,128]{2,1,0:T(8,128)(2,1)S(1)}, u32[]{:S(2)}, u32[]{:S(2)}) collective-permute-start(bf16[1,144,128]{2,1,0:T(8,128)(2,1)S(1)} %maximum_bitcast_fusion), channel_id=1, source_target_pairs={{0,24},{1,25},{2,26},{3,27},{4,28},{5,29},{6,30},{7,31},{8,16},{9,... | collective-permute-start | bytes 110600 | tf_op jit(solution)/shard_map/ppermute | solution.py:35
  8.4 4.0 %collective-permute-start.2 = (bf16[1,144,128]{2,1,0:T(8,128)(2,1)S(1)}, bf16[1,144,128]{2,1,0:T(8,128)(2,1)S(1)}, u32[]{:S(2)}, u32[]{:S(2)}) collective-permute-start(bf16[1,144,128]{2,1,0:T(8,128)(2,1)S(1)} %maximum_bitcast_fusion), channel_id=1, source_target_pairs={{0,8},{1,17},{2,10},{3,19},{4,12},{5,21},{6,14},{7,23},{8,0},{9,25... | collective-permute-start | bytes 110600 | tf_op jit(solution)/shard_map/ppermute | solution.py:35
  8.4 4.9 %collective-permute-start.1 = (bf16[1,144,128]{2,1,0:T(8,128)(2,1)S(1)}, bf16[1,144,128]{2,1,0:T(8,128)(2,1)S(1)}, u32[]{:S(2)}, u32[]{:S(2)}) collective-permute-start(bf16[1,144,128]{2,1,0:T(8,128)(2,1)S(1)} %maximum_bitcast_fusion), channel_id=1, source_target_pairs={{0,16},{1,9},{2,18},{3,11},{4,20},{5,13},{6,22},{7,15},{8,24},{9,1... | collective-permute-start | bytes 110600 | tf_op jit(solution)/shard_map/ppermute | solution.py:35
  9.3 16.9 %copy-start = (bf16[1040,128]{1,0:T(8,128)(2,1)}, bf16[1040,128]{1,0:T(8,128)(2,1)S(1)}, u32[]{:S(2)}) copy-start(bf16[1040,128]{1,0:T(8,128)(2,1)S(1)} %pad_maximum_fusion.cols_a_ref) | copy-start | bytes 798724
  9.3 18.4 %collective-permute-start = (bf16[1040,128]{1,0:T(8,128)(2,1)S(1)}, bf16[1040,128]{1,0:T(8,128)(2,1)S(1)}, u32[]{:S(2)}, u32[]{:S(2)}) collective-permute-start(bf16[1040,128]{1,0:T(8,128)(2,1)S(1)} %pad_maximum_fusion.cols_a_ref), channel_id=1, source_target_pairs={{0,1},{1,0},{2,3},{3,2},{4,5},{5,4},{6,7},{7,6},{8,9},{9,8},{10,11... | collective-permute-start | bytes 798728 | tf_op jit(solution)/shard_map/ppermute | solution.py:111
  13.3 5.2 %collective-permute-start.4 = (bf16[4,144,128]{2,1,0:T(8,128)(2,1)S(1)}, bf16[4,144,128]{2,1,0:T(8,128)(2,1)S(1)}, u32[]{:S(2)}, u32[]{:S(2)}) collective-permute-start(bf16[4,144,128]{2,1,0:T(8,128)(2,1)S(1)} %pad_maximum_fusion.1), channel_id=1, source_target_pairs={{0,4},{1,3},{2,6},{3,1},{4,0},{5,7},{6,2},{7,5},{8,12},{9,11},{10,... | collective-permute-start | bytes 442376 | tf_op jit(solution)/shard_map/ppermute | solution.py:35
  18.6 6.8 %collective-permute-start.5 = (bf16[8,144,128]{2,1,0:T(8,128)(2,1)S(1)}, bf16[8,144,128]{2,1,0:T(8,128)(2,1)S(1)}, u32[]{:S(2)}, u32[]{:S(2)}) collective-permute-start(bf16[8,144,128]{2,1,0:T(8,128)(2,1)S(1)} %get-tuple-element.22), channel_id=1, source_target_pairs={{0,2},{1,5},{2,0},{3,7},{4,6},{5,1},{6,4},{7,3},{8,10},{9,13},{10,... | collective-permute-start | bytes 884744 | tf_op jit(solution)/shard_map/ppermute | solution.py:35
  26.1 1.7 %collective-permute-start.6 = (bf16[9,144,128]{2,1,0:T(8,128)(2,1)S(1)}, bf16[9,144,128]{2,1,0:T(8,128)(2,1)S(1)}, u32[]{:S(2)}, u32[]{:S(2)}) collective-permute-start(bf16[9,144,128]{2,1,0:T(8,128)(2,1)S(1)} %broadcast_select_fusion), channel_id=1, source_target_pairs={{0,1},{1,0},{2,3},{3,2},{4,5},{5,4},{6,7},{7,6},{8,9},{9,8},{10,11... | collective-permute-start | bytes 995336 | tf_op jit(solution)/shard_map/ppermute | solution.py:114
  27.7 0.7 %copy-start.2 = (bf16[1040,128]{1,0:T(8,128)(2,1)}, bf16[1040,128]{1,0:T(8,128)(2,1)S(1)}, u32[]{:S(2)}) copy-start(bf16[1040,128]{1,0:T(8,128)(2,1)S(1)} %collective-permute-done.cols_b_ref) | copy-start | bytes 798724
  28.4 0.7 %copy-start.1 = (bf16[9,144,128]{2,1,0:T(8,128)(2,1)}, bf16[9,144,128]{2,1,0:T(8,128)(2,1)S(1)}, u32[]{:S(2)}) copy-start(bf16[9,144,128]{2,1,0:T(8,128)(2,1)S(1)} %collective-permute-done.6.pieces_b_ref) | copy-start | bytes 995332

commit v7 on v6

--- a/solution.py
+++ b/solution.py
@@ -35,17 +35,13 @@
         return lax.ppermute(value, ("row", "col"), perm)
 
     held = piece[None]
-    first = 0
-    if bits >= 2:
+    for start in range(0, bits, 2):
+        groups = ((start,), (start + 1,), (start, start + 1)) if start + 1 < bits else ((start,),)
         parts = [held]
-        for chosen in ((0,), (1,), (0, 1)):
+        for chosen in groups:
             masks = [sum(1 << order[p] for p in chosen) for order in (even, odd)]
             parts.append(exchange(held, masks))
         held = jnp.concatenate(parts, axis=0)
-        first = 2
-    for step in range(first, bits):
-        masks = [1 << order[step] for order in (even, odd)]
-        held = jnp.concatenate((held, exchange(held, masks)), axis=0)
 
     def slot_of(owner, order_parity):
         diff = jnp.bitwise_xor(owner, me)

time: 34.6 us -> 31.5 us (0.910)
  waiting for transfers between devices: 10.6 us -> 7.1 us
  starting transfers between devices: 9.04 us -> 9.46 us
    ppermute x5 -> x6, waiting for transfers between devices: 10.4 us -> 6.97 us  [exchange(): return lax.ppermute(value, ('row', 'col'), perm)]
    ppermute x5 -> x6, starting transfers between devices: 8.9 us -> 9.31 us  [exchange(): return lax.ppermute(value, ('row', 'col'), perm)]
    unnamed x9 -> x11, local copies, waits for them, and re-layouts: 1.33 us -> 1.39 us
  transfers between devices with their start and end apart: 7 -> 8, of which waited for: 5 -> 5; matrix products, arithmetic and copies ran while one was open for 14% -> 15% of each run, Pallas kernels for 0% -> 0%
where the time goes in v7:
time: 31.5 us; the launch traced here: 31.3 us
  starting transfers between devices  9.46 us (30%)
  waiting for transfers between devices  7.1 us (23%)
  Pallas kernels  5.24 us (17%)
  local copies, waits for them, and re-layouts  5.2 us (17%)
  other arithmetic  3.69 us (12%)
  matrix products  0.38 us (1%)
    ppermute x6, starting transfers between devices, exchange(): return lax.ppermute(value, ('row', 'col'), perm)  9.31 us
    ppermute x6, waiting for transfers between devices, exchange(): return lax.ppermute(value, ('row', 'col'), perm)  6.97 us
    pallas_call x1, Pallas kernels, factor_call(): pl.pallas_call(functools.partial(factor_kernel, by_col=by_col), out_shape...  5.24 us
    unnamed x11, local copies, waits for them, and re-layouts  1.39 us
    gather x2, local copies, waits for them, and re-layouts, pick(): slots = slot_of(owner_row[wanted], order_parity)  1.32 us
    gather x2, local copies, waits for them, and re-layouts, pick(): return jnp.take(pieces, slots, axis=0)  1.22 us
    slice x1, local copies, waits for them, and re-layouts, shards(): payload = jnp.concatenate((matrix[:, :PW], mask_rows), axis=0)  0.97 us
    select_n x2, other arithmetic, pick(): return jnp.take(pieces, slots, axis=0)  0.94 us
  transfers between devices with their start and end apart: 8, of which 5 were waited for; matrix products, arithmetic and copies ran while one was open for 15% of the time, Pallas kernels for 0%

profile of v7, /device:TPU:0, one launch (start us, length us, event | category | flops | bytes accessed | tf_op | source)
XLA Modules:
  0.0 31.3 jit_solution(15271587988318351538)
XLA Ops:
  0.0 0.7 %convert_element_type.25 = bf16[4,8]{1,0:T(4,128)(2,1)S(1)} convert(s32[4,8]{1,0:T(4,128)} %mask_ref.1) | non-fusion elementwise | flops 32 | bytes 192 | tf_op jit(solution)/shard_map/convert_element_type | solution.py:67
  1.0 0.8 %convert_reduce_fusion = s32[8]{0:T(128)S(1)} fusion(s32[16]{0:T(128)} %param.10, s32[8]{0:T(128)S(1)} %iota_add_fusion), kind=kLoop, calls=%fused_computation.27 | loop fusion | flops 376 | bytes 128 | tf_op jit(solution)/shard_map/reduce_sum | solution.py:71
  2.0 1.0 %slice.25 = bf16[1024,128]{1,0:T(8,128)(2,1)S(1)} slice(bf16[1024,1024]{1,0:T(8,128)(2,1)} %matrix_ref.1), slice={[0:1024], [0:128]} | slice | bytes 524288 | tf_op jit(solution)/shard_map/slice | solution.py:93
  3.0 0.3 fusion
  3.3 5.1 %collective-permute-start.3 = (bf16[1,144,128]{2,1,0:T(8,128)(2,1)S(1)}, bf16[1,144,128]{2,1,0:T(8,128)(2,1)S(1)}, u32[]{:S(2)}, u32[]{:S(2)}) collective-permute-start(bf16[1,144,128]{2,1,0:T(8,128)(2,1)S(1)} %maximum_bitcast_fusion), channel_id=1, source_target_pairs={{0,24},{1,25},{2,26},{3,27},{4,28},{5,29},{6,30},{7,31},{8,16},{9,... | collective-permute-start | bytes 110600 | tf_op jit(solution)/shard_map/ppermute | solution.py:35
  8.4 0.6 %collective-permute-start.1 = (bf16[1,144,128]{2,1,0:T(8,128)(2,1)S(1)}, bf16[1,144,128]{2,1,0:T(8,128)(2,1)S(1)}, u32[]{:S(2)}, u32[]{:S(2)}) collective-permute-start(bf16[1,144,128]{2,1,0:T(8,128)(2,1)S(1)} %maximum_bitcast_fusion), channel_id=1, source_target_pairs={{0,16},{1,9},{2,18},{3,11},{4,20},{5,13},{6,22},{7,15},{8,24},{9,1... | collective-permute-start | bytes 110600 | tf_op jit(solution)/shard_map/ppermute | solution.py:35
  9.1 0.2 pad_maximum_fusion.cols_a_ref
  9.4 0.7 %and_select_fusion = s32[16]{0:T(128)S(1)} fusion(s32[16]{0:T(128)} %param.10), kind=kLoop, calls=%fused_computation.34 | loop fusion | flops 240 | bytes 128 | tf_op jit(solution)/shard_map/jit(floor_divide)/jit(_where)/select_n | solution.py:69
  10.3 0.7 %gather_fusion.1 = s32[9]{0:T(128)S(1)} fusion(s32[16]{0:T(128)S(1)} %and_select_fusion, s32[1024]{0:T(1024)S(1)} %pad_clamp_fusion.1), kind=kCustom, calls=%fused_computation.3 | custom fusion | bytes 108 | tf_op jit(solution)/shard_map/gather | solution.py:100
  10.9 0.7 %gather_fusion = s32[9]{0:T(128)S(1)} fusion(s32[16]{0:T(128)S(1)} %and_select_fusion, s32[1024]{0:T(1024)S(1)} %pad_clamp_fusion.3), kind=kCustom, calls=%fused_computation.2 | custom fusion | bytes 108 | tf_op jit(solution)/shard_map/gather | solution.py:100
  11.6 0.7 %collective-permute-done.2 = bf16[1,144,128]{2,1,0:T(8,128)(2,1)S(1)} collective-permute-done((bf16[1,144,128]{2,1,0:T(8,128)(2,1)S(1)}, bf16[1,144,128]{2,1,0:T(8,128)(2,1)S(1)}, u32[]{:S(2)}, u32[]{:S(2)}) %collective-permute-start.2) | collective-permute-done | bytes 36896 | tf_op jit(solution)/shard_map/ppermute | solution.py:35
  12.4 0.9 %collective-permute-done.1 = bf16[1,144,128]{2,1,0:T(8,128)(2,1)S(1)} collective-permute-done((bf16[1,144,128]{2,1,0:T(8,128)(2,1)S(1)}, bf16[1,144,128]{2,1,0:T(8,128)(2,1)S(1)}, u32[]{:S(2)}, u32[]{:S(2)}) %collective-permute-start.1) | collective-permute-done | bytes 36896 | tf_op jit(solution)/shard_map/ppermute | solution.py:35
  13.3 2.5 %collective-permute-start.6 = (bf16[4,144,128]{2,1,0:T(8,128)(2,1)S(1)}, bf16[4,144,128]{2,1,0:T(8,128)(2,1)S(1)}, u32[]{:S(2)}, u32[]{:S(2)}) collective-permute-start(bf16[4,144,128]{2,1,0:T(8,128)(2,1)S(1)} %pad_maximum_fusion.1), channel_id=1, source_target_pairs={{0,6},{1,7},{2,4},{3,5},{4,2},{5,3},{6,0},{7,1},{8,14},{9,15},{10,... | collective-permute-start | bytes 442376 | tf_op jit(solution)/shard_map/ppermute | solution.py:35
  15.8 0.5 %collective-permute-start.5 = (bf16[4,144,128]{2,1,0:T(8,128)(2,1)S(1)}, bf16[4,144,128]{2,1,0:T(8,128)(2,1)S(1)}, u32[]{:S(2)}, u32[]{:S(2)}) collective-permute-start(bf16[4,144,128]{2,1,0:T(8,128)(2,1)S(1)} %pad_maximum_fusion.1), channel_id=1, source_target_pairs={{0,2},{1,5},{2,0},{3,7},{4,6},{5,1},{6,4},{7,3},{8,10},{9,13},{10,... | collective-permute-start | bytes 442376 | tf_op jit(solution)/shard_map/ppermute | solution.py:35
  16.3 0.5 %collective-permute-start.4 = (bf16[4,144,128]{2,1,0:T(8,128)(2,1)S(1)}, bf16[4,144,128]{2,1,0:T(8,128)(2,1)S(1)}, u32[]{:S(2)}, u32[]{:S(2)}) collective-permute-start(bf16[4,144,128]{2,1,0:T(8,128)(2,1)S(1)} %pad_maximum_fusion.1), channel_id=1, source_target_pairs={{0,4},{1,3},{2,6},{3,1},{4,0},{5,7},{6,2},{7,5},{8,12},{9,11},{10,... | collective-permute-start | bytes 442376 | tf_op jit(solution)/shard_map/ppermute | solution.py:35
  16.9 5.2 %collective-permute-done.4 = bf16[4,144,128]{2,1,0:T(8,128)(2,1)S(1)} collective-permute-done((bf16[4,144,128]{2,1,0:T(8,128)(2,1)S(1)}, bf16[4,144,128]{2,1,0:T(8,128)(2,1)S(1)}, u32[]{:S(2)}, u32[]{:S(2)}) %collective-permute-start.4) | collective-permute-done | bytes 147488 | tf_op jit(solution)/shard_map/ppermute | solution.py:35
  22.1 0.2 collective-permute-done.5
  22.3 0.6 %gather_fusion.3 = bf16[9,144,128]{2,1,0:T(8,128)(2,1)S(1)} fusion(bf16[16,144,128]{2,1,0:T(8,128)(2,1)S(1)} %constant_dynamic-update-slice_fusion, s32[1024]{0:T(1024)S(1)} %pad_clamp_fusion), kind=kCustom, calls=%fused_computation.1.clone | custom fusion | bytes 663588 | tf_op jit(solution)/shard_map/jit(_take)/gather | solution.py:101
  23.1 0.6 %gather_fusion.2 = bf16[9,144,128]{2,1,0:T(8,128)(2,1)S(1)} fusion(bf16[16,144,128]{2,1,0:T(8,128)(2,1)S(1)} %constant_dynamic-update-slice_fusion, s32[1024]{0:T(1024)S(1)} %pad_clamp_fusion.2), kind=kCustom, calls=%fused_computation.clone | custom fusion | bytes 663588 | tf_op jit(solution)/shard_map/jit(_take)/gather | solution.py:101
  23.8 0.8 %broadcast_select_fusion.1.pieces_a_ref = bf16[9,144,128]{2,1,0:T(8,128)(2,1)} fusion(bf16[9,144,128]{2,1,0:T(8,128)(2,1)S(1)} %gather_fusion.2, pred[9]{0:T(512)(128)(4,1)S(1)} %get-tuple-element.22), kind=kLoop, calls=%fused_computation.5 | loop fusion | flops 165888 | bytes 663561 | tf_op jit(solution)/shard_map/jit(_take)/select_n | solution.py:101
  24.6 0.1 collective-permute-done.7.pieces_b_ref
  24.7 0.6 %copy-done.2 = bf16[1040,128]{1,0:T(8,128)(2,1)} copy-done((bf16[1040,128]{1,0:T(8,128)(2,1)}, bf16[1040,128]{1,0:T(8,128)(2,1)S(1)}, u32[]{:S(2)}) %copy-start.2) | copy-done | bytes 266264
  25.3 0.7 %copy-done.1 = bf16[9,144,128]{2,1,0:T(8,128)(2,1)} copy-done((bf16[9,144,128]{2,1,0:T(8,128)(2,1)}, bf16[9,144,128]{2,1,0:T(8,128)(2,1)S(1)}, u32[]{:S(2)}) %copy-start.1) | copy-done | bytes 331800
  26.0 5.2 %shard_map.46 = bf16[1024,1024]{1,0:T(8,128)(2,1)} custom-call(bf16[1024,1024]{1,0:T(8,128)(2,1)} %matrix_ref.1, bf16[1040,128]{1,0:T(8,128)(2,1)} %copy-done, bf16[1040,128]{1,0:T(8,128)(2,1)} %copy-done.2, bf16[9,144,128]{2,1,0:T(8,128)(2,1)} %broadcast_select_fusion.1.pieces_a_ref, bf16[9,144,128]{2,1,0:T(8,128)(2,1)} %copy-done.1, ...), custom_call_target="tpu_custom_call" | custom-call | flops 637534208 | bytes 4194304 | tf_op jit(solution)/shard_map/pallas_call | solution.py:213
  (39 shorter events, 1.1 us)
Async XLA Ops:
  3.3 8.3 %collective-permute-start.3 = (bf16[1,144,128]{2,1,0:T(8,128)(2,1)S(1)}, bf16[1,144,128]{2,1,0:T(8,128)(2,1)S(1)}, u32[]{:S(2)}, u32[]{:S(2)}) collective-permute-start(bf16[1,144,128]{2,1,0:T(8,128)(2,1)S(1)} %maximum_bitcast_fusion), channel_id=1, source_target_pairs={{0,24},{1,25},{2,26},{3,27},{4,28},{5,29},{6,30},{7,31},{8,16},{9,... | collective-permute-start | bytes 110600 | tf_op jit(solution)/shard_map/ppermute | solution.py:35
  8.4 4.0 %collective-permute-start.2 = (bf16[1,144,128]{2,1,0:T(8,128)(2,1)S(1)}, bf16[1,144,128]{2,1,0:T(8,128)(2,1)S(1)}, u32[]{:S(2)}, u32[]{:S(2)}) collective-permute-start(bf16[1,144,128]{2,1,0:T(8,128)(2,1)S(1)} %maximum_bitcast_fusion), channel_id=1, source_target_pairs={{0,8},{1,17},{2,10},{3,19},{4,12},{5,21},{6,14},{7,23},{8,0},{9,25... | collective-permute-start | bytes 110600 | tf_op jit(solution)/shard_map/ppermute | solution.py:35
  8.4 4.9 %collective-permute-start.1 = (bf16[1,144,128]{2,1,0:T(8,128)(2,1)S(1)}, bf16[1,144,128]{2,1,0:T(8,128)(2,1)S(1)}, u32[]{:S(2)}, u32[]{:S(2)}) collective-permute-start(bf16[1,144,128]{2,1,0:T(8,128)(2,1)S(1)} %maximum_bitcast_fusion), channel_id=1, source_target_pairs={{0,16},{1,9},{2,18},{3,11},{4,20},{5,13},{6,22},{7,15},{8,24},{9,1... | collective-permute-start | bytes 110600 | tf_op jit(solution)/shard_map/ppermute | solution.py:35
  9.3 14.5 %copy-start = (bf16[1040,128]{1,0:T(8,128)(2,1)}, bf16[1040,128]{1,0:T(8,128)(2,1)S(1)}, u32[]{:S(2)}) copy-start(bf16[1040,128]{1,0:T(8,128)(2,1)S(1)} %pad_maximum_fusion.cols_a_ref) | copy-start | bytes 798724
  9.3 15.3 %collective-permute-start = (bf16[1040,128]{1,0:T(8,128)(2,1)S(1)}, bf16[1040,128]{1,0:T(8,128)(2,1)S(1)}, u32[]{:S(2)}, u32[]{:S(2)}) collective-permute-start(bf16[1040,128]{1,0:T(8,128)(2,1)S(1)} %pad_maximum_fusion.cols_a_ref), channel_id=1, source_target_pairs={{0,1},{1,0},{2,3},{3,2},{4,5},{5,4},{6,7},{7,6},{8,9},{9,8},{10,11... | collective-permute-start | bytes 798728 | tf_op jit(solution)/shard_map/ppermute | solution.py:107
  13.3 9.0 %collective-permute-start.6 = (bf16[4,144,128]{2,1,0:T(8,128)(2,1)S(1)}, bf16[4,144,128]{2,1,0:T(8,128)(2,1)S(1)}, u32[]{:S(2)}, u32[]{:S(2)}) collective-permute-start(bf16[4,144,128]{2,1,0:T(8,128)(2,1)S(1)} %pad_maximum_fusion.1), channel_id=1, source_target_pairs={{0,6},{1,7},{2,4},{3,5},{4,2},{5,3},{6,0},{7,1},{8,14},{9,15},{10,... | collective-permute-start | bytes 442376 | tf_op jit(solution)/shard_map/ppermute | solution.py:35
  15.8 6.4 %collective-permute-start.5 = (bf16[4,144,128]{2,1,0:T(8,128)(2,1)S(1)}, bf16[4,144,128]{2,1,0:T(8,128)(2,1)S(1)}, u32[]{:S(2)}, u32[]{:S(2)}) collective-permute-start(bf16[4,144,128]{2,1,0:T(8,128)(2,1)S(1)} %pad_maximum_fusion.1), channel_id=1, source_target_pairs={{0,2},{1,5},{2,0},{3,7},{4,6},{5,1},{6,4},{7,3},{8,10},{9,13},{10,... | collective-permute-start | bytes 442376 | tf_op jit(solution)/shard_map/ppermute | solution.py:35
  16.3 5.7 %collective-permute-start.4 = (bf16[4,144,128]{2,1,0:T(8,128)(2,1)S(1)}, bf16[4,144,128]{2,1,0:T(8,128)(2,1)S(1)}, u32[]{:S(2)}, u32[]{:S(2)}) collective-permute-start(bf16[4,144,128]{2,1,0:T(8,128)(2,1)S(1)} %pad_maximum_fusion.1), channel_id=1, source_target_pairs={{0,4},{1,3},{2,6},{3,1},{4,0},{5,7},{6,2},{7,5},{8,12},{9,11},{10,... | collective-permute-start | bytes 442376 | tf_op jit(solution)/shard_map/ppermute | solution.py:35
  23.0 1.7 %collective-permute-start.7 = (bf16[9,144,128]{2,1,0:T(8,128)(2,1)S(1)}, bf16[9,144,128]{2,1,0:T(8,128)(2,1)S(1)}, u32[]{:S(2)}, u32[]{:S(2)}) collective-permute-start(bf16[9,144,128]{2,1,0:T(8,128)(2,1)S(1)} %broadcast_select_fusion), channel_id=1, source_target_pairs={{0,1},{1,0},{2,3},{3,2},{4,5},{5,4},{6,7},{7,6},{8,9},{9,8},{10,11... | collective-permute-start | bytes 995336 | tf_op jit(solution)/shard_map/ppermute | solution.py:110
  24.6 0.7 %copy-start.2 = (bf16[1040,128]{1,0:T(8,128)(2,1)}, bf16[1040,128]{1,0:T(8,128)(2,1)S(1)}, u32[]{:S(2)}) copy-start(bf16[1040,128]{1,0:T(8,128)(2,1)S(1)} %collective-permute-done.cols_b_ref) | copy-start | bytes 798724
  25.3 0.7 %copy-start.1 = (bf16[9,144,128]{2,1,0:T(8,128)(2,1)}, bf16[9,144,128]{2,1,0:T(8,128)(2,1)S(1)}, u32[]{:S(2)}) copy-start(bf16[9,144,128]{2,1,0:T(8,128)(2,1)S(1)} %collective-permute-done.7.pieces_b_ref) | copy-start | bytes 995332

commit v8 on v7

--- a/solution.py
+++ b/solution.py
@@ -121,12 +121,35 @@
 
 
 def factor_kernel(
-    matrix_ref, cols_a_ref, cols_b_ref, pieces_a_ref, pieces_b_ref, inv_ref, mask_ref, out_ref, *, by_col
+    matrix_hbm, cols_a_hbm, cols_b_hbm, pieces_a_hbm, pieces_b_hbm, inv_ref, mask_ref, out_hbm,
+    matrix_ref, cols_a_ref, cols_b_ref, pieces_a_ref, pieces_b_ref, out_ref, in_sems, matrix_sems, out_sems,
+    *, by_col
 ):
     local_rows, width = matrix_ref.shape
     col_panels = width // PW
     block_rows = local_rows // RB
     picks = pieces_a_ref.shape[0]
+    small = [
+        pltpu.make_async_copy(src, dst, in_sems.at[i])
+        for i, (src, dst) in enumerate(
+            (
+                (pieces_a_hbm, pieces_a_ref),
+                (pieces_b_hbm, pieces_b_ref),
+                (cols_a_hbm, cols_a_ref),
+                (cols_b_hbm, cols_b_ref),
+            )
+        )
+    ]
+    for copy in small:
+        copy.start()
+    matrix_in = []
+    for b in range(block_rows):
+        rows = pl.ds(b * RB, RB)
+        copy = pltpu.make_async_copy(matrix_hbm.at[rows], matrix_ref.at[rows], matrix_sems.at[b])
+        copy.start()
+        matrix_in.append(copy)
+    small[0].wait()
+    small[1].wait()
     col_index = lax.axis_index("col")
     swapped = (col_index != FIRST_COL) if by_col else False
 
@@ -172,6 +195,8 @@
         * flags_second[:col_panels].astype(jnp.float32)
     ).astype(jnp.bfloat16)
 
+    small[2].wait()
+    small[3].wait()
     cols_first, cols_second = first_second(cols_a_ref, cols_b_ref, slice(0, local_rows))
     rows_first, rows_second = first_second(
         cols_a_ref, cols_b_ref, slice(local_rows, local_rows + block_rows)
@@ -189,13 +214,18 @@
     ).astype(jnp.bfloat16).reshape(local_rows, PW)
     both_panels = jnp.concatenate((first_panel, second_panel), axis=1)
 
-    for j in range(col_panels):
-        cols = slice(j * PW, (j + 1) * PW)
-        both_diag = jnp.concatenate((diag_first[j], diag_second[j]), axis=1)
-        schur = matrix_ref[:, cols].astype(jnp.float32) - dot_t(both_panels, both_diag)
-        for b in range(block_rows):
-            rows = slice(b * RB, (b + 1) * RB)
-            tile = (schur[rows] * mask_ref[b, j].astype(jnp.float32)).astype(jnp.bfloat16)
+    both_diag = [
+        jnp.concatenate((diag_first[j], diag_second[j]), axis=1) for j in range(col_panels)
+    ]
+    matrix_out = []
+    for b in range(block_rows):
+        rows = slice(b * RB, (b + 1) * RB)
+        matrix_in[b].wait()
+        panels_rows = both_panels[rows]
+        for j in range(col_panels):
+            cols = slice(j * PW, (j + 1) * PW)
+            schur = matrix_ref[rows, cols].astype(jnp.float32) - dot_t(panels_rows, both_diag[j])
+            tile = (schur * mask_ref[b, j].astype(jnp.float32)).astype(jnp.bfloat16)
             if j == 0:
                 tile = jnp.where(
                     col_index == FIRST_COL,
@@ -203,18 +233,37 @@
                     jnp.where(col_index == SECOND_COL, second_panel[rows], tile),
                 )
             out_ref[rows, cols] = tile
+        copy = pltpu.make_async_copy(
+            out_ref.at[pl.ds(b * RB, RB)], out_hbm.at[pl.ds(b * RB, RB)], out_sems.at[b]
+        )
+        copy.start()
+        matrix_out.append(copy)
+    for copy in matrix_out:
+        copy.wait()
 
 
 def factor_call(matrix, cols_a, cols_b, pieces_a, pieces_b, inverses, fill_mask, by_col):
     local_rows, width = matrix.shape
     vmem = pl.BlockSpec(memory_space=pltpu.VMEM)
     smem = pl.BlockSpec(memory_space=pltpu.SMEM)
+    hbm = pl.BlockSpec(memory_space=pl.ANY)
     flops = 2 * local_rows * width * 2 * PW + 6 * local_rows * PW * PW
     return pl.pallas_call(
         functools.partial(factor_kernel, by_col=by_col),
         out_shape=jax.ShapeDtypeStruct((local_rows, width), jnp.bfloat16),
-        in_specs=[vmem] * 6 + [smem],
-        out_specs=vmem,
+        in_specs=[hbm] * 5 + [vmem, smem],
+        out_specs=hbm,
+        scratch_shapes=[
+            pltpu.VMEM((local_rows, width), jnp.bfloat16),
+            pltpu.VMEM(cols_a.shape, jnp.bfloat16),
+            pltpu.VMEM(cols_b.shape, jnp.bfloat16),
+            pltpu.VMEM(pieces_a.shape, jnp.bfloat16),
+            pltpu.VMEM(pieces_b.shape, jnp.bfloat16),
+            pltpu.VMEM((local_rows, width), jnp.bfloat16),
+            pltpu.SemaphoreType.DMA((4,)),
+            pltpu.SemaphoreType.DMA((local_rows // RB,)),
+            pltpu.SemaphoreType.DMA((local_rows // RB,)),
+        ],
         cost_estimate=pl.CostEstimate(
             flops=flops, bytes_accessed=4 * local_rows * width, transcendentals=0
         ),

time: 31.5 us -> 32.2 us (1.022)
  Pallas kernels: 5.24 us -> 5.92 us
    pallas_call x1, Pallas kernels: 5.24 us -> 5.92 us  [factor_call(): pl.pallas_call(functools.partial(factor_kernel, by_col=by_col), out_shape...]
where the time goes in v8:
time: 32.2 us; the launch traced here: 32 us
  starting transfers between devices  9.46 us (29%)
  waiting for transfers between devices  7.1 us (22%)
  Pallas kernels  5.92 us (18%)
  local copies, waits for them, and re-layouts  5.2 us (16%)
  other arithmetic  3.69 us (11%)
  matrix products  0.38 us (1%)
    ppermute x6, starting transfers between devices, exchange(): return lax.ppermute(value, ('row', 'col'), perm)  9.31 us
    ppermute x6, waiting for transfers between devices, exchange(): return lax.ppermute(value, ('row', 'col'), perm)  6.97 us
    pallas_call x1, Pallas kernels, factor_call(): pl.pallas_call(functools.partial(factor_kernel, by_col=by_col), out_shape...  5.92 us
    unnamed x11, local copies, waits for them, and re-layouts  1.39 us
    gather x2, local copies, waits for them, and re-layouts, pick(): slots = slot_of(owner_row[wanted], order_parity)  1.32 us
    gather x2, local copies, waits for them, and re-layouts, pick(): return jnp.take(pieces, slots, axis=0)  1.22 us
    slice x1, local copies, waits for them, and re-layouts, shards(): payload = jnp.concatenate((matrix[:, :PW], mask_rows), axis=0)  0.97 us
    select_n x2, other arithmetic, pick(): return jnp.take(pieces, slots, axis=0)  0.94 us
  transfers between devices with their start and end apart: 8, of which 5 were waited for; matrix products, arithmetic and copies ran while one was open for 15% of the time, Pallas kernels for 0%

profile of v8, /device:TPU:0, one launch (start us, length us, event | category | flops | bytes accessed | tf_op | source)
XLA Modules:
  0.0 32.0 jit_solution(2557136951891832383)
XLA Ops:
  0.0 0.7 %convert_element_type.25 = bf16[4,8]{1,0:T(4,128)(2,1)S(1)} convert(s32[4,8]{1,0:T(4,128)} %mask_ref.1) | non-fusion elementwise | flops 32 | bytes 192 | tf_op jit(solution)/shard_map/convert_element_type | solution.py:67
  1.0 0.8 %convert_reduce_fusion = s32[8]{0:T(128)S(1)} fusion(s32[16]{0:T(128)} %param.10, s32[8]{0:T(128)S(1)} %iota_add_fusion), kind=kLoop, calls=%fused_computation.27 | loop fusion | flops 376 | bytes 128 | tf_op jit(solution)/shard_map/reduce_sum | solution.py:71
  2.0 1.0 %slice.25 = bf16[1024,128]{1,0:T(8,128)(2,1)S(1)} slice(bf16[1024,1024]{1,0:T(8,128)(2,1)} %matrix_hbm.1), slice={[0:1024], [0:128]} | slice | bytes 524288 | tf_op jit(solution)/shard_map/slice | solution.py:93
  3.0 0.3 fusion
  3.3 5.1 %collective-permute-start.3 = (bf16[1,144,128]{2,1,0:T(8,128)(2,1)S(1)}, bf16[1,144,128]{2,1,0:T(8,128)(2,1)S(1)}, u32[]{:S(2)}, u32[]{:S(2)}) collective-permute-start(bf16[1,144,128]{2,1,0:T(8,128)(2,1)S(1)} %maximum_bitcast_fusion), channel_id=1, source_target_pairs={{0,24},{1,25},{2,26},{3,27},{4,28},{5,29},{6,30},{7,31},{8,16},{9,... | collective-permute-start | bytes 110600 | tf_op jit(solution)/shard_map/ppermute | solution.py:35
  8.4 0.6 %collective-permute-start.1 = (bf16[1,144,128]{2,1,0:T(8,128)(2,1)S(1)}, bf16[1,144,128]{2,1,0:T(8,128)(2,1)S(1)}, u32[]{:S(2)}, u32[]{:S(2)}) collective-permute-start(bf16[1,144,128]{2,1,0:T(8,128)(2,1)S(1)} %maximum_bitcast_fusion), channel_id=1, source_target_pairs={{0,16},{1,9},{2,18},{3,11},{4,20},{5,13},{6,22},{7,15},{8,24},{9,1... | collective-permute-start | bytes 110600 | tf_op jit(solution)/shard_map/ppermute | solution.py:35
  9.1 0.2 pad_maximum_fusion.cols_a_hbm
  9.4 0.7 %and_select_fusion = s32[16]{0:T(128)S(1)} fusion(s32[16]{0:T(128)} %param.10), kind=kLoop, calls=%fused_computation.34 | loop fusion | flops 240 | bytes 128 | tf_op jit(solution)/shard_map/jit(floor_divide)/jit(_where)/select_n | solution.py:69
  10.3 0.7 %gather_fusion.1 = s32[9]{0:T(128)S(1)} fusion(s32[16]{0:T(128)S(1)} %and_select_fusion, s32[1024]{0:T(1024)S(1)} %pad_clamp_fusion.1), kind=kCustom, calls=%fused_computation.3 | custom fusion | bytes 108 | tf_op jit(solution)/shard_map/gather | solution.py:100
  10.9 0.7 %gather_fusion = s32[9]{0:T(128)S(1)} fusion(s32[16]{0:T(128)S(1)} %and_select_fusion, s32[1024]{0:T(1024)S(1)} %pad_clamp_fusion.3), kind=kCustom, calls=%fused_computation.2 | custom fusion | bytes 108 | tf_op jit(solution)/shard_map/gather | solution.py:100
  11.6 0.7 %collective-permute-done.2 = bf16[1,144,128]{2,1,0:T(8,128)(2,1)S(1)} collective-permute-done((bf16[1,144,128]{2,1,0:T(8,128)(2,1)S(1)}, bf16[1,144,128]{2,1,0:T(8,128)(2,1)S(1)}, u32[]{:S(2)}, u32[]{:S(2)}) %collective-permute-start.2) | collective-permute-done | bytes 36896 | tf_op jit(solution)/shard_map/ppermute | solution.py:35
  12.4 0.9 %collective-permute-done.1 = bf16[1,144,128]{2,1,0:T(8,128)(2,1)S(1)} collective-permute-done((bf16[1,144,128]{2,1,0:T(8,128)(2,1)S(1)}, bf16[1,144,128]{2,1,0:T(8,128)(2,1)S(1)}, u32[]{:S(2)}, u32[]{:S(2)}) %collective-permute-start.1) | collective-permute-done | bytes 36896 | tf_op jit(solution)/shard_map/ppermute | solution.py:35
  13.3 2.5 %collective-permute-start.6 = (bf16[4,144,128]{2,1,0:T(8,128)(2,1)S(1)}, bf16[4,144,128]{2,1,0:T(8,128)(2,1)S(1)}, u32[]{:S(2)}, u32[]{:S(2)}) collective-permute-start(bf16[4,144,128]{2,1,0:T(8,128)(2,1)S(1)} %pad_maximum_fusion.1), channel_id=1, source_target_pairs={{0,6},{1,7},{2,4},{3,5},{4,2},{5,3},{6,0},{7,1},{8,14},{9,15},{10,... | collective-permute-start | bytes 442376 | tf_op jit(solution)/shard_map/ppermute | solution.py:35
  15.8 0.5 %collective-permute-start.5 = (bf16[4,144,128]{2,1,0:T(8,128)(2,1)S(1)}, bf16[4,144,128]{2,1,0:T(8,128)(2,1)S(1)}, u32[]{:S(2)}, u32[]{:S(2)}) collective-permute-start(bf16[4,144,128]{2,1,0:T(8,128)(2,1)S(1)} %pad_maximum_fusion.1), channel_id=1, source_target_pairs={{0,2},{1,5},{2,0},{3,7},{4,6},{5,1},{6,4},{7,3},{8,10},{9,13},{10,... | collective-permute-start | bytes 442376 | tf_op jit(solution)/shard_map/ppermute | solution.py:35
  16.3 0.5 %collective-permute-start.4 = (bf16[4,144,128]{2,1,0:T(8,128)(2,1)S(1)}, bf16[4,144,128]{2,1,0:T(8,128)(2,1)S(1)}, u32[]{:S(2)}, u32[]{:S(2)}) collective-permute-start(bf16[4,144,128]{2,1,0:T(8,128)(2,1)S(1)} %pad_maximum_fusion.1), channel_id=1, source_target_pairs={{0,4},{1,3},{2,6},{3,1},{4,0},{5,7},{6,2},{7,5},{8,12},{9,11},{10,... | collective-permute-start | bytes 442376 | tf_op jit(solution)/shard_map/ppermute | solution.py:35
  16.9 5.2 %collective-permute-done.4 = bf16[4,144,128]{2,1,0:T(8,128)(2,1)S(1)} collective-permute-done((bf16[4,144,128]{2,1,0:T(8,128)(2,1)S(1)}, bf16[4,144,128]{2,1,0:T(8,128)(2,1)S(1)}, u32[]{:S(2)}, u32[]{:S(2)}) %collective-permute-start.4) | collective-permute-done | bytes 147488 | tf_op jit(solution)/shard_map/ppermute | solution.py:35
  22.1 0.2 collective-permute-done.5
  22.3 0.6 %gather_fusion.3 = bf16[9,144,128]{2,1,0:T(8,128)(2,1)S(1)} fusion(bf16[16,144,128]{2,1,0:T(8,128)(2,1)S(1)} %constant_dynamic-update-slice_fusion, s32[1024]{0:T(1024)S(1)} %pad_clamp_fusion), kind=kCustom, calls=%fused_computation.1.clone | custom fusion | bytes 663588 | tf_op jit(solution)/shard_map/jit(_take)/gather | solution.py:101
  23.1 0.6 %gather_fusion.2 = bf16[9,144,128]{2,1,0:T(8,128)(2,1)S(1)} fusion(bf16[16,144,128]{2,1,0:T(8,128)(2,1)S(1)} %constant_dynamic-update-slice_fusion, s32[1024]{0:T(1024)S(1)} %pad_clamp_fusion.2), kind=kCustom, calls=%fused_computation.clone | custom fusion | bytes 663588 | tf_op jit(solution)/shard_map/jit(_take)/gather | solution.py:101
  23.8 0.8 %broadcast_select_fusion.1.pieces_a_hbm = bf16[9,144,128]{2,1,0:T(8,128)(2,1)} fusion(bf16[9,144,128]{2,1,0:T(8,128)(2,1)S(1)} %gather_fusion.2, pred[9]{0:T(512)(128)(4,1)S(1)} %get-tuple-element.22), kind=kLoop, calls=%fused_computation.5 | loop fusion | flops 165888 | bytes 663561 | tf_op jit(solution)/shard_map/jit(_take)/select_n | solution.py:101
  24.6 0.1 collective-permute-done.7.pieces_b_hbm
  24.7 0.6 %copy-done.2 = bf16[1040,128]{1,0:T(8,128)(2,1)} copy-done((bf16[1040,128]{1,0:T(8,128)(2,1)}, bf16[1040,128]{1,0:T(8,128)(2,1)S(1)}, u32[]{:S(2)}) %copy-start.2) | copy-done | bytes 266264
  25.3 0.7 %copy-done.1 = bf16[9,144,128]{2,1,0:T(8,128)(2,1)} copy-done((bf16[9,144,128]{2,1,0:T(8,128)(2,1)}, bf16[9,144,128]{2,1,0:T(8,128)(2,1)S(1)}, u32[]{:S(2)}) %copy-start.1) | copy-done | bytes 331800
  26.0 5.9 %shard_map.46 = bf16[1024,1024]{1,0:T(8,128)(2,1)} custom-call(bf16[1024,1024]{1,0:T(8,128)(2,1)} %matrix_hbm.1, bf16[1040,128]{1,0:T(8,128)(2,1)} %copy-done, bf16[1040,128]{1,0:T(8,128)(2,1)} %copy-done.2, bf16[9,144,128]{2,1,0:T(8,128)(2,1)} %broadcast_select_fusion.1.pieces_a_hbm, bf16[9,144,128]{2,1,0:T(8,128)(2,1)} %copy-done.1, ...), custom_call_target="tpu_custom_call" | custom-call | flops 637534208 | bytes 4194304 | tf_op jit(solution)/shard_map/pallas_call | solution.py:251
  (39 shorter events, 1.1 us)
Async XLA Ops:
  3.3 8.3 %collective-permute-start.3 = (bf16[1,144,128]{2,1,0:T(8,128)(2,1)S(1)}, bf16[1,144,128]{2,1,0:T(8,128)(2,1)S(1)}, u32[]{:S(2)}, u32[]{:S(2)}) collective-permute-start(bf16[1,144,128]{2,1,0:T(8,128)(2,1)S(1)} %maximum_bitcast_fusion), channel_id=1, source_target_pairs={{0,24},{1,25},{2,26},{3,27},{4,28},{5,29},{6,30},{7,31},{8,16},{9,... | collective-permute-start | bytes 110600 | tf_op jit(solution)/shard_map/ppermute | solution.py:35
  8.4 4.0 %collective-permute-start.2 = (bf16[1,144,128]{2,1,0:T(8,128)(2,1)S(1)}, bf16[1,144,128]{2,1,0:T(8,128)(2,1)S(1)}, u32[]{:S(2)}, u32[]{:S(2)}) collective-permute-start(bf16[1,144,128]{2,1,0:T(8,128)(2,1)S(1)} %maximum_bitcast_fusion), channel_id=1, source_target_pairs={{0,8},{1,17},{2,10},{3,19},{4,12},{5,21},{6,14},{7,23},{8,0},{9,25... | collective-permute-start | bytes 110600 | tf_op jit(solution)/shard_map/ppermute | solution.py:35
  8.4 4.9 %collective-permute-start.1 = (bf16[1,144,128]{2,1,0:T(8,128)(2,1)S(1)}, bf16[1,144,128]{2,1,0:T(8,128)(2,1)S(1)}, u32[]{:S(2)}, u32[]{:S(2)}) collective-permute-start(bf16[1,144,128]{2,1,0:T(8,128)(2,1)S(1)} %maximum_bitcast_fusion), channel_id=1, source_target_pairs={{0,16},{1,9},{2,18},{3,11},{4,20},{5,13},{6,22},{7,15},{8,24},{9,1... | collective-permute-start | bytes 110600 | tf_op jit(solution)/shard_map/ppermute | solution.py:35
  9.3 14.5 %copy-start = (bf16[1040,128]{1,0:T(8,128)(2,1)}, bf16[1040,128]{1,0:T(8,128)(2,1)S(1)}, u32[]{:S(2)}) copy-start(bf16[1040,128]{1,0:T(8,128)(2,1)S(1)} %pad_maximum_fusion.cols_a_hbm) | copy-start | bytes 798724
  9.3 15.3 %collective-permute-start = (bf16[1040,128]{1,0:T(8,128)(2,1)S(1)}, bf16[1040,128]{1,0:T(8,128)(2,1)S(1)}, u32[]{:S(2)}, u32[]{:S(2)}) collective-permute-start(bf16[1040,128]{1,0:T(8,128)(2,1)S(1)} %pad_maximum_fusion.cols_a_hbm), channel_id=1, source_target_pairs={{0,1},{1,0},{2,3},{3,2},{4,5},{5,4},{6,7},{7,6},{8,9},{9,8},{10,11... | collective-permute-start | bytes 798728 | tf_op jit(solution)/shard_map/ppermute | solution.py:107
  13.3 9.0 %collective-permute-start.6 = (bf16[4,144,128]{2,1,0:T(8,128)(2,1)S(1)}, bf16[4,144,128]{2,1,0:T(8,128)(2,1)S(1)}, u32[]{:S(2)}, u32[]{:S(2)}) collective-permute-start(bf16[4,144,128]{2,1,0:T(8,128)(2,1)S(1)} %pad_maximum_fusion.1), channel_id=1, source_target_pairs={{0,6},{1,7},{2,4},{3,5},{4,2},{5,3},{6,0},{7,1},{8,14},{9,15},{10,... | collective-permute-start | bytes 442376 | tf_op jit(solution)/shard_map/ppermute | solution.py:35
  15.8 6.4 %collective-permute-start.5 = (bf16[4,144,128]{2,1,0:T(8,128)(2,1)S(1)}, bf16[4,144,128]{2,1,0:T(8,128)(2,1)S(1)}, u32[]{:S(2)}, u32[]{:S(2)}) collective-permute-start(bf16[4,144,128]{2,1,0:T(8,128)(2,1)S(1)} %pad_maximum_fusion.1), channel_id=1, source_target_pairs={{0,2},{1,5},{2,0},{3,7},{4,6},{5,1},{6,4},{7,3},{8,10},{9,13},{10,... | collective-permute-start | bytes 442376 | tf_op jit(solution)/shard_map/ppermute | solution.py:35
  16.3 5.7 %collective-permute-start.4 = (bf16[4,144,128]{2,1,0:T(8,128)(2,1)S(1)}, bf16[4,144,128]{2,1,0:T(8,128)(2,1)S(1)}, u32[]{:S(2)}, u32[]{:S(2)}) collective-permute-start(bf16[4,144,128]{2,1,0:T(8,128)(2,1)S(1)} %pad_maximum_fusion.1), channel_id=1, source_target_pairs={{0,4},{1,3},{2,6},{3,1},{4,0},{5,7},{6,2},{7,5},{8,12},{9,11},{10,... | collective-permute-start | bytes 442376 | tf_op jit(solution)/shard_map/ppermute | solution.py:35
  23.0 1.7 %collective-permute-start.7 = (bf16[9,144,128]{2,1,0:T(8,128)(2,1)S(1)}, bf16[9,144,128]{2,1,0:T(8,128)(2,1)S(1)}, u32[]{:S(2)}, u32[]{:S(2)}) collective-permute-start(bf16[9,144,128]{2,1,0:T(8,128)(2,1)S(1)} %broadcast_select_fusion), channel_id=1, source_target_pairs={{0,1},{1,0},{2,3},{3,2},{4,5},{5,4},{6,7},{7,6},{8,9},{9,8},{10,11... | collective-permute-start | bytes 995336 | tf_op jit(solution)/shard_map/ppermute | solution.py:110
  24.6 0.7 %copy-start.2 = (bf16[1040,128]{1,0:T(8,128)(2,1)}, bf16[1040,128]{1,0:T(8,128)(2,1)S(1)}, u32[]{:S(2)}) copy-start(bf16[1040,128]{1,0:T(8,128)(2,1)S(1)} %collective-permute-done.cols_b_hbm) | copy-start | bytes 798724
  25.3 0.7 %copy-start.1 = (bf16[9,144,128]{2,1,0:T(8,128)(2,1)}, bf16[9,144,128]{2,1,0:T(8,128)(2,1)S(1)}, u32[]{:S(2)}) copy-start(bf16[9,144,128]{2,1,0:T(8,128)(2,1)S(1)} %collective-permute-done.7.pieces_b_hbm) | copy-start | bytes 995332

commit v9 on v7

--- a/solution.py
+++ b/solution.py
@@ -64,33 +64,10 @@
     col_panels = width // PW
     block_rows = local_rows // RB
     local_slabs = local_rows // PW
-    mask_f = fill_mask.astype(jnp.bfloat16)
 
     owner_row = col_rows // local_slabs
-    local_ids = row_index * local_slabs + jnp.arange(local_slabs, dtype=jnp.int32)
-    choose = jnp.sum((col_rows[None, :] == local_ids[:, None]).astype(jnp.int32), axis=1)
-    choose_f = choose.astype(jnp.bfloat16)
-    own_slab = jnp.einsum(
-        "s,sij->ij",
-        choose_f,
-        matrix[:, :PW].reshape(local_slabs, PW, PW),
-        preferred_element_type=jnp.float32,
-    ).astype(jnp.bfloat16)
-    slab_mask = jnp.repeat(fill_mask[:, 0], RB // PW).astype(jnp.bfloat16)
-    flag_block = jnp.where(
-        lax.broadcasted_iota(jnp.int32, (local_slabs, MASK_ROWS, PW), 1) == 0,
-        slab_mask[:, None, None],
-        jnp.bfloat16(0),
-    )
-    flag_rows = jnp.einsum(
-        "s,sij->ij", choose_f, flag_block, preferred_element_type=jnp.float32
-    ).astype(jnp.bfloat16)
-    piece = jnp.concatenate((own_slab, flag_rows), axis=0)
+    piece, payload = prep_call(matrix, col_rows, fill_mask)
     held, slot_of, parity = gather_rows(piece, row_count, col_count)
-
-    mask_rows = jnp.zeros((MASK_ROWS, PW), jnp.bfloat16)
-    mask_rows = mask_rows.at[:block_rows].set(jnp.broadcast_to(mask_f[:, 0:1], (block_rows, PW)))
-    payload = jnp.concatenate((matrix[:, :PW], mask_rows), axis=0)
 
     def wanted_of(group):
         own = group * col_panels + jnp.arange(col_panels, dtype=jnp.int32)
@@ -120,6 +97,49 @@
     )
 
 
+def prep_kernel(lead_ref, col_rows_ref, mask_ref, piece_ref, payload_ref):
+    local_rows = lead_ref.shape[0]
+    local_slabs = local_rows // PW
+    block_rows = local_rows // RB
+    row_index = lax.axis_index("row")
+    place = jnp.int32(0)
+    for c in range(col_rows_ref.shape[0]):
+        entry = col_rows_ref[c]
+        place = place + jnp.where(entry // local_slabs == row_index, entry % local_slabs, 0)
+    place = jnp.minimum(place, local_slabs - 1)
+    start = pl.multiple_of(place * PW, PW)
+    piece_ref[0:PW, :] = lead_ref[pl.ds(start, PW), :]
+    flag = mask_ref[place // (RB // PW), 0].astype(jnp.float32)
+    row_ids = lax.broadcasted_iota(jnp.int32, (MASK_ROWS, PW), 0)
+    piece_ref[PW : PW + MASK_ROWS, :] = jnp.where(row_ids == 0, flag, 0.0).astype(jnp.bfloat16)
+    payload_ref[0:local_rows, :] = lead_ref[...]
+    mask_rows = jnp.zeros((MASK_ROWS, PW), jnp.float32)
+    for b in range(block_rows):
+        mask_rows = jnp.where(row_ids == b, mask_ref[b, 0].astype(jnp.float32), mask_rows)
+    payload_ref[local_rows : local_rows + MASK_ROWS, :] = mask_rows.astype(jnp.bfloat16)
+
+
+def prep_call(matrix, col_rows, fill_mask):
+    local_rows = matrix.shape[0]
+    smem = pl.BlockSpec(memory_space=pltpu.SMEM)
+    return pl.pallas_call(
+        prep_kernel,
+        out_shape=(
+            jax.ShapeDtypeStruct((PW + MASK_ROWS, PW), jnp.bfloat16),
+            jax.ShapeDtypeStruct((local_rows + MASK_ROWS, PW), jnp.bfloat16),
+        ),
+        grid=(1,),
+        in_specs=[pl.BlockSpec((local_rows, PW), lambda i: (0, 0)), smem, smem],
+        out_specs=(
+            pl.BlockSpec((PW + MASK_ROWS, PW), lambda i: (0, 0)),
+            pl.BlockSpec((local_rows + MASK_ROWS, PW), lambda i: (0, 0)),
+        ),
+        cost_estimate=pl.CostEstimate(
+            flops=0, bytes_accessed=4 * local_rows * PW, transcendentals=0
+        ),
+    )(matrix, col_rows, fill_mask)
+
+
 def factor_kernel(
     matrix_ref, cols_a_ref, cols_b_ref, pieces_a_ref, pieces_b_ref, inv_ref, mask_ref, out_ref, *, by_col
 ):

time: 31.5 us -> 30.8 us (0.978)
  other arithmetic: 3.69 us -> 1.87 us
  Pallas kernels: 5.24 us -> 7.03 us
  local copies, waits for them, and re-layouts: 5.2 us -> 4.71 us
  waiting for transfers between devices: 7.1 us -> 7.49 us
  matrix products: 0.38 us -> 0 us
    pallas_call x0 -> x1, Pallas kernels: none -> 1.79 us  [prep_call(): pl.pallas_call(prep_kernel, out_shape=(jax.ShapeDtypeStruct((PW + MASK_RO...]
    slice x2 -> x0, local copies, waits for them, and re-layouts: 1.09 us -> none  [the longest x1 0.97 us: shards(): payload = jnp.concatenate((matrix[:, :PW], mask_rows), axis=0)]
    reduce_sum x1 -> x0, other arithmetic: 0.84 us -> none  [shards(): jnp.sum((col_rows[None, :] == local_ids[:, None]).astype(jnp.int32), axis=1)]
    concatenate x1, other arithmetic: 0.02 us -> 0.79 us  [gather_rows(): held = jnp.concatenate(parts, axis=0)]
    unnamed x11 -> x12, local copies, waits for them, and re-layouts: 1.39 us -> 2.14 us
    convert_element_type x3 -> x0, other arithmetic: 0.7 us -> none  [the longest x1 0.68 us: shards(): mask_f = fill_mask.astype(jnp.bfloat16)]
    select_n x1, other arithmetic: 0.68 us -> 0.01 us  [shards(): owner_row = col_rows // local_slabs]
    dot_general x2 -> x0, matrix products: 0.38 us -> none  [the longest x1 0.26 us: shards(): jnp.einsum('s,sij->ij', choose_f, matrix[:, :PW].reshape(local_slabs, PW,...]
  transfers between devices with their start and end apart: 8 -> 8, of which waited for: 5 -> 4; matrix products, arithmetic and copies ran while one was open for 15% -> 17% of each run, Pallas kernels for 0% -> 0%
where the time goes in v9:
time: 30.8 us; the launch traced here: 30.5 us
  starting transfers between devices  9.24 us (30%)
  waiting for transfers between devices  7.49 us (24%)
  Pallas kernels  7.03 us (23%)
  local copies, waits for them, and re-layouts  4.71 us (15%)
  other arithmetic  1.87 us (6%)
    ppermute x6, starting transfers between devices, exchange(): return lax.ppermute(value, ('row', 'col'), perm)  9.17 us
    ppermute x6, waiting for transfers between devices, exchange(): return lax.ppermute(value, ('row', 'col'), perm)  7.33 us
    pallas_call x1, Pallas kernels, factor_call(): pl.pallas_call(functools.partial(factor_kernel, by_col=by_col), out_shape...  5.24 us
    unnamed x12, local copies, waits for them, and re-layouts  2.14 us
    pallas_call x1, Pallas kernels, prep_call(): pl.pallas_call(prep_kernel, out_shape=(jax.ShapeDtypeStruct((PW + MASK_RO...  1.79 us
    gather x2, local copies, waits for them, and re-layouts, pick(): slots = slot_of(owner_row[wanted], order_parity)  1.32 us
    gather x2, local copies, waits for them, and re-layouts, pick(): return jnp.take(pieces, slots, axis=0)  1.22 us
    select_n x2, other arithmetic, pick(): return jnp.take(pieces, slots, axis=0)  0.92 us
  transfers between devices with their start and end apart: 8, of which 4 were waited for; matrix products, arithmetic and copies ran while one was open for 17% of the time, Pallas kernels for 0%

profile of v9, /device:TPU:0, one launch (start us, length us, event | category | flops | bytes accessed | tf_op | source)
XLA Modules:
  0.0 30.5 jit_solution(14802258021381287669)
XLA Ops:
  0.0 1.8 %shard_map.46 = (bf16[144,128]{1,0:T(8,128)(2,1)}, bf16[1040,128]{1,0:T(8,128)(2,1)}) custom-call(bf16[1024,1024]{1,0:T(8,128)(2,1)} %matrix_ref.1, s32[16]{0:T(128)} %col_rows_ref.1, s32[4,8]{1,0:T(4,128)} %mask_ref.3), custom_call_target="tpu_custom_call" | custom-call | bytes 524288 | tf_op jit(solution)/shard_map/pallas_call | solution.py:125
  1.8 5.0 %collective-permute-start.3 = (bf16[1,144,128]{2,1,0:T(8,128)(2,1)}, bf16[1,144,128]{2,1,0:T(8,128)(2,1)S(1)}, u32[]{:S(2)}, u32[]{:S(2)}) collective-permute-start(bf16[1,144,128]{2,1,0:T(8,128)(2,1)} %bitcast.10), channel_id=1, source_target_pairs={{0,24},{1,25},{2,26},{3,27},{4,28},{5,29},{6,30},{7,31},{8,16},{9,... | collective-permute-start | bytes 110600 | tf_op jit(solution)/shard_map/ppermute | solution.py:35
  6.8 0.0 collective-permute-start.2
  6.8 0.6 %collective-permute-start.1 = (bf16[1,144,128]{2,1,0:T(8,128)(2,1)}, bf16[1,144,128]{2,1,0:T(8,128)(2,1)S(1)}, u32[]{:S(2)}, u32[]{:S(2)}) collective-permute-start(bf16[1,144,128]{2,1,0:T(8,128)(2,1)} %bitcast.12), channel_id=1, source_target_pairs={{0,16},{1,9},{2,18},{3,11},{4,20},{5,13},{6,22},{7,15},{8,24},{9,1... | collective-permute-start | bytes 110600 | tf_op jit(solution)/shard_map/ppermute | solution.py:35
  7.4 0.8 %constant_dynamic-update-slice_fusion.6 = bf16[16,144,128]{2,1,0:T(8,128)(2,1)S(1)} fusion(bf16[144,128]{1,0:T(8,128)(2,1)} %get-tuple-element.9), kind=kLoop, calls=%fused_computation.13 | loop fusion | bytes 73728
  8.2 0.1 fusion
  8.3 0.7 %gather_fusion = s32[9]{0:T(128)S(1)} fusion(s32[16]{0:T(128)S(1)} %and_select_fusion, s32[1024]{0:T(1024)S(1)} %pad_clamp_fusion.3), kind=kCustom, calls=%fused_computation.2 | custom fusion | bytes 108 | tf_op jit(solution)/shard_map/gather | solution.py:77
  9.0 0.7 %gather_fusion.1 = s32[9]{0:T(128)S(1)} fusion(s32[16]{0:T(128)S(1)} %and_select_fusion, s32[1024]{0:T(1024)S(1)} %pad_clamp_fusion.1), kind=kCustom, calls=%fused_computation.3 | custom fusion | bytes 108 | tf_op jit(solution)/shard_map/gather | solution.py:77
  9.7 1.3 %collective-permute-done.2 = bf16[1,144,128]{2,1,0:T(8,128)(2,1)S(1)} collective-permute-done((bf16[1,144,128]{2,1,0:T(8,128)(2,1)}, bf16[1,144,128]{2,1,0:T(8,128)(2,1)S(1)}, u32[]{:S(2)}, u32[]{:S(2)}) %collective-permute-start.2) | collective-permute-done | bytes 36896 | tf_op jit(solution)/shard_map/ppermute | solution.py:35
  11.0 0.9 %collective-permute-done.1 = bf16[1,144,128]{2,1,0:T(8,128)(2,1)S(1)} collective-permute-done((bf16[1,144,128]{2,1,0:T(8,128)(2,1)}, bf16[1,144,128]{2,1,0:T(8,128)(2,1)S(1)}, u32[]{:S(2)}, u32[]{:S(2)}) %collective-permute-start.1) | collective-permute-done | bytes 36896 | tf_op jit(solution)/shard_map/ppermute | solution.py:35
  11.9 0.8 %pad_maximum_fusion = bf16[4,144,128]{2,1,0:T(8,128)(2,1)S(1)} fusion(bf16[1,144,128]{2,1,0:T(8,128)(2,1)S(1)} %collective-permute-done.3, bf16[1,144,128]{2,1,0:T(8,128)(2,1)S(1)} %collective-permute-done.2, bf16[1,144,128]{2,1,0:T(8,128)(2,1)S(1)} %collective-permute-done.1, bf16[1,144,128]{2,1,0:T(8,128)(2,1)} %bitcast.13), kind=kLoop, calls=%fused_computation.6 | loop fusion | flops 221184 | bytes 294912 | tf_op jit(solution)/shard_map/concatenate | solution.py:44
  12.7 2.5 %collective-permute-start.6 = (bf16[4,144,128]{2,1,0:T(8,128)(2,1)S(1)}, bf16[4,144,128]{2,1,0:T(8,128)(2,1)S(1)}, u32[]{:S(2)}, u32[]{:S(2)}) collective-permute-start(bf16[4,144,128]{2,1,0:T(8,128)(2,1)S(1)} %pad_maximum_fusion), channel_id=1, source_target_pairs={{0,6},{1,7},{2,4},{3,5},{4,2},{5,3},{6,0},{7,1},{8,14},{9,15},{10,... | collective-permute-start | bytes 442376 | tf_op jit(solution)/shard_map/ppermute | solution.py:35
  15.2 0.5 %collective-permute-start.5 = (bf16[4,144,128]{2,1,0:T(8,128)(2,1)S(1)}, bf16[4,144,128]{2,1,0:T(8,128)(2,1)S(1)}, u32[]{:S(2)}, u32[]{:S(2)}) collective-permute-start(bf16[4,144,128]{2,1,0:T(8,128)(2,1)S(1)} %pad_maximum_fusion), channel_id=1, source_target_pairs={{0,2},{1,5},{2,0},{3,7},{4,6},{5,1},{6,4},{7,3},{8,10},{9,13},{10,... | collective-permute-start | bytes 442376 | tf_op jit(solution)/shard_map/ppermute | solution.py:35
  15.8 0.5 %collective-permute-start.4 = (bf16[4,144,128]{2,1,0:T(8,128)(2,1)S(1)}, bf16[4,144,128]{2,1,0:T(8,128)(2,1)S(1)}, u32[]{:S(2)}, u32[]{:S(2)}) collective-permute-start(bf16[4,144,128]{2,1,0:T(8,128)(2,1)S(1)} %pad_maximum_fusion), channel_id=1, source_target_pairs={{0,4},{1,3},{2,6},{3,1},{4,0},{5,7},{6,2},{7,5},{8,12},{9,11},{10,... | collective-permute-start | bytes 442376 | tf_op jit(solution)/shard_map/ppermute | solution.py:35
  16.3 5.1 %collective-permute-done.4 = bf16[4,144,128]{2,1,0:T(8,128)(2,1)S(1)} collective-permute-done((bf16[4,144,128]{2,1,0:T(8,128)(2,1)S(1)}, bf16[4,144,128]{2,1,0:T(8,128)(2,1)S(1)}, u32[]{:S(2)}, u32[]{:S(2)}) %collective-permute-start.4) | collective-permute-done | bytes 147488 | tf_op jit(solution)/shard_map/ppermute | solution.py:35
  21.5 0.6 %gather_fusion.3 = bf16[9,144,128]{2,1,0:T(8,128)(2,1)S(1)} fusion(bf16[16,144,128]{2,1,0:T(8,128)(2,1)S(1)} %constant_dynamic-update-slice_fusion, s32[1024]{0:T(1024)S(1)} %pad_clamp_fusion), kind=kCustom, calls=%fused_computation.1.clone | custom fusion | bytes 663588 | tf_op jit(solution)/shard_map/jit(_take)/gather | solution.py:78
  22.1 0.1 broadcast_select_fusion
  22.3 0.1 collective-permute-start.7
  22.3 0.6 %gather_fusion.2 = bf16[9,144,128]{2,1,0:T(8,128)(2,1)S(1)} fusion(bf16[16,144,128]{2,1,0:T(8,128)(2,1)S(1)} %constant_dynamic-update-slice_fusion, s32[1024]{0:T(1024)S(1)} %pad_clamp_fusion.2), kind=kCustom, calls=%fused_computation.clone | custom fusion | bytes 663588 | tf_op jit(solution)/shard_map/jit(_take)/gather | solution.py:78
  23.0 0.8 %broadcast_select_fusion.1.pieces_a_ref = bf16[9,144,128]{2,1,0:T(8,128)(2,1)} fusion(bf16[9,144,128]{2,1,0:T(8,128)(2,1)S(1)} %gather_fusion.2, pred[9]{0:T(512)(128)(4,1)S(1)} %get-tuple-element.12), kind=kLoop, calls=%fused_computation.5 | loop fusion | flops 165888 | bytes 663561 | tf_op jit(solution)/shard_map/jit(_take)/select_n | solution.py:78
  23.8 0.2 collective-permute-done.7.pieces_b_ref
  24.0 0.5 %copy-done.1 = bf16[1040,128]{1,0:T(8,128)(2,1)} copy-done((bf16[1040,128]{1,0:T(8,128)(2,1)}, bf16[1040,128]{1,0:T(8,128)(2,1)S(1)}, u32[]{:S(2)}) %copy-start.1) | copy-done | bytes 266264
  24.5 0.7 %copy-done = bf16[9,144,128]{2,1,0:T(8,128)(2,1)} copy-done((bf16[9,144,128]{2,1,0:T(8,128)(2,1)}, bf16[9,144,128]{2,1,0:T(8,128)(2,1)S(1)}, u32[]{:S(2)}) %copy-start) | copy-done | bytes 331800
  25.2 5.2 %shard_map.47 = bf16[1024,1024]{1,0:T(8,128)(2,1)} custom-call(bf16[1024,1024]{1,0:T(8,128)(2,1)} %matrix_ref.1, bf16[1040,128]{1,0:T(8,128)(2,1)} %get-tuple-element.8.cols_a_ref, bf16[1040,128]{1,0:T(8,128)(2,1)} %copy-done.1, bf16[9,144,128]{2,1,0:T(8,128)(2,1)} %broadcast_select_fusion.1.pieces_a_ref, bf16[9,144,128]{2,1,0:T(8,128)(2,1)} %copy-done, ...), custom_call_target="tpu_custom_call" | custom-call | flops 637534208 | bytes 4194304 | tf_op jit(solution)/shard_map/pallas_call | solution.py:233
  (24 shorter events, 0.2 us)
Async XLA Ops:
  0.0 7.4 %copy-start.2 = (s32[16]{0:T(128)S(1)}, s32[16]{0:T(128)}, u32[]{:S(2)}) copy-start(s32[16]{0:T(128)} %col_rows_ref.1) | copy-start | bytes 196
  1.8 7.9 %collective-permute-start.3 = (bf16[1,144,128]{2,1,0:T(8,128)(2,1)}, bf16[1,144,128]{2,1,0:T(8,128)(2,1)S(1)}, u32[]{:S(2)}, u32[]{:S(2)}) collective-permute-start(bf16[1,144,128]{2,1,0:T(8,128)(2,1)} %bitcast.10), channel_id=1, source_target_pairs={{0,24},{1,25},{2,26},{3,27},{4,28},{5,29},{6,30},{7,31},{8,16},{9,... | collective-permute-start | bytes 110600 | tf_op jit(solution)/shard_map/ppermute | solution.py:35
  6.8 4.2 %collective-permute-start.2 = (bf16[1,144,128]{2,1,0:T(8,128)(2,1)}, bf16[1,144,128]{2,1,0:T(8,128)(2,1)S(1)}, u32[]{:S(2)}, u32[]{:S(2)}) collective-permute-start(bf16[1,144,128]{2,1,0:T(8,128)(2,1)} %bitcast.11), channel_id=1, source_target_pairs={{0,8},{1,17},{2,10},{3,19},{4,12},{5,21},{6,14},{7,23},{8,0},{9,25... | collective-permute-start | bytes 110600 | tf_op jit(solution)/shard_map/ppermute | solution.py:35
  6.8 5.1 %collective-permute-start.1 = (bf16[1,144,128]{2,1,0:T(8,128)(2,1)}, bf16[1,144,128]{2,1,0:T(8,128)(2,1)S(1)}, u32[]{:S(2)}, u32[]{:S(2)}) collective-permute-start(bf16[1,144,128]{2,1,0:T(8,128)(2,1)} %bitcast.12), channel_id=1, source_target_pairs={{0,16},{1,9},{2,18},{3,11},{4,20},{5,13},{6,22},{7,15},{8,24},{9,1... | collective-permute-start | bytes 110600 | tf_op jit(solution)/shard_map/ppermute | solution.py:35
  7.4 16.4 %collective-permute-start = (bf16[1040,128]{1,0:T(8,128)(2,1)}, bf16[1040,128]{1,0:T(8,128)(2,1)S(1)}, u32[]{:S(2)}, u32[]{:S(2)}) collective-permute-start(bf16[1040,128]{1,0:T(8,128)(2,1)} %get-tuple-element.8.cols_a_ref), channel_id=1, source_target_pairs={{0,1},{1,0},{2,3},{3,2},{4,5},{5,4},{6,7},{7,6},{8,9},{9,8},{10,11... | collective-permute-start | bytes 798728 | tf_op jit(solution)/shard_map/ppermute | solution.py:84
  12.7 8.8 %collective-permute-start.6 = (bf16[4,144,128]{2,1,0:T(8,128)(2,1)S(1)}, bf16[4,144,128]{2,1,0:T(8,128)(2,1)S(1)}, u32[]{:S(2)}, u32[]{:S(2)}) collective-permute-start(bf16[4,144,128]{2,1,0:T(8,128)(2,1)S(1)} %pad_maximum_fusion), channel_id=1, source_target_pairs={{0,6},{1,7},{2,4},{3,5},{4,2},{5,3},{6,0},{7,1},{8,14},{9,15},{10,... | collective-permute-start | bytes 442376 | tf_op jit(solution)/shard_map/ppermute | solution.py:35
  15.2 6.2 %collective-permute-start.5 = (bf16[4,144,128]{2,1,0:T(8,128)(2,1)S(1)}, bf16[4,144,128]{2,1,0:T(8,128)(2,1)S(1)}, u32[]{:S(2)}, u32[]{:S(2)}) collective-permute-start(bf16[4,144,128]{2,1,0:T(8,128)(2,1)S(1)} %pad_maximum_fusion), channel_id=1, source_target_pairs={{0,2},{1,5},{2,0},{3,7},{4,6},{5,1},{6,4},{7,3},{8,10},{9,13},{10,... | collective-permute-start | bytes 442376 | tf_op jit(solution)/shard_map/ppermute | solution.py:35
  15.8 5.7 %collective-permute-start.4 = (bf16[4,144,128]{2,1,0:T(8,128)(2,1)S(1)}, bf16[4,144,128]{2,1,0:T(8,128)(2,1)S(1)}, u32[]{:S(2)}, u32[]{:S(2)}) collective-permute-start(bf16[4,144,128]{2,1,0:T(8,128)(2,1)S(1)} %pad_maximum_fusion), channel_id=1, source_target_pairs={{0,4},{1,3},{2,6},{3,1},{4,0},{5,7},{6,2},{7,5},{8,12},{9,11},{10,... | collective-permute-start | bytes 442376 | tf_op jit(solution)/shard_map/ppermute | solution.py:35
  22.3 1.7 %collective-permute-start.7 = (bf16[9,144,128]{2,1,0:T(8,128)(2,1)S(1)}, bf16[9,144,128]{2,1,0:T(8,128)(2,1)S(1)}, u32[]{:S(2)}, u32[]{:S(2)}) collective-permute-start(bf16[9,144,128]{2,1,0:T(8,128)(2,1)S(1)} %broadcast_select_fusion), channel_id=1, source_target_pairs={{0,1},{1,0},{2,3},{3,2},{4,5},{5,4},{6,7},{7,6},{8,9},{9,8},{10,11... | collective-permute-start | bytes 995336 | tf_op jit(solution)/shard_map/ppermute | solution.py:87
  23.8 0.7 %copy-start.1 = (bf16[1040,128]{1,0:T(8,128)(2,1)}, bf16[1040,128]{1,0:T(8,128)(2,1)S(1)}, u32[]{:S(2)}) copy-start(bf16[1040,128]{1,0:T(8,128)(2,1)S(1)} %collective-permute-done.cols_b_ref) | copy-start | bytes 798724
  24.5 0.7 %copy-start = (bf16[9,144,128]{2,1,0:T(8,128)(2,1)}, bf16[9,144,128]{2,1,0:T(8,128)(2,1)S(1)}, u32[]{:S(2)}) copy-start(bf16[9,144,128]{2,1,0:T(8,128)(2,1)S(1)} %collective-permute-done.7.pieces_b_ref) | copy-start | bytes 995332

commit v10 on v9

--- a/solution.py
+++ b/solution.py
@@ -141,9 +141,12 @@
 
 
 def factor_kernel(
-    matrix_ref, cols_a_ref, cols_b_ref, pieces_a_ref, pieces_b_ref, inv_ref, mask_ref, out_ref, *, by_col
+    matrix_hbm, cols_a_ref, cols_b_ref, pieces_a_ref, pieces_b_ref, inv_ref, mask_ref, out_hbm,
+    matrix_ref, out_ref, sems, *, by_col
 ):
     local_rows, width = matrix_ref.shape
+    matrix_in = pltpu.make_async_copy(matrix_hbm, matrix_ref, sems.at[0])
+    matrix_in.start()
     col_panels = width // PW
     block_rows = local_rows // RB
     picks = pieces_a_ref.shape[0]
@@ -209,6 +212,8 @@
     ).astype(jnp.bfloat16).reshape(local_rows, PW)
     both_panels = jnp.concatenate((first_panel, second_panel), axis=1)
 
+    matrix_in.wait()
+    panels_out = []
     for j in range(col_panels):
         cols = slice(j * PW, (j + 1) * PW)
         both_diag = jnp.concatenate((diag_first[j], diag_second[j]), axis=1)
@@ -223,6 +228,13 @@
                     jnp.where(col_index == SECOND_COL, second_panel[rows], tile),
                 )
             out_ref[rows, cols] = tile
+        copy = pltpu.make_async_copy(
+            out_ref.at[:, pl.ds(j * PW, PW)], out_hbm.at[:, pl.ds(j * PW, PW)], sems.at[1 + j]
+        )
+        copy.start()
+        panels_out.append(copy)
+    for copy in panels_out:
+        copy.wait()
 
 
 def factor_call(matrix, cols_a, cols_b, pieces_a, pieces_b, inverses, fill_mask, by_col):
@@ -233,8 +245,13 @@
     return pl.pallas_call(
         functools.partial(factor_kernel, by_col=by_col),
         out_shape=jax.ShapeDtypeStruct((local_rows, width), jnp.bfloat16),
-        in_specs=[vmem] * 6 + [smem],
-        out_specs=vmem,
+        in_specs=[pl.BlockSpec(memory_space=pl.ANY)] + [vmem] * 5 + [smem],
+        out_specs=pl.BlockSpec(memory_space=pl.ANY),
+        scratch_shapes=[
+            pltpu.VMEM((local_rows, width), jnp.bfloat16),
+            pltpu.VMEM((local_rows, width), jnp.bfloat16),
+            pltpu.SemaphoreType.DMA((1 + width // PW,)),
+        ],
         cost_estimate=pl.CostEstimate(
             flops=flops, bytes_accessed=4 * local_rows * width, transcendentals=0
         ),

time: 30.8 us -> 30.9 us (level)
  no operation moved by 1% of the time
where the time goes in v10:
time: 30.9 us; the launch traced here: 30.5 us
  starting transfers between devices  9.24 us (30%)
  waiting for transfers between devices  7.49 us (24%)
  Pallas kernels  7.11 us (23%)
  local copies, waits for them, and re-layouts  4.71 us (15%)
  other arithmetic  1.87 us (6%)
    ppermute x6, starting transfers between devices, exchange(): return lax.ppermute(value, ('row', 'col'), perm)  9.17 us
    ppermute x6, waiting for transfers between devices, exchange(): return lax.ppermute(value, ('row', 'col'), perm)  7.33 us
    pallas_call x1, Pallas kernels, factor_call(): pl.pallas_call(functools.partial(factor_kernel, by_col=by_col), out_shape...  5.32 us
    unnamed x12, local copies, waits for them, and re-layouts  2.14 us
    pallas_call x1, Pallas kernels, prep_call(): pl.pallas_call(prep_kernel, out_shape=(jax.ShapeDtypeStruct((PW + MASK_RO...  1.79 us
    gather x2, local copies, waits for them, and re-layouts, pick(): slots = slot_of(owner_row[wanted], order_parity)  1.32 us
    gather x2, local copies, waits for them, and re-layouts, pick(): return jnp.take(pieces, slots, axis=0)  1.22 us
    select_n x2, other arithmetic, pick(): return jnp.take(pieces, slots, axis=0)  0.92 us
  transfers between devices with their start and end apart: 8, of which 4 were waited for; matrix products, arithmetic and copies ran while one was open for 17% of the time, Pallas kernels for 0%

profile of v10, /device:TPU:0, one launch (start us, length us, event | category | flops | bytes accessed | tf_op | source)
XLA Modules:
  0.0 30.5 jit_solution(15166459257315226750)
XLA Ops:
  0.0 1.8 %shard_map.46 = (bf16[144,128]{1,0:T(8,128)(2,1)}, bf16[1040,128]{1,0:T(8,128)(2,1)}) custom-call(bf16[1024,1024]{1,0:T(8,128)(2,1)} %matrix_hbm.1, s32[16]{0:T(128)} %col_rows_ref.1, s32[4,8]{1,0:T(4,128)} %mask_ref.3), custom_call_target="tpu_custom_call" | custom-call | bytes 524288 | tf_op jit(solution)/shard_map/pallas_call | solution.py:125
  1.8 5.0 %collective-permute-start.3 = (bf16[1,144,128]{2,1,0:T(8,128)(2,1)}, bf16[1,144,128]{2,1,0:T(8,128)(2,1)S(1)}, u32[]{:S(2)}, u32[]{:S(2)}) collective-permute-start(bf16[1,144,128]{2,1,0:T(8,128)(2,1)} %bitcast.10), channel_id=1, source_target_pairs={{0,24},{1,25},{2,26},{3,27},{4,28},{5,29},{6,30},{7,31},{8,16},{9,... | collective-permute-start | bytes 110600 | tf_op jit(solution)/shard_map/ppermute | solution.py:35
  6.8 0.0 collective-permute-start.2
  6.8 0.6 %collective-permute-start.1 = (bf16[1,144,128]{2,1,0:T(8,128)(2,1)}, bf16[1,144,128]{2,1,0:T(8,128)(2,1)S(1)}, u32[]{:S(2)}, u32[]{:S(2)}) collective-permute-start(bf16[1,144,128]{2,1,0:T(8,128)(2,1)} %bitcast.12), channel_id=1, source_target_pairs={{0,16},{1,9},{2,18},{3,11},{4,20},{5,13},{6,22},{7,15},{8,24},{9,1... | collective-permute-start | bytes 110600 | tf_op jit(solution)/shard_map/ppermute | solution.py:35
  7.4 0.8 %constant_dynamic-update-slice_fusion.6 = bf16[16,144,128]{2,1,0:T(8,128)(2,1)S(1)} fusion(bf16[144,128]{1,0:T(8,128)(2,1)} %get-tuple-element.9), kind=kLoop, calls=%fused_computation.13 | loop fusion | bytes 73728
  8.2 0.1 fusion
  8.3 0.7 %gather_fusion = s32[9]{0:T(128)S(1)} fusion(s32[16]{0:T(128)S(1)} %and_select_fusion, s32[1024]{0:T(1024)S(1)} %pad_clamp_fusion.3), kind=kCustom, calls=%fused_computation.2 | custom fusion | bytes 108 | tf_op jit(solution)/shard_map/gather | solution.py:77
  9.0 0.7 %gather_fusion.1 = s32[9]{0:T(128)S(1)} fusion(s32[16]{0:T(128)S(1)} %and_select_fusion, s32[1024]{0:T(1024)S(1)} %pad_clamp_fusion.1), kind=kCustom, calls=%fused_computation.3 | custom fusion | bytes 108 | tf_op jit(solution)/shard_map/gather | solution.py:77
  9.7 1.3 %collective-permute-done.2 = bf16[1,144,128]{2,1,0:T(8,128)(2,1)S(1)} collective-permute-done((bf16[1,144,128]{2,1,0:T(8,128)(2,1)}, bf16[1,144,128]{2,1,0:T(8,128)(2,1)S(1)}, u32[]{:S(2)}, u32[]{:S(2)}) %collective-permute-start.2) | collective-permute-done | bytes 36896 | tf_op jit(solution)/shard_map/ppermute | solution.py:35
  11.0 0.9 %collective-permute-done.1 = bf16[1,144,128]{2,1,0:T(8,128)(2,1)S(1)} collective-permute-done((bf16[1,144,128]{2,1,0:T(8,128)(2,1)}, bf16[1,144,128]{2,1,0:T(8,128)(2,1)S(1)}, u32[]{:S(2)}, u32[]{:S(2)}) %collective-permute-start.1) | collective-permute-done | bytes 36896 | tf_op jit(solution)/shard_map/ppermute | solution.py:35
  11.9 0.8 %pad_maximum_fusion = bf16[4,144,128]{2,1,0:T(8,128)(2,1)S(1)} fusion(bf16[1,144,128]{2,1,0:T(8,128)(2,1)S(1)} %collective-permute-done.3, bf16[1,144,128]{2,1,0:T(8,128)(2,1)S(1)} %collective-permute-done.2, bf16[1,144,128]{2,1,0:T(8,128)(2,1)S(1)} %collective-permute-done.1, bf16[1,144,128]{2,1,0:T(8,128)(2,1)} %bitcast.13), kind=kLoop, calls=%fused_computation.6 | loop fusion | flops 221184 | bytes 294912 | tf_op jit(solution)/shard_map/concatenate | solution.py:44
  12.7 2.5 %collective-permute-start.6 = (bf16[4,144,128]{2,1,0:T(8,128)(2,1)S(1)}, bf16[4,144,128]{2,1,0:T(8,128)(2,1)S(1)}, u32[]{:S(2)}, u32[]{:S(2)}) collective-permute-start(bf16[4,144,128]{2,1,0:T(8,128)(2,1)S(1)} %pad_maximum_fusion), channel_id=1, source_target_pairs={{0,6},{1,7},{2,4},{3,5},{4,2},{5,3},{6,0},{7,1},{8,14},{9,15},{10,... | collective-permute-start | bytes 442376 | tf_op jit(solution)/shard_map/ppermute | solution.py:35
  15.2 0.5 %collective-permute-start.5 = (bf16[4,144,128]{2,1,0:T(8,128)(2,1)S(1)}, bf16[4,144,128]{2,1,0:T(8,128)(2,1)S(1)}, u32[]{:S(2)}, u32[]{:S(2)}) collective-permute-start(bf16[4,144,128]{2,1,0:T(8,128)(2,1)S(1)} %pad_maximum_fusion), channel_id=1, source_target_pairs={{0,2},{1,5},{2,0},{3,7},{4,6},{5,1},{6,4},{7,3},{8,10},{9,13},{10,... | collective-permute-start | bytes 442376 | tf_op jit(solution)/shard_map/ppermute | solution.py:35
  15.8 0.5 %collective-permute-start.4 = (bf16[4,144,128]{2,1,0:T(8,128)(2,1)S(1)}, bf16[4,144,128]{2,1,0:T(8,128)(2,1)S(1)}, u32[]{:S(2)}, u32[]{:S(2)}) collective-permute-start(bf16[4,144,128]{2,1,0:T(8,128)(2,1)S(1)} %pad_maximum_fusion), channel_id=1, source_target_pairs={{0,4},{1,3},{2,6},{3,1},{4,0},{5,7},{6,2},{7,5},{8,12},{9,11},{10,... | collective-permute-start | bytes 442376 | tf_op jit(solution)/shard_map/ppermute | solution.py:35
  16.3 5.1 %collective-permute-done.4 = bf16[4,144,128]{2,1,0:T(8,128)(2,1)S(1)} collective-permute-done((bf16[4,144,128]{2,1,0:T(8,128)(2,1)S(1)}, bf16[4,144,128]{2,1,0:T(8,128)(2,1)S(1)}, u32[]{:S(2)}, u32[]{:S(2)}) %collective-permute-start.4) | collective-permute-done | bytes 147488 | tf_op jit(solution)/shard_map/ppermute | solution.py:35
  21.5 0.6 %gather_fusion.3 = bf16[9,144,128]{2,1,0:T(8,128)(2,1)S(1)} fusion(bf16[16,144,128]{2,1,0:T(8,128)(2,1)S(1)} %constant_dynamic-update-slice_fusion, s32[1024]{0:T(1024)S(1)} %pad_clamp_fusion), kind=kCustom, calls=%fused_computation.1.clone | custom fusion | bytes 663588 | tf_op jit(solution)/shard_map/jit(_take)/gather | solution.py:78
  22.1 0.1 broadcast_select_fusion
  22.3 0.1 collective-permute-start.7
  22.3 0.6 %gather_fusion.2 = bf16[9,144,128]{2,1,0:T(8,128)(2,1)S(1)} fusion(bf16[16,144,128]{2,1,0:T(8,128)(2,1)S(1)} %constant_dynamic-update-slice_fusion, s32[1024]{0:T(1024)S(1)} %pad_clamp_fusion.2), kind=kCustom, calls=%fused_computation.clone | custom fusion | bytes 663588 | tf_op jit(solution)/shard_map/jit(_take)/gather | solution.py:78
  23.0 0.8 %broadcast_select_fusion.1.pieces_a_ref = bf16[9,144,128]{2,1,0:T(8,128)(2,1)} fusion(bf16[9,144,128]{2,1,0:T(8,128)(2,1)S(1)} %gather_fusion.2, pred[9]{0:T(512)(128)(4,1)S(1)} %get-tuple-element.12), kind=kLoop, calls=%fused_computation.5 | loop fusion | flops 165888 | bytes 663561 | tf_op jit(solution)/shard_map/jit(_take)/select_n | solution.py:78
  23.8 0.2 collective-permute-done.7.pieces_b_ref
  24.0 0.5 %copy-done.1 = bf16[1040,128]{1,0:T(8,128)(2,1)} copy-done((bf16[1040,128]{1,0:T(8,128)(2,1)}, bf16[1040,128]{1,0:T(8,128)(2,1)S(1)}, u32[]{:S(2)}) %copy-start.1) | copy-done | bytes 266264
  24.5 0.7 %copy-done = bf16[9,144,128]{2,1,0:T(8,128)(2,1)} copy-done((bf16[9,144,128]{2,1,0:T(8,128)(2,1)}, bf16[9,144,128]{2,1,0:T(8,128)(2,1)S(1)}, u32[]{:S(2)}) %copy-start) | copy-done | bytes 331800
  25.2 5.3 %shard_map.47 = bf16[1024,1024]{1,0:T(8,128)(2,1)} custom-call(bf16[1024,1024]{1,0:T(8,128)(2,1)} %matrix_hbm.1, bf16[1040,128]{1,0:T(8,128)(2,1)} %get-tuple-element.8.cols_a_ref, bf16[1040,128]{1,0:T(8,128)(2,1)} %copy-done.1, bf16[9,144,128]{2,1,0:T(8,128)(2,1)} %broadcast_select_fusion.1.pieces_a_ref, bf16[9,144,128]{2,1,0:T(8,128)(2,1)} %copy-done, ...), custom_call_target="tpu_custom_call" | custom-call | flops 637534208 | bytes 4194304 | tf_op jit(solution)/shard_map/pallas_call | solution.py:245
  (24 shorter events, 0.2 us)
Async XLA Ops:
  0.0 7.4 %copy-start.2 = (s32[16]{0:T(128)S(1)}, s32[16]{0:T(128)}, u32[]{:S(2)}) copy-start(s32[16]{0:T(128)} %col_rows_ref.1) | copy-start | bytes 196
  1.8 7.9 %collective-permute-start.3 = (bf16[1,144,128]{2,1,0:T(8,128)(2,1)}, bf16[1,144,128]{2,1,0:T(8,128)(2,1)S(1)}, u32[]{:S(2)}, u32[]{:S(2)}) collective-permute-start(bf16[1,144,128]{2,1,0:T(8,128)(2,1)} %bitcast.10), channel_id=1, source_target_pairs={{0,24},{1,25},{2,26},{3,27},{4,28},{5,29},{6,30},{7,31},{8,16},{9,... | collective-permute-start | bytes 110600 | tf_op jit(solution)/shard_map/ppermute | solution.py:35
  6.8 4.2 %collective-permute-start.2 = (bf16[1,144,128]{2,1,0:T(8,128)(2,1)}, bf16[1,144,128]{2,1,0:T(8,128)(2,1)S(1)}, u32[]{:S(2)}, u32[]{:S(2)}) collective-permute-start(bf16[1,144,128]{2,1,0:T(8,128)(2,1)} %bitcast.11), channel_id=1, source_target_pairs={{0,8},{1,17},{2,10},{3,19},{4,12},{5,21},{6,14},{7,23},{8,0},{9,25... | collective-permute-start | bytes 110600 | tf_op jit(solution)/shard_map/ppermute | solution.py:35
  6.8 5.1 %collective-permute-start.1 = (bf16[1,144,128]{2,1,0:T(8,128)(2,1)}, bf16[1,144,128]{2,1,0:T(8,128)(2,1)S(1)}, u32[]{:S(2)}, u32[]{:S(2)}) collective-permute-start(bf16[1,144,128]{2,1,0:T(8,128)(2,1)} %bitcast.12), channel_id=1, source_target_pairs={{0,16},{1,9},{2,18},{3,11},{4,20},{5,13},{6,22},{7,15},{8,24},{9,1... | collective-permute-start | bytes 110600 | tf_op jit(solution)/shard_map/ppermute | solution.py:35
  7.4 16.4 %collective-permute-start = (bf16[1040,128]{1,0:T(8,128)(2,1)}, bf16[1040,128]{1,0:T(8,128)(2,1)S(1)}, u32[]{:S(2)}, u32[]{:S(2)}) collective-permute-start(bf16[1040,128]{1,0:T(8,128)(2,1)} %get-tuple-element.8.cols_a_ref), channel_id=1, source_target_pairs={{0,1},{1,0},{2,3},{3,2},{4,5},{5,4},{6,7},{7,6},{8,9},{9,8},{10,11... | collective-permute-start | bytes 798728 | tf_op jit(solution)/shard_map/ppermute | solution.py:84
  12.7 8.8 %collective-permute-start.6 = (bf16[4,144,128]{2,1,0:T(8,128)(2,1)S(1)}, bf16[4,144,128]{2,1,0:T(8,128)(2,1)S(1)}, u32[]{:S(2)}, u32[]{:S(2)}) collective-permute-start(bf16[4,144,128]{2,1,0:T(8,128)(2,1)S(1)} %pad_maximum_fusion), channel_id=1, source_target_pairs={{0,6},{1,7},{2,4},{3,5},{4,2},{5,3},{6,0},{7,1},{8,14},{9,15},{10,... | collective-permute-start | bytes 442376 | tf_op jit(solution)/shard_map/ppermute | solution.py:35
  15.2 6.2 %collective-permute-start.5 = (bf16[4,144,128]{2,1,0:T(8,128)(2,1)S(1)}, bf16[4,144,128]{2,1,0:T(8,128)(2,1)S(1)}, u32[]{:S(2)}, u32[]{:S(2)}) collective-permute-start(bf16[4,144,128]{2,1,0:T(8,128)(2,1)S(1)} %pad_maximum_fusion), channel_id=1, source_target_pairs={{0,2},{1,5},{2,0},{3,7},{4,6},{5,1},{6,4},{7,3},{8,10},{9,13},{10,... | collective-permute-start | bytes 442376 | tf_op jit(solution)/shard_map/ppermute | solution.py:35
  15.8 5.7 %collective-permute-start.4 = (bf16[4,144,128]{2,1,0:T(8,128)(2,1)S(1)}, bf16[4,144,128]{2,1,0:T(8,128)(2,1)S(1)}, u32[]{:S(2)}, u32[]{:S(2)}) collective-permute-start(bf16[4,144,128]{2,1,0:T(8,128)(2,1)S(1)} %pad_maximum_fusion), channel_id=1, source_target_pairs={{0,4},{1,3},{2,6},{3,1},{4,0},{5,7},{6,2},{7,5},{8,12},{9,11},{10,... | collective-permute-start | bytes 442376 | tf_op jit(solution)/shard_map/ppermute | solution.py:35
  22.3 1.7 %collective-permute-start.7 = (bf16[9,144,128]{2,1,0:T(8,128)(2,1)S(1)}, bf16[9,144,128]{2,1,0:T(8,128)(2,1)S(1)}, u32[]{:S(2)}, u32[]{:S(2)}) collective-permute-start(bf16[9,144,128]{2,1,0:T(8,128)(2,1)S(1)} %broadcast_select_fusion), channel_id=1, source_target_pairs={{0,1},{1,0},{2,3},{3,2},{4,5},{5,4},{6,7},{7,6},{8,9},{9,8},{10,11... | collective-permute-start | bytes 995336 | tf_op jit(solution)/shard_map/ppermute | solution.py:87
  23.8 0.7 %copy-start.1 = (bf16[1040,128]{1,0:T(8,128)(2,1)}, bf16[1040,128]{1,0:T(8,128)(2,1)S(1)}, u32[]{:S(2)}) copy-start(bf16[1040,128]{1,0:T(8,128)(2,1)S(1)} %collective-permute-done.cols_b_ref) | copy-start | bytes 798724
  24.5 0.7 %copy-start = (bf16[9,144,128]{2,1,0:T(8,128)(2,1)}, bf16[9,144,128]{2,1,0:T(8,128)(2,1)S(1)}, u32[]{:S(2)}) copy-start(bf16[9,144,128]{2,1,0:T(8,128)(2,1)S(1)} %collective-permute-done.7.pieces_b_ref) | copy-start | bytes 995332

commit v11 on v9

--- a/solution.py
+++ b/solution.py
@@ -209,20 +209,24 @@
     ).astype(jnp.bfloat16).reshape(local_rows, PW)
     both_panels = jnp.concatenate((first_panel, second_panel), axis=1)
 
-    for j in range(col_panels):
-        cols = slice(j * PW, (j + 1) * PW)
-        both_diag = jnp.concatenate((diag_first[j], diag_second[j]), axis=1)
-        schur = matrix_ref[:, cols].astype(jnp.float32) - dot_t(both_panels, both_diag)
-        for b in range(block_rows):
-            rows = slice(b * RB, (b + 1) * RB)
-            tile = (schur[rows] * mask_ref[b, j].astype(jnp.float32)).astype(jnp.bfloat16)
-            if j == 0:
-                tile = jnp.where(
-                    col_index == FIRST_COL,
-                    first_panel[rows],
-                    jnp.where(col_index == SECOND_COL, second_panel[rows], tile),
-                )
-            out_ref[rows, cols] = tile
+    all_diag = jnp.concatenate(
+        (diag_first[:col_panels].reshape(width, PW), diag_second.reshape(width, PW)), axis=1
+    )
+    product = dot_t(both_panels, all_diag)
+    lane_panel = lax.broadcasted_iota(jnp.int32, (1, width), 1) // PW
+    for b in range(block_rows):
+        rows = slice(b * RB, (b + 1) * RB)
+        scale = jnp.zeros((1, width), jnp.float32)
+        for j in range(col_panels):
+            scale = jnp.where(lane_panel == j, mask_ref[b, j].astype(jnp.float32), scale)
+        schur = matrix_ref[rows, :].astype(jnp.float32) - product[rows]
+        out_ref[rows, :] = (schur * scale).astype(jnp.bfloat16)
+        lead = out_ref[rows, 0:PW]
+        out_ref[rows, 0:PW] = jnp.where(
+            col_index == FIRST_COL,
+            first_panel[rows],
+            jnp.where(col_index == SECOND_COL, second_panel[rows], lead),
+        )
 
 
 def factor_call(matrix, cols_a, cols_b, pieces_a, pieces_b, inverses, fill_mask, by_col):

time: 30.8 us -> 30.3 us (0.984)
  Pallas kernels: 7.03 us -> 6.61 us
    pallas_call x1, Pallas kernels: 5.24 us -> 4.82 us  [factor_call(): pl.pallas_call(functools.partial(factor_kernel, by_col=by_col), out_shape...]
  transfers between devices with their start and end apart: 8 -> 8, of which waited for: 4 -> 4; matrix products, arithmetic and copies ran while one was open for 17% -> 18% of each run, Pallas kernels for 0% -> 0%
where the time goes in v11:
time: 30.3 us; the launch traced here: 30 us
  starting transfers between devices  9.24 us (30%)
  waiting for transfers between devices  7.49 us (25%)
  Pallas kernels  6.61 us (22%)
  local copies, waits for them, and re-layouts  4.71 us (16%)
  other arithmetic  1.87 us (6%)
    ppermute x6, starting transfers between devices, exchange(): return lax.ppermute(value, ('row', 'col'), perm)  9.17 us
    ppermute x6, waiting for transfers between devices, exchange(): return lax.ppermute(value, ('row', 'col'), perm)  7.33 us
    pallas_call x1, Pallas kernels, factor_call(): pl.pallas_call(functools.partial(factor_kernel, by_col=by_col), out_shape...  4.82 us
    unnamed x12, local copies, waits for them, and re-layouts  2.14 us
    pallas_call x1, Pallas kernels, prep_call(): pl.pallas_call(prep_kernel, out_shape=(jax.ShapeDtypeStruct((PW + MASK_RO...  1.79 us
    gather x2, local copies, waits for them, and re-layouts, pick(): slots = slot_of(owner_row[wanted], order_parity)  1.32 us
    gather x2, local copies, waits for them, and re-layouts, pick(): return jnp.take(pieces, slots, axis=0)  1.22 us
    select_n x2, other arithmetic, pick(): return jnp.take(pieces, slots, axis=0)  0.92 us
  transfers between devices with their start and end apart: 8, of which 4 were waited for; matrix products, arithmetic and copies ran while one was open for 18% of the time, Pallas kernels for 0%

profile of v11, /device:TPU:0, one launch (start us, length us, event | category | flops | bytes accessed | tf_op | source)
XLA Modules:
  0.0 30.0 jit_solution(14613436791770038581)
XLA Ops:
  0.0 1.8 %shard_map.46 = (bf16[144,128]{1,0:T(8,128)(2,1)}, bf16[1040,128]{1,0:T(8,128)(2,1)}) custom-call(bf16[1024,1024]{1,0:T(8,128)(2,1)} %matrix_ref.1, s32[16]{0:T(128)} %col_rows_ref.1, s32[4,8]{1,0:T(4,128)} %mask_ref.3), custom_call_target="tpu_custom_call" | custom-call | bytes 524288 | tf_op jit(solution)/shard_map/pallas_call | solution.py:125
  1.8 5.0 %collective-permute-start.3 = (bf16[1,144,128]{2,1,0:T(8,128)(2,1)}, bf16[1,144,128]{2,1,0:T(8,128)(2,1)S(1)}, u32[]{:S(2)}, u32[]{:S(2)}) collective-permute-start(bf16[1,144,128]{2,1,0:T(8,128)(2,1)} %bitcast.10), channel_id=1, source_target_pairs={{0,24},{1,25},{2,26},{3,27},{4,28},{5,29},{6,30},{7,31},{8,16},{9,... | collective-permute-start | bytes 110600 | tf_op jit(solution)/shard_map/ppermute | solution.py:35
  6.8 0.0 collective-permute-start.2
  6.8 0.6 %collective-permute-start.1 = (bf16[1,144,128]{2,1,0:T(8,128)(2,1)}, bf16[1,144,128]{2,1,0:T(8,128)(2,1)S(1)}, u32[]{:S(2)}, u32[]{:S(2)}) collective-permute-start(bf16[1,144,128]{2,1,0:T(8,128)(2,1)} %bitcast.12), channel_id=1, source_target_pairs={{0,16},{1,9},{2,18},{3,11},{4,20},{5,13},{6,22},{7,15},{8,24},{9,1... | collective-permute-start | bytes 110600 | tf_op jit(solution)/shard_map/ppermute | solution.py:35
  7.4 0.8 %constant_dynamic-update-slice_fusion.6 = bf16[16,144,128]{2,1,0:T(8,128)(2,1)S(1)} fusion(bf16[144,128]{1,0:T(8,128)(2,1)} %get-tuple-element.9), kind=kLoop, calls=%fused_computation.13 | loop fusion | bytes 73728
  8.2 0.1 fusion
  8.3 0.7 %gather_fusion = s32[9]{0:T(128)S(1)} fusion(s32[16]{0:T(128)S(1)} %and_select_fusion, s32[1024]{0:T(1024)S(1)} %pad_clamp_fusion.3), kind=kCustom, calls=%fused_computation.2 | custom fusion | bytes 108 | tf_op jit(solution)/shard_map/gather | solution.py:77
  9.0 0.7 %gather_fusion.1 = s32[9]{0:T(128)S(1)} fusion(s32[16]{0:T(128)S(1)} %and_select_fusion, s32[1024]{0:T(1024)S(1)} %pad_clamp_fusion.1), kind=kCustom, calls=%fused_computation.3 | custom fusion | bytes 108 | tf_op jit(solution)/shard_map/gather | solution.py:77
  9.7 1.3 %collective-permute-done.2 = bf16[1,144,128]{2,1,0:T(8,128)(2,1)S(1)} collective-permute-done((bf16[1,144,128]{2,1,0:T(8,128)(2,1)}, bf16[1,144,128]{2,1,0:T(8,128)(2,1)S(1)}, u32[]{:S(2)}, u32[]{:S(2)}) %collective-permute-start.2) | collective-permute-done | bytes 36896 | tf_op jit(solution)/shard_map/ppermute | solution.py:35
  11.0 0.9 %collective-permute-done.1 = bf16[1,144,128]{2,1,0:T(8,128)(2,1)S(1)} collective-permute-done((bf16[1,144,128]{2,1,0:T(8,128)(2,1)}, bf16[1,144,128]{2,1,0:T(8,128)(2,1)S(1)}, u32[]{:S(2)}, u32[]{:S(2)}) %collective-permute-start.1) | collective-permute-done | bytes 36896 | tf_op jit(solution)/shard_map/ppermute | solution.py:35
  11.9 0.8 %pad_maximum_fusion = bf16[4,144,128]{2,1,0:T(8,128)(2,1)S(1)} fusion(bf16[1,144,128]{2,1,0:T(8,128)(2,1)S(1)} %collective-permute-done.3, bf16[1,144,128]{2,1,0:T(8,128)(2,1)S(1)} %collective-permute-done.2, bf16[1,144,128]{2,1,0:T(8,128)(2,1)S(1)} %collective-permute-done.1, bf16[1,144,128]{2,1,0:T(8,128)(2,1)} %bitcast.13), kind=kLoop, calls=%fused_computation.6 | loop fusion | flops 221184 | bytes 294912 | tf_op jit(solution)/shard_map/concatenate | solution.py:44
  12.7 2.5 %collective-permute-start.6 = (bf16[4,144,128]{2,1,0:T(8,128)(2,1)S(1)}, bf16[4,144,128]{2,1,0:T(8,128)(2,1)S(1)}, u32[]{:S(2)}, u32[]{:S(2)}) collective-permute-start(bf16[4,144,128]{2,1,0:T(8,128)(2,1)S(1)} %pad_maximum_fusion), channel_id=1, source_target_pairs={{0,6},{1,7},{2,4},{3,5},{4,2},{5,3},{6,0},{7,1},{8,14},{9,15},{10,... | collective-permute-start | bytes 442376 | tf_op jit(solution)/shard_map/ppermute | solution.py:35
  15.2 0.5 %collective-permute-start.5 = (bf16[4,144,128]{2,1,0:T(8,128)(2,1)S(1)}, bf16[4,144,128]{2,1,0:T(8,128)(2,1)S(1)}, u32[]{:S(2)}, u32[]{:S(2)}) collective-permute-start(bf16[4,144,128]{2,1,0:T(8,128)(2,1)S(1)} %pad_maximum_fusion), channel_id=1, source_target_pairs={{0,2},{1,5},{2,0},{3,7},{4,6},{5,1},{6,4},{7,3},{8,10},{9,13},{10,... | collective-permute-start | bytes 442376 | tf_op jit(solution)/shard_map/ppermute | solution.py:35
  15.8 0.5 %collective-permute-start.4 = (bf16[4,144,128]{2,1,0:T(8,128)(2,1)S(1)}, bf16[4,144,128]{2,1,0:T(8,128)(2,1)S(1)}, u32[]{:S(2)}, u32[]{:S(2)}) collective-permute-start(bf16[4,144,128]{2,1,0:T(8,128)(2,1)S(1)} %pad_maximum_fusion), channel_id=1, source_target_pairs={{0,4},{1,3},{2,6},{3,1},{4,0},{5,7},{6,2},{7,5},{8,12},{9,11},{10,... | collective-permute-start | bytes 442376 | tf_op jit(solution)/shard_map/ppermute | solution.py:35
  16.3 5.1 %collective-permute-done.4 = bf16[4,144,128]{2,1,0:T(8,128)(2,1)S(1)} collective-permute-done((bf16[4,144,128]{2,1,0:T(8,128)(2,1)S(1)}, bf16[4,144,128]{2,1,0:T(8,128)(2,1)S(1)}, u32[]{:S(2)}, u32[]{:S(2)}) %collective-permute-start.4) | collective-permute-done | bytes 147488 | tf_op jit(solution)/shard_map/ppermute | solution.py:35
  21.5 0.6 %gather_fusion.3 = bf16[9,144,128]{2,1,0:T(8,128)(2,1)S(1)} fusion(bf16[16,144,128]{2,1,0:T(8,128)(2,1)S(1)} %constant_dynamic-update-slice_fusion, s32[1024]{0:T(1024)S(1)} %pad_clamp_fusion), kind=kCustom, calls=%fused_computation.1.clone | custom fusion | bytes 663588 | tf_op jit(solution)/shard_map/jit(_take)/gather | solution.py:78
  22.1 0.1 broadcast_select_fusion
  22.3 0.1 collective-permute-start.7
  22.3 0.6 %gather_fusion.2 = bf16[9,144,128]{2,1,0:T(8,128)(2,1)S(1)} fusion(bf16[16,144,128]{2,1,0:T(8,128)(2,1)S(1)} %constant_dynamic-update-slice_fusion, s32[1024]{0:T(1024)S(1)} %pad_clamp_fusion.2), kind=kCustom, calls=%fused_computation.clone | custom fusion | bytes 663588 | tf_op jit(solution)/shard_map/jit(_take)/gather | solution.py:78
  23.0 0.8 %broadcast_select_fusion.1.pieces_a_ref = bf16[9,144,128]{2,1,0:T(8,128)(2,1)} fusion(bf16[9,144,128]{2,1,0:T(8,128)(2,1)S(1)} %gather_fusion.2, pred[9]{0:T(512)(128)(4,1)S(1)} %get-tuple-element.12), kind=kLoop, calls=%fused_computation.5 | loop fusion | flops 165888 | bytes 663561 | tf_op jit(solution)/shard_map/jit(_take)/select_n | solution.py:78
  23.8 0.2 collective-permute-done.7.pieces_b_ref
  24.0 0.5 %copy-done.1 = bf16[1040,128]{1,0:T(8,128)(2,1)} copy-done((bf16[1040,128]{1,0:T(8,128)(2,1)}, bf16[1040,128]{1,0:T(8,128)(2,1)S(1)}, u32[]{:S(2)}) %copy-start.1) | copy-done | bytes 266264
  24.5 0.7 %copy-done = bf16[9,144,128]{2,1,0:T(8,128)(2,1)} copy-done((bf16[9,144,128]{2,1,0:T(8,128)(2,1)}, bf16[9,144,128]{2,1,0:T(8,128)(2,1)S(1)}, u32[]{:S(2)}) %copy-start) | copy-done | bytes 331800
  25.2 4.8 %shard_map.47 = bf16[1024,1024]{1,0:T(8,128)(2,1)} custom-call(bf16[1024,1024]{1,0:T(8,128)(2,1)} %matrix_ref.1, bf16[1040,128]{1,0:T(8,128)(2,1)} %get-tuple-element.8.cols_a_ref, bf16[1040,128]{1,0:T(8,128)(2,1)} %copy-done.1, bf16[9,144,128]{2,1,0:T(8,128)(2,1)} %broadcast_select_fusion.1.pieces_a_ref, bf16[9,144,128]{2,1,0:T(8,128)(2,1)} %copy-done, ...), custom_call_target="tpu_custom_call" | custom-call | flops 637534208 | bytes 4194304 | tf_op jit(solution)/shard_map/pallas_call | solution.py:237
  (24 shorter events, 0.2 us)
Async XLA Ops:
  0.0 7.4 %copy-start.2 = (s32[16]{0:T(128)S(1)}, s32[16]{0:T(128)}, u32[]{:S(2)}) copy-start(s32[16]{0:T(128)} %col_rows_ref.1) | copy-start | bytes 196
  1.8 7.9 %collective-permute-start.3 = (bf16[1,144,128]{2,1,0:T(8,128)(2,1)}, bf16[1,144,128]{2,1,0:T(8,128)(2,1)S(1)}, u32[]{:S(2)}, u32[]{:S(2)}) collective-permute-start(bf16[1,144,128]{2,1,0:T(8,128)(2,1)} %bitcast.10), channel_id=1, source_target_pairs={{0,24},{1,25},{2,26},{3,27},{4,28},{5,29},{6,30},{7,31},{8,16},{9,... | collective-permute-start | bytes 110600 | tf_op jit(solution)/shard_map/ppermute | solution.py:35
  6.8 4.2 %collective-permute-start.2 = (bf16[1,144,128]{2,1,0:T(8,128)(2,1)}, bf16[1,144,128]{2,1,0:T(8,128)(2,1)S(1)}, u32[]{:S(2)}, u32[]{:S(2)}) collective-permute-start(bf16[1,144,128]{2,1,0:T(8,128)(2,1)} %bitcast.11), channel_id=1, source_target_pairs={{0,8},{1,17},{2,10},{3,19},{4,12},{5,21},{6,14},{7,23},{8,0},{9,25... | collective-permute-start | bytes 110600 | tf_op jit(solution)/shard_map/ppermute | solution.py:35
  6.8 5.1 %collective-permute-start.1 = (bf16[1,144,128]{2,1,0:T(8,128)(2,1)}, bf16[1,144,128]{2,1,0:T(8,128)(2,1)S(1)}, u32[]{:S(2)}, u32[]{:S(2)}) collective-permute-start(bf16[1,144,128]{2,1,0:T(8,128)(2,1)} %bitcast.12), channel_id=1, source_target_pairs={{0,16},{1,9},{2,18},{3,11},{4,20},{5,13},{6,22},{7,15},{8,24},{9,1... | collective-permute-start | bytes 110600 | tf_op jit(solution)/shard_map/ppermute | solution.py:35
  7.4 16.4 %collective-permute-start = (bf16[1040,128]{1,0:T(8,128)(2,1)}, bf16[1040,128]{1,0:T(8,128)(2,1)S(1)}, u32[]{:S(2)}, u32[]{:S(2)}) collective-permute-start(bf16[1040,128]{1,0:T(8,128)(2,1)} %get-tuple-element.8.cols_a_ref), channel_id=1, source_target_pairs={{0,1},{1,0},{2,3},{3,2},{4,5},{5,4},{6,7},{7,6},{8,9},{9,8},{10,11... | collective-permute-start | bytes 798728 | tf_op jit(solution)/shard_map/ppermute | solution.py:84
  12.7 8.8 %collective-permute-start.6 = (bf16[4,144,128]{2,1,0:T(8,128)(2,1)S(1)}, bf16[4,144,128]{2,1,0:T(8,128)(2,1)S(1)}, u32[]{:S(2)}, u32[]{:S(2)}) collective-permute-start(bf16[4,144,128]{2,1,0:T(8,128)(2,1)S(1)} %pad_maximum_fusion), channel_id=1, source_target_pairs={{0,6},{1,7},{2,4},{3,5},{4,2},{5,3},{6,0},{7,1},{8,14},{9,15},{10,... | collective-permute-start | bytes 442376 | tf_op jit(solution)/shard_map/ppermute | solution.py:35
  15.2 6.2 %collective-permute-start.5 = (bf16[4,144,128]{2,1,0:T(8,128)(2,1)S(1)}, bf16[4,144,128]{2,1,0:T(8,128)(2,1)S(1)}, u32[]{:S(2)}, u32[]{:S(2)}) collective-permute-start(bf16[4,144,128]{2,1,0:T(8,128)(2,1)S(1)} %pad_maximum_fusion), channel_id=1, source_target_pairs={{0,2},{1,5},{2,0},{3,7},{4,6},{5,1},{6,4},{7,3},{8,10},{9,13},{10,... | collective-permute-start | bytes 442376 | tf_op jit(solution)/shard_map/ppermute | solution.py:35
  15.8 5.7 %collective-permute-start.4 = (bf16[4,144,128]{2,1,0:T(8,128)(2,1)S(1)}, bf16[4,144,128]{2,1,0:T(8,128)(2,1)S(1)}, u32[]{:S(2)}, u32[]{:S(2)}) collective-permute-start(bf16[4,144,128]{2,1,0:T(8,128)(2,1)S(1)} %pad_maximum_fusion), channel_id=1, source_target_pairs={{0,4},{1,3},{2,6},{3,1},{4,0},{5,7},{6,2},{7,5},{8,12},{9,11},{10,... | collective-permute-start | bytes 442376 | tf_op jit(solution)/shard_map/ppermute | solution.py:35
  22.3 1.7 %collective-permute-start.7 = (bf16[9,144,128]{2,1,0:T(8,128)(2,1)S(1)}, bf16[9,144,128]{2,1,0:T(8,128)(2,1)S(1)}, u32[]{:S(2)}, u32[]{:S(2)}) collective-permute-start(bf16[9,144,128]{2,1,0:T(8,128)(2,1)S(1)} %broadcast_select_fusion), channel_id=1, source_target_pairs={{0,1},{1,0},{2,3},{3,2},{4,5},{5,4},{6,7},{7,6},{8,9},{9,8},{10,11... | collective-permute-start | bytes 995336 | tf_op jit(solution)/shard_map/ppermute | solution.py:87
  23.8 0.7 %copy-start.1 = (bf16[1040,128]{1,0:T(8,128)(2,1)}, bf16[1040,128]{1,0:T(8,128)(2,1)S(1)}, u32[]{:S(2)}) copy-start(bf16[1040,128]{1,0:T(8,128)(2,1)S(1)} %collective-permute-done.cols_b_ref) | copy-start | bytes 798724
  24.5 0.7 %copy-start = (bf16[9,144,128]{2,1,0:T(8,128)(2,1)}, bf16[9,144,128]{2,1,0:T(8,128)(2,1)S(1)}, u32[]{:S(2)}) copy-start(bf16[9,144,128]{2,1,0:T(8,128)(2,1)S(1)} %collective-permute-done.7.pieces_b_ref) | copy-start | bytes 995332

commit v12 on v11

--- a/solution.py
+++ b/solution.py
@@ -177,36 +177,49 @@
     flags_first, flags_second = first_second(
         pieces_a_ref, pieces_b_ref, (slice(None), slice(PW, PW + 1), slice(None))
     )
-    diag_first = (
-        dot(slabs_first.reshape(picks * PW, PW), upper_first).reshape(picks, PW, PW)
-        * flags_first.astype(jnp.float32)
-    ).astype(jnp.bfloat16)
-    pivot = diag_first[col_panels]
-    own_first = diag_first[:col_panels].reshape(col_panels * PW, PW)
-    diag_update = (
-        slabs_second[:col_panels].reshape(col_panels * PW, PW).astype(jnp.float32)
-        - dot_t(own_first, pivot)
-    ).astype(jnp.bfloat16)
-    diag_second = (
-        dot(diag_update, upper_second).reshape(col_panels, PW, PW)
-        * flags_second[:col_panels].astype(jnp.float32)
-    ).astype(jnp.bfloat16)
-
     cols_first, cols_second = first_second(cols_a_ref, cols_b_ref, slice(0, local_rows))
     rows_first, rows_second = first_second(
         cols_a_ref, cols_b_ref, slice(local_rows, local_rows + block_rows)
     )
-    first_panel = (
-        dot(cols_first, upper_first).reshape(block_rows, RB, PW)
-        * rows_first.astype(jnp.float32)[:, None, :]
-    ).astype(jnp.bfloat16).reshape(local_rows, PW)
-    panel_update = (
-        cols_second.astype(jnp.float32) - dot_t(first_panel, pivot)
+    diag_rows = picks * PW
+    own_rows = col_panels * PW
+    scale_first = jnp.concatenate(
+        (
+            jnp.broadcast_to(flags_first.astype(jnp.float32), (picks, PW, PW)).reshape(diag_rows, PW),
+            jnp.broadcast_to(rows_first.astype(jnp.float32)[:, None, :], (block_rows, RB, PW)).reshape(
+                local_rows, PW
+            ),
+        ),
+        axis=0,
+    )
+    stacked_first = (
+        dot(jnp.concatenate((slabs_first.reshape(diag_rows, PW), cols_first), axis=0), upper_first)
+        * scale_first
     ).astype(jnp.bfloat16)
-    second_panel = (
-        dot(panel_update, upper_second).reshape(block_rows, RB, PW)
-        * rows_second.astype(jnp.float32)[:, None, :]
-    ).astype(jnp.bfloat16).reshape(local_rows, PW)
+    diag_first = stacked_first[:diag_rows].reshape(picks, PW, PW)
+    first_panel = stacked_first[diag_rows:]
+    pivot = diag_first[col_panels]
+    stacked_left = jnp.concatenate((stacked_first[:own_rows], first_panel), axis=0)
+    stacked_raw = jnp.concatenate(
+        (slabs_second[:col_panels].reshape(own_rows, PW), cols_second), axis=0
+    )
+    stacked_update = (
+        stacked_raw.astype(jnp.float32) - dot_t(stacked_left, pivot)
+    ).astype(jnp.bfloat16)
+    scale_second = jnp.concatenate(
+        (
+            jnp.broadcast_to(
+                flags_second[:col_panels].astype(jnp.float32), (col_panels, PW, PW)
+            ).reshape(own_rows, PW),
+            jnp.broadcast_to(rows_second.astype(jnp.float32)[:, None, :], (block_rows, RB, PW)).reshape(
+                local_rows, PW
+            ),
+        ),
+        axis=0,
+    )
+    stacked_second = (dot(stacked_update, upper_second) * scale_second).astype(jnp.bfloat16)
+    diag_second = stacked_second[:own_rows].reshape(col_panels, PW, PW)
+    second_panel = stacked_second[own_rows:]
     both_panels = jnp.concatenate((first_panel, second_panel), axis=1)
 
     all_diag = jnp.concatenate(

time: 30.3 us -> 30.2 us (level)
  no operation moved by 1% of the time
where the time goes in v12:
time: 30.2 us; the launch traced here: 29.9 us
  starting transfers between devices  9.24 us (31%)
  waiting for transfers between devices  7.49 us (25%)
  Pallas kernels  6.5 us (22%)
  local copies, waits for them, and re-layouts  4.71 us (16%)
  other arithmetic  1.87 us (6%)
    ppermute x6, starting transfers between devices, exchange(): return lax.ppermute(value, ('row', 'col'), perm)  9.17 us
    ppermute x6, waiting for transfers between devices, exchange(): return lax.ppermute(value, ('row', 'col'), perm)  7.33 us
    pallas_call x1, Pallas kernels, factor_call(): pl.pallas_call(functools.partial(factor_kernel, by_col=by_col), out_shape...  4.71 us
    unnamed x12, local copies, waits for them, and re-layouts  2.14 us
    pallas_call x1, Pallas kernels, prep_call(): pl.pallas_call(prep_kernel, out_shape=(jax.ShapeDtypeStruct((PW + MASK_RO...  1.79 us
    gather x2, local copies, waits for them, and re-layouts, pick(): slots = slot_of(owner_row[wanted], order_parity)  1.32 us
    gather x2, local copies, waits for them, and re-layouts, pick(): return jnp.take(pieces, slots, axis=0)  1.22 us
    select_n x2, other arithmetic, pick(): return jnp.take(pieces, slots, axis=0)  0.92 us
  transfers between devices with their start and end apart: 8, of which 4 were waited for; matrix products, arithmetic and copies ran while one was open for 18% of the time, Pallas kernels for 0%

profile of v12, /device:TPU:0, one launch (start us, length us, event | category | flops | bytes accessed | tf_op | source)
XLA Modules:
  0.0 29.9 jit_solution(8245419927899522605)
XLA Ops:
  0.0 1.8 %shard_map.46 = (bf16[144,128]{1,0:T(8,128)(2,1)}, bf16[1040,128]{1,0:T(8,128)(2,1)}) custom-call(bf16[1024,1024]{1,0:T(8,128)(2,1)} %matrix_ref.1, s32[16]{0:T(128)} %col_rows_ref.1, s32[4,8]{1,0:T(4,128)} %mask_ref.3), custom_call_target="tpu_custom_call" | custom-call | bytes 524288 | tf_op jit(solution)/shard_map/pallas_call | solution.py:125
  1.8 5.0 %collective-permute-start.3 = (bf16[1,144,128]{2,1,0:T(8,128)(2,1)}, bf16[1,144,128]{2,1,0:T(8,128)(2,1)S(1)}, u32[]{:S(2)}, u32[]{:S(2)}) collective-permute-start(bf16[1,144,128]{2,1,0:T(8,128)(2,1)} %bitcast.10), channel_id=1, source_target_pairs={{0,24},{1,25},{2,26},{3,27},{4,28},{5,29},{6,30},{7,31},{8,16},{9,... | collective-permute-start | bytes 110600 | tf_op jit(solution)/shard_map/ppermute | solution.py:35
  6.8 0.6 %collective-permute-start.1 = (bf16[1,144,128]{2,1,0:T(8,128)(2,1)}, bf16[1,144,128]{2,1,0:T(8,128)(2,1)S(1)}, u32[]{:S(2)}, u32[]{:S(2)}) collective-permute-start(bf16[1,144,128]{2,1,0:T(8,128)(2,1)} %bitcast.12), channel_id=1, source_target_pairs={{0,16},{1,9},{2,18},{3,11},{4,20},{5,13},{6,22},{7,15},{8,24},{9,1... | collective-permute-start | bytes 110600 | tf_op jit(solution)/shard_map/ppermute | solution.py:35
  7.4 0.0 collective-permute-start
  7.4 0.8 %constant_dynamic-update-slice_fusion.6 = bf16[16,144,128]{2,1,0:T(8,128)(2,1)S(1)} fusion(bf16[144,128]{1,0:T(8,128)(2,1)} %get-tuple-element.9), kind=kLoop, calls=%fused_computation.13 | loop fusion | bytes 73728
  8.2 0.1 fusion
  8.3 0.7 %gather_fusion = s32[9]{0:T(128)S(1)} fusion(s32[16]{0:T(128)S(1)} %and_select_fusion, s32[1024]{0:T(1024)S(1)} %pad_clamp_fusion.3), kind=kCustom, calls=%fused_computation.2 | custom fusion | bytes 108 | tf_op jit(solution)/shard_map/gather | solution.py:77
  9.0 0.7 %gather_fusion.1 = s32[9]{0:T(128)S(1)} fusion(s32[16]{0:T(128)S(1)} %and_select_fusion, s32[1024]{0:T(1024)S(1)} %pad_clamp_fusion.1), kind=kCustom, calls=%fused_computation.3 | custom fusion | bytes 108 | tf_op jit(solution)/shard_map/gather | solution.py:77
  9.7 1.3 %collective-permute-done.2 = bf16[1,144,128]{2,1,0:T(8,128)(2,1)S(1)} collective-permute-done((bf16[1,144,128]{2,1,0:T(8,128)(2,1)}, bf16[1,144,128]{2,1,0:T(8,128)(2,1)S(1)}, u32[]{:S(2)}, u32[]{:S(2)}) %collective-permute-start.2) | collective-permute-done | bytes 36896 | tf_op jit(solution)/shard_map/ppermute | solution.py:35
  11.0 0.9 %collective-permute-done.1 = bf16[1,144,128]{2,1,0:T(8,128)(2,1)S(1)} collective-permute-done((bf16[1,144,128]{2,1,0:T(8,128)(2,1)}, bf16[1,144,128]{2,1,0:T(8,128)(2,1)S(1)}, u32[]{:S(2)}, u32[]{:S(2)}) %collective-permute-start.1) | collective-permute-done | bytes 36896 | tf_op jit(solution)/shard_map/ppermute | solution.py:35
  11.9 0.8 %pad_maximum_fusion = bf16[4,144,128]{2,1,0:T(8,128)(2,1)S(1)} fusion(bf16[1,144,128]{2,1,0:T(8,128)(2,1)S(1)} %collective-permute-done.3, bf16[1,144,128]{2,1,0:T(8,128)(2,1)S(1)} %collective-permute-done.2, bf16[1,144,128]{2,1,0:T(8,128)(2,1)S(1)} %collective-permute-done.1, bf16[1,144,128]{2,1,0:T(8,128)(2,1)} %bitcast.13), kind=kLoop, calls=%fused_computation.6 | loop fusion | flops 221184 | bytes 294912 | tf_op jit(solution)/shard_map/concatenate | solution.py:44
  12.7 2.5 %collective-permute-start.6 = (bf16[4,144,128]{2,1,0:T(8,128)(2,1)S(1)}, bf16[4,144,128]{2,1,0:T(8,128)(2,1)S(1)}, u32[]{:S(2)}, u32[]{:S(2)}) collective-permute-start(bf16[4,144,128]{2,1,0:T(8,128)(2,1)S(1)} %pad_maximum_fusion), channel_id=1, source_target_pairs={{0,6},{1,7},{2,4},{3,5},{4,2},{5,3},{6,0},{7,1},{8,14},{9,15},{10,... | collective-permute-start | bytes 442376 | tf_op jit(solution)/shard_map/ppermute | solution.py:35
  15.2 0.5 %collective-permute-start.5 = (bf16[4,144,128]{2,1,0:T(8,128)(2,1)S(1)}, bf16[4,144,128]{2,1,0:T(8,128)(2,1)S(1)}, u32[]{:S(2)}, u32[]{:S(2)}) collective-permute-start(bf16[4,144,128]{2,1,0:T(8,128)(2,1)S(1)} %pad_maximum_fusion), channel_id=1, source_target_pairs={{0,2},{1,5},{2,0},{3,7},{4,6},{5,1},{6,4},{7,3},{8,10},{9,13},{10,... | collective-permute-start | bytes 442376 | tf_op jit(solution)/shard_map/ppermute | solution.py:35
  15.8 0.5 %collective-permute-start.4 = (bf16[4,144,128]{2,1,0:T(8,128)(2,1)S(1)}, bf16[4,144,128]{2,1,0:T(8,128)(2,1)S(1)}, u32[]{:S(2)}, u32[]{:S(2)}) collective-permute-start(bf16[4,144,128]{2,1,0:T(8,128)(2,1)S(1)} %pad_maximum_fusion), channel_id=1, source_target_pairs={{0,4},{1,3},{2,6},{3,1},{4,0},{5,7},{6,2},{7,5},{8,12},{9,11},{10,... | collective-permute-start | bytes 442376 | tf_op jit(solution)/shard_map/ppermute | solution.py:35
  16.3 5.1 %collective-permute-done.4 = bf16[4,144,128]{2,1,0:T(8,128)(2,1)S(1)} collective-permute-done((bf16[4,144,128]{2,1,0:T(8,128)(2,1)S(1)}, bf16[4,144,128]{2,1,0:T(8,128)(2,1)S(1)}, u32[]{:S(2)}, u32[]{:S(2)}) %collective-permute-start.4) | collective-permute-done | bytes 147488 | tf_op jit(solution)/shard_map/ppermute | solution.py:35
  21.5 0.6 %gather_fusion.3 = bf16[9,144,128]{2,1,0:T(8,128)(2,1)S(1)} fusion(bf16[16,144,128]{2,1,0:T(8,128)(2,1)S(1)} %constant_dynamic-update-slice_fusion, s32[1024]{0:T(1024)S(1)} %pad_clamp_fusion), kind=kCustom, calls=%fused_computation.1.clone | custom fusion | bytes 663588 | tf_op jit(solution)/shard_map/jit(_take)/gather | solution.py:78
  22.1 0.1 broadcast_select_fusion
  22.3 0.1 collective-permute-start.7
  22.3 0.6 %gather_fusion.2 = bf16[9,144,128]{2,1,0:T(8,128)(2,1)S(1)} fusion(bf16[16,144,128]{2,1,0:T(8,128)(2,1)S(1)} %constant_dynamic-update-slice_fusion, s32[1024]{0:T(1024)S(1)} %pad_clamp_fusion.2), kind=kCustom, calls=%fused_computation.clone | custom fusion | bytes 663588 | tf_op jit(solution)/shard_map/jit(_take)/gather | solution.py:78
  23.0 0.8 %broadcast_select_fusion.1.pieces_a_ref = bf16[9,144,128]{2,1,0:T(8,128)(2,1)} fusion(bf16[9,144,128]{2,1,0:T(8,128)(2,1)S(1)} %gather_fusion.2, pred[9]{0:T(512)(128)(4,1)S(1)} %get-tuple-element.12), kind=kLoop, calls=%fused_computation.5 | loop fusion | flops 165888 | bytes 663561 | tf_op jit(solution)/shard_map/jit(_take)/select_n | solution.py:78
  23.8 0.2 collective-permute-done.7.pieces_b_ref
  24.0 0.5 %copy-done.1 = bf16[1040,128]{1,0:T(8,128)(2,1)} copy-done((bf16[1040,128]{1,0:T(8,128)(2,1)}, bf16[1040,128]{1,0:T(8,128)(2,1)S(1)}, u32[]{:S(2)}) %copy-start.1) | copy-done | bytes 266264
  24.5 0.7 %copy-done = bf16[9,144,128]{2,1,0:T(8,128)(2,1)} copy-done((bf16[9,144,128]{2,1,0:T(8,128)(2,1)}, bf16[9,144,128]{2,1,0:T(8,128)(2,1)S(1)}, u32[]{:S(2)}) %copy-start) | copy-done | bytes 331800
  25.2 4.7 %shard_map.47 = bf16[1024,1024]{1,0:T(8,128)(2,1)} custom-call(bf16[1024,1024]{1,0:T(8,128)(2,1)} %matrix_ref.1, bf16[1040,128]{1,0:T(8,128)(2,1)} %get-tuple-element.8.cols_a_ref, bf16[1040,128]{1,0:T(8,128)(2,1)} %copy-done.1, bf16[9,144,128]{2,1,0:T(8,128)(2,1)} %broadcast_select_fusion.1.pieces_a_ref, bf16[9,144,128]{2,1,0:T(8,128)(2,1)} %copy-done, ...), custom_call_target="tpu_custom_call" | custom-call | flops 637534208 | bytes 4194304 | tf_op jit(solution)/shard_map/pallas_call | solution.py:250
  (24 shorter events, 0.2 us)
Async XLA Ops:
  0.0 7.4 %copy-start.2 = (s32[16]{0:T(128)S(1)}, s32[16]{0:T(128)}, u32[]{:S(2)}) copy-start(s32[16]{0:T(128)} %col_rows_ref.1) | copy-start | bytes 196
  1.8 7.9 %collective-permute-start.3 = (bf16[1,144,128]{2,1,0:T(8,128)(2,1)}, bf16[1,144,128]{2,1,0:T(8,128)(2,1)S(1)}, u32[]{:S(2)}, u32[]{:S(2)}) collective-permute-start(bf16[1,144,128]{2,1,0:T(8,128)(2,1)} %bitcast.10), channel_id=1, source_target_pairs={{0,24},{1,25},{2,26},{3,27},{4,28},{5,29},{6,30},{7,31},{8,16},{9,... | collective-permute-start | bytes 110600 | tf_op jit(solution)/shard_map/ppermute | solution.py:35
  6.8 4.2 %collective-permute-start.2 = (bf16[1,144,128]{2,1,0:T(8,128)(2,1)}, bf16[1,144,128]{2,1,0:T(8,128)(2,1)S(1)}, u32[]{:S(2)}, u32[]{:S(2)}) collective-permute-start(bf16[1,144,128]{2,1,0:T(8,128)(2,1)} %bitcast.11), channel_id=1, source_target_pairs={{0,8},{1,17},{2,10},{3,19},{4,12},{5,21},{6,14},{7,23},{8,0},{9,25... | collective-permute-start | bytes 110600 | tf_op jit(solution)/shard_map/ppermute | solution.py:35
  6.8 5.1 %collective-permute-start.1 = (bf16[1,144,128]{2,1,0:T(8,128)(2,1)}, bf16[1,144,128]{2,1,0:T(8,128)(2,1)S(1)}, u32[]{:S(2)}, u32[]{:S(2)}) collective-permute-start(bf16[1,144,128]{2,1,0:T(8,128)(2,1)} %bitcast.12), channel_id=1, source_target_pairs={{0,16},{1,9},{2,18},{3,11},{4,20},{5,13},{6,22},{7,15},{8,24},{9,1... | collective-permute-start | bytes 110600 | tf_op jit(solution)/shard_map/ppermute | solution.py:35
  7.4 16.4 %collective-permute-start = (bf16[1040,128]{1,0:T(8,128)(2,1)}, bf16[1040,128]{1,0:T(8,128)(2,1)S(1)}, u32[]{:S(2)}, u32[]{:S(2)}) collective-permute-start(bf16[1040,128]{1,0:T(8,128)(2,1)} %get-tuple-element.8.cols_a_ref), channel_id=1, source_target_pairs={{0,1},{1,0},{2,3},{3,2},{4,5},{5,4},{6,7},{7,6},{8,9},{9,8},{10,11... | collective-permute-start | bytes 798728 | tf_op jit(solution)/shard_map/ppermute | solution.py:84
  12.7 8.8 %collective-permute-start.6 = (bf16[4,144,128]{2,1,0:T(8,128)(2,1)S(1)}, bf16[4,144,128]{2,1,0:T(8,128)(2,1)S(1)}, u32[]{:S(2)}, u32[]{:S(2)}) collective-permute-start(bf16[4,144,128]{2,1,0:T(8,128)(2,1)S(1)} %pad_maximum_fusion), channel_id=1, source_target_pairs={{0,6},{1,7},{2,4},{3,5},{4,2},{5,3},{6,0},{7,1},{8,14},{9,15},{10,... | collective-permute-start | bytes 442376 | tf_op jit(solution)/shard_map/ppermute | solution.py:35
  15.2 6.2 %collective-permute-start.5 = (bf16[4,144,128]{2,1,0:T(8,128)(2,1)S(1)}, bf16[4,144,128]{2,1,0:T(8,128)(2,1)S(1)}, u32[]{:S(2)}, u32[]{:S(2)}) collective-permute-start(bf16[4,144,128]{2,1,0:T(8,128)(2,1)S(1)} %pad_maximum_fusion), channel_id=1, source_target_pairs={{0,2},{1,5},{2,0},{3,7},{4,6},{5,1},{6,4},{7,3},{8,10},{9,13},{10,... | collective-permute-start | bytes 442376 | tf_op jit(solution)/shard_map/ppermute | solution.py:35
  15.8 5.7 %collective-permute-start.4 = (bf16[4,144,128]{2,1,0:T(8,128)(2,1)S(1)}, bf16[4,144,128]{2,1,0:T(8,128)(2,1)S(1)}, u32[]{:S(2)}, u32[]{:S(2)}) collective-permute-start(bf16[4,144,128]{2,1,0:T(8,128)(2,1)S(1)} %pad_maximum_fusion), channel_id=1, source_target_pairs={{0,4},{1,3},{2,6},{3,1},{4,0},{5,7},{6,2},{7,5},{8,12},{9,11},{10,... | collective-permute-start | bytes 442376 | tf_op jit(solution)/shard_map/ppermute | solution.py:35
  22.3 1.7 %collective-permute-start.7 = (bf16[9,144,128]{2,1,0:T(8,128)(2,1)S(1)}, bf16[9,144,128]{2,1,0:T(8,128)(2,1)S(1)}, u32[]{:S(2)}, u32[]{:S(2)}) collective-permute-start(bf16[9,144,128]{2,1,0:T(8,128)(2,1)S(1)} %broadcast_select_fusion), channel_id=1, source_target_pairs={{0,1},{1,0},{2,3},{3,2},{4,5},{5,4},{6,7},{7,6},{8,9},{9,8},{10,11... | collective-permute-start | bytes 995336 | tf_op jit(solution)/shard_map/ppermute | solution.py:87
  23.8 0.7 %copy-start.1 = (bf16[1040,128]{1,0:T(8,128)(2,1)}, bf16[1040,128]{1,0:T(8,128)(2,1)S(1)}, u32[]{:S(2)}) copy-start(bf16[1040,128]{1,0:T(8,128)(2,1)S(1)} %collective-permute-done.cols_b_ref) | copy-start | bytes 798724
  24.5 0.7 %copy-start = (bf16[9,144,128]{2,1,0:T(8,128)(2,1)}, bf16[9,144,128]{2,1,0:T(8,128)(2,1)S(1)}, u32[]{:S(2)}) copy-start(bf16[9,144,128]{2,1,0:T(8,128)(2,1)S(1)} %collective-permute-done.7.pieces_b_ref) | copy-start | bytes 995332

commit v13 on v11

--- a/solution.py
+++ b/solution.py
@@ -22,7 +22,7 @@
     return even, odd
 
 
-def gather_rows(piece, row_count, col_count):
+def gather_rows(piece, row_count, col_count, companion):
     me = lax.axis_index("row")
     parity = lax.axis_index("col") % 2
     bits = row_count.bit_length() - 1
@@ -42,6 +42,8 @@
             masks = [sum(1 << order[p] for p in chosen) for order in (even, odd)]
             parts.append(exchange(held, masks))
         held = jnp.concatenate(parts, axis=0)
+        if start == 0:
+            held, companion = lax.optimization_barrier((held, companion))
 
     def slot_of(owner, order_parity):
         diff = jnp.bitwise_xor(owner, me)
@@ -52,7 +54,7 @@
             slot_odd = slot_odd + ((diff >> odd[position]) & 1) * (1 << position)
         return jnp.where(order_parity == 0, slot_even, slot_odd)
 
-    return held, slot_of, parity
+    return held, slot_of, parity, companion
 
 
 def shards(matrix, fill_mask, col_rows, inverses):
@@ -67,7 +69,12 @@
 
     owner_row = col_rows // local_slabs
     piece, payload = prep_call(matrix, col_rows, fill_mask)
-    held, slot_of, parity = gather_rows(piece, row_count, col_count)
+    if col_count == 2:
+        swap = [(0, 1), (1, 0)]
+        swapped_cols = lax.ppermute(payload, "col", swap)
+    else:
+        swapped_cols = payload
+    held, slot_of, parity, swapped_cols = gather_rows(piece, row_count, col_count, swapped_cols)
 
     def wanted_of(group):
         own = group * col_panels + jnp.arange(col_panels, dtype=jnp.int32)
@@ -79,9 +86,8 @@
 
     wanted = wanted_of(col_index)
     if col_count == 2:
-        swap = [(0, 1), (1, 0)]
         cols_a = payload
-        cols_b = lax.ppermute(payload, "col", swap)
+        cols_b = swapped_cols
         pieces_a = pick(held, wanted, parity)
         for_partner = pick(held, wanted_of(1 - col_index), parity)
         pieces_b = lax.ppermute(for_partner, "col", swap)

time: 30.3 us -> 30.8 us (1.017)
  waiting for transfers between devices: 7.49 us -> 9.39 us
  local copies, waits for them, and re-layouts: 4.71 us -> 3.36 us
    ppermute x6, waiting for transfers between devices: 7.33 us -> 9.22 us  [exchange(): return lax.ppermute(value, ('row', 'col'), perm)]
    unnamed x12 -> x9, local copies, waits for them, and re-layouts: 2.14 us -> 0.79 us
  transfers between devices with their start and end apart: 8 -> 8, of which waited for: 4 -> 5; matrix products, arithmetic and copies ran while one was open for 18% -> 12% of each run, Pallas kernels for 0% -> 0%
where the time goes in v13:
time: 30.8 us; the launch traced here: 30.6 us
  waiting for transfers between devices  9.39 us (30%)
  starting transfers between devices  9.24 us (30%)
  Pallas kernels  6.6 us (21%)
  local copies, waits for them, and re-layouts  3.36 us (11%)
  other arithmetic  1.87 us (6%)
    ppermute x6, waiting for transfers between devices, exchange(): return lax.ppermute(value, ('row', 'col'), perm)  9.22 us
    ppermute x6, starting transfers between devices, exchange(): return lax.ppermute(value, ('row', 'col'), perm)  9.17 us
    pallas_call x1, Pallas kernels, factor_call(): pl.pallas_call(functools.partial(factor_kernel, by_col=by_col), out_shape...  4.82 us
    pallas_call x1, Pallas kernels, prep_call(): pl.pallas_call(prep_kernel, out_shape=(jax.ShapeDtypeStruct((PW + MASK_RO...  1.79 us
    gather x2, local copies, waits for them, and re-layouts, pick(): slots = slot_of(owner_row[wanted], order_parity)  1.32 us
    gather x2, local copies, waits for them, and re-layouts, pick(): return jnp.take(pieces, slots, axis=0)  1.22 us
    select_n x2, other arithmetic, pick(): return jnp.take(pieces, slots, axis=0)  0.92 us
    unnamed x9, local copies, waits for them, and re-layouts  0.79 us
  transfers between devices with their start and end apart: 8, of which 5 were waited for; matrix products, arithmetic and copies ran while one was open for 12% of the time, Pallas kernels for 0%

profile of v13, /device:TPU:0, one launch (start us, length us, event | category | flops | bytes accessed | tf_op | source)
XLA Modules:
  0.0 30.6 jit_solution(16010284091865098146)
XLA Ops:
  0.0 1.8 %shard_map.46 = (bf16[144,128]{1,0:T(8,128)(2,1)}, bf16[1040,128]{1,0:T(8,128)(2,1)}) custom-call(bf16[1024,1024]{1,0:T(8,128)(2,1)} %matrix_ref.1, s32[16]{0:T(128)} %col_rows_ref.1, s32[4,8]{1,0:T(4,128)} %mask_ref.3), custom_call_target="tpu_custom_call" | custom-call | bytes 524288 | tf_op jit(solution)/shard_map/pallas_call | solution.py:131
  1.8 5.0 %collective-permute-start.2 = (bf16[1,144,128]{2,1,0:T(8,128)(2,1)}, bf16[1,144,128]{2,1,0:T(8,128)(2,1)S(1)}, u32[]{:S(2)}, u32[]{:S(2)}) collective-permute-start(bf16[1,144,128]{2,1,0:T(8,128)(2,1)} %bitcast.9), channel_id=1, source_target_pairs={{0,24},{1,25},{2,26},{3,27},{4,28},{5,29},{6,30},{7,31},{8,16},{9,... | collective-permute-start | bytes 110600 | tf_op jit(solution)/shard_map/ppermute | solution.py:35
  6.8 0.6 %collective-permute-start = (bf16[1,144,128]{2,1,0:T(8,128)(2,1)}, bf16[1,144,128]{2,1,0:T(8,128)(2,1)S(1)}, u32[]{:S(2)}, u32[]{:S(2)}) collective-permute-start(bf16[1,144,128]{2,1,0:T(8,128)(2,1)} %bitcast.11), channel_id=1, source_target_pairs={{0,16},{1,9},{2,18},{3,11},{4,20},{5,13},{6,22},{7,15},{8,24},{9,1... | collective-permute-start | bytes 110600 | tf_op jit(solution)/shard_map/ppermute | solution.py:35
  7.4 0.0 collective-permute-start.3
  7.5 0.1 fusion
  7.6 0.7 %gather_fusion = s32[9]{0:T(128)S(1)} fusion(s32[16]{0:T(128)S(1)} %and_select_fusion, s32[1024]{0:T(1024)S(1)} %pad_clamp_fusion.3), kind=kCustom, calls=%fused_computation.2 | custom fusion | bytes 108 | tf_op jit(solution)/shard_map/gather | solution.py:84
  8.2 0.7 %gather_fusion.1 = s32[9]{0:T(128)S(1)} fusion(s32[16]{0:T(128)S(1)} %and_select_fusion, s32[1024]{0:T(1024)S(1)} %pad_clamp_fusion.1), kind=kCustom, calls=%fused_computation.3 | custom fusion | bytes 108 | tf_op jit(solution)/shard_map/gather | solution.py:84
  8.9 0.1 collective-permute-done.2
  9.0 2.0 %collective-permute-done.1 = bf16[1,144,128]{2,1,0:T(8,128)(2,1)S(1)} collective-permute-done((bf16[1,144,128]{2,1,0:T(8,128)(2,1)}, bf16[1,144,128]{2,1,0:T(8,128)(2,1)S(1)}, u32[]{:S(2)}, u32[]{:S(2)}) %collective-permute-start.1) | collective-permute-done | bytes 36896 | tf_op jit(solution)/shard_map/ppermute | solution.py:35
  11.0 0.9 %collective-permute-done = bf16[1,144,128]{2,1,0:T(8,128)(2,1)S(1)} collective-permute-done((bf16[1,144,128]{2,1,0:T(8,128)(2,1)}, bf16[1,144,128]{2,1,0:T(8,128)(2,1)S(1)}, u32[]{:S(2)}, u32[]{:S(2)}) %collective-permute-start) | collective-permute-done | bytes 36896 | tf_op jit(solution)/shard_map/ppermute | solution.py:35
  11.9 0.8 %pad_maximum_fusion = bf16[4,144,128]{2,1,0:T(8,128)(2,1)S(1)} fusion(bf16[1,144,128]{2,1,0:T(8,128)(2,1)S(1)} %collective-permute-done.2, bf16[1,144,128]{2,1,0:T(8,128)(2,1)S(1)} %collective-permute-done.1, bf16[1,144,128]{2,1,0:T(8,128)(2,1)S(1)} %collective-permute-done, bf16[1,144,128]{2,1,0:T(8,128)(2,1)} %bitcast.12), kind=kLoop, calls=%fused_computation.6 | loop fusion | flops 221184 | bytes 294912 | tf_op jit(solution)/shard_map/concatenate | solution.py:44
  12.7 0.0 collective-permute-done.3.cols_b_ref
  12.7 1.6 %collective-permute-start.4 = (bf16[4,144,128]{2,1,0:T(8,128)(2,1)S(1)}, bf16[4,144,128]{2,1,0:T(8,128)(2,1)S(1)}, u32[]{:S(2)}, u32[]{:S(2)}) collective-permute-start(bf16[4,144,128]{2,1,0:T(8,128)(2,1)S(1)} %pad_maximum_fusion), channel_id=1, source_target_pairs={{0,4},{1,3},{2,6},{3,1},{4,0},{5,7},{6,2},{7,5},{8,12},{9,11},{10,... | collective-permute-start | bytes 442376 | tf_op jit(solution)/shard_map/ppermute | solution.py:35
  14.3 1.4 %collective-permute-start.6 = (bf16[4,144,128]{2,1,0:T(8,128)(2,1)S(1)}, bf16[4,144,128]{2,1,0:T(8,128)(2,1)S(1)}, u32[]{:S(2)}, u32[]{:S(2)}) collective-permute-start(bf16[4,144,128]{2,1,0:T(8,128)(2,1)S(1)} %pad_maximum_fusion), channel_id=1, source_target_pairs={{0,6},{1,7},{2,4},{3,5},{4,2},{5,3},{6,0},{7,1},{8,14},{9,15},{10,... | collective-permute-start | bytes 442376 | tf_op jit(solution)/shard_map/ppermute | solution.py:35
  15.8 0.5 %collective-permute-start.5 = (bf16[4,144,128]{2,1,0:T(8,128)(2,1)S(1)}, bf16[4,144,128]{2,1,0:T(8,128)(2,1)S(1)}, u32[]{:S(2)}, u32[]{:S(2)}) collective-permute-start(bf16[4,144,128]{2,1,0:T(8,128)(2,1)S(1)} %pad_maximum_fusion), channel_id=1, source_target_pairs={{0,2},{1,5},{2,0},{3,7},{4,6},{5,1},{6,4},{7,3},{8,10},{9,13},{10,... | collective-permute-start | bytes 442376 | tf_op jit(solution)/shard_map/ppermute | solution.py:35
  16.3 6.2 %collective-permute-done.4 = bf16[4,144,128]{2,1,0:T(8,128)(2,1)S(1)} collective-permute-done((bf16[4,144,128]{2,1,0:T(8,128)(2,1)S(1)}, bf16[4,144,128]{2,1,0:T(8,128)(2,1)S(1)}, u32[]{:S(2)}, u32[]{:S(2)}) %collective-permute-start.4) | collective-permute-done | bytes 147488 | tf_op jit(solution)/shard_map/ppermute | solution.py:35
  22.6 0.6 %gather_fusion.3 = bf16[9,144,128]{2,1,0:T(8,128)(2,1)S(1)} fusion(bf16[16,144,128]{2,1,0:T(8,128)(2,1)S(1)} %constant_dynamic-update-slice_fusion, s32[1024]{0:T(1024)S(1)} %pad_clamp_fusion), kind=kCustom, calls=%fused_computation.1.clone | custom fusion | bytes 663588 | tf_op jit(solution)/shard_map/jit(_take)/gather | solution.py:85
  23.3 0.1 broadcast_select_fusion
  23.4 0.1 collective-permute-start.7
  23.5 0.6 %gather_fusion.2 = bf16[9,144,128]{2,1,0:T(8,128)(2,1)S(1)} fusion(bf16[16,144,128]{2,1,0:T(8,128)(2,1)S(1)} %constant_dynamic-update-slice_fusion, s32[1024]{0:T(1024)S(1)} %pad_clamp_fusion.2), kind=kCustom, calls=%fused_computation.clone | custom fusion | bytes 663588 | tf_op jit(solution)/shard_map/jit(_take)/gather | solution.py:85
  24.1 0.8 %broadcast_select_fusion.1.pieces_a_ref = bf16[9,144,128]{2,1,0:T(8,128)(2,1)} fusion(bf16[9,144,128]{2,1,0:T(8,128)(2,1)S(1)} %gather_fusion.2, pred[9]{0:T(512)(128)(4,1)S(1)} %get-tuple-element.16), kind=kLoop, calls=%fused_computation.5 | loop fusion | flops 165888 | bytes 663561 | tf_op jit(solution)/shard_map/jit(_take)/select_n | solution.py:85
  24.9 0.2 collective-permute-done.7.pieces_b_ref
  25.1 0.7 %copy-done = bf16[9,144,128]{2,1,0:T(8,128)(2,1)} copy-done((bf16[9,144,128]{2,1,0:T(8,128)(2,1)}, bf16[9,144,128]{2,1,0:T(8,128)(2,1)S(1)}, u32[]{:S(2)}) %copy-start) | copy-done | bytes 331800
  25.8 4.8 %shard_map.47 = bf16[1024,1024]{1,0:T(8,128)(2,1)} custom-call(bf16[1024,1024]{1,0:T(8,128)(2,1)} %matrix_ref.1, bf16[1040,128]{1,0:T(8,128)(2,1)} %get-tuple-element.10.cols_a_ref, bf16[1040,128]{1,0:T(8,128)(2,1)} %copy-done.1, bf16[9,144,128]{2,1,0:T(8,128)(2,1)} %broadcast_select_fusion.1.pieces_a_ref, bf16[9,144,128]{2,1,0:T(8,128)(2,1)} %copy-done, ...), custom_call_target="tpu_custom_call" | custom-call | flops 637534208 | bytes 4194304 | tf_op jit(solution)/shard_map/pallas_call | solution.py:243
  (21 shorter events, 0.2 us)
Async XLA Ops:
  0.0 7.4 %copy-start.2 = (s32[16]{0:T(128)S(1)}, s32[16]{0:T(128)}, u32[]{:S(2)}) copy-start(s32[16]{0:T(128)} %col_rows_ref.1) | copy-start | bytes 196
  1.8 7.2 %collective-permute-start.2 = (bf16[1,144,128]{2,1,0:T(8,128)(2,1)}, bf16[1,144,128]{2,1,0:T(8,128)(2,1)S(1)}, u32[]{:S(2)}, u32[]{:S(2)}) collective-permute-start(bf16[1,144,128]{2,1,0:T(8,128)(2,1)} %bitcast.9), channel_id=1, source_target_pairs={{0,24},{1,25},{2,26},{3,27},{4,28},{5,29},{6,30},{7,31},{8,16},{9,... | collective-permute-start | bytes 110600 | tf_op jit(solution)/shard_map/ppermute | solution.py:35
  6.8 4.2 %collective-permute-start.1 = (bf16[1,144,128]{2,1,0:T(8,128)(2,1)}, bf16[1,144,128]{2,1,0:T(8,128)(2,1)S(1)}, u32[]{:S(2)}, u32[]{:S(2)}) collective-permute-start(bf16[1,144,128]{2,1,0:T(8,128)(2,1)} %bitcast.10), channel_id=1, source_target_pairs={{0,8},{1,17},{2,10},{3,19},{4,12},{5,21},{6,14},{7,23},{8,0},{9,25... | collective-permute-start | bytes 110600 | tf_op jit(solution)/shard_map/ppermute | solution.py:35
  6.8 5.1 %collective-permute-start = (bf16[1,144,128]{2,1,0:T(8,128)(2,1)}, bf16[1,144,128]{2,1,0:T(8,128)(2,1)S(1)}, u32[]{:S(2)}, u32[]{:S(2)}) collective-permute-start(bf16[1,144,128]{2,1,0:T(8,128)(2,1)} %bitcast.11), channel_id=1, source_target_pairs={{0,16},{1,9},{2,18},{3,11},{4,20},{5,13},{6,22},{7,15},{8,24},{9,1... | collective-permute-start | bytes 110600 | tf_op jit(solution)/shard_map/ppermute | solution.py:35
  7.4 5.3 %collective-permute-start.3 = (bf16[1040,128]{1,0:T(8,128)(2,1)}, bf16[1040,128]{1,0:T(8,128)(2,1)S(1)}, u32[]{:S(2)}, u32[]{:S(2)}) collective-permute-start(bf16[1040,128]{1,0:T(8,128)(2,1)} %get-tuple-element.10.cols_a_ref), channel_id=1, source_target_pairs={{0,1},{1,0},{2,3},{3,2},{4,5},{5,4},{6,7},{7,6},{8,9},{9,8},{10,11... | collective-permute-start | bytes 798728 | tf_op jit(solution)/shard_map/ppermute | solution.py:74
  12.7 12.4 %copy-start.1 = (bf16[1040,128]{1,0:T(8,128)(2,1)}, bf16[1040,128]{1,0:T(8,128)(2,1)S(1)}, u32[]{:S(2)}) copy-start(bf16[1040,128]{1,0:T(8,128)(2,1)S(1)} %collective-permute-done.3.cols_b_ref) | copy-start | bytes 798724
  12.7 9.8 %collective-permute-start.4 = (bf16[4,144,128]{2,1,0:T(8,128)(2,1)S(1)}, bf16[4,144,128]{2,1,0:T(8,128)(2,1)S(1)}, u32[]{:S(2)}, u32[]{:S(2)}) collective-permute-start(bf16[4,144,128]{2,1,0:T(8,128)(2,1)S(1)} %pad_maximum_fusion), channel_id=1, source_target_pairs={{0,4},{1,3},{2,6},{3,1},{4,0},{5,7},{6,2},{7,5},{8,12},{9,11},{10,... | collective-permute-start | bytes 442376 | tf_op jit(solution)/shard_map/ppermute | solution.py:35
  14.3 8.3 %collective-permute-start.6 = (bf16[4,144,128]{2,1,0:T(8,128)(2,1)S(1)}, bf16[4,144,128]{2,1,0:T(8,128)(2,1)S(1)}, u32[]{:S(2)}, u32[]{:S(2)}) collective-permute-start(bf16[4,144,128]{2,1,0:T(8,128)(2,1)S(1)} %pad_maximum_fusion), channel_id=1, source_target_pairs={{0,6},{1,7},{2,4},{3,5},{4,2},{5,3},{6,0},{7,1},{8,14},{9,15},{10,... | collective-permute-start | bytes 442376 | tf_op jit(solution)/shard_map/ppermute | solution.py:35
  15.8 6.8 %collective-permute-start.5 = (bf16[4,144,128]{2,1,0:T(8,128)(2,1)S(1)}, bf16[4,144,128]{2,1,0:T(8,128)(2,1)S(1)}, u32[]{:S(2)}, u32[]{:S(2)}) collective-permute-start(bf16[4,144,128]{2,1,0:T(8,128)(2,1)S(1)} %pad_maximum_fusion), channel_id=1, source_target_pairs={{0,2},{1,5},{2,0},{3,7},{4,6},{5,1},{6,4},{7,3},{8,10},{9,13},{10,... | collective-permute-start | bytes 442376 | tf_op jit(solution)/shard_map/ppermute | solution.py:35
  23.4 1.7 %collective-permute-start.7 = (bf16[9,144,128]{2,1,0:T(8,128)(2,1)S(1)}, bf16[9,144,128]{2,1,0:T(8,128)(2,1)S(1)}, u32[]{:S(2)}, u32[]{:S(2)}) collective-permute-start(bf16[9,144,128]{2,1,0:T(8,128)(2,1)S(1)} %broadcast_select_fusion), channel_id=1, source_target_pairs={{0,1},{1,0},{2,3},{3,2},{4,5},{5,4},{6,7},{7,6},{8,9},{9,8},{10,11... | collective-permute-start | bytes 995336 | tf_op jit(solution)/shard_map/ppermute | solution.py:93
  25.1 0.7 %copy-start = (bf16[9,144,128]{2,1,0:T(8,128)(2,1)}, bf16[9,144,128]{2,1,0:T(8,128)(2,1)S(1)}, u32[]{:S(2)}) copy-start(bf16[9,144,128]{2,1,0:T(8,128)(2,1)S(1)} %collective-permute-done.7.pieces_b_ref) | copy-start | bytes 995332

commit v14 on v11

--- a/solution.py
+++ b/solution.py
@@ -108,10 +108,13 @@
         place = place + jnp.where(entry // local_slabs == row_index, entry % local_slabs, 0)
     place = jnp.minimum(place, local_slabs - 1)
     start = pl.multiple_of(place * PW, PW)
-    piece_ref[0:PW, :] = lead_ref[pl.ds(start, PW), :]
-    flag = mask_ref[place // (RB // PW), 0].astype(jnp.float32)
+    flag = mask_ref[place // (RB // PW), 0]
+    slab = lead_ref[pl.ds(start, PW), :].astype(jnp.float32)
+    corner = (lax.broadcasted_iota(jnp.int32, (PW, PW), 0) == 0) & (
+        lax.broadcasted_iota(jnp.int32, (PW, PW), 1) == 0
+    )
+    piece_ref[...] = jnp.where(corner & (flag == 0), jnp.nan, slab).astype(jnp.bfloat16)
     row_ids = lax.broadcasted_iota(jnp.int32, (MASK_ROWS, PW), 0)
-    piece_ref[PW : PW + MASK_ROWS, :] = jnp.where(row_ids == 0, flag, 0.0).astype(jnp.bfloat16)
     payload_ref[0:local_rows, :] = lead_ref[...]
     mask_rows = jnp.zeros((MASK_ROWS, PW), jnp.float32)
     for b in range(block_rows):
@@ -125,13 +128,13 @@
     return pl.pallas_call(
         prep_kernel,
         out_shape=(
-            jax.ShapeDtypeStruct((PW + MASK_ROWS, PW), jnp.bfloat16),
+            jax.ShapeDtypeStruct((PW, PW), jnp.bfloat16),
             jax.ShapeDtypeStruct((local_rows + MASK_ROWS, PW), jnp.bfloat16),
         ),
         grid=(1,),
         in_specs=[pl.BlockSpec((local_rows, PW), lambda i: (0, 0)), smem, smem],
         out_specs=(
-            pl.BlockSpec((PW + MASK_ROWS, PW), lambda i: (0, 0)),
+            pl.BlockSpec((PW, PW), lambda i: (0, 0)),
             pl.BlockSpec((local_rows + MASK_ROWS, PW), lambda i: (0, 0)),
         ),
         cost_estimate=pl.CostEstimate(
@@ -172,14 +175,17 @@
     upper_second = jnp.where(upper, inv_ref[1], zero)
 
     slabs_first, slabs_second = first_second(
-        pieces_a_ref, pieces_b_ref, (slice(None), slice(0, PW), slice(None))
-    )
-    flags_first, flags_second = first_second(
-        pieces_a_ref, pieces_b_ref, (slice(None), slice(PW, PW + 1), slice(None))
-    )
-    diag_first = (
-        dot(slabs_first.reshape(picks * PW, PW), upper_first).reshape(picks, PW, PW)
-        * flags_first.astype(jnp.float32)
+        pieces_a_ref, pieces_b_ref, (slice(None), slice(None), slice(None))
+    )
+
+    def filled(slabs):
+        corner = slabs[:, 0:1, 0:1].astype(jnp.float32)
+        return jnp.broadcast_to(corner == corner, slabs.shape)
+
+    diag_first = jnp.where(
+        filled(slabs_first),
+        dot(slabs_first.reshape(picks * PW, PW), upper_first).reshape(picks, PW, PW),
+        0.0,
     ).astype(jnp.bfloat16)
     pivot = diag_first[col_panels]
     own_first = diag_first[:col_panels].reshape(col_panels * PW, PW)
@@ -187,9 +193,10 @@
         slabs_second[:col_panels].reshape(col_panels * PW, PW).astype(jnp.float32)
         - dot_t(own_first, pivot)
     ).astype(jnp.bfloat16)
-    diag_second = (
-        dot(diag_update, upper_second).reshape(col_panels, PW, PW)
-        * flags_second[:col_panels].astype(jnp.float32)
+    diag_second = jnp.where(
+        filled(slabs_second[:col_panels]),
+        dot(diag_update, upper_second).reshape(col_panels, PW, PW),
+        0.0,
     ).astype(jnp.bfloat16)
 
     cols_first, cols_second = first_second(cols_a_ref, cols_b_ref, slice(0, local_rows))

time: 30.3 us -> 29.9 us (0.987)
  waiting for transfers between devices: 7.49 us -> 7.07 us
    ppermute x6, waiting for transfers between devices: 7.33 us -> 6.93 us  [exchange(): return lax.ppermute(value, ('row', 'col'), perm)]
where the time goes in v14:
time: 29.9 us; the launch traced here: 29.5 us
  starting transfers between devices  9.24 us (31%)
  waiting for transfers between devices  7.07 us (24%)
  Pallas kernels  6.61 us (22%)
  local copies, waits for them, and re-layouts  4.66 us (16%)
  other arithmetic  1.83 us (6%)
    ppermute x6, starting transfers between devices, exchange(): return lax.ppermute(value, ('row', 'col'), perm)  9.17 us
    ppermute x6, waiting for transfers between devices, exchange(): return lax.ppermute(value, ('row', 'col'), perm)  6.93 us
    pallas_call x1, Pallas kernels, factor_call(): pl.pallas_call(functools.partial(factor_kernel, by_col=by_col), out_shape...  4.82 us
    unnamed x12, local copies, waits for them, and re-layouts  2.11 us
    pallas_call x1, Pallas kernels, prep_call(): pl.pallas_call(prep_kernel, out_shape=(jax.ShapeDtypeStruct((PW, PW), jnp...  1.79 us
    gather x2, local copies, waits for them, and re-layouts, pick(): slots = slot_of(owner_row[wanted], order_parity)  1.32 us
    gather x2, local copies, waits for them, and re-layouts, pick(): return jnp.take(pieces, slots, axis=0)  1.21 us
    select_n x2, other arithmetic, pick(): return jnp.take(pieces, slots, axis=0)  0.9 us
  transfers between devices with their start and end apart: 8, of which 4 were waited for; matrix products, arithmetic and copies ran while one was open for 18% of the time, Pallas kernels for 0%

profile of v14, /device:TPU:0, one launch (start us, length us, event | category | flops | bytes accessed | tf_op | source)
XLA Modules:
  0.0 29.5 jit_solution(4015911389992385155)
XLA Ops:
  0.0 1.8 %shard_map.46 = (bf16[128,128]{1,0:T(8,128)(2,1)}, bf16[1040,128]{1,0:T(8,128)(2,1)}) custom-call(bf16[1024,1024]{1,0:T(8,128)(2,1)} %matrix_ref.1, s32[16]{0:T(128)} %col_rows_ref.1, s32[4,8]{1,0:T(4,128)} %mask_ref.3), custom_call_target="tpu_custom_call" | custom-call | bytes 524288 | tf_op jit(solution)/shard_map/pallas_call | solution.py:128
  1.8 5.0 %collective-permute-start.3 = (bf16[1,128,128]{2,1,0:T(8,128)(2,1)}, bf16[1,128,128]{2,1,0:T(8,128)(2,1)S(1)}, u32[]{:S(2)}, u32[]{:S(2)}) collective-permute-start(bf16[1,128,128]{2,1,0:T(8,128)(2,1)} %bitcast.10), channel_id=1, source_target_pairs={{0,24},{1,25},{2,26},{3,27},{4,28},{5,29},{6,30},{7,31},{8,16},{9,... | collective-permute-start | bytes 98312 | tf_op jit(solution)/shard_map/ppermute | solution.py:35
  6.8 0.0 collective-permute-start.2
  6.8 0.6 %collective-permute-start.1 = (bf16[1,128,128]{2,1,0:T(8,128)(2,1)}, bf16[1,128,128]{2,1,0:T(8,128)(2,1)S(1)}, u32[]{:S(2)}, u32[]{:S(2)}) collective-permute-start(bf16[1,128,128]{2,1,0:T(8,128)(2,1)} %bitcast.12), channel_id=1, source_target_pairs={{0,16},{1,9},{2,18},{3,11},{4,20},{5,13},{6,22},{7,15},{8,24},{9,1... | collective-permute-start | bytes 98312 | tf_op jit(solution)/shard_map/ppermute | solution.py:35
  7.4 0.8 %constant_dynamic-update-slice_fusion.6 = bf16[16,128,128]{2,1,0:T(8,128)(2,1)S(1)} fusion(bf16[128,128]{1,0:T(8,128)(2,1)} %get-tuple-element.9), kind=kLoop, calls=%fused_computation.13 | loop fusion | bytes 65536
  8.2 0.1 fusion
  8.3 0.7 %gather_fusion = s32[9]{0:T(128)S(1)} fusion(s32[16]{0:T(128)S(1)} %and_select_fusion, s32[1024]{0:T(1024)S(1)} %pad_clamp_fusion.3), kind=kCustom, calls=%fused_computation.2 | custom fusion | bytes 108 | tf_op jit(solution)/shard_map/gather | solution.py:77
  9.0 0.7 %gather_fusion.1 = s32[9]{0:T(128)S(1)} fusion(s32[16]{0:T(128)S(1)} %and_select_fusion, s32[1024]{0:T(1024)S(1)} %pad_clamp_fusion.1), kind=kCustom, calls=%fused_computation.3 | custom fusion | bytes 108 | tf_op jit(solution)/shard_map/gather | solution.py:77
  9.7 1.3 %collective-permute-done.2 = bf16[1,128,128]{2,1,0:T(8,128)(2,1)S(1)} collective-permute-done((bf16[1,128,128]{2,1,0:T(8,128)(2,1)}, bf16[1,128,128]{2,1,0:T(8,128)(2,1)S(1)}, u32[]{:S(2)}, u32[]{:S(2)}) %collective-permute-start.2) | collective-permute-done | bytes 32800 | tf_op jit(solution)/shard_map/ppermute | solution.py:35
  11.0 0.9 %collective-permute-done.1 = bf16[1,128,128]{2,1,0:T(8,128)(2,1)S(1)} collective-permute-done((bf16[1,128,128]{2,1,0:T(8,128)(2,1)}, bf16[1,128,128]{2,1,0:T(8,128)(2,1)S(1)}, u32[]{:S(2)}, u32[]{:S(2)}) %collective-permute-start.1) | collective-permute-done | bytes 32800 | tf_op jit(solution)/shard_map/ppermute | solution.py:35
  11.9 0.8 %pad_maximum_fusion = bf16[4,128,128]{2,1,0:T(8,128)(2,1)S(1)} fusion(bf16[1,128,128]{2,1,0:T(8,128)(2,1)S(1)} %collective-permute-done.3, bf16[1,128,128]{2,1,0:T(8,128)(2,1)S(1)} %collective-permute-done.2, bf16[1,128,128]{2,1,0:T(8,128)(2,1)S(1)} %collective-permute-done.1, bf16[1,128,128]{2,1,0:T(8,128)(2,1)} %bitcast.13), kind=kLoop, calls=%fused_computation.6 | loop fusion | flops 196608 | bytes 262144 | tf_op jit(solution)/shard_map/concatenate | solution.py:44
  12.7 2.5 %collective-permute-start.6 = (bf16[4,128,128]{2,1,0:T(8,128)(2,1)S(1)}, bf16[4,128,128]{2,1,0:T(8,128)(2,1)S(1)}, u32[]{:S(2)}, u32[]{:S(2)}) collective-permute-start(bf16[4,128,128]{2,1,0:T(8,128)(2,1)S(1)} %pad_maximum_fusion), channel_id=1, source_target_pairs={{0,6},{1,7},{2,4},{3,5},{4,2},{5,3},{6,0},{7,1},{8,14},{9,15},{10,... | collective-permute-start | bytes 393224 | tf_op jit(solution)/shard_map/ppermute | solution.py:35
  15.2 0.5 %collective-permute-start.5 = (bf16[4,128,128]{2,1,0:T(8,128)(2,1)S(1)}, bf16[4,128,128]{2,1,0:T(8,128)(2,1)S(1)}, u32[]{:S(2)}, u32[]{:S(2)}) collective-permute-start(bf16[4,128,128]{2,1,0:T(8,128)(2,1)S(1)} %pad_maximum_fusion), channel_id=1, source_target_pairs={{0,2},{1,5},{2,0},{3,7},{4,6},{5,1},{6,4},{7,3},{8,10},{9,13},{10,... | collective-permute-start | bytes 393224 | tf_op jit(solution)/shard_map/ppermute | solution.py:35
  15.7 0.5 %collective-permute-start.4 = (bf16[4,128,128]{2,1,0:T(8,128)(2,1)S(1)}, bf16[4,128,128]{2,1,0:T(8,128)(2,1)S(1)}, u32[]{:S(2)}, u32[]{:S(2)}) collective-permute-start(bf16[4,128,128]{2,1,0:T(8,128)(2,1)S(1)} %pad_maximum_fusion), channel_id=1, source_target_pairs={{0,4},{1,3},{2,6},{3,1},{4,0},{5,7},{6,2},{7,5},{8,12},{9,11},{10,... | collective-permute-start | bytes 393224 | tf_op jit(solution)/shard_map/ppermute | solution.py:35
  16.2 4.8 %collective-permute-done.4 = bf16[4,128,128]{2,1,0:T(8,128)(2,1)S(1)} collective-permute-done((bf16[4,128,128]{2,1,0:T(8,128)(2,1)S(1)}, bf16[4,128,128]{2,1,0:T(8,128)(2,1)S(1)}, u32[]{:S(2)}, u32[]{:S(2)}) %collective-permute-start.4) | collective-permute-done | bytes 131104 | tf_op jit(solution)/shard_map/ppermute | solution.py:35
  21.1 0.6 %gather_fusion.3 = bf16[9,128,128]{2,1,0:T(8,128)(2,1)S(1)} fusion(bf16[16,128,128]{2,1,0:T(8,128)(2,1)S(1)} %constant_dynamic-update-slice_fusion, s32[1024]{0:T(1024)S(1)} %pad_clamp_fusion), kind=kCustom, calls=%fused_computation.1.clone | custom fusion | bytes 589860 | tf_op jit(solution)/shard_map/jit(_take)/gather | solution.py:78
  21.7 0.1 broadcast_select_fusion
  21.8 0.1 collective-permute-start.7
  21.9 0.6 %gather_fusion.2 = bf16[9,128,128]{2,1,0:T(8,128)(2,1)S(1)} fusion(bf16[16,128,128]{2,1,0:T(8,128)(2,1)S(1)} %constant_dynamic-update-slice_fusion, s32[1024]{0:T(1024)S(1)} %pad_clamp_fusion.2), kind=kCustom, calls=%fused_computation.clone | custom fusion | bytes 589860 | tf_op jit(solution)/shard_map/jit(_take)/gather | solution.py:78
  22.5 0.8 %broadcast_select_fusion.1.pieces_a_ref = bf16[9,128,128]{2,1,0:T(8,128)(2,1)} fusion(bf16[9,128,128]{2,1,0:T(8,128)(2,1)S(1)} %gather_fusion.2, pred[9]{0:T(512)(128)(4,1)S(1)} %get-tuple-element.12), kind=kLoop, calls=%fused_computation.5 | loop fusion | flops 147456 | bytes 589833 | tf_op jit(solution)/shard_map/jit(_take)/select_n | solution.py:78
  23.3 0.1 collective-permute-done.7.pieces_b_ref
  23.5 0.6 %copy-done.1 = bf16[1040,128]{1,0:T(8,128)(2,1)} copy-done((bf16[1040,128]{1,0:T(8,128)(2,1)}, bf16[1040,128]{1,0:T(8,128)(2,1)S(1)}, u32[]{:S(2)}) %copy-start.1) | copy-done | bytes 266264
  24.0 0.7 %copy-done = bf16[9,128,128]{2,1,0:T(8,128)(2,1)} copy-done((bf16[9,128,128]{2,1,0:T(8,128)(2,1)}, bf16[9,128,128]{2,1,0:T(8,128)(2,1)S(1)}, u32[]{:S(2)}) %copy-start) | copy-done | bytes 294936
  24.7 4.8 %shard_map.47 = bf16[1024,1024]{1,0:T(8,128)(2,1)} custom-call(bf16[1024,1024]{1,0:T(8,128)(2,1)} %matrix_ref.1, bf16[1040,128]{1,0:T(8,128)(2,1)} %get-tuple-element.8.cols_a_ref, bf16[1040,128]{1,0:T(8,128)(2,1)} %copy-done.1, bf16[9,128,128]{2,1,0:T(8,128)(2,1)} %broadcast_select_fusion.1.pieces_a_ref, bf16[9,128,128]{2,1,0:T(8,128)(2,1)} %copy-done, ...), custom_call_target="tpu_custom_call" | custom-call | flops 637534208 | bytes 4194304 | tf_op jit(solution)/shard_map/pallas_call | solution.py:244
  (24 shorter events, 0.2 us)
Async XLA Ops:
  0.0 7.4 %copy-start.2 = (s32[16]{0:T(128)S(1)}, s32[16]{0:T(128)}, u32[]{:S(2)}) copy-start(s32[16]{0:T(128)} %col_rows_ref.1) | copy-start | bytes 196
  1.8 7.9 %collective-permute-start.3 = (bf16[1,128,128]{2,1,0:T(8,128)(2,1)}, bf16[1,128,128]{2,1,0:T(8,128)(2,1)S(1)}, u32[]{:S(2)}, u32[]{:S(2)}) collective-permute-start(bf16[1,128,128]{2,1,0:T(8,128)(2,1)} %bitcast.10), channel_id=1, source_target_pairs={{0,24},{1,25},{2,26},{3,27},{4,28},{5,29},{6,30},{7,31},{8,16},{9,... | collective-permute-start | bytes 98312 | tf_op jit(solution)/shard_map/ppermute | solution.py:35
  6.8 4.1 %collective-permute-start.2 = (bf16[1,128,128]{2,1,0:T(8,128)(2,1)}, bf16[1,128,128]{2,1,0:T(8,128)(2,1)S(1)}, u32[]{:S(2)}, u32[]{:S(2)}) collective-permute-start(bf16[1,128,128]{2,1,0:T(8,128)(2,1)} %bitcast.11), channel_id=1, source_target_pairs={{0,8},{1,17},{2,10},{3,19},{4,12},{5,21},{6,14},{7,23},{8,0},{9,25... | collective-permute-start | bytes 98312 | tf_op jit(solution)/shard_map/ppermute | solution.py:35
  6.8 5.0 %collective-permute-start.1 = (bf16[1,128,128]{2,1,0:T(8,128)(2,1)}, bf16[1,128,128]{2,1,0:T(8,128)(2,1)S(1)}, u32[]{:S(2)}, u32[]{:S(2)}) collective-permute-start(bf16[1,128,128]{2,1,0:T(8,128)(2,1)} %bitcast.12), channel_id=1, source_target_pairs={{0,16},{1,9},{2,18},{3,11},{4,20},{5,13},{6,22},{7,15},{8,24},{9,1... | collective-permute-start | bytes 98312 | tf_op jit(solution)/shard_map/ppermute | solution.py:35
  7.4 15.9 %collective-permute-start = (bf16[1040,128]{1,0:T(8,128)(2,1)}, bf16[1040,128]{1,0:T(8,128)(2,1)S(1)}, u32[]{:S(2)}, u32[]{:S(2)}) collective-permute-start(bf16[1040,128]{1,0:T(8,128)(2,1)} %get-tuple-element.8.cols_a_ref), channel_id=1, source_target_pairs={{0,1},{1,0},{2,3},{3,2},{4,5},{5,4},{6,7},{7,6},{8,9},{9,8},{10,11... | collective-permute-start | bytes 798728 | tf_op jit(solution)/shard_map/ppermute | solution.py:84
  12.7 8.4 %collective-permute-start.6 = (bf16[4,128,128]{2,1,0:T(8,128)(2,1)S(1)}, bf16[4,128,128]{2,1,0:T(8,128)(2,1)S(1)}, u32[]{:S(2)}, u32[]{:S(2)}) collective-permute-start(bf16[4,128,128]{2,1,0:T(8,128)(2,1)S(1)} %pad_maximum_fusion), channel_id=1, source_target_pairs={{0,6},{1,7},{2,4},{3,5},{4,2},{5,3},{6,0},{7,1},{8,14},{9,15},{10,... | collective-permute-start | bytes 393224 | tf_op jit(solution)/shard_map/ppermute | solution.py:35
  15.2 5.9 %collective-permute-start.5 = (bf16[4,128,128]{2,1,0:T(8,128)(2,1)S(1)}, bf16[4,128,128]{2,1,0:T(8,128)(2,1)S(1)}, u32[]{:S(2)}, u32[]{:S(2)}) collective-permute-start(bf16[4,128,128]{2,1,0:T(8,128)(2,1)S(1)} %pad_maximum_fusion), channel_id=1, source_target_pairs={{0,2},{1,5},{2,0},{3,7},{4,6},{5,1},{6,4},{7,3},{8,10},{9,13},{10,... | collective-permute-start | bytes 393224 | tf_op jit(solution)/shard_map/ppermute | solution.py:35
  15.7 5.3 %collective-permute-start.4 = (bf16[4,128,128]{2,1,0:T(8,128)(2,1)S(1)}, bf16[4,128,128]{2,1,0:T(8,128)(2,1)S(1)}, u32[]{:S(2)}, u32[]{:S(2)}) collective-permute-start(bf16[4,128,128]{2,1,0:T(8,128)(2,1)S(1)} %pad_maximum_fusion), channel_id=1, source_target_pairs={{0,4},{1,3},{2,6},{3,1},{4,0},{5,7},{6,2},{7,5},{8,12},{9,11},{10,... | collective-permute-start | bytes 393224 | tf_op jit(solution)/shard_map/ppermute | solution.py:35
  21.8 1.6 %collective-permute-start.7 = (bf16[9,128,128]{2,1,0:T(8,128)(2,1)S(1)}, bf16[9,128,128]{2,1,0:T(8,128)(2,1)S(1)}, u32[]{:S(2)}, u32[]{:S(2)}) collective-permute-start(bf16[9,128,128]{2,1,0:T(8,128)(2,1)S(1)} %broadcast_select_fusion), channel_id=1, source_target_pairs={{0,1},{1,0},{2,3},{3,2},{4,5},{5,4},{6,7},{7,6},{8,9},{9,8},{10,11... | collective-permute-start | bytes 884744 | tf_op jit(solution)/shard_map/ppermute | solution.py:87
  23.3 0.7 %copy-start.1 = (bf16[1040,128]{1,0:T(8,128)(2,1)}, bf16[1040,128]{1,0:T(8,128)(2,1)S(1)}, u32[]{:S(2)}) copy-start(bf16[1040,128]{1,0:T(8,128)(2,1)S(1)} %collective-permute-done.cols_b_ref) | copy-start | bytes 798724
  24.0 0.7 %copy-start = (bf16[9,128,128]{2,1,0:T(8,128)(2,1)}, bf16[9,128,128]{2,1,0:T(8,128)(2,1)S(1)}, u32[]{:S(2)}) copy-start(bf16[9,128,128]{2,1,0:T(8,128)(2,1)S(1)} %collective-permute-done.7.pieces_b_ref) | copy-start | bytes 884740

commit v15 on v14

--- a/solution.py
+++ b/solution.py
@@ -22,7 +22,7 @@
     return even, odd
 
 
-def gather_rows(piece, row_count, col_count):
+def gather_rows(piece, row_count, col_count, companion):
     me = lax.axis_index("row")
     parity = lax.axis_index("col") % 2
     bits = row_count.bit_length() - 1
@@ -42,6 +42,8 @@
             masks = [sum(1 << order[p] for p in chosen) for order in (even, odd)]
             parts.append(exchange(held, masks))
         held = jnp.concatenate(parts, axis=0)
+        if start == 0:
+            held, companion = lax.optimization_barrier((held, companion))
 
     def slot_of(owner, order_parity):
         diff = jnp.bitwise_xor(owner, me)
@@ -52,7 +54,7 @@
             slot_odd = slot_odd + ((diff >> odd[position]) & 1) * (1 << position)
         return jnp.where(order_parity == 0, slot_even, slot_odd)
 
-    return held, slot_of, parity
+    return held, slot_of, parity, companion
 
 
 def shards(matrix, fill_mask, col_rows, inverses):
@@ -67,7 +69,12 @@
 
     owner_row = col_rows // local_slabs
     piece, payload = prep_call(matrix, col_rows, fill_mask)
-    held, slot_of, parity = gather_rows(piece, row_count, col_count)
+    if col_count == 2:
+        swap = [(0, 1), (1, 0)]
+        swapped_cols = lax.ppermute(payload, "col", swap)
+    else:
+        swapped_cols = payload
+    held, slot_of, parity, swapped_cols = gather_rows(piece, row_count, col_count, swapped_cols)
 
     def wanted_of(group):
         own = group * col_panels + jnp.arange(col_panels, dtype=jnp.int32)
@@ -79,9 +86,8 @@
 
     wanted = wanted_of(col_index)
     if col_count == 2:
-        swap = [(0, 1), (1, 0)]
         cols_a = payload
-        cols_b = lax.ppermute(payload, "col", swap)
+        cols_b = swapped_cols
         pieces_a = pick(held, wanted, parity)
         for_partner = pick(held, wanted_of(1 - col_index), parity)
         pieces_b = lax.ppermute(for_partner, "col", swap)

time: 29.9 us -> 29.9 us (level)
  waiting for transfers between devices: 7.07 us -> 8.51 us
  local copies, waits for them, and re-layouts: 4.66 us -> 3.31 us
    ppermute x6, waiting for transfers between devices: 6.93 us -> 8.4 us  [exchange(): return lax.ppermute(value, ('row', 'col'), perm)]
    unnamed x12 -> x9, local copies, waits for them, and re-layouts: 2.11 us -> 0.76 us
  transfers between devices with their start and end apart: 8 -> 8, of which waited for: 4 -> 4; matrix products, arithmetic and copies ran while one was open for 18% -> 12% of each run, Pallas kernels for 0% -> 0%
where the time goes in v15:
time: 29.9 us; the launch traced here: 29.7 us
  starting transfers between devices  9.3 us (31%)
  waiting for transfers between devices  8.51 us (28%)
  Pallas kernels  6.6 us (22%)
  local copies, waits for them, and re-layouts  3.31 us (11%)
  other arithmetic  1.83 us (6%)
    ppermute x6, starting transfers between devices, exchange(): return lax.ppermute(value, ('row', 'col'), perm)  9.17 us
    ppermute x6, waiting for transfers between devices, exchange(): return lax.ppermute(value, ('row', 'col'), perm)  8.4 us
    pallas_call x1, Pallas kernels, factor_call(): pl.pallas_call(functools.partial(factor_kernel, by_col=by_col), out_shape...  4.81 us
    pallas_call x1, Pallas kernels, prep_call(): pl.pallas_call(prep_kernel, out_shape=(jax.ShapeDtypeStruct((PW, PW), jnp...  1.79 us
    gather x2, local copies, waits for them, and re-layouts, pick(): slots = slot_of(owner_row[wanted], order_parity)  1.32 us
    gather x2, local copies, waits for them, and re-layouts, pick(): return jnp.take(pieces, slots, axis=0)  1.2 us
    select_n x2, other arithmetic, pick(): return jnp.take(pieces, slots, axis=0)  0.9 us
    concatenate x1, other arithmetic, gather_rows(): held = jnp.concatenate(parts, axis=0)  0.78 us
  transfers between devices with their start and end apart: 8, of which 4 were waited for; matrix products, arithmetic and copies ran while one was open for 12% of the time, Pallas kernels for 0%

profile of v15, /device:TPU:0, one launch (start us, length us, event | category | flops | bytes accessed | tf_op | source)
XLA Modules:
  0.0 29.7 jit_solution(10462433584635664443)
XLA Ops:
  0.0 1.8 %shard_map.46 = (bf16[128,128]{1,0:T(8,128)(2,1)}, bf16[1040,128]{1,0:T(8,128)(2,1)}) custom-call(bf16[1024,1024]{1,0:T(8,128)(2,1)} %matrix_ref.1, s32[16]{0:T(128)} %col_rows_ref.1, s32[4,8]{1,0:T(4,128)} %mask_ref.3), custom_call_target="tpu_custom_call" | custom-call | bytes 524288 | tf_op jit(solution)/shard_map/pallas_call | solution.py:134
  1.8 5.0 %collective-permute-start.2 = (bf16[1,128,128]{2,1,0:T(8,128)(2,1)}, bf16[1,128,128]{2,1,0:T(8,128)(2,1)S(1)}, u32[]{:S(2)}, u32[]{:S(2)}) collective-permute-start(bf16[1,128,128]{2,1,0:T(8,128)(2,1)} %bitcast.9), channel_id=1, source_target_pairs={{0,24},{1,25},{2,26},{3,27},{4,28},{5,29},{6,30},{7,31},{8,16},{9,... | collective-permute-start | bytes 98312 | tf_op jit(solution)/shard_map/ppermute | solution.py:35
  6.8 0.0 collective-permute-start.1
  6.8 0.6 %collective-permute-start = (bf16[1,128,128]{2,1,0:T(8,128)(2,1)}, bf16[1,128,128]{2,1,0:T(8,128)(2,1)S(1)}, u32[]{:S(2)}, u32[]{:S(2)}) collective-permute-start(bf16[1,128,128]{2,1,0:T(8,128)(2,1)} %bitcast.11), channel_id=1, source_target_pairs={{0,16},{1,9},{2,18},{3,11},{4,20},{5,13},{6,22},{7,15},{8,24},{9,1... | collective-permute-start | bytes 98312 | tf_op jit(solution)/shard_map/ppermute | solution.py:35
  7.5 0.1 fusion
  7.6 0.7 %gather_fusion = s32[9]{0:T(128)S(1)} fusion(s32[16]{0:T(128)S(1)} %and_select_fusion, s32[1024]{0:T(1024)S(1)} %pad_clamp_fusion.3), kind=kCustom, calls=%fused_computation.2 | custom fusion | bytes 108 | tf_op jit(solution)/shard_map/gather | solution.py:84
  8.2 0.7 %gather_fusion.1 = s32[9]{0:T(128)S(1)} fusion(s32[16]{0:T(128)S(1)} %and_select_fusion, s32[1024]{0:T(1024)S(1)} %pad_clamp_fusion.1), kind=kCustom, calls=%fused_computation.3 | custom fusion | bytes 108 | tf_op jit(solution)/shard_map/gather | solution.py:84
  8.9 0.0 collective-permute-done.2
  8.9 2.0 %collective-permute-done.1 = bf16[1,128,128]{2,1,0:T(8,128)(2,1)S(1)} collective-permute-done((bf16[1,128,128]{2,1,0:T(8,128)(2,1)}, bf16[1,128,128]{2,1,0:T(8,128)(2,1)S(1)}, u32[]{:S(2)}, u32[]{:S(2)}) %collective-permute-start.1) | collective-permute-done | bytes 32800 | tf_op jit(solution)/shard_map/ppermute | solution.py:35
  11.0 0.9 %collective-permute-done = bf16[1,128,128]{2,1,0:T(8,128)(2,1)S(1)} collective-permute-done((bf16[1,128,128]{2,1,0:T(8,128)(2,1)}, bf16[1,128,128]{2,1,0:T(8,128)(2,1)S(1)}, u32[]{:S(2)}, u32[]{:S(2)}) %collective-permute-start) | collective-permute-done | bytes 32800 | tf_op jit(solution)/shard_map/ppermute | solution.py:35
  11.9 0.8 %pad_maximum_fusion = bf16[4,128,128]{2,1,0:T(8,128)(2,1)S(1)} fusion(bf16[1,128,128]{2,1,0:T(8,128)(2,1)S(1)} %collective-permute-done.2, bf16[1,128,128]{2,1,0:T(8,128)(2,1)S(1)} %collective-permute-done.1, bf16[1,128,128]{2,1,0:T(8,128)(2,1)S(1)} %collective-permute-done, bf16[1,128,128]{2,1,0:T(8,128)(2,1)} %bitcast.12), kind=kLoop, calls=%fused_computation.6 | loop fusion | flops 196608 | bytes 262144 | tf_op jit(solution)/shard_map/concatenate | solution.py:44
  12.7 0.0 collective-permute-done.3.cols_b_ref
  12.7 1.6 %collective-permute-start.4 = (bf16[4,128,128]{2,1,0:T(8,128)(2,1)S(1)}, bf16[4,128,128]{2,1,0:T(8,128)(2,1)S(1)}, u32[]{:S(2)}, u32[]{:S(2)}) collective-permute-start(bf16[4,128,128]{2,1,0:T(8,128)(2,1)S(1)} %pad_maximum_fusion), channel_id=1, source_target_pairs={{0,4},{1,3},{2,6},{3,1},{4,0},{5,7},{6,2},{7,5},{8,12},{9,11},{10,... | collective-permute-start | bytes 393224 | tf_op jit(solution)/shard_map/ppermute | solution.py:35
  14.3 1.4 %collective-permute-start.6 = (bf16[4,128,128]{2,1,0:T(8,128)(2,1)S(1)}, bf16[4,128,128]{2,1,0:T(8,128)(2,1)S(1)}, u32[]{:S(2)}, u32[]{:S(2)}) collective-permute-start(bf16[4,128,128]{2,1,0:T(8,128)(2,1)S(1)} %pad_maximum_fusion), channel_id=1, source_target_pairs={{0,6},{1,7},{2,4},{3,5},{4,2},{5,3},{6,0},{7,1},{8,14},{9,15},{10,... | collective-permute-start | bytes 393224 | tf_op jit(solution)/shard_map/ppermute | solution.py:35
  15.7 0.5 %collective-permute-start.5 = (bf16[4,128,128]{2,1,0:T(8,128)(2,1)S(1)}, bf16[4,128,128]{2,1,0:T(8,128)(2,1)S(1)}, u32[]{:S(2)}, u32[]{:S(2)}) collective-permute-start(bf16[4,128,128]{2,1,0:T(8,128)(2,1)S(1)} %pad_maximum_fusion), channel_id=1, source_target_pairs={{0,2},{1,5},{2,0},{3,7},{4,6},{5,1},{6,4},{7,3},{8,10},{9,13},{10,... | collective-permute-start | bytes 393224 | tf_op jit(solution)/shard_map/ppermute | solution.py:35
  16.2 5.5 %collective-permute-done.4 = bf16[4,128,128]{2,1,0:T(8,128)(2,1)S(1)} collective-permute-done((bf16[4,128,128]{2,1,0:T(8,128)(2,1)S(1)}, bf16[4,128,128]{2,1,0:T(8,128)(2,1)S(1)}, u32[]{:S(2)}, u32[]{:S(2)}) %collective-permute-start.4) | collective-permute-done | bytes 131104 | tf_op jit(solution)/shard_map/ppermute | solution.py:35
  21.8 0.6 %gather_fusion.3 = bf16[9,128,128]{2,1,0:T(8,128)(2,1)S(1)} fusion(bf16[16,128,128]{2,1,0:T(8,128)(2,1)S(1)} %constant_dynamic-update-slice_fusion, s32[1024]{0:T(1024)S(1)} %pad_clamp_fusion), kind=kCustom, calls=%fused_computation.1.clone | custom fusion | bytes 589860 | tf_op jit(solution)/shard_map/jit(_take)/gather | solution.py:85
  22.4 0.1 broadcast_select_fusion
  22.5 0.1 collective-permute-start.7
  22.7 0.6 %gather_fusion.2 = bf16[9,128,128]{2,1,0:T(8,128)(2,1)S(1)} fusion(bf16[16,128,128]{2,1,0:T(8,128)(2,1)S(1)} %constant_dynamic-update-slice_fusion, s32[1024]{0:T(1024)S(1)} %pad_clamp_fusion.2), kind=kCustom, calls=%fused_computation.clone | custom fusion | bytes 589860 | tf_op jit(solution)/shard_map/jit(_take)/gather | solution.py:85
  23.3 0.8 %broadcast_select_fusion.1.pieces_a_ref = bf16[9,128,128]{2,1,0:T(8,128)(2,1)} fusion(bf16[9,128,128]{2,1,0:T(8,128)(2,1)S(1)} %gather_fusion.2, pred[9]{0:T(512)(128)(4,1)S(1)} %get-tuple-element.16), kind=kLoop, calls=%fused_computation.5 | loop fusion | flops 147456 | bytes 589833 | tf_op jit(solution)/shard_map/jit(_take)/select_n | solution.py:85
  24.1 0.1 collective-permute-done.7.pieces_b_ref
  24.2 0.7 %copy-done = bf16[9,128,128]{2,1,0:T(8,128)(2,1)} copy-done((bf16[9,128,128]{2,1,0:T(8,128)(2,1)}, bf16[9,128,128]{2,1,0:T(8,128)(2,1)S(1)}, u32[]{:S(2)}) %copy-start) | copy-done | bytes 294936
  24.9 4.8 %shard_map.47 = bf16[1024,1024]{1,0:T(8,128)(2,1)} custom-call(bf16[1024,1024]{1,0:T(8,128)(2,1)} %matrix_ref.1, bf16[1040,128]{1,0:T(8,128)(2,1)} %get-tuple-element.10.cols_a_ref, bf16[1040,128]{1,0:T(8,128)(2,1)} %copy-done.1, bf16[9,128,128]{2,1,0:T(8,128)(2,1)} %broadcast_select_fusion.1.pieces_a_ref, bf16[9,128,128]{2,1,0:T(8,128)(2,1)} %copy-done, ...), custom_call_target="tpu_custom_call" | custom-call | flops 637534208 | bytes 4194304 | tf_op jit(solution)/shard_map/pallas_call | solution.py:250
  (21 shorter events, 0.2 us)
Async XLA Ops:
  0.0 7.4 %copy-start.2 = (s32[16]{0:T(128)S(1)}, s32[16]{0:T(128)}, u32[]{:S(2)}) copy-start(s32[16]{0:T(128)} %col_rows_ref.1) | copy-start | bytes 196
  1.8 7.2 %collective-permute-start.2 = (bf16[1,128,128]{2,1,0:T(8,128)(2,1)}, bf16[1,128,128]{2,1,0:T(8,128)(2,1)S(1)}, u32[]{:S(2)}, u32[]{:S(2)}) collective-permute-start(bf16[1,128,128]{2,1,0:T(8,128)(2,1)} %bitcast.9), channel_id=1, source_target_pairs={{0,24},{1,25},{2,26},{3,27},{4,28},{5,29},{6,30},{7,31},{8,16},{9,... | collective-permute-start | bytes 98312 | tf_op jit(solution)/shard_map/ppermute | solution.py:35
  6.8 4.1 %collective-permute-start.1 = (bf16[1,128,128]{2,1,0:T(8,128)(2,1)}, bf16[1,128,128]{2,1,0:T(8,128)(2,1)S(1)}, u32[]{:S(2)}, u32[]{:S(2)}) collective-permute-start(bf16[1,128,128]{2,1,0:T(8,128)(2,1)} %bitcast.10), channel_id=1, source_target_pairs={{0,8},{1,17},{2,10},{3,19},{4,12},{5,21},{6,14},{7,23},{8,0},{9,25... | collective-permute-start | bytes 98312 | tf_op jit(solution)/shard_map/ppermute | solution.py:35
  6.8 5.0 %collective-permute-start = (bf16[1,128,128]{2,1,0:T(8,128)(2,1)}, bf16[1,128,128]{2,1,0:T(8,128)(2,1)S(1)}, u32[]{:S(2)}, u32[]{:S(2)}) collective-permute-start(bf16[1,128,128]{2,1,0:T(8,128)(2,1)} %bitcast.11), channel_id=1, source_target_pairs={{0,16},{1,9},{2,18},{3,11},{4,20},{5,13},{6,22},{7,15},{8,24},{9,1... | collective-permute-start | bytes 98312 | tf_op jit(solution)/shard_map/ppermute | solution.py:35
  7.4 5.2 %collective-permute-start.3 = (bf16[1040,128]{1,0:T(8,128)(2,1)}, bf16[1040,128]{1,0:T(8,128)(2,1)S(1)}, u32[]{:S(2)}, u32[]{:S(2)}) collective-permute-start(bf16[1040,128]{1,0:T(8,128)(2,1)} %get-tuple-element.10.cols_a_ref), channel_id=1, source_target_pairs={{0,1},{1,0},{2,3},{3,2},{4,5},{5,4},{6,7},{7,6},{8,9},{9,8},{10,11... | collective-permute-start | bytes 798728 | tf_op jit(solution)/shard_map/ppermute | solution.py:74
  12.7 11.5 %copy-start.1 = (bf16[1040,128]{1,0:T(8,128)(2,1)}, bf16[1040,128]{1,0:T(8,128)(2,1)S(1)}, u32[]{:S(2)}) copy-start(bf16[1040,128]{1,0:T(8,128)(2,1)S(1)} %collective-permute-done.3.cols_b_ref) | copy-start | bytes 798724
  12.7 9.0 %collective-permute-start.4 = (bf16[4,128,128]{2,1,0:T(8,128)(2,1)S(1)}, bf16[4,128,128]{2,1,0:T(8,128)(2,1)S(1)}, u32[]{:S(2)}, u32[]{:S(2)}) collective-permute-start(bf16[4,128,128]{2,1,0:T(8,128)(2,1)S(1)} %pad_maximum_fusion), channel_id=1, source_target_pairs={{0,4},{1,3},{2,6},{3,1},{4,0},{5,7},{6,2},{7,5},{8,12},{9,11},{10,... | collective-permute-start | bytes 393224 | tf_op jit(solution)/shard_map/ppermute | solution.py:35
  14.3 7.5 %collective-permute-start.6 = (bf16[4,128,128]{2,1,0:T(8,128)(2,1)S(1)}, bf16[4,128,128]{2,1,0:T(8,128)(2,1)S(1)}, u32[]{:S(2)}, u32[]{:S(2)}) collective-permute-start(bf16[4,128,128]{2,1,0:T(8,128)(2,1)S(1)} %pad_maximum_fusion), channel_id=1, source_target_pairs={{0,6},{1,7},{2,4},{3,5},{4,2},{5,3},{6,0},{7,1},{8,14},{9,15},{10,... | collective-permute-start | bytes 393224 | tf_op jit(solution)/shard_map/ppermute | solution.py:35
  15.7 6.0 %collective-permute-start.5 = (bf16[4,128,128]{2,1,0:T(8,128)(2,1)S(1)}, bf16[4,128,128]{2,1,0:T(8,128)(2,1)S(1)}, u32[]{:S(2)}, u32[]{:S(2)}) collective-permute-start(bf16[4,128,128]{2,1,0:T(8,128)(2,1)S(1)} %pad_maximum_fusion), channel_id=1, source_target_pairs={{0,2},{1,5},{2,0},{3,7},{4,6},{5,1},{6,4},{7,3},{8,10},{9,13},{10,... | collective-permute-start | bytes 393224 | tf_op jit(solution)/shard_map/ppermute | solution.py:35
  22.5 1.6 %collective-permute-start.7 = (bf16[9,128,128]{2,1,0:T(8,128)(2,1)S(1)}, bf16[9,128,128]{2,1,0:T(8,128)(2,1)S(1)}, u32[]{:S(2)}, u32[]{:S(2)}) collective-permute-start(bf16[9,128,128]{2,1,0:T(8,128)(2,1)S(1)} %broadcast_select_fusion), channel_id=1, source_target_pairs={{0,1},{1,0},{2,3},{3,2},{4,5},{5,4},{6,7},{7,6},{8,9},{9,8},{10,11... | collective-permute-start | bytes 884744 | tf_op jit(solution)/shard_map/ppermute | solution.py:93
  24.2 0.7 %copy-start = (bf16[9,128,128]{2,1,0:T(8,128)(2,1)}, bf16[9,128,128]{2,1,0:T(8,128)(2,1)S(1)}, u32[]{:S(2)}) copy-start(bf16[9,128,128]{2,1,0:T(8,128)(2,1)S(1)} %collective-permute-done.7.pieces_b_ref) | copy-start | bytes 884740

commit v16 on v14

--- a/solution.py
+++ b/solution.py
@@ -97,10 +97,9 @@
     )
 
 
-def prep_kernel(lead_ref, col_rows_ref, mask_ref, piece_ref, payload_ref):
-    local_rows = lead_ref.shape[0]
+def prep_kernel(matrix_hbm, col_rows_ref, mask_ref, piece_ref, slab_ref, sem):
+    local_rows = matrix_hbm.shape[0]
     local_slabs = local_rows // PW
-    block_rows = local_rows // RB
     row_index = lax.axis_index("row")
     place = jnp.int32(0)
     for c in range(col_rows_ref.shape[0]):
@@ -108,39 +107,35 @@
         place = place + jnp.where(entry // local_slabs == row_index, entry % local_slabs, 0)
     place = jnp.minimum(place, local_slabs - 1)
     start = pl.multiple_of(place * PW, PW)
+    copy = pltpu.make_async_copy(matrix_hbm.at[pl.ds(start, PW), pl.ds(0, PW)], slab_ref, sem.at[0])
+    copy.start()
     flag = mask_ref[place // (RB // PW), 0]
-    slab = lead_ref[pl.ds(start, PW), :].astype(jnp.float32)
     corner = (lax.broadcasted_iota(jnp.int32, (PW, PW), 0) == 0) & (
         lax.broadcasted_iota(jnp.int32, (PW, PW), 1) == 0
     )
+    copy.wait()
+    slab = slab_ref[...].astype(jnp.float32)
     piece_ref[...] = jnp.where(corner & (flag == 0), jnp.nan, slab).astype(jnp.bfloat16)
-    row_ids = lax.broadcasted_iota(jnp.int32, (MASK_ROWS, PW), 0)
-    payload_ref[0:local_rows, :] = lead_ref[...]
-    mask_rows = jnp.zeros((MASK_ROWS, PW), jnp.float32)
-    for b in range(block_rows):
-        mask_rows = jnp.where(row_ids == b, mask_ref[b, 0].astype(jnp.float32), mask_rows)
-    payload_ref[local_rows : local_rows + MASK_ROWS, :] = mask_rows.astype(jnp.bfloat16)
 
 
 def prep_call(matrix, col_rows, fill_mask):
     local_rows = matrix.shape[0]
+    block_rows = local_rows // RB
     smem = pl.BlockSpec(memory_space=pltpu.SMEM)
-    return pl.pallas_call(
+    piece = pl.pallas_call(
         prep_kernel,
-        out_shape=(
-            jax.ShapeDtypeStruct((PW, PW), jnp.bfloat16),
-            jax.ShapeDtypeStruct((local_rows + MASK_ROWS, PW), jnp.bfloat16),
-        ),
-        grid=(1,),
-        in_specs=[pl.BlockSpec((local_rows, PW), lambda i: (0, 0)), smem, smem],
-        out_specs=(
-            pl.BlockSpec((PW, PW), lambda i: (0, 0)),
-            pl.BlockSpec((local_rows + MASK_ROWS, PW), lambda i: (0, 0)),
-        ),
-        cost_estimate=pl.CostEstimate(
-            flops=0, bytes_accessed=4 * local_rows * PW, transcendentals=0
-        ),
+        out_shape=jax.ShapeDtypeStruct((PW, PW), jnp.bfloat16),
+        in_specs=[pl.BlockSpec(memory_space=pltpu.HBM), smem, smem],
+        out_specs=pl.BlockSpec(memory_space=pltpu.VMEM),
+        scratch_shapes=[pltpu.VMEM((PW, PW), jnp.bfloat16), pltpu.SemaphoreType.DMA((1,))],
+        cost_estimate=pl.CostEstimate(flops=0, bytes_accessed=4 * PW * PW, transcendentals=0),
     )(matrix, col_rows, fill_mask)
+    mask_rows = jnp.zeros((MASK_ROWS, PW), jnp.bfloat16)
+    mask_rows = mask_rows.at[:block_rows].set(
+        jnp.broadcast_to(fill_mask[:, 0:1].astype(jnp.bfloat16), (block_rows, PW))
+    )
+    payload = jnp.concatenate((matrix[:, :PW], mask_rows), axis=0)
+    return piece, payload
 
 
 def factor_kernel(

time: 29.9 us -> 29.7 us (level)
  waiting for transfers between devices: 7.07 us -> 6.44 us
  other arithmetic: 1.83 us -> 1.3 us
  Pallas kernels: 6.61 us -> 7.14 us
    concatenate x1, other arithmetic: 0.78 us -> 0.02 us  [gather_rows(): held = jnp.concatenate(parts, axis=0)]
    ppermute x6, waiting for transfers between devices: 6.93 us -> 6.32 us  [exchange(): return lax.ppermute(value, ('row', 'col'), perm)]
    pallas_call x1, Pallas kernels: 1.79 us -> 2.32 us  [prep_call(): pl.pallas_call(prep_kernel, out_shape=jax.ShapeDtypeStruct((PW, PW), jnp....]
    unnamed x12 -> x18, local copies, waits for them, and re-layouts: 2.11 us -> 2.13 us
  transfers between devices with their start and end apart: 8 -> 8, of which waited for: 4 -> 5; matrix products, arithmetic and copies ran while one was open for 18% -> 16% of each run, Pallas kernels for 0% -> 0%
where the time goes in v16:
time: 29.7 us; the launch traced here: 29.3 us
  starting transfers between devices  9.46 us (32%)
  Pallas kernels  7.14 us (24%)
  waiting for transfers between devices  6.44 us (22%)
  local copies, waits for them, and re-layouts  4.81 us (16%)
  other arithmetic  1.3 us (4%)
    ppermute x6, starting transfers between devices, exchange(): return lax.ppermute(value, ('row', 'col'), perm)  9.31 us
    ppermute x6, waiting for transfers between devices, exchange(): return lax.ppermute(value, ('row', 'col'), perm)  6.32 us
    pallas_call x1, Pallas kernels, factor_call(): pl.pallas_call(functools.partial(factor_kernel, by_col=by_col), out_shape...  4.82 us
    pallas_call x1, Pallas kernels, prep_call(): pl.pallas_call(prep_kernel, out_shape=jax.ShapeDtypeStruct((PW, PW), jnp....  2.32 us
    unnamed x18, local copies, waits for them, and re-layouts  2.13 us
    gather x2, local copies, waits for them, and re-layouts, pick(): slots = slot_of(owner_row[wanted], order_parity)  1.32 us
    gather x2, local copies, waits for them, and re-layouts, pick(): return jnp.take(pieces, slots, axis=0)  1.21 us
    select_n x2, other arithmetic, pick(): return jnp.take(pieces, slots, axis=0)  0.9 us
  transfers between devices with their start and end apart: 8, of which 5 were waited for; matrix products, arithmetic and copies ran while one was open for 16% of the time, Pallas kernels for 0%

profile of v16, /device:TPU:0, one launch (start us, length us, event | category | flops | bytes accessed | tf_op | source)
XLA Modules:
  0.0 29.3 jit_solution(4729459304107375404)
XLA Ops:
  0.0 2.3 %shard_map.46 = bf16[128,128]{1,0:T(8,128)(2,1)} custom-call(bf16[1024,1024]{1,0:T(8,128)(2,1)} %matrix_ref.1, s32[16]{0:T(128)} %col_rows_ref.1, s32[4,8]{1,0:T(4,128)} %mask_ref.3), custom_call_target="tpu_custom_call" | custom-call | bytes 65536 | tf_op jit(solution)/shard_map/pallas_call | solution.py:125
  2.4 5.1 %collective-permute-start.3 = (bf16[1,128,128]{2,1,0:T(8,128)(2,1)}, bf16[1,128,128]{2,1,0:T(8,128)(2,1)S(1)}, u32[]{:S(2)}, u32[]{:S(2)}) collective-permute-start(bf16[1,128,128]{2,1,0:T(8,128)(2,1)} %bitcast.10), channel_id=1, source_target_pairs={{0,24},{1,25},{2,26},{3,27},{4,28},{5,29},{6,30},{7,31},{8,16},{9,... | collective-permute-start | bytes 98312 | tf_op jit(solution)/shard_map/ppermute | solution.py:35
  7.5 0.6 %collective-permute-start.1 = (bf16[1,128,128]{2,1,0:T(8,128)(2,1)}, bf16[1,128,128]{2,1,0:T(8,128)(2,1)S(1)}, u32[]{:S(2)}, u32[]{:S(2)}) collective-permute-start(bf16[1,128,128]{2,1,0:T(8,128)(2,1)} %bitcast.12), channel_id=1, source_target_pairs={{0,16},{1,9},{2,18},{3,11},{4,20},{5,13},{6,22},{7,15},{8,24},{9,1... | collective-permute-start | bytes 98312 | tf_op jit(solution)/shard_map/ppermute | solution.py:35
  8.1 0.1 slice_reduce_fusion
  8.3 0.2 pad_maximum_fusion.cols_a_ref
  8.6 0.8 %constant_dynamic-update-slice_fusion.6 = bf16[16,128,128]{2,1,0:T(8,128)(2,1)S(1)} fusion(bf16[128,128]{1,0:T(8,128)(2,1)} %shard_map.46), kind=kLoop, calls=%fused_computation.14 | loop fusion | bytes 65536
  9.4 0.1 fusion.1
  9.5 0.7 %gather_fusion = s32[9]{0:T(128)S(1)} fusion(s32[16]{0:T(128)S(1)} %and_select_fusion, s32[1024]{0:T(1024)S(1)} %pad_clamp_fusion.3), kind=kCustom, calls=%fused_computation.2 | custom fusion | bytes 108 | tf_op jit(solution)/shard_map/gather | solution.py:77
  10.1 0.7 %gather_fusion.1 = s32[9]{0:T(128)S(1)} fusion(s32[16]{0:T(128)S(1)} %and_select_fusion, s32[1024]{0:T(1024)S(1)} %pad_clamp_fusion.1), kind=kCustom, calls=%fused_computation.3 | custom fusion | bytes 108 | tf_op jit(solution)/shard_map/gather | solution.py:77
  10.9 0.7 %collective-permute-done.2 = bf16[1,128,128]{2,1,0:T(8,128)(2,1)S(1)} collective-permute-done((bf16[1,128,128]{2,1,0:T(8,128)(2,1)}, bf16[1,128,128]{2,1,0:T(8,128)(2,1)S(1)}, u32[]{:S(2)}, u32[]{:S(2)}) %collective-permute-start.2) | collective-permute-done | bytes 32800 | tf_op jit(solution)/shard_map/ppermute | solution.py:35
  11.6 0.9 %collective-permute-done.1 = bf16[1,128,128]{2,1,0:T(8,128)(2,1)S(1)} collective-permute-done((bf16[1,128,128]{2,1,0:T(8,128)(2,1)}, bf16[1,128,128]{2,1,0:T(8,128)(2,1)S(1)}, u32[]{:S(2)}, u32[]{:S(2)}) %collective-permute-start.1) | collective-permute-done | bytes 32800 | tf_op jit(solution)/shard_map/ppermute | solution.py:35
  12.5 2.5 %collective-permute-start.6 = (bf16[4,128,128]{2,1,0:T(8,128)(2,1)S(1)}, bf16[4,128,128]{2,1,0:T(8,128)(2,1)S(1)}, u32[]{:S(2)}, u32[]{:S(2)}) collective-permute-start(bf16[4,128,128]{2,1,0:T(8,128)(2,1)S(1)} %pad_maximum_fusion.1), channel_id=1, source_target_pairs={{0,6},{1,7},{2,4},{3,5},{4,2},{5,3},{6,0},{7,1},{8,14},{9,15},{10,... | collective-permute-start | bytes 393224 | tf_op jit(solution)/shard_map/ppermute | solution.py:35
  15.0 0.5 %collective-permute-start.5 = (bf16[4,128,128]{2,1,0:T(8,128)(2,1)S(1)}, bf16[4,128,128]{2,1,0:T(8,128)(2,1)S(1)}, u32[]{:S(2)}, u32[]{:S(2)}) collective-permute-start(bf16[4,128,128]{2,1,0:T(8,128)(2,1)S(1)} %pad_maximum_fusion.1), channel_id=1, source_target_pairs={{0,2},{1,5},{2,0},{3,7},{4,6},{5,1},{6,4},{7,3},{8,10},{9,13},{10,... | collective-permute-start | bytes 393224 | tf_op jit(solution)/shard_map/ppermute | solution.py:35
  15.6 0.5 %collective-permute-start.4 = (bf16[4,128,128]{2,1,0:T(8,128)(2,1)S(1)}, bf16[4,128,128]{2,1,0:T(8,128)(2,1)S(1)}, u32[]{:S(2)}, u32[]{:S(2)}) collective-permute-start(bf16[4,128,128]{2,1,0:T(8,128)(2,1)S(1)} %pad_maximum_fusion.1), channel_id=1, source_target_pairs={{0,4},{1,3},{2,6},{3,1},{4,0},{5,7},{6,2},{7,5},{8,12},{9,11},{10,... | collective-permute-start | bytes 393224 | tf_op jit(solution)/shard_map/ppermute | solution.py:35
  16.1 4.6 %collective-permute-done.4 = bf16[4,128,128]{2,1,0:T(8,128)(2,1)S(1)} collective-permute-done((bf16[4,128,128]{2,1,0:T(8,128)(2,1)S(1)}, bf16[4,128,128]{2,1,0:T(8,128)(2,1)S(1)}, u32[]{:S(2)}, u32[]{:S(2)}) %collective-permute-start.4) | collective-permute-done | bytes 131104 | tf_op jit(solution)/shard_map/ppermute | solution.py:35
  20.7 0.1 collective-permute-done.5
  20.9 0.6 %gather_fusion.3 = bf16[9,128,128]{2,1,0:T(8,128)(2,1)S(1)} fusion(bf16[16,128,128]{2,1,0:T(8,128)(2,1)S(1)} %constant_dynamic-update-slice_fusion, s32[1024]{0:T(1024)S(1)} %pad_clamp_fusion), kind=kCustom, calls=%fused_computation.1.clone | custom fusion | bytes 589860 | tf_op jit(solution)/shard_map/jit(_take)/gather | solution.py:78
  21.5 0.1 broadcast_select_fusion
  21.7 0.6 %gather_fusion.2 = bf16[9,128,128]{2,1,0:T(8,128)(2,1)S(1)} fusion(bf16[16,128,128]{2,1,0:T(8,128)(2,1)S(1)} %constant_dynamic-update-slice_fusion, s32[1024]{0:T(1024)S(1)} %pad_clamp_fusion.2), kind=kCustom, calls=%fused_computation.clone | custom fusion | bytes 589860 | tf_op jit(solution)/shard_map/jit(_take)/gather | solution.py:78
  22.3 0.8 %broadcast_select_fusion.1.pieces_a_ref = bf16[9,128,128]{2,1,0:T(8,128)(2,1)} fusion(bf16[9,128,128]{2,1,0:T(8,128)(2,1)S(1)} %gather_fusion.2, pred[9]{0:T(512)(128)(4,1)S(1)} %get-tuple-element.20), kind=kLoop, calls=%fused_computation.5 | loop fusion | flops 147456 | bytes 589833 | tf_op jit(solution)/shard_map/jit(_take)/select_n | solution.py:78
  23.1 0.1 collective-permute-done.7.pieces_b_ref
  23.2 0.6 %copy-done.3 = bf16[1040,128]{1,0:T(8,128)(2,1)} copy-done((bf16[1040,128]{1,0:T(8,128)(2,1)}, bf16[1040,128]{1,0:T(8,128)(2,1)S(1)}, u32[]{:S(2)}) %copy-start.3) | copy-done | bytes 266264
  23.8 0.7 %copy-done.2 = bf16[9,128,128]{2,1,0:T(8,128)(2,1)} copy-done((bf16[9,128,128]{2,1,0:T(8,128)(2,1)}, bf16[9,128,128]{2,1,0:T(8,128)(2,1)S(1)}, u32[]{:S(2)}) %copy-start.2) | copy-done | bytes 294936
  24.5 4.8 %shard_map.47 = bf16[1024,1024]{1,0:T(8,128)(2,1)} custom-call(bf16[1024,1024]{1,0:T(8,128)(2,1)} %matrix_ref.1, bf16[1040,128]{1,0:T(8,128)(2,1)} %copy-done, bf16[1040,128]{1,0:T(8,128)(2,1)} %copy-done.3, bf16[9,128,128]{2,1,0:T(8,128)(2,1)} %broadcast_select_fusion.1.pieces_a_ref, bf16[9,128,128]{2,1,0:T(8,128)(2,1)} %copy-done.2, ...), custom_call_target="tpu_custom_call" | custom-call | flops 637534208 | bytes 4194304 | tf_op jit(solution)/shard_map/pallas_call | solution.py:239
  (36 shorter events, 0.4 us)
Async XLA Ops:
  0.0 8.1 %copy-start.4 = (s32[4,8]{1,0:T(4,128)S(1)}, s32[4,8]{1,0:T(4,128)}, u32[]{:S(2)}) copy-start(s32[4,8]{1,0:T(4,128)} %mask_ref.3) | copy-start | bytes 388
  0.0 8.2 %slice-start = ((bf16[1024,1024]{1,0:T(8,128)(2,1)}), bf16[1024,128]{1,0:T(8,128)(2,1)S(1)}, s32[]{:S(2)}) async-start(bf16[1024,1024]{1,0:T(8,128)(2,1)} %matrix_ref.1), calls=%async_computation | async-start | bytes 524288 | tf_op jit(solution)/shard_map/slice | solution.py:137
  0.0 8.6 %copy-start.5 = (s32[16]{0:T(128)S(1)}, s32[16]{0:T(128)}, u32[]{:S(2)}) copy-start(s32[16]{0:T(128)} %col_rows_ref.1) | copy-start | bytes 196
  2.3 10.2 %copy-start.1 = (bf16[128,128]{1,0:T(8,128)(2,1)S(1)}, bf16[128,128]{1,0:T(8,128)(2,1)}, u32[]{:S(2)}) copy-start(bf16[128,128]{1,0:T(8,128)(2,1)} %shard_map.46) | copy-start | bytes 98308
  2.4 8.5 %collective-permute-start.3 = (bf16[1,128,128]{2,1,0:T(8,128)(2,1)}, bf16[1,128,128]{2,1,0:T(8,128)(2,1)S(1)}, u32[]{:S(2)}, u32[]{:S(2)}) collective-permute-start(bf16[1,128,128]{2,1,0:T(8,128)(2,1)} %bitcast.10), channel_id=1, source_target_pairs={{0,24},{1,25},{2,26},{3,27},{4,28},{5,29},{6,30},{7,31},{8,16},{9,... | collective-permute-start | bytes 98312 | tf_op jit(solution)/shard_map/ppermute | solution.py:35
  7.5 4.1 %collective-permute-start.2 = (bf16[1,128,128]{2,1,0:T(8,128)(2,1)}, bf16[1,128,128]{2,1,0:T(8,128)(2,1)S(1)}, u32[]{:S(2)}, u32[]{:S(2)}) collective-permute-start(bf16[1,128,128]{2,1,0:T(8,128)(2,1)} %bitcast.11), channel_id=1, source_target_pairs={{0,8},{1,17},{2,10},{3,19},{4,12},{5,21},{6,14},{7,23},{8,0},{9,25... | collective-permute-start | bytes 98312 | tf_op jit(solution)/shard_map/ppermute | solution.py:35
  7.5 5.0 %collective-permute-start.1 = (bf16[1,128,128]{2,1,0:T(8,128)(2,1)}, bf16[1,128,128]{2,1,0:T(8,128)(2,1)S(1)}, u32[]{:S(2)}, u32[]{:S(2)}) collective-permute-start(bf16[1,128,128]{2,1,0:T(8,128)(2,1)} %bitcast.12), channel_id=1, source_target_pairs={{0,16},{1,9},{2,18},{3,11},{4,20},{5,13},{6,22},{7,15},{8,24},{9,1... | collective-permute-start | bytes 98312 | tf_op jit(solution)/shard_map/ppermute | solution.py:35
  8.5 13.8 %copy-start = (bf16[1040,128]{1,0:T(8,128)(2,1)}, bf16[1040,128]{1,0:T(8,128)(2,1)S(1)}, u32[]{:S(2)}) copy-start(bf16[1040,128]{1,0:T(8,128)(2,1)S(1)} %pad_maximum_fusion.cols_a_ref) | copy-start | bytes 798724
  8.5 14.6 %collective-permute-start = (bf16[1040,128]{1,0:T(8,128)(2,1)S(1)}, bf16[1040,128]{1,0:T(8,128)(2,1)S(1)}, u32[]{:S(2)}, u32[]{:S(2)}) collective-permute-start(bf16[1040,128]{1,0:T(8,128)(2,1)S(1)} %pad_maximum_fusion.cols_a_ref), channel_id=1, source_target_pairs={{0,1},{1,0},{2,3},{3,2},{4,5},{5,4},{6,7},{7,6},{8,9},{9,8},{10,11... | collective-permute-start | bytes 798728 | tf_op jit(solution)/shard_map/ppermute | solution.py:84
  12.5 8.3 %collective-permute-start.6 = (bf16[4,128,128]{2,1,0:T(8,128)(2,1)S(1)}, bf16[4,128,128]{2,1,0:T(8,128)(2,1)S(1)}, u32[]{:S(2)}, u32[]{:S(2)}) collective-permute-start(bf16[4,128,128]{2,1,0:T(8,128)(2,1)S(1)} %pad_maximum_fusion.1), channel_id=1, source_target_pairs={{0,6},{1,7},{2,4},{3,5},{4,2},{5,3},{6,0},{7,1},{8,14},{9,15},{10,... | collective-permute-start | bytes 393224 | tf_op jit(solution)/shard_map/ppermute | solution.py:35
  15.0 5.8 %collective-permute-start.5 = (bf16[4,128,128]{2,1,0:T(8,128)(2,1)S(1)}, bf16[4,128,128]{2,1,0:T(8,128)(2,1)S(1)}, u32[]{:S(2)}, u32[]{:S(2)}) collective-permute-start(bf16[4,128,128]{2,1,0:T(8,128)(2,1)S(1)} %pad_maximum_fusion.1), channel_id=1, source_target_pairs={{0,2},{1,5},{2,0},{3,7},{4,6},{5,1},{6,4},{7,3},{8,10},{9,13},{10,... | collective-permute-start | bytes 393224 | tf_op jit(solution)/shard_map/ppermute | solution.py:35
  15.6 5.1 %collective-permute-start.4 = (bf16[4,128,128]{2,1,0:T(8,128)(2,1)S(1)}, bf16[4,128,128]{2,1,0:T(8,128)(2,1)S(1)}, u32[]{:S(2)}, u32[]{:S(2)}) collective-permute-start(bf16[4,128,128]{2,1,0:T(8,128)(2,1)S(1)} %pad_maximum_fusion.1), channel_id=1, source_target_pairs={{0,4},{1,3},{2,6},{3,1},{4,0},{5,7},{6,2},{7,5},{8,12},{9,11},{10,... | collective-permute-start | bytes 393224 | tf_op jit(solution)/shard_map/ppermute | solution.py:35
  21.6 1.6 %collective-permute-start.7 = (bf16[9,128,128]{2,1,0:T(8,128)(2,1)S(1)}, bf16[9,128,128]{2,1,0:T(8,128)(2,1)S(1)}, u32[]{:S(2)}, u32[]{:S(2)}) collective-permute-start(bf16[9,128,128]{2,1,0:T(8,128)(2,1)S(1)} %broadcast_select_fusion), channel_id=1, source_target_pairs={{0,1},{1,0},{2,3},{3,2},{4,5},{5,4},{6,7},{7,6},{8,9},{9,8},{10,11... | collective-permute-start | bytes 884744 | tf_op jit(solution)/shard_map/ppermute | solution.py:87
  23.1 0.7 %copy-start.3 = (bf16[1040,128]{1,0:T(8,128)(2,1)}, bf16[1040,128]{1,0:T(8,128)(2,1)S(1)}, u32[]{:S(2)}) copy-start(bf16[1040,128]{1,0:T(8,128)(2,1)S(1)} %collective-permute-done.cols_b_ref) | copy-start | bytes 798724
  23.8 0.7 %copy-start.2 = (bf16[9,128,128]{2,1,0:T(8,128)(2,1)}, bf16[9,128,128]{2,1,0:T(8,128)(2,1)S(1)}, u32[]{:S(2)}) copy-start(bf16[9,128,128]{2,1,0:T(8,128)(2,1)S(1)} %collective-permute-done.7.pieces_b_ref) | copy-start | bytes 884740

commit v17 on v16

--- a/solution.py
+++ b/solution.py
@@ -41,7 +41,10 @@
         for chosen in groups:
             masks = [sum(1 << order[p] for p in chosen) for order in (even, odd)]
             parts.append(exchange(held, masks))
-        held = jnp.concatenate(parts, axis=0)
+        joined = jnp.zeros((len(parts) * held.shape[0],) + held.shape[1:], held.dtype)
+        for index, part in enumerate(parts):
+            joined = lax.dynamic_update_slice_in_dim(joined, part, index * held.shape[0], 0)
+        held = joined
 
     def slot_of(owner, order_parity):
         diff = jnp.bitwise_xor(owner, me)

time: 29.7 us -> 30.3 us (1.020)
  waiting for transfers between devices: 6.44 us -> 7.74 us
  local copies, waits for them, and re-layouts: 4.81 us -> 4.13 us
    ppermute x6, waiting for transfers between devices: 6.32 us -> 7.61 us  [exchange(): return lax.ppermute(value, ('row', 'col'), perm)]
    unnamed x18 -> x12, local copies, waits for them, and re-layouts: 2.13 us -> 1.3 us
  transfers between devices with their start and end apart: 8 -> 8, of which waited for: 5 -> 5; matrix products, arithmetic and copies ran while one was open for 16% -> 14% of each run, Pallas kernels for 0% -> 0%
where the time goes in v17:
time: 30.3 us; the launch traced here: 30.1 us
  starting transfers between devices  9.52 us (31%)
  waiting for transfers between devices  7.74 us (26%)
  Pallas kernels  7.14 us (24%)
  local copies, waits for them, and re-layouts  4.13 us (14%)
  other arithmetic  1.33 us (4%)
    ppermute x6, starting transfers between devices, exchange(): return lax.ppermute(value, ('row', 'col'), perm)  9.38 us
    ppermute x6, waiting for transfers between devices, exchange(): return lax.ppermute(value, ('row', 'col'), perm)  7.61 us
    pallas_call x1, Pallas kernels, factor_call(): pl.pallas_call(functools.partial(factor_kernel, by_col=by_col), out_shape...  4.82 us
    pallas_call x1, Pallas kernels, prep_call(): pl.pallas_call(prep_kernel, out_shape=jax.ShapeDtypeStruct((PW, PW), jnp....  2.32 us
    gather x2, local copies, waits for them, and re-layouts, pick(): slots = slot_of(owner_row[wanted], order_parity)  1.32 us
    unnamed x12, local copies, waits for them, and re-layouts  1.3 us
    gather x2, local copies, waits for them, and re-layouts, pick(): return jnp.take(pieces, slots, axis=0)  1.21 us
    select_n x2, other arithmetic, pick(): return jnp.take(pieces, slots, axis=0)  0.9 us
  transfers between devices with their start and end apart: 8, of which 5 were waited for; matrix products, arithmetic and copies ran while one was open for 14% of the time, Pallas kernels for 0%

profile of v17, /device:TPU:0, one launch (start us, length us, event | category | flops | bytes accessed | tf_op | source)
XLA Modules:
  0.0 30.1 jit_solution(11098049643010097134)
XLA Ops:
  0.0 2.3 %shard_map.46 = bf16[128,128]{1,0:T(8,128)(2,1)} custom-call(bf16[1024,1024]{1,0:T(8,128)(2,1)} %matrix_ref.1, s32[16]{0:T(128)} %col_rows_ref.1, s32[4,8]{1,0:T(4,128)} %mask_ref.3), custom_call_target="tpu_custom_call" | custom-call | bytes 65536 | tf_op jit(solution)/shard_map/pallas_call | solution.py:128
  2.4 5.1 %collective-permute-start.3 = (bf16[1,128,128]{2,1,0:T(8,128)(2,1)}, bf16[1,128,128]{2,1,0:T(8,128)(2,1)S(1)}, u32[]{:S(2)}, u32[]{:S(2)}) collective-permute-start(bf16[1,128,128]{2,1,0:T(8,128)(2,1)} %bitcast.9), channel_id=1, source_target_pairs={{0,24},{1,25},{2,26},{3,27},{4,28},{5,29},{6,30},{7,31},{8,16},{9,... | collective-permute-start | bytes 98312 | tf_op jit(solution)/shard_map/ppermute | solution.py:35
  7.5 0.6 %collective-permute-start.1 = (bf16[1,128,128]{2,1,0:T(8,128)(2,1)}, bf16[1,128,128]{2,1,0:T(8,128)(2,1)S(1)}, u32[]{:S(2)}, u32[]{:S(2)}) collective-permute-start(bf16[1,128,128]{2,1,0:T(8,128)(2,1)} %bitcast.11), channel_id=1, source_target_pairs={{0,16},{1,9},{2,18},{3,11},{4,20},{5,13},{6,22},{7,15},{8,24},{9,1... | collective-permute-start | bytes 98312 | tf_op jit(solution)/shard_map/ppermute | solution.py:35
  8.1 0.1 slice_reduce_fusion
  8.3 0.2 pad_maximum_fusion.cols_a_ref
  8.6 0.1 fusion.2
  8.8 0.7 %gather_fusion = s32[9]{0:T(128)S(1)} fusion(s32[16]{0:T(128)S(1)} %and_select_fusion, s32[1024]{0:T(1024)S(1)} %pad_clamp_fusion.3), kind=kCustom, calls=%fused_computation.2 | custom fusion | bytes 108 | tf_op jit(solution)/shard_map/gather | solution.py:80
  9.5 0.7 %gather_fusion.1 = s32[9]{0:T(128)S(1)} fusion(s32[16]{0:T(128)S(1)} %and_select_fusion, s32[1024]{0:T(1024)S(1)} %pad_clamp_fusion.1), kind=kCustom, calls=%fused_computation.3 | custom fusion | bytes 108 | tf_op jit(solution)/shard_map/gather | solution.py:80
  10.2 2.3 %collective-permute-done.1 = bf16[1,128,128]{2,1,0:T(8,128)(2,1)S(1)} collective-permute-done((bf16[1,128,128]{2,1,0:T(8,128)(2,1)}, bf16[1,128,128]{2,1,0:T(8,128)(2,1)S(1)}, u32[]{:S(2)}, u32[]{:S(2)}) %collective-permute-start.1) | collective-permute-done | bytes 32800 | tf_op jit(solution)/shard_map/ppermute | solution.py:35
  12.6 1.6 %collective-permute-start.4 = (bf16[4,128,128]{2,1,0:T(8,128)(2,1)S(1)}, bf16[4,128,128]{2,1,0:T(8,128)(2,1)S(1)}, u32[]{:S(2)}, u32[]{:S(2)}) collective-permute-start(bf16[4,128,128]{2,1,0:T(8,128)(2,1)S(1)} %constant_dynamic-update-slice_fusion.3), channel_id=1, source_target_pairs={{0,4},{1,3},{2,6},{3,1},{4,0},{5,7},{6,2},{7,5},{8,12},{9,11},{10,... | collective-permute-start | bytes 393224 | tf_op jit(solution)/shard_map/ppermute | solution.py:35
  14.2 1.6 %collective-permute-start.5 = (bf16[4,128,128]{2,1,0:T(8,128)(2,1)S(1)}, bf16[4,128,128]{2,1,0:T(8,128)(2,1)S(1)}, u32[]{:S(2)}, u32[]{:S(2)}) collective-permute-start(bf16[4,128,128]{2,1,0:T(8,128)(2,1)S(1)} %constant_dynamic-update-slice_fusion.3), channel_id=1, source_target_pairs={{0,2},{1,5},{2,0},{3,7},{4,6},{5,1},{6,4},{7,3},{8,10},{9,13},{10,... | collective-permute-start | bytes 393224 | tf_op jit(solution)/shard_map/ppermute | solution.py:35
  15.7 0.5 %collective-permute-start.6 = (bf16[4,128,128]{2,1,0:T(8,128)(2,1)S(1)}, bf16[4,128,128]{2,1,0:T(8,128)(2,1)S(1)}, u32[]{:S(2)}, u32[]{:S(2)}) collective-permute-start(bf16[4,128,128]{2,1,0:T(8,128)(2,1)S(1)} %constant_dynamic-update-slice_fusion.3), channel_id=1, source_target_pairs={{0,6},{1,7},{2,4},{3,5},{4,2},{5,3},{6,0},{7,1},{8,14},{9,15},{10,... | collective-permute-start | bytes 393224 | tf_op jit(solution)/shard_map/ppermute | solution.py:35
  16.2 0.1 dynamic_update_slice.28
  16.3 2.7 %collective-permute-done.4 = bf16[4,128,128]{2,1,0:T(8,128)(2,1)S(1)} collective-permute-done((bf16[4,128,128]{2,1,0:T(8,128)(2,1)S(1)}, bf16[4,128,128]{2,1,0:T(8,128)(2,1)S(1)}, u32[]{:S(2)}, u32[]{:S(2)}) %collective-permute-start.4) | collective-permute-done | bytes 131104 | tf_op jit(solution)/shard_map/ppermute | solution.py:35
  19.0 0.2 collective-permute-done.5
  19.2 2.4 %collective-permute-done.6 = bf16[4,128,128]{2,1,0:T(8,128)(2,1)S(1)} collective-permute-done((bf16[4,128,128]{2,1,0:T(8,128)(2,1)S(1)}, bf16[4,128,128]{2,1,0:T(8,128)(2,1)S(1)}, u32[]{:S(2)}, u32[]{:S(2)}) %collective-permute-start.6) | collective-permute-done | bytes 131104 | tf_op jit(solution)/shard_map/ppermute | solution.py:35
  21.6 0.6 %gather_fusion.3 = bf16[9,128,128]{2,1,0:T(8,128)(2,1)S(1)} fusion(bf16[16,128,128]{2,1,0:T(8,128)(2,1)S(1)} %constant_dynamic-update-slice_fusion, s32[1024]{0:T(1024)S(1)} %pad_clamp_fusion), kind=kCustom, calls=%fused_computation.1.clone | custom fusion | bytes 589860 | tf_op jit(solution)/shard_map/jit(_take)/gather | solution.py:81
  22.2 0.1 broadcast_select_fusion
  22.4 0.6 %gather_fusion.2 = bf16[9,128,128]{2,1,0:T(8,128)(2,1)S(1)} fusion(bf16[16,128,128]{2,1,0:T(8,128)(2,1)S(1)} %constant_dynamic-update-slice_fusion, s32[1024]{0:T(1024)S(1)} %pad_clamp_fusion.2), kind=kCustom, calls=%fused_computation.clone | custom fusion | bytes 589860 | tf_op jit(solution)/shard_map/jit(_take)/gather | solution.py:81
  23.0 0.8 %broadcast_select_fusion.1.pieces_a_ref = bf16[9,128,128]{2,1,0:T(8,128)(2,1)} fusion(bf16[9,128,128]{2,1,0:T(8,128)(2,1)S(1)} %gather_fusion.2, pred[9]{0:T(512)(128)(4,1)S(1)} %get-tuple-element.22), kind=kLoop, calls=%fused_computation.5 | loop fusion | flops 147456 | bytes 589833 | tf_op jit(solution)/shard_map/jit(_take)/select_n | solution.py:81
  23.8 0.1 collective-permute-done.7.pieces_b_ref
  24.0 0.6 %copy-done.2 = bf16[1040,128]{1,0:T(8,128)(2,1)} copy-done((bf16[1040,128]{1,0:T(8,128)(2,1)}, bf16[1040,128]{1,0:T(8,128)(2,1)S(1)}, u32[]{:S(2)}) %copy-start.2) | copy-done | bytes 266264
  24.5 0.7 %copy-done.1 = bf16[9,128,128]{2,1,0:T(8,128)(2,1)} copy-done((bf16[9,128,128]{2,1,0:T(8,128)(2,1)}, bf16[9,128,128]{2,1,0:T(8,128)(2,1)S(1)}, u32[]{:S(2)}) %copy-start.1) | copy-done | bytes 294936
  25.2 4.8 %shard_map.47 = bf16[1024,1024]{1,0:T(8,128)(2,1)} custom-call(bf16[1024,1024]{1,0:T(8,128)(2,1)} %matrix_ref.1, bf16[1040,128]{1,0:T(8,128)(2,1)} %copy-done, bf16[1040,128]{1,0:T(8,128)(2,1)} %copy-done.2, bf16[9,128,128]{2,1,0:T(8,128)(2,1)} %broadcast_select_fusion.1.pieces_a_ref, bf16[9,128,128]{2,1,0:T(8,128)(2,1)} %copy-done.1, ...), custom_call_target="tpu_custom_call" | custom-call | flops 637534208 | bytes 4194304 | tf_op jit(solution)/shard_map/pallas_call | solution.py:242
  (36 shorter events, 0.4 us)
Async XLA Ops:
  0.0 8.1 %copy-start.4 = (s32[4,8]{1,0:T(4,128)S(1)}, s32[4,8]{1,0:T(4,128)}, u32[]{:S(2)}) copy-start(s32[4,8]{1,0:T(4,128)} %mask_ref.3) | copy-start | bytes 388
  0.0 8.2 %slice-start = ((bf16[1024,1024]{1,0:T(8,128)(2,1)}), bf16[1024,128]{1,0:T(8,128)(2,1)S(1)}, s32[]{:S(2)}) async-start(bf16[1024,1024]{1,0:T(8,128)(2,1)} %matrix_ref.1), calls=%async_computation | async-start | bytes 524288 | tf_op jit(solution)/shard_map/slice | solution.py:140
  0.0 8.6 %copy-start.5 = (s32[16]{0:T(128)S(1)}, s32[16]{0:T(128)}, u32[]{:S(2)}) copy-start(s32[16]{0:T(128)} %col_rows_ref.1) | copy-start | bytes 196
  2.3 7.8 %copy-start.3 = (bf16[128,128]{1,0:T(8,128)(2,1)S(1)}, bf16[128,128]{1,0:T(8,128)(2,1)}, u32[]{:S(2)}) copy-start(bf16[128,128]{1,0:T(8,128)(2,1)} %shard_map.46) | copy-start | bytes 98308
  2.4 10.2 %collective-permute-start.3 = (bf16[1,128,128]{2,1,0:T(8,128)(2,1)}, bf16[1,128,128]{2,1,0:T(8,128)(2,1)S(1)}, u32[]{:S(2)}, u32[]{:S(2)}) collective-permute-start(bf16[1,128,128]{2,1,0:T(8,128)(2,1)} %bitcast.9), channel_id=1, source_target_pairs={{0,24},{1,25},{2,26},{3,27},{4,28},{5,29},{6,30},{7,31},{8,16},{9,... | collective-permute-start | bytes 98312 | tf_op jit(solution)/shard_map/ppermute | solution.py:35
  7.5 5.0 %collective-permute-start.2 = (bf16[1,128,128]{2,1,0:T(8,128)(2,1)}, bf16[1,128,128]{2,1,0:T(8,128)(2,1)S(1)}, u32[]{:S(2)}, u32[]{:S(2)}) collective-permute-start(bf16[1,128,128]{2,1,0:T(8,128)(2,1)} %bitcast.10), channel_id=1, source_target_pairs={{0,8},{1,17},{2,10},{3,19},{4,12},{5,21},{6,14},{7,23},{8,0},{9,25... | collective-permute-start | bytes 98312 | tf_op jit(solution)/shard_map/ppermute | solution.py:35
  7.5 5.0 %collective-permute-start.1 = (bf16[1,128,128]{2,1,0:T(8,128)(2,1)}, bf16[1,128,128]{2,1,0:T(8,128)(2,1)S(1)}, u32[]{:S(2)}, u32[]{:S(2)}) collective-permute-start(bf16[1,128,128]{2,1,0:T(8,128)(2,1)} %bitcast.11), channel_id=1, source_target_pairs={{0,16},{1,9},{2,18},{3,11},{4,20},{5,13},{6,22},{7,15},{8,24},{9,1... | collective-permute-start | bytes 98312 | tf_op jit(solution)/shard_map/ppermute | solution.py:35
  8.5 14.6 %copy-start = (bf16[1040,128]{1,0:T(8,128)(2,1)}, bf16[1040,128]{1,0:T(8,128)(2,1)S(1)}, u32[]{:S(2)}) copy-start(bf16[1040,128]{1,0:T(8,128)(2,1)S(1)} %pad_maximum_fusion.cols_a_ref) | copy-start | bytes 798724
  8.5 15.4 %collective-permute-start = (bf16[1040,128]{1,0:T(8,128)(2,1)S(1)}, bf16[1040,128]{1,0:T(8,128)(2,1)S(1)}, u32[]{:S(2)}, u32[]{:S(2)}) collective-permute-start(bf16[1040,128]{1,0:T(8,128)(2,1)S(1)} %pad_maximum_fusion.cols_a_ref), channel_id=1, source_target_pairs={{0,1},{1,0},{2,3},{3,2},{4,5},{5,4},{6,7},{7,6},{8,9},{9,8},{10,11... | collective-permute-start | bytes 798728 | tf_op jit(solution)/shard_map/ppermute | solution.py:87
  12.6 6.5 %collective-permute-start.4 = (bf16[4,128,128]{2,1,0:T(8,128)(2,1)S(1)}, bf16[4,128,128]{2,1,0:T(8,128)(2,1)S(1)}, u32[]{:S(2)}, u32[]{:S(2)}) collective-permute-start(bf16[4,128,128]{2,1,0:T(8,128)(2,1)S(1)} %constant_dynamic-update-slice_fusion.3), channel_id=1, source_target_pairs={{0,4},{1,3},{2,6},{3,1},{4,0},{5,7},{6,2},{7,5},{8,12},{9,11},{10,... | collective-permute-start | bytes 393224 | tf_op jit(solution)/shard_map/ppermute | solution.py:35
  14.2 5.0 %collective-permute-start.5 = (bf16[4,128,128]{2,1,0:T(8,128)(2,1)S(1)}, bf16[4,128,128]{2,1,0:T(8,128)(2,1)S(1)}, u32[]{:S(2)}, u32[]{:S(2)}) collective-permute-start(bf16[4,128,128]{2,1,0:T(8,128)(2,1)S(1)} %constant_dynamic-update-slice_fusion.3), channel_id=1, source_target_pairs={{0,2},{1,5},{2,0},{3,7},{4,6},{5,1},{6,4},{7,3},{8,10},{9,13},{10,... | collective-permute-start | bytes 393224 | tf_op jit(solution)/shard_map/ppermute | solution.py:35
  15.7 5.9 %collective-permute-start.6 = (bf16[4,128,128]{2,1,0:T(8,128)(2,1)S(1)}, bf16[4,128,128]{2,1,0:T(8,128)(2,1)S(1)}, u32[]{:S(2)}, u32[]{:S(2)}) collective-permute-start(bf16[4,128,128]{2,1,0:T(8,128)(2,1)S(1)} %constant_dynamic-update-slice_fusion.3), channel_id=1, source_target_pairs={{0,6},{1,7},{2,4},{3,5},{4,2},{5,3},{6,0},{7,1},{8,14},{9,15},{10,... | collective-permute-start | bytes 393224 | tf_op jit(solution)/shard_map/ppermute | solution.py:35
  22.3 1.6 %collective-permute-start.7 = (bf16[9,128,128]{2,1,0:T(8,128)(2,1)S(1)}, bf16[9,128,128]{2,1,0:T(8,128)(2,1)S(1)}, u32[]{:S(2)}, u32[]{:S(2)}) collective-permute-start(bf16[9,128,128]{2,1,0:T(8,128)(2,1)S(1)} %broadcast_select_fusion), channel_id=1, source_target_pairs={{0,1},{1,0},{2,3},{3,2},{4,5},{5,4},{6,7},{7,6},{8,9},{9,8},{10,11... | collective-permute-start | bytes 884744 | tf_op jit(solution)/shard_map/ppermute | solution.py:90
  23.8 0.7 %copy-start.2 = (bf16[1040,128]{1,0:T(8,128)(2,1)}, bf16[1040,128]{1,0:T(8,128)(2,1)S(1)}, u32[]{:S(2)}) copy-start(bf16[1040,128]{1,0:T(8,128)(2,1)S(1)} %collective-permute-done.cols_b_ref) | copy-start | bytes 798724
  24.5 0.7 %copy-start.1 = (bf16[9,128,128]{2,1,0:T(8,128)(2,1)}, bf16[9,128,128]{2,1,0:T(8,128)(2,1)S(1)}, u32[]{:S(2)}) copy-start(bf16[9,128,128]{2,1,0:T(8,128)(2,1)S(1)} %collective-permute-done.7.pieces_b_ref) | copy-start | bytes 884740
